TPU v7x, 32 devices: a whole 2x2x4 slice. The times are simulated.
32 devices in a mesh: groups: 2 (over x), ctx: 8 (over z, y), heads: 2 (over core).
Axes of the slice: x: 2, y: 2, z: 4, core: 2. Of those that a mesh axis runs over, the one named last changes fastest.
Arguments:
- query_vectors: bfloat16 [2048, 16, 128], P(('groups', 'ctx'), 'heads'), parts along dimension 0, may hold values from -5.5 to 5.5
- key_vectors: bfloat16 [2048, 4, 128], P(('groups', 'ctx'), 'heads'), parts along dimension 0, may hold values from -5.5 to 5.5
- value_rows: bfloat16 [2048, 4, 128], P(('groups', 'ctx'), 'heads'), parts along dimension 0, may hold values from -6 to 6
- forward_out: bfloat16 [2048, 16, 128], P(('groups', 'ctx'), 'heads'), parts along dimension 0, may hold values from -3 to 3
- out_grad: bfloat16 [2048, 16, 128], P(('groups', 'ctx'), 'heads'), parts along dimension 0, may hold values from -24 to 24
- block_offsets: int32 [16], P(('groups', 'ctx')), parts along dimension 0, may hold values from 0 to 7, each once
Outputs:
- query_grad: float32 [2048, 16, 128], P(('groups', 'ctx'), 'heads'), parts along dimension 0
- key_gradient_array: float32 [2048, 4, 128], P(('groups', 'ctx'), 'heads'), parts along dimension 0
- value_gradient_array: float32 [2048, 4, 128], P(('groups', 'ctx'), 'heads'), parts along dimension 0
There are 2 independent parts, one for each index of `groups`. A program takes and returns all parts, laid end to end along the dimension named above; each array names one. Nothing has to cross between parts.
Inputs may be any that keep to these rules, and one draw needn't show every extreme that they name: block_offsets is a permutation of 0 to 7.
All inputs are finite; a program needn't handle non-finite values.
Results may differ from a plain program's by a relative error of at most 0.0029.
Values may be sent and summed in bfloat16 or wider, within the bound.
No kernel may reach another device: no remote copies, remote signals or barrier semaphores. Data moves between devices by JAX's collectives and lax.ppermute only.
A program may use at most 64 MiB of HBM per device.

v0:
```python
import jax
import jax.numpy as jnp
from jax import lax
from jax.sharding import PartitionSpec as P


def passed_along(value, axis, by):
    peers = lax.axis_size(axis)
    return lax.ppermute(value, axis, [(i, (i + by) % peers) for i in range(peers)])


def on_device(query_vectors, key_vectors, value_rows, forward_out, out_grad, block_offsets):
    tok_rows, q_heads, head_width = query_vectors.shape
    kv_heads = key_vectors.shape[1]
    heads_per_group = q_heads // kv_heads
    cycle_size = lax.axis_size("ctx")
    cycle_index = lax.axis_index("ctx")
    block_starts = lax.all_gather(block_offsets, "ctx", axis=0, tiled=True)
    score_scale = head_width ** (-0.5)
    row_index = jnp.arange(tok_rows, dtype=jnp.int32)
    own_positions = block_offsets[0] * tok_rows + row_index
    grouped_query = query_vectors.reshape(tok_rows, kv_heads, heads_per_group, head_width)
    grouped_grad = out_grad.reshape(tok_rows, kv_heads, heads_per_group, head_width)
    row_delta = jnp.sum(out_grad.astype(jnp.float32) * forward_out.astype(jnp.float32), axis=2)
    row_delta = row_delta.reshape(tok_rows, kv_heads, heads_per_group).transpose(1, 2, 0)

    def masked_scores(key_block, source_block):
        key_positions = block_starts[source_block] * tok_rows + row_index
        visible = key_positions[None, :] <= own_positions[:, None]
        scores = (
            jnp.einsum(
                "ighd,jgd->ghij", grouped_query, key_block, preferred_element_type=jnp.float32
            )
            * score_scale
        )
        return (jnp.where(visible, scores, -1e30), visible)

    def stats_update(running, key_block, source_block):
        run_max, run_total = running
        scores, visible = masked_scores(key_block, source_block)
        new_max = jnp.maximum(run_max, jnp.max(scores, axis=3))
        new_total = run_total * jnp.exp(run_max - new_max) + jnp.sum(
            jnp.exp(scores - new_max[..., None]), axis=3
        )
        return (new_max, new_total)

    def stats_step(running, key_block, source_block):
        return stats_update(running, key_block, source_block)

    head_shape = (kv_heads, heads_per_group, tok_rows)
    running = (jnp.full(head_shape, -1e30, jnp.float32), jnp.zeros(head_shape, jnp.float32))
    pair_shape = (2, tok_rows, kv_heads, head_width)
    zero_pair = jnp.zeros(pair_shape, jnp.float32)
    query_grad = jnp.zeros((tok_rows, kv_heads, heads_per_group, head_width), jnp.float32)

    def grad_update(grad_state, key_block, value_block, source_block, log_total):
        query_grad, grad_pair = grad_state
        scores, visible = masked_scores(key_block, source_block)
        probs = jnp.where(visible, jnp.exp(scores - log_total[..., None]), 0.0)
        probs_low = probs.astype(jnp.bfloat16)
        prob_grad = jnp.einsum(
            "ighd,jgd->ghij", grouped_grad, value_block, preferred_element_type=jnp.float32
        )
        score_grad = (probs * (prob_grad - row_delta[..., None])).astype(jnp.bfloat16)
        query_grad = query_grad + score_scale * jnp.einsum(
            "ghij,jgd->ighd", score_grad, key_block, preferred_element_type=jnp.float32
        )
        key_part = score_scale * jnp.einsum(
            "ghij,ighd->jgd", score_grad, grouped_query, preferred_element_type=jnp.float32
        )
        value_part = jnp.einsum(
            "ghij,ighd->jgd", probs_low, grouped_grad, preferred_element_type=jnp.float32
        )
        return (query_grad, grad_pair + jnp.stack([key_part, value_part]))

    def grad_step(grad_state, key_block, value_block, source_block, log_total):
        return grad_update(grad_state, key_block, value_block, source_block, log_total)

    running = stats_step(running, key_vectors, cycle_index)

    def stats_loop(cycle_step, loop_carry):
        running, key_block = loop_carry
        key_block = passed_along(key_block, "ctx", 1)
        source_block = (cycle_index - cycle_step) % cycle_size
        running = stats_step(running, key_block, source_block)
        return (running, key_block)

    running, unused_block = lax.fori_loop(1, cycle_size, stats_loop, (running, key_vectors))
    log_total = running[0] + jnp.log(running[1])
    travelling = jnp.stack([key_vectors, value_rows])
    grad_pair = zero_pair

    def cycle_update(query_grad, grad_pair, travelling, source_block):
        key_block, value_block = (travelling[0], travelling[1])
        return grad_step((query_grad, grad_pair), key_block, value_block, source_block, log_total)

    query_grad, grad_pair = cycle_update(query_grad, grad_pair, travelling, cycle_index)

    def back_loop(cycle_step, loop_carry):
        query_grad, grad_pair, travelling = loop_carry
        travelling = passed_along(travelling, "ctx", 1)
        grad_pair = passed_along(grad_pair, "ctx", 1)
        source_block = (cycle_index - cycle_step) % cycle_size
        query_grad, grad_pair = cycle_update(query_grad, grad_pair, travelling, source_block)
        return (query_grad, grad_pair, travelling)

    query_grad, grad_pair, travelling = lax.fori_loop(
        1, cycle_size, back_loop, (query_grad, grad_pair, travelling)
    )
    grad_pair = passed_along(grad_pair, "ctx", 1)
    return (query_grad.reshape(tok_rows, q_heads, head_width), grad_pair[0], grad_pair[1])


def solution(mesh):
    in_specs = (
        P(("groups", "ctx"), "heads", None),
        P(("groups", "ctx"), "heads", None),
        P(("groups", "ctx"), "heads", None),
        P(("groups", "ctx"), "heads", None),
        P(("groups", "ctx"), "heads", None),
        P(("groups", "ctx")),
    )
    out_specs = (
        P(("groups", "ctx"), "heads", None),
        P(("groups", "ctx"), "heads", None),
        P(("groups", "ctx"), "heads", None),
    )
    return jax.shard_map(
        on_device, mesh=mesh, in_specs=in_specs, out_specs=out_specs, check_vma=False
    )
```

profile of v0, /device:TPU:0, one launch (start us, length us, event | category | flops | bytes accessed | tf_op | source)
XLA Modules:
  0.0 167.6 jit_solution(2116778922920582532)
XLA Ops:
  1.9 0.8 dynamic-update-slice
  2.7 13.1 %all-reduce = s32[8]{0:T(128)S(1)} all-reduce(s32[8]{0:T(128)S(1)} %dynamic-update-slice), channel_id=1, replica_groups=mesh['groups'=2,'ctx'=8,'heads'=2] {'ctx'}, use_global_device_ids=true, to_apply=%add | all-reduce | flops 8 | bytes 64
  17.0 0.9 copy.77
  17.9 0.6 copy-done.1
  18.5 0.9 copy-done.6
  19.7 0.8 copy-done.5
  20.7 0.7 copy-done.4
  21.8 0.7 copy-done.3
  22.5 53.4 %while.40 = (s32[]{:T(128)}, f32[2,4,128]{2,1,0:T(4,128)S(1)}, f32[2,4,128]{2,1,0:T(4,128)S(1)}, bf16[128,2,128]{2,0,1:T(8,128)(2,1)S(1)}, s32[]{:T(128)}, /*ind...) while((s32[]{:T(128)}, f32[2,4,128]{2,1,0:T(4,128)S(1)}, ...), condition=%wide.region_5.6_spmd.clone, body=%wide.region_2.5_spmd.clone.sunk | while | flops 34228496 | bytes 1857888 | solution.py:88
  22.5 1.5 collective-permute-start
  24.0 0.6 dynamic_slice.29
  25.3 4.1 %collective-permute-done = bf16[128,2,128]{2,0,1:T(8,128)(2,1)S(1)} collective-permute-done((bf16[128,2,128]{2,0,1:T(8,128)(2,1)S(1)}, bf16[128,2,128]{2,0,1:T(8,128)(2,1)S(1)}, u32[]{:S(2)}, u32[]{:S(2)}) %collective-permute-start) | collective-permute-done | bytes 65568 | tf_op jit(solution)/shard_map/while/body/eval_jaxpr/ppermute | solution.py:9
  29.9 0.6 dynamic_slice.29
  31.3 5.6 %collective-permute-done = bf16[128,2,128]{2,0,1:T(8,128)(2,1)S(1)} collective-permute-done((bf16[128,2,128]{2,0,1:T(8,128)(2,1)S(1)}, bf16[128,2,128]{2,0,1:T(8,128)(2,1)S(1)}, u32[]{:S(2)}, u32[]{:S(2)}) %collective-permute-start) | collective-permute-done | bytes 65568 | tf_op jit(solution)/shard_map/while/body/eval_jaxpr/ppermute | solution.py:9
  37.4 0.6 dynamic_slice.29
  38.7 6.3 %collective-permute-done = bf16[128,2,128]{2,0,1:T(8,128)(2,1)S(1)} collective-permute-done((bf16[128,2,128]{2,0,1:T(8,128)(2,1)S(1)}, bf16[128,2,128]{2,0,1:T(8,128)(2,1)S(1)}, u32[]{:S(2)}, u32[]{:S(2)}) %collective-permute-start) | collective-permute-done | bytes 65568 | tf_op jit(solution)/shard_map/while/body/eval_jaxpr/ppermute | solution.py:9
  45.4 0.6 dynamic_slice.29
  46.8 5.6 %collective-permute-done = bf16[128,2,128]{2,0,1:T(8,128)(2,1)S(1)} collective-permute-done((bf16[128,2,128]{2,0,1:T(8,128)(2,1)S(1)}, bf16[128,2,128]{2,0,1:T(8,128)(2,1)S(1)}, u32[]{:S(2)}, u32[]{:S(2)}) %collective-permute-start) | collective-permute-done | bytes 65568 | tf_op jit(solution)/shard_map/while/body/eval_jaxpr/ppermute | solution.py:9
  52.9 0.6 dynamic_slice.29
  54.2 5.6 %collective-permute-done = bf16[128,2,128]{2,0,1:T(8,128)(2,1)S(1)} collective-permute-done((bf16[128,2,128]{2,0,1:T(8,128)(2,1)S(1)}, bf16[128,2,128]{2,0,1:T(8,128)(2,1)S(1)}, u32[]{:S(2)}, u32[]{:S(2)}) %collective-permute-start) | collective-permute-done | bytes 65568 | tf_op jit(solution)/shard_map/while/body/eval_jaxpr/ppermute | solution.py:9
  60.3 0.6 dynamic_slice.29
  61.6 5.6 %collective-permute-done = bf16[128,2,128]{2,0,1:T(8,128)(2,1)S(1)} collective-permute-done((bf16[128,2,128]{2,0,1:T(8,128)(2,1)S(1)}, bf16[128,2,128]{2,0,1:T(8,128)(2,1)S(1)}, u32[]{:S(2)}, u32[]{:S(2)}) %collective-permute-start) | collective-permute-done | bytes 65568 | tf_op jit(solution)/shard_map/while/body/eval_jaxpr/ppermute | solution.py:9
  67.7 0.6 dynamic_slice.29
  69.1 6.4 %collective-permute-done = bf16[128,2,128]{2,0,1:T(8,128)(2,1)S(1)} collective-permute-done((bf16[128,2,128]{2,0,1:T(8,128)(2,1)S(1)}, bf16[128,2,128]{2,0,1:T(8,128)(2,1)S(1)}, u32[]{:S(2)}, u32[]{:S(2)}) %collective-permute-start) | collective-permute-done | bytes 65568 | tf_op jit(solution)/shard_map/while/body/eval_jaxpr/ppermute | solution.py:9
  77.4 80.1 %while.41 = (s32[]{:T(128)}, f32[128,2,4,128]{3,0,2,1:T(8,128)S(1)}, f32[2,128,2,128]{3,1,2,0:T(8,128)S(1)}, bf16[2,128,2,128]{3,1,2,0:T(8,128)(2,1)S(1)}, s32[]...) while((s32[]{:T(128)}, ...), condition=%wide.region_8.9_spmd.clone, body=%wide.region_7.8_spmd.clone.sunk | while | flops 169263376 | bytes 7580064 | solution.py:107
  77.6 0.6 dynamic_slice.30
  79.0 7.7 %collective-permute-done.1 = bf16[2,128,2,128]{3,1,2,0:T(8,128)(2,1)S(1)} collective-permute-done((bf16[2,128,2,128]{3,1,2,0:T(8,128)(2,1)S(1)}, bf16[2,128,2,128]{3,1,2,0:T(8,128)(2,1)S(1)}, u32[]{:S(2)}, u32[]{:S(2)}) %collective-permute-start.1) | collective-permute-done | bytes 131104 | tf_op jit(solution)/shard_map/while/body/eval_jaxpr/ppermute | solution.py:9
  87.9 1.8 %collective-permute-done.2 = f32[2,128,2,128]{3,1,2,0:T(8,128)S(1)} collective-permute-done((f32[2,128,2,128]{3,1,2,0:T(8,128)S(1)}, f32[2,128,2,128]{3,1,2,0:T(8,128)S(1)}, u32[]{:S(2)}, u32[]{:S(2)}) %collective-permute-start.2) | collective-permute-done | bytes 262176 | tf_op jit(solution)/shard_map/while/body/eval_jaxpr/ppermute | solution.py:9
  90.0 0.6 dynamic_slice.30
  91.3 7.1 %collective-permute-done.1 = bf16[2,128,2,128]{3,1,2,0:T(8,128)(2,1)S(1)} collective-permute-done((bf16[2,128,2,128]{3,1,2,0:T(8,128)(2,1)S(1)}, bf16[2,128,2,128]{3,1,2,0:T(8,128)(2,1)S(1)}, u32[]{:S(2)}, u32[]{:S(2)}) %collective-permute-start.1) | collective-permute-done | bytes 131104 | tf_op jit(solution)/shard_map/while/body/eval_jaxpr/ppermute | solution.py:9
  99.7 1.5 collective-permute-done.2
  101.4 0.6 dynamic_slice.30
  102.8 6.2 %collective-permute-done.1 = bf16[2,128,2,128]{3,1,2,0:T(8,128)(2,1)S(1)} collective-permute-done((bf16[2,128,2,128]{3,1,2,0:T(8,128)(2,1)S(1)}, bf16[2,128,2,128]{3,1,2,0:T(8,128)(2,1)S(1)}, u32[]{:S(2)}, u32[]{:S(2)}) %collective-permute-start.1) | collective-permute-done | bytes 131104 | tf_op jit(solution)/shard_map/while/body/eval_jaxpr/ppermute | solution.py:9
  110.3 1.5 collective-permute-done.2
  112.0 0.6 dynamic_slice.30
  113.3 6.2 %collective-permute-done.1 = bf16[2,128,2,128]{3,1,2,0:T(8,128)(2,1)S(1)} collective-permute-done((bf16[2,128,2,128]{3,1,2,0:T(8,128)(2,1)S(1)}, bf16[2,128,2,128]{3,1,2,0:T(8,128)(2,1)S(1)}, u32[]{:S(2)}, u32[]{:S(2)}) %collective-permute-start.1) | collective-permute-done | bytes 131104 | tf_op jit(solution)/shard_map/while/body/eval_jaxpr/ppermute | solution.py:9
  120.9 1.6 collective-permute-done.2
  122.7 0.6 dynamic_slice.30
  124.1 6.2 %collective-permute-done.1 = bf16[2,128,2,128]{3,1,2,0:T(8,128)(2,1)S(1)} collective-permute-done((bf16[2,128,2,128]{3,1,2,0:T(8,128)(2,1)S(1)}, bf16[2,128,2,128]{3,1,2,0:T(8,128)(2,1)S(1)}, u32[]{:S(2)}, u32[]{:S(2)}) %collective-permute-start.1) | collective-permute-done | bytes 131104 | tf_op jit(solution)/shard_map/while/body/eval_jaxpr/ppermute | solution.py:9
  131.6 2.7 %collective-permute-done.2 = f32[2,128,2,128]{3,1,2,0:T(8,128)S(1)} collective-permute-done((f32[2,128,2,128]{3,1,2,0:T(8,128)S(1)}, f32[2,128,2,128]{3,1,2,0:T(8,128)S(1)}, u32[]{:S(2)}, u32[]{:S(2)}) %collective-permute-start.2) | collective-permute-done | bytes 262176 | tf_op jit(solution)/shard_map/while/body/eval_jaxpr/ppermute | solution.py:9
  134.5 0.6 dynamic_slice.30
  135.8 6.2 %collective-permute-done.1 = bf16[2,128,2,128]{3,1,2,0:T(8,128)(2,1)S(1)} collective-permute-done((bf16[2,128,2,128]{3,1,2,0:T(8,128)(2,1)S(1)}, bf16[2,128,2,128]{3,1,2,0:T(8,128)(2,1)S(1)}, u32[]{:S(2)}, u32[]{:S(2)}) %collective-permute-start.1) | collective-permute-done | bytes 131104 | tf_op jit(solution)/shard_map/while/body/eval_jaxpr/ppermute | solution.py:9
  143.4 3.6 %collective-permute-done.2 = f32[2,128,2,128]{3,1,2,0:T(8,128)S(1)} collective-permute-done((f32[2,128,2,128]{3,1,2,0:T(8,128)S(1)}, f32[2,128,2,128]{3,1,2,0:T(8,128)S(1)}, u32[]{:S(2)}, u32[]{:S(2)}) %collective-permute-start.2) | collective-permute-done | bytes 262176 | tf_op jit(solution)/shard_map/while/body/eval_jaxpr/ppermute | solution.py:9
  148.5 6.2 %collective-permute-done.1 = bf16[2,128,2,128]{3,1,2,0:T(8,128)(2,1)S(1)} collective-permute-done((bf16[2,128,2,128]{3,1,2,0:T(8,128)(2,1)S(1)}, bf16[2,128,2,128]{3,1,2,0:T(8,128)(2,1)S(1)}, u32[]{:S(2)}, u32[]{:S(2)}) %collective-permute-start.1) | collective-permute-done | bytes 131104 | tf_op jit(solution)/shard_map/while/body/eval_jaxpr/ppermute | solution.py:9
  156.0 1.5 collective-permute-done.2
  157.8 1.1 copy.45
  159.0 7.9 %collective-permute-done.3 = f32[2,128,2,128]{3,2,1,0:T(2,128)S(1)} collective-permute-done((f32[2,128,2,128]{3,2,1,0:T(2,128)S(1)}, f32[2,128,2,128]{3,2,1,0:T(2,128)S(1)}, u32[]{:S(2)}, u32[]{:S(2)}) %collective-permute-start.3) | collective-permute-done | bytes 262176 | tf_op jit(solution)/shard_map/ppermute | solution.py:9
  166.9 0.7 slice_bitcast_fusion.5
  (183 shorter events, 18.5 us)
Async XLA Ops:
  0.6 0.7 copy-start.8
  0.6 17.8 %copy-start = (bf16[128,8,128]{2,1,0:T(8,128)(2,1)S(1)}, bf16[128,8,128]{2,1,0:T(8,128)(2,1)}, u32[]{:S(2)}) copy-start(bf16[128,8,128]{2,1,0:T(8,128)(2,1)} %param.14) | copy-start | bytes 786436
  17.8 0.6 copy-start.1
  18.5 1.0 copy-start.6
  19.4 1.1 copy-start.7
  19.7 0.8 copy-start.5
  20.5 0.8 copy-start.4
  21.6 0.8 copy-start.3
  22.5 7.0 %collective-permute-start = (bf16[128,2,128]{2,0,1:T(8,128)(2,1)S(1)}, bf16[128,2,128]{2,0,1:T(8,128)(2,1)S(1)}, u32[]{:S(2)}, u32[]{:S(2)}) collective-permute-start(bf16[128,2,128]{2,0,1:T(8,128)(2,1)S(1)} %get-tuple-element.777), channel_id=1, source_target_pairs={{0,2},{2,4},{4,6},{6,8},{8,10},{10,12},{12,14},{14,0},{1,3},{3,5},... | collective-permute-start | bytes 196616 | tf_op jit(solution)/shard_map/while/body/eval_jaxpr/ppermute | solution.py:9
  29.8 7.0 %collective-permute-start = (bf16[128,2,128]{2,0,1:T(8,128)(2,1)S(1)}, bf16[128,2,128]{2,0,1:T(8,128)(2,1)S(1)}, u32[]{:S(2)}, u32[]{:S(2)}) collective-permute-start(bf16[128,2,128]{2,0,1:T(8,128)(2,1)S(1)} %get-tuple-element.777), channel_id=1, source_target_pairs={{0,2},{2,4},{4,6},{6,8},{8,10},{10,12},{12,14},{14,0},{1,3},{3,5},... | collective-permute-start | bytes 196616 | tf_op jit(solution)/shard_map/while/body/eval_jaxpr/ppermute | solution.py:9
  37.3 7.7 %collective-permute-start = (bf16[128,2,128]{2,0,1:T(8,128)(2,1)S(1)}, bf16[128,2,128]{2,0,1:T(8,128)(2,1)S(1)}, u32[]{:S(2)}, u32[]{:S(2)}) collective-permute-start(bf16[128,2,128]{2,0,1:T(8,128)(2,1)S(1)} %get-tuple-element.777), channel_id=1, source_target_pairs={{0,2},{2,4},{4,6},{6,8},{8,10},{10,12},{12,14},{14,0},{1,3},{3,5},... | collective-permute-start | bytes 196616 | tf_op jit(solution)/shard_map/while/body/eval_jaxpr/ppermute | solution.py:9
  45.4 7.0 %collective-permute-start = (bf16[128,2,128]{2,0,1:T(8,128)(2,1)S(1)}, bf16[128,2,128]{2,0,1:T(8,128)(2,1)S(1)}, u32[]{:S(2)}, u32[]{:S(2)}) collective-permute-start(bf16[128,2,128]{2,0,1:T(8,128)(2,1)S(1)} %get-tuple-element.777), channel_id=1, source_target_pairs={{0,2},{2,4},{4,6},{6,8},{8,10},{10,12},{12,14},{14,0},{1,3},{3,5},... | collective-permute-start | bytes 196616 | tf_op jit(solution)/shard_map/while/body/eval_jaxpr/ppermute | solution.py:9
  52.8 7.0 %collective-permute-start = (bf16[128,2,128]{2,0,1:T(8,128)(2,1)S(1)}, bf16[128,2,128]{2,0,1:T(8,128)(2,1)S(1)}, u32[]{:S(2)}, u32[]{:S(2)}) collective-permute-start(bf16[128,2,128]{2,0,1:T(8,128)(2,1)S(1)} %get-tuple-element.777), channel_id=1, source_target_pairs={{0,2},{2,4},{4,6},{6,8},{8,10},{10,12},{12,14},{14,0},{1,3},{3,5},... | collective-permute-start | bytes 196616 | tf_op jit(solution)/shard_map/while/body/eval_jaxpr/ppermute | solution.py:9
  60.2 7.0 %collective-permute-start = (bf16[128,2,128]{2,0,1:T(8,128)(2,1)S(1)}, bf16[128,2,128]{2,0,1:T(8,128)(2,1)S(1)}, u32[]{:S(2)}, u32[]{:S(2)}) collective-permute-start(bf16[128,2,128]{2,0,1:T(8,128)(2,1)S(1)} %get-tuple-element.777), channel_id=1, source_target_pairs={{0,2},{2,4},{4,6},{6,8},{8,10},{10,12},{12,14},{14,0},{1,3},{3,5},... | collective-permute-start | bytes 196616 | tf_op jit(solution)/shard_map/while/body/eval_jaxpr/ppermute | solution.py:9
  67.6 7.8 %collective-permute-start = (bf16[128,2,128]{2,0,1:T(8,128)(2,1)S(1)}, bf16[128,2,128]{2,0,1:T(8,128)(2,1)S(1)}, u32[]{:S(2)}, u32[]{:S(2)}) collective-permute-start(bf16[128,2,128]{2,0,1:T(8,128)(2,1)S(1)} %get-tuple-element.777), channel_id=1, source_target_pairs={{0,2},{2,4},{4,6},{6,8},{8,10},{10,12},{12,14},{14,0},{1,3},{3,5},... | collective-permute-start | bytes 196616 | tf_op jit(solution)/shard_map/while/body/eval_jaxpr/ppermute | solution.py:9
  76.5 0.8 copy-start.2
  77.4 9.2 %collective-permute-start.1 = (bf16[2,128,2,128]{3,1,2,0:T(8,128)(2,1)S(1)}, bf16[2,128,2,128]{3,1,2,0:T(8,128)(2,1)S(1)}, u32[]{:S(2)}, u32[]{:S(2)}) collective-permute-start(bf16[2,128,2,128]{3,1,2,0:T(8,128)(2,1)S(1)} %get-tuple-element.819), channel_id=1, source_target_pairs={{0,2},{2,4},{4,6},{6,8},{8,10},{10,12},{12,14},{14,0},{1,3},{3,5},... | collective-permute-start | bytes 393224 | tf_op jit(solution)/shard_map/while/body/eval_jaxpr/ppermute | solution.py:9
  77.5 12.3 %collective-permute-start.2 = (f32[2,128,2,128]{3,1,2,0:T(8,128)S(1)}, f32[2,128,2,128]{3,1,2,0:T(8,128)S(1)}, u32[]{:S(2)}, u32[]{:S(2)}) collective-permute-start(f32[2,128,2,128]{3,1,2,0:T(8,128)S(1)} %get-tuple-element.818), channel_id=1, source_target_pairs={{0,2},{2,4},{4,6},{6,8},{8,10},{10,12},{12,14},{14,0},{1,3},{3,5},... | collective-permute-start | bytes 786440 | tf_op jit(solution)/shard_map/while/body/eval_jaxpr/ppermute | solution.py:9
  89.8 8.6 %collective-permute-start.1 = (bf16[2,128,2,128]{3,1,2,0:T(8,128)(2,1)S(1)}, bf16[2,128,2,128]{3,1,2,0:T(8,128)(2,1)S(1)}, u32[]{:S(2)}, u32[]{:S(2)}) collective-permute-start(bf16[2,128,2,128]{3,1,2,0:T(8,128)(2,1)S(1)} %get-tuple-element.819), channel_id=1, source_target_pairs={{0,2},{2,4},{4,6},{6,8},{8,10},{10,12},{12,14},{14,0},{1,3},{3,5},... | collective-permute-start | bytes 393224 | tf_op jit(solution)/shard_map/while/body/eval_jaxpr/ppermute | solution.py:9
  89.9 11.3 %collective-permute-start.2 = (f32[2,128,2,128]{3,1,2,0:T(8,128)S(1)}, f32[2,128,2,128]{3,1,2,0:T(8,128)S(1)}, u32[]{:S(2)}, u32[]{:S(2)}) collective-permute-start(f32[2,128,2,128]{3,1,2,0:T(8,128)S(1)} %get-tuple-element.818), channel_id=1, source_target_pairs={{0,2},{2,4},{4,6},{6,8},{8,10},{10,12},{12,14},{14,0},{1,3},{3,5},... | collective-permute-start | bytes 786440 | tf_op jit(solution)/shard_map/while/body/eval_jaxpr/ppermute | solution.py:9
  101.3 7.7 %collective-permute-start.1 = (bf16[2,128,2,128]{3,1,2,0:T(8,128)(2,1)S(1)}, bf16[2,128,2,128]{3,1,2,0:T(8,128)(2,1)S(1)}, u32[]{:S(2)}, u32[]{:S(2)}) collective-permute-start(bf16[2,128,2,128]{3,1,2,0:T(8,128)(2,1)S(1)} %get-tuple-element.819), channel_id=1, source_target_pairs={{0,2},{2,4},{4,6},{6,8},{8,10},{10,12},{12,14},{14,0},{1,3},{3,5},... | collective-permute-start | bytes 393224 | tf_op jit(solution)/shard_map/while/body/eval_jaxpr/ppermute | solution.py:9
  101.3 10.5 %collective-permute-start.2 = (f32[2,128,2,128]{3,1,2,0:T(8,128)S(1)}, f32[2,128,2,128]{3,1,2,0:T(8,128)S(1)}, u32[]{:S(2)}, u32[]{:S(2)}) collective-permute-start(f32[2,128,2,128]{3,1,2,0:T(8,128)S(1)} %get-tuple-element.818), channel_id=1, source_target_pairs={{0,2},{2,4},{4,6},{6,8},{8,10},{10,12},{12,14},{14,0},{1,3},{3,5},... | collective-permute-start | bytes 786440 | tf_op jit(solution)/shard_map/while/body/eval_jaxpr/ppermute | solution.py:9
  111.8 7.7 %collective-permute-start.1 = (bf16[2,128,2,128]{3,1,2,0:T(8,128)(2,1)S(1)}, bf16[2,128,2,128]{3,1,2,0:T(8,128)(2,1)S(1)}, u32[]{:S(2)}, u32[]{:S(2)}) collective-permute-start(bf16[2,128,2,128]{3,1,2,0:T(8,128)(2,1)S(1)} %get-tuple-element.819), channel_id=1, source_target_pairs={{0,2},{2,4},{4,6},{6,8},{8,10},{10,12},{12,14},{14,0},{1,3},{3,5},... | collective-permute-start | bytes 393224 | tf_op jit(solution)/shard_map/while/body/eval_jaxpr/ppermute | solution.py:9
  111.9 10.6 %collective-permute-start.2 = (f32[2,128,2,128]{3,1,2,0:T(8,128)S(1)}, f32[2,128,2,128]{3,1,2,0:T(8,128)S(1)}, u32[]{:S(2)}, u32[]{:S(2)}) collective-permute-start(f32[2,128,2,128]{3,1,2,0:T(8,128)S(1)} %get-tuple-element.818), channel_id=1, source_target_pairs={{0,2},{2,4},{4,6},{6,8},{8,10},{10,12},{12,14},{14,0},{1,3},{3,5},... | collective-permute-start | bytes 786440 | tf_op jit(solution)/shard_map/while/body/eval_jaxpr/ppermute | solution.py:9
  122.5 7.7 %collective-permute-start.1 = (bf16[2,128,2,128]{3,1,2,0:T(8,128)(2,1)S(1)}, bf16[2,128,2,128]{3,1,2,0:T(8,128)(2,1)S(1)}, u32[]{:S(2)}, u32[]{:S(2)}) collective-permute-start(bf16[2,128,2,128]{3,1,2,0:T(8,128)(2,1)S(1)} %get-tuple-element.819), channel_id=1, source_target_pairs={{0,2},{2,4},{4,6},{6,8},{8,10},{10,12},{12,14},{14,0},{1,3},{3,5},... | collective-permute-start | bytes 393224 | tf_op jit(solution)/shard_map/while/body/eval_jaxpr/ppermute | solution.py:9
  122.6 11.7 %collective-permute-start.2 = (f32[2,128,2,128]{3,1,2,0:T(8,128)S(1)}, f32[2,128,2,128]{3,1,2,0:T(8,128)S(1)}, u32[]{:S(2)}, u32[]{:S(2)}) collective-permute-start(f32[2,128,2,128]{3,1,2,0:T(8,128)S(1)} %get-tuple-element.818), channel_id=1, source_target_pairs={{0,2},{2,4},{4,6},{6,8},{8,10},{10,12},{12,14},{14,0},{1,3},{3,5},... | collective-permute-start | bytes 786440 | tf_op jit(solution)/shard_map/while/body/eval_jaxpr/ppermute | solution.py:9
  134.3 7.7 %collective-permute-start.1 = (bf16[2,128,2,128]{3,1,2,0:T(8,128)(2,1)S(1)}, bf16[2,128,2,128]{3,1,2,0:T(8,128)(2,1)S(1)}, u32[]{:S(2)}, u32[]{:S(2)}) collective-permute-start(bf16[2,128,2,128]{3,1,2,0:T(8,128)(2,1)S(1)} %get-tuple-element.819), channel_id=1, source_target_pairs={{0,2},{2,4},{4,6},{6,8},{8,10},{10,12},{12,14},{14,0},{1,3},{3,5},... | collective-permute-start | bytes 393224 | tf_op jit(solution)/shard_map/while/body/eval_jaxpr/ppermute | solution.py:9
  134.4 12.5 %collective-permute-start.2 = (f32[2,128,2,128]{3,1,2,0:T(8,128)S(1)}, f32[2,128,2,128]{3,1,2,0:T(8,128)S(1)}, u32[]{:S(2)}, u32[]{:S(2)}) collective-permute-start(f32[2,128,2,128]{3,1,2,0:T(8,128)S(1)} %get-tuple-element.818), channel_id=1, source_target_pairs={{0,2},{2,4},{4,6},{6,8},{8,10},{10,12},{12,14},{14,0},{1,3},{3,5},... | collective-permute-start | bytes 786440 | tf_op jit(solution)/shard_map/while/body/eval_jaxpr/ppermute | solution.py:9
  147.0 7.7 %collective-permute-start.1 = (bf16[2,128,2,128]{3,1,2,0:T(8,128)(2,1)S(1)}, bf16[2,128,2,128]{3,1,2,0:T(8,128)(2,1)S(1)}, u32[]{:S(2)}, u32[]{:S(2)}) collective-permute-start(bf16[2,128,2,128]{3,1,2,0:T(8,128)(2,1)S(1)} %get-tuple-element.819), channel_id=1, source_target_pairs={{0,2},{2,4},{4,6},{6,8},{8,10},{10,12},{12,14},{14,0},{1,3},{3,5},... | collective-permute-start | bytes 393224 | tf_op jit(solution)/shard_map/while/body/eval_jaxpr/ppermute | solution.py:9
  147.1 10.5 %collective-permute-start.2 = (f32[2,128,2,128]{3,1,2,0:T(8,128)S(1)}, f32[2,128,2,128]{3,1,2,0:T(8,128)S(1)}, u32[]{:S(2)}, u32[]{:S(2)}) collective-permute-start(f32[2,128,2,128]{3,1,2,0:T(8,128)S(1)} %get-tuple-element.818), channel_id=1, source_target_pairs={{0,2},{2,4},{4,6},{6,8},{8,10},{10,12},{12,14},{14,0},{1,3},{3,5},... | collective-permute-start | bytes 786440 | tf_op jit(solution)/shard_map/while/body/eval_jaxpr/ppermute | solution.py:9
  157.8 9.1 %collective-permute-start.3 = (f32[2,128,2,128]{3,2,1,0:T(2,128)S(1)}, f32[2,128,2,128]{3,2,1,0:T(2,128)S(1)}, u32[]{:S(2)}, u32[]{:S(2)}) collective-permute-start(f32[2,128,2,128]{3,2,1,0:T(2,128)S(1)} %copy.46), channel_id=1, source_target_pairs={{0,2},{2,4},{4,6},{6,8},{8,10},{10,12},{12,14},{14,0},{1,3},{3,5},... | collective-permute-start | bytes 786440 | tf_op jit(solution)/shard_map/ppermute | solution.py:9
where the time goes:
time: 168 us
  waiting for transfers between devices  107 us (64%)
  local copies, waits for them, and re-layouts  17.7 us (11%)
  blocking collectives  13.1 us (8%)
  matrix products  11.7 us (7%)
  loops' own time  10.4 us (6%)
  starting transfers between devices  2.75 us (2%)
  other arithmetic  2.71 us (2%)
  between operations  2.19 us (1%)
    ppermute x22, waiting for transfers between devices, passed_along(): lax.ppermute(value, axis, [(i, (i + by) % peers) for i in range(peers)])  107 us
    unnamed x1, blocking collectives  13.1 us
    dynamic_slice x15, local copies, waits for them, and re-layouts, masked_scores(): key_positions = block_starts[source_block] * tok_rows + row_index  8.86 us
    unnamed x24, local copies, waits for them, and re-layouts  5.71 us
    another operation x1, loops' own time, on_device(): lax.fori_loop(1, cycle_size, back_loop, (query_grad, grad_pair, travelling))  5.4 us
    another operation x1, loops' own time, on_device(): lax.fori_loop(1, cycle_size, stats_loop, (running, key_vectors))  4.98 us
    dot_general x15, matrix products, masked_scores(): jnp.einsum('ighd,jgd->ghij', grouped_query, key_block, preferred_element_...  3.92 us
  transfers between devices with their start and end apart: 22, of which 22 were waited for; matrix products, arithmetic and copies ran while one was open for 12% of the time, Pallas kernels for 0%

commit v1 on v0

v1 whole, which is shorter than its diff:
```python
import jax
import jax.numpy as jnp
from jax import lax
from jax.sharding import PartitionSpec as P

OFFSET_ROWS = 16


def on_device(query_vectors, key_vectors, value_rows, forward_out, out_grad, block_offsets):
    tok_rows, q_heads, head_width = query_vectors.shape
    kv_heads = key_vectors.shape[1]
    heads_per_group = q_heads // kv_heads
    cycle_size = lax.axis_size("ctx")
    score_scale = head_width ** (-0.5)
    kv_rows = tok_rows * kv_heads

    offset_rows = jnp.full((OFFSET_ROWS, head_width), block_offsets[0], jnp.float32).astype(jnp.bfloat16)
    slab = jnp.concatenate(
        [
            key_vectors.reshape(kv_rows, head_width),
            value_rows.reshape(kv_rows, head_width),
            offset_rows,
        ],
        axis=0,
    )
    gathered = lax.all_gather(slab, "ctx", axis=0, tiled=False)
    all_keys = gathered[:, :kv_rows].reshape(cycle_size * tok_rows, kv_heads, head_width)
    all_values = gathered[:, kv_rows : 2 * kv_rows].reshape(cycle_size * tok_rows, kv_heads, head_width)
    all_offsets = gathered[:, 2 * kv_rows, 0].astype(jnp.float32).astype(jnp.int32)

    row_index = jnp.arange(tok_rows, dtype=jnp.int32)
    key_positions = (all_offsets[:, None] * tok_rows + row_index[None, :]).reshape(-1)
    own_positions = block_offsets[0] * tok_rows + row_index
    visible = key_positions[None, :] <= own_positions[:, None]

    grouped_query = query_vectors.reshape(tok_rows, kv_heads, heads_per_group, head_width)
    grouped_grad = out_grad.reshape(tok_rows, kv_heads, heads_per_group, head_width)
    row_delta = jnp.sum(out_grad.astype(jnp.float32) * forward_out.astype(jnp.float32), axis=2)
    row_delta = row_delta.reshape(tok_rows, kv_heads, heads_per_group).transpose(1, 2, 0)

    scores = (
        jnp.einsum("tgrd,ugd->grtu", grouped_query, all_keys, preferred_element_type=jnp.float32)
        * score_scale
    )
    scores = jnp.where(visible, scores, -1e30)
    row_max = jnp.max(scores, axis=3, keepdims=True)
    log_total = row_max + jnp.log(jnp.sum(jnp.exp(scores - row_max), axis=3, keepdims=True))
    probs = jnp.where(visible, jnp.exp(scores - log_total), 0.0)
    probs_low = probs.astype(jnp.bfloat16)
    prob_grad = jnp.einsum(
        "tgrd,ugd->grtu", grouped_grad, all_values, preferred_element_type=jnp.float32
    )
    score_grad = (probs * (prob_grad - row_delta[..., None])).astype(jnp.bfloat16)
    query_grad = score_scale * jnp.einsum(
        "grtu,ugd->tgrd", score_grad, all_keys, preferred_element_type=jnp.float32
    )
    key_part = score_scale * jnp.einsum(
        "grtu,tgrd->ugd", score_grad, grouped_query, preferred_element_type=jnp.float32
    )
    value_part = jnp.einsum(
        "grtu,tgrd->ugd", probs_low, grouped_grad, preferred_element_type=jnp.float32
    )
    parts = jnp.concatenate([key_part, value_part], axis=1)
    owned = lax.psum_scatter(parts, "ctx", scatter_dimension=0, tiled=True)
    return (
        query_grad.reshape(tok_rows, q_heads, head_width),
        owned[:, :kv_heads],
        owned[:, kv_heads:],
    )


def solution(mesh):
    in_specs = (
        P(("groups", "ctx"), "heads", None),
        P(("groups", "ctx"), "heads", None),
        P(("groups", "ctx"), "heads", None),
        P(("groups", "ctx"), "heads", None),
        P(("groups", "ctx"), "heads", None),
        P(("groups", "ctx")),
    )
    out_specs = (
        P(("groups", "ctx"), "heads", None),
        P(("groups", "ctx"), "heads", None),
        P(("groups", "ctx"), "heads", None),
    )
    return jax.shard_map(
        on_device, mesh=mesh, in_specs=in_specs, out_specs=out_specs, check_vma=False
    )
```

time: 168 us -> 140 us (0.83)
  blocking collectives: 13.1 us -> 0 us
  between operations: 2.19 us -> 14.8 us
  local copies, waits for them, and re-layouts: 17.7 us -> 5.26 us
  loops' own time: 10.4 us -> 0 us
  matrix products: 11.7 us -> 4.62 us
  other arithmetic: 2.71 us -> 6.51 us
  starting transfers between devices: 2.75 us -> 0.08 us
    ppermute x22 -> x0, waiting for transfers between devices: 107 us -> none  [passed_along(): lax.ppermute(value, axis, [(i, (i + by) % peers) for i in range(peers)])]
    reduce_scatter x0 -> x1, waiting for transfers between devices: none -> 65.6 us  [on_device(): owned = lax.psum_scatter(parts, 'ctx', scatter_dimension=0, tiled=True)]
    all_gather x0 -> x1, waiting for transfers between devices: none -> 42.8 us  [on_device(): gathered = lax.all_gather(slab, 'ctx', axis=0, tiled=False)]
    unnamed x1 -> x0, blocking collectives: 13.1 us -> none
    another operation x2 -> x0, loops' own time: 10.4 us -> none  [the longest x1 5.4 us: on_device(): lax.fori_loop(1, cycle_size, back_loop, (query_grad, grad_pair, travelling))]
    dynamic_slice x15 -> x0, local copies, waits for them, and re-layouts: 8.86 us -> none  [masked_scores(): key_positions = block_starts[source_block] * tok_rows + row_index]
    dot_general x47 -> x5, matrix products: 11.7 us -> 4.62 us  [the longest x1 1.56 us: on_device(): jnp.einsum('tgrd,ugd->grtu', grouped_grad, all_values, preferred_element_...]
    unnamed x24 -> x7, local copies, waits for them, and re-layouts: 5.71 us -> 2.53 us
  transfers between devices with their start and end apart: 22 -> 2, of which waited for: 22 -> 2; matrix products, arithmetic and copies ran while one was open for 12% -> 2% of each run, Pallas kernels for 0% -> 0%
where the time goes in v1:
time: 140 us
  waiting for transfers between devices  108 us (77%)
  between operations  14.8 us (11%)
  other arithmetic  6.51 us (5%)
  local copies, waits for them, and re-layouts  5.26 us (4%)
  matrix products  4.62 us (3%)
    reduce_scatter x1, waiting for transfers between devices, on_device(): owned = lax.psum_scatter(parts, 'ctx', scatter_dimension=0, tiled=True)  65.6 us
    all_gather x1, waiting for transfers between devices, on_device(): gathered = lax.all_gather(slab, 'ctx', axis=0, tiled=False)  42.8 us
  transfers between devices with their start and end apart: 2, of which 2 were waited for; matrix products, arithmetic and copies ran while one was open for 2% of the time, Pallas kernels for 0%

profile of v1, /device:TPU:0, one launch (start us, length us, event | category | flops | bytes accessed | tf_op | source)
XLA Modules:
  0.0 139.8 jit_solution(11926490216184304033)
XLA Ops:
  7.2 0.0 copy-start
  7.2 0.0 all-gather.3.cloned.1.call-start
  7.9 1.7 %maximum_maximum_fusion = bf16[528,128]{1,0:T(8,128)(2,1)} fusion(bf16[256,128]{1,0:T(8,128)(2,1)} %bitcast.71, bf16[256,128]{1,0:T(8,128)(2,1)} %bitcast.72, bf16[528]{0:T(1024)(128)(2,1)S(1)} %pad.4.clone), kind=kLoop, calls=%fused_computation.24 | loop fusion | flops 405504 | bytes 267296 | tf_op jit(solution)/shard_map/concatenate | solution.py:18
  9.6 0.0 all-gather.3.cloned.1.call-update
  9.6 0.0 reduce-scatter.2.cloned.1.call-start
  9.7 1.2 multiply_reduce_fusion
  11.0 42.8 %all-gather.3.cloned.1.call-done = bf16[4224,128]{1,0:T(8,128)(2,1)} async-done(((bf16[528,128]{1,0:T(8,128)(2,1)}), bf16[4224,128]{1,0:T(8,128)(2,1)}) %all-gather.3.cloned.1.call-update) | async-done | bytes 1081360 | tf_op jit(solution)/shard_map/all_gather | solution.py:26
  53.8 1.3 fusion.24
  55.1 1.0 fusion.20
  56.0 0.4 copy.66
  56.5 0.1 add_bitcast_fusion
  56.5 0.2 broadcast_compare_fusion
  56.7 0.0 copy-done
  56.8 0.0 copy-start.1
  56.8 0.9 fusion.3
  57.6 0.9 exponential_reduce_fusion
  58.5 0.0 copy-done.1
  58.5 1.0 fusion.8
  59.6 1.6 %fusion.1 = bf16[2,4,128,1024]{2,3,1,0:T(8,128)(2,1)S(1)} fusion(f32[2,1024,128,4]{2,1,3,0:T(8,128)S(1)} %get-tuple-element.23, f32[2,4,128]{2,1,0:T(4,128)S(1)} %bitcast.75, f32[2,4,128]{2,1,0:T(4,128)S(1)} %bitcast.77, pred[128,1024]{0,1:T(8,128)(4,1)S(1)} %broadcast_compare_fusion, bf16[1024,2,128,1]{2,1,0,3:T(2,128)(2,1)S(1)} %bitcast.68, ...), kind=kOutput, calls=%fused_computation.2 | convolution fusion | flops 275775488 | bytes 7217152 | tf_op jit(solution)/shard_map/tgrd,ugd->grtu/dot_general | solution.py:50
  61.1 0.7 fusion.11
  61.9 1.5 %pad_maximum_fusion = f32[1024,4,128]{2,0,1:T(8,128)} fusion(f32[1024,2,128]{2,0,1:T(8,128)S(1)} %fusion.8, f32[1024,2,128]{2,0,1:T(8,128)S(1)} %fusion.11), kind=kLoop, calls=%fused_computation.8 | loop fusion | flops 524288 | bytes 4194304 | tf_op jit(solution)/shard_map/concatenate | solution.py:63
  63.3 0.0 reduce-scatter.2.cloned.1.call-update
  63.4 0.4 convolution_multiply_fusion
  63.8 1.0 copy.61
  64.8 65.6 %reduce-scatter.2.cloned.1.call-done = f32[128,4,128]{2,0,1:T(8,128)} async-done(((f32[1024,4,128]{2,0,1:T(8,128)}), f32[128,4,128]{2,0,1:T(8,128)}) %reduce-scatter.2.cloned.1.call-update) | async-done | bytes 262160 | tf_op jit(solution)/shard_map/reduce_scatter | solution.py:64
  130.5 1.0 fusion.25
  131.4 0.8 copy.62
  132.2 0.8 copy.63
  (5 shorter events, 0.1 us)
Async XLA Ops:
  7.2 49.6 %copy-start = (bf16[128,8,128]{2,1,0:T(8,128)(2,1)S(1)}, bf16[128,8,128]{2,1,0:T(8,128)(2,1)}, u32[]{:S(2)}) copy-start(bf16[128,8,128]{2,1,0:T(8,128)(2,1)} %param.6) | copy-start | bytes 786436
  7.2 46.6 %all-gather.3.cloned.1.call-start = ((), (), s32[]{:S(2)}) async-start(), calls=%async_computation.2 | async-start | bytes 1216512 | tf_op jit(solution)/shard_map/all_gather | solution.py:26
  9.6 120.8 %reduce-scatter.2.cloned.1.call-start = ((), (), s32[]{:S(2)}) async-start(), calls=%async_computation.1 | async-start | bytes 2359296 | tf_op jit(solution)/shard_map/reduce_scatter | solution.py:64
  56.8 1.8 %copy-start.1 = (bf16[128,8,128]{2,1,0:T(8,128)(2,1)S(1)}, bf16[128,8,128]{2,1,0:T(8,128)(2,1)}, u32[]{:S(2)}) copy-start(bf16[128,8,128]{2,1,0:T(8,128)(2,1)} %param.10) | copy-start | bytes 786436
Sparse Core Ops, SparseCore 0:
  10.8 42.9 all-gather.2
  63.5 66.9 reduce-scatter.1

commit v2 on v1

--- a/solution.py
+++ b/solution.py
@@ -4,6 +4,11 @@
 from jax.sharding import PartitionSpec as P
 
 OFFSET_ROWS = 16
+
+
+def passed_along(value, axis, by):
+    peers = lax.axis_size(axis)
+    return lax.ppermute(value, axis, [(i, (i + by) % peers) for i in range(peers)])
 
 
 def on_device(query_vectors, key_vectors, value_rows, forward_out, out_grad, block_offsets):
@@ -23,7 +28,7 @@
         ],
         axis=0,
     )
-    gathered = lax.all_gather(slab, "ctx", axis=0, tiled=False)
+    gathered = jnp.stack([slab] + [passed_along(slab, "ctx", s) for s in range(1, cycle_size)])
     all_keys = gathered[:, :kv_rows].reshape(cycle_size * tok_rows, kv_heads, head_width)
     all_values = gathered[:, kv_rows : 2 * kv_rows].reshape(cycle_size * tok_rows, kv_heads, head_width)
     all_offsets = gathered[:, 2 * kv_rows, 0].astype(jnp.float32).astype(jnp.int32)
@@ -60,8 +65,12 @@
     value_part = jnp.einsum(
         "grtu,tgrd->ugd", probs_low, grouped_grad, preferred_element_type=jnp.float32
     )
-    parts = jnp.concatenate([key_part, value_part], axis=1)
-    owned = lax.psum_scatter(parts, "ctx", scatter_dimension=0, tiled=True)
+    parts = jnp.concatenate([key_part, value_part], axis=1).reshape(
+        cycle_size, tok_rows, 2 * kv_heads, head_width
+    )
+    owned = parts[0]
+    for s in range(1, cycle_size):
+        owned = owned + passed_along(parts[s], "ctx", -s)
     return (
         query_grad.reshape(tok_rows, q_heads, head_width),
         owned[:, :kv_heads],

time: 140 us -> 88.3 us (0.63)
  the two profiles are of different devices: /device:TPU:0 before, /device:TPU:30 now
where the time goes in v2:
time: 88.3 us; the launch traced here: 88 us
  waiting for transfers between devices  57.1 us (65%)
  starting transfers between devices  13.4 us (15%)
  other arithmetic  7.27 us (8%)
  matrix products  4.63 us (5%)
  local copies, waits for them, and re-layouts  4.01 us (5%)
  between operations  1.54 us (2%)
    ppermute x14, waiting for transfers between devices, passed_along(): lax.ppermute(value, axis, [(i, (i + by) % peers) for i in range(peers)])  57.1 us
    ppermute x14, starting transfers between devices, passed_along(): lax.ppermute(value, axis, [(i, (i + by) % peers) for i in range(peers)])  13.4 us
    unnamed x17, local copies, waits for them, and re-layouts  3.4 us
  transfers between devices with their start and end apart: 14, of which 7 were waited for; matrix products, arithmetic and copies ran while one was open for 4% of the time, Pallas kernels for 0%

profile of v2, /device:TPU:30, one launch (start us, length us, event | category | flops | bytes accessed | tf_op | source)
XLA Modules:
  0.0 88.0 jit_solution(325643415719789707)
XLA Ops:
  0.6 0.0 copy-start
  1.4 1.0 %maximum_maximum_fusion = bf16[528,128]{1,0:T(8,128)(2,1)S(1)} fusion(bf16[256,128]{1,0:T(8,128)(2,1)} %bitcast.84, bf16[256,128]{1,0:T(8,128)(2,1)} %bitcast.86, bf16[528]{0:T(1024)(128)(2,1)S(1)} %pad.4.clone), kind=kLoop, calls=%fused_computation.52 | loop fusion | flops 405504 | bytes 267296 | tf_op jit(solution)/shard_map/concatenate | solution.py:23
  2.4 0.2 collective-permute-start
  2.6 1.6 %collective-permute-start.1 = (bf16[528,128]{1,0:T(8,128)(2,1)S(1)}, bf16[528,128]{1,0:T(8,128)(2,1)S(1)}, u32[]{:S(2)}, u32[]{:S(2)}) collective-permute-start(bf16[528,128]{1,0:T(8,128)(2,1)S(1)} %maximum_maximum_fusion), channel_id=1, source_target_pairs={{0,4},{2,6},{4,8},{6,10},{8,12},{10,14},{12,0},{14,2},{1,5},{3,7},... | collective-permute-start | bytes 405512 | tf_op jit(solution)/shard_map/ppermute | solution.py:11
  4.2 1.6 %collective-permute-start.2 = (bf16[528,128]{1,0:T(8,128)(2,1)S(1)}, bf16[528,128]{1,0:T(8,128)(2,1)S(1)}, u32[]{:S(2)}, u32[]{:S(2)}) collective-permute-start(bf16[528,128]{1,0:T(8,128)(2,1)S(1)} %maximum_maximum_fusion), channel_id=1, source_target_pairs={{0,6},{2,8},{4,10},{6,12},{8,14},{10,0},{12,2},{14,4},{1,7},{3,9},... | collective-permute-start | bytes 405512 | tf_op jit(solution)/shard_map/ppermute | solution.py:11
  5.8 1.2 %collective-permute-start.3 = (bf16[528,128]{1,0:T(8,128)(2,1)S(1)}, bf16[528,128]{1,0:T(8,128)(2,1)S(1)}, u32[]{:S(2)}, u32[]{:S(2)}) collective-permute-start(bf16[528,128]{1,0:T(8,128)(2,1)S(1)} %maximum_maximum_fusion), channel_id=1, source_target_pairs={{0,8},{2,10},{4,12},{6,14},{8,0},{10,2},{12,4},{14,6},{1,9},{3,11}... | collective-permute-start | bytes 405512 | tf_op jit(solution)/shard_map/ppermute | solution.py:11
  7.0 1.7 %collective-permute-start.4 = (bf16[528,128]{1,0:T(8,128)(2,1)S(1)}, bf16[528,128]{1,0:T(8,128)(2,1)S(1)}, u32[]{:S(2)}, u32[]{:S(2)}) collective-permute-start(bf16[528,128]{1,0:T(8,128)(2,1)S(1)} %maximum_maximum_fusion), channel_id=1, source_target_pairs={{0,10},{2,12},{4,14},{6,0},{8,2},{10,4},{12,6},{14,8},{1,11},{3,13... | collective-permute-start | bytes 405512 | tf_op jit(solution)/shard_map/ppermute | solution.py:11
  8.8 1.0 %bitcast_dynamic-update-slice_fusion.7 = bf16[8,528,128]{2,1,0:T(8,128)(2,1)S(1)} fusion(bf16[528]{0:T(1024)(128)(2,1)S(1)} %pad.4.clone, bf16[256,128]{1,0:T(8,128)(2,1)} %bitcast.85, bf16[256,128]{1,0:T(8,128)(2,1)} %bitcast.87), kind=kLoop, calls=%fused_computation.60 | loop fusion | flops 405503 | bytes 267296
  9.8 1.2 %multiply_reduce_fusion = f32[128,8]{1,0:T(8,128)S(1)} fusion(bf16[128,8,128]{2,1,0:T(8,128)(2,1)} %param.9, bf16[128,8,128]{2,1,0:T(8,128)(2,1)} %param.10), kind=kLoop, calls=%fused_computation.30 | loop fusion | flops 523264 | bytes 528384 | tf_op jit(solution)/shard_map/reduce_sum | solution.py:43
  11.1 0.0 collective-permute-done
  11.1 1.4 %collective-permute-start.5 = (bf16[528,128]{1,0:T(8,128)(2,1)S(1)}, bf16[528,128]{1,0:T(8,128)(2,1)S(1)}, u32[]{:S(2)}, u32[]{:S(2)}) collective-permute-start(bf16[528,128]{1,0:T(8,128)(2,1)S(1)} %maximum_maximum_fusion), channel_id=1, source_target_pairs={{0,12},{2,14},{4,0},{6,2},{8,4},{10,6},{12,8},{14,10},{1,13},{3,15... | collective-permute-start | bytes 405512 | tf_op jit(solution)/shard_map/ppermute | solution.py:11
  12.5 0.0 collective-permute-done.1
  12.5 0.6 collective-permute-start.6
  13.1 0.0 collective-permute-done.2
  13.1 14.7 %collective-permute-done.3 = bf16[528,128]{1,0:T(8,128)(2,1)S(1)} collective-permute-done((bf16[528,128]{1,0:T(8,128)(2,1)S(1)}, bf16[528,128]{1,0:T(8,128)(2,1)S(1)}, u32[]{:S(2)}, u32[]{:S(2)}) %collective-permute-start.3) | collective-permute-done | bytes 135200 | tf_op jit(solution)/shard_map/ppermute | solution.py:11
  27.9 1.2 %collective-permute-done.4 = bf16[528,128]{1,0:T(8,128)(2,1)S(1)} collective-permute-done((bf16[528,128]{1,0:T(8,128)(2,1)S(1)}, bf16[528,128]{1,0:T(8,128)(2,1)S(1)}, u32[]{:S(2)}, u32[]{:S(2)}) %collective-permute-start.4) | collective-permute-done | bytes 135200 | tf_op jit(solution)/shard_map/ppermute | solution.py:11
  29.1 0.0 collective-permute-done.5
  29.2 0.1 fusion.38
  29.3 0.2 fusion.34
  29.5 0.4 copy.73
  30.0 0.1 add_bitcast_fusion
  30.0 0.2 broadcast_compare_fusion
  30.3 0.9 fusion.3
  31.1 0.0 copy-start.3
  31.1 0.9 exponential_reduce_fusion
  32.0 0.1 copy-done.3
  32.1 1.0 %fusion.8 = f32[1024,2,128]{2,0,1:T(8,128)S(1)} fusion(f32[2,1024,128,4]{2,1,3,0:T(8,128)S(1)} %get-tuple-element.30, f32[2,4,128]{2,1,0:T(4,128)S(1)} %bitcast.91, pred[128,1024]{0,1:T(8,128)(4,1)S(1)} %broadcast_compare_fusion, bf16[128,2,4,128]{3,2,1,0:T(4,128)(2,1)S(1)} %bitcast.82), kind=kOutput, calls=%fused_computation.26 | convolution fusion | flops 273678336 | bytes 5640192 | tf_op jit(solution)/shard_map/grtu,tgrd->ugd/dot_general | solution.py:65
  33.1 1.6 %fusion.1 = bf16[2,4,128,1024]{2,3,1,0:T(8,128)(2,1)S(1)} fusion(f32[2,1024,128,4]{2,1,3,0:T(8,128)S(1)} %get-tuple-element.30, f32[2,4,128]{2,1,0:T(4,128)S(1)} %bitcast.90, f32[2,4,128]{2,1,0:T(4,128)S(1)} %bitcast.92, pred[128,1024]{0,1:T(8,128)(4,1)S(1)} %broadcast_compare_fusion, bf16[1024,2,128,1]{2,1,0,3:T(2,128)(2,1)S(1)} %bitcast.81, ...), kind=kOutput, calls=%fused_computation.16 | convolution fusion | flops 275775488 | bytes 7217152 | tf_op jit(solution)/shard_map/tgrd,ugd->grtu/dot_general | solution.py:55
  34.7 0.7 fusion.11
  35.4 1.1 %fusion.22 = (f32[128,4,128]{2,0,1:T(8,128)}, f32[128,4,128]{2,0,1:T(8,128)}, f32[128,4,128]{2,0,1:T(8,128)}, f32[128,4,128]{2,0,1:T(8,128)}, f32[128,4,128]{2,0...) fusion(f32[1024,2,128]{2,0,1:T(8,128)S(1)} %fusion.11, f32[1024,2,128]{2,0,1:T(8,128)S(1)} %fusion.8), kind=kLoop, calls=%fused_computation.40 | loop fusion | flops 458752 | bytes 3932160 | tf_op jit(solution)/shard_map/concatenate | solution.py:68
  36.5 0.0 collective-permute-start.13
  36.5 1.0 %collective-permute-start.12 = (f32[128,4,128]{2,0,1:T(8,128)S(1)}, f32[128,4,128]{2,0,1:T(8,128)S(1)}, u32[]{:S(2)}, u32[]{:S(2)}) collective-permute-start(f32[128,4,128]{2,0,1:T(8,128)S(1)} %get-tuple-element.24), channel_id=1, source_target_pairs={{0,4},{2,6},{4,8},{6,10},{8,12},{10,14},{12,0},{14,2},{1,5},{3,7},... | collective-permute-start | bytes 786440 | tf_op jit(solution)/shard_map/ppermute | solution.py:11
  37.5 2.4 %collective-permute-start.11 = (f32[128,4,128]{2,0,1:T(8,128)}, f32[128,4,128]{2,0,1:T(8,128)}, u32[]{:S(2)}, u32[]{:S(2)}) collective-permute-start(f32[128,4,128]{2,0,1:T(8,128)} %get-tuple-element.22), channel_id=1, source_target_pairs={{0,6},{2,8},{4,10},{6,12},{8,14},{10,0},{12,2},{14,4},{1,7},{3,9},... | collective-permute-start | bytes 786440 | tf_op jit(solution)/shard_map/ppermute | solution.py:11
  39.9 1.0 %collective-permute-start.10 = (f32[128,4,128]{2,0,1:T(8,128)}, f32[128,4,128]{2,0,1:T(8,128)}, u32[]{:S(2)}, u32[]{:S(2)}) collective-permute-start(f32[128,4,128]{2,0,1:T(8,128)} %get-tuple-element.21), channel_id=1, source_target_pairs={{0,8},{2,10},{4,12},{6,14},{8,0},{10,2},{12,4},{14,6},{1,9},{3,11}... | collective-permute-start | bytes 786440 | tf_op jit(solution)/shard_map/ppermute | solution.py:11
  40.9 0.6 collective-permute-start.9
  41.5 3.4 %collective-permute-done.13 = f32[128,4,128]{2,0,1:T(8,128)S(1)} collective-permute-done((f32[128,4,128]{2,0,1:T(8,128)S(1)}, f32[128,4,128]{2,0,1:T(8,128)S(1)}, u32[]{:S(2)}, u32[]{:S(2)}) %collective-permute-start.13) | collective-permute-done | bytes 262176 | tf_op jit(solution)/shard_map/ppermute | solution.py:11
  44.9 4.1 %collective-permute-done.12 = f32[128,4,128]{2,0,1:T(8,128)S(1)} collective-permute-done((f32[128,4,128]{2,0,1:T(8,128)S(1)}, f32[128,4,128]{2,0,1:T(8,128)S(1)}, u32[]{:S(2)}, u32[]{:S(2)}) %collective-permute-start.12) | collective-permute-done | bytes 262176 | tf_op jit(solution)/shard_map/ppermute | solution.py:11
  49.0 0.7 copy-done.2
  49.7 0.5 convolution_multiply_fusion
  50.2 1.0 %copy.68 = f32[128,8,128]{2,1,0:T(8,128)} copy(f32[128,8,128]{0,2,1:T(8,128)S(1)} %bitcast.80) | data formatting | bytes 1048576
  51.2 3.5 %collective-permute-done.11 = f32[128,4,128]{2,0,1:T(8,128)} collective-permute-done((f32[128,4,128]{2,0,1:T(8,128)}, f32[128,4,128]{2,0,1:T(8,128)}, u32[]{:S(2)}, u32[]{:S(2)}) %collective-permute-start.11) | collective-permute-done | bytes 262176 | tf_op jit(solution)/shard_map/ppermute | solution.py:11
  54.7 29.0 %collective-permute-done.10 = f32[128,4,128]{2,0,1:T(8,128)} collective-permute-done((f32[128,4,128]{2,0,1:T(8,128)}, f32[128,4,128]{2,0,1:T(8,128)}, u32[]{:S(2)}, u32[]{:S(2)}) %collective-permute-start.10) | collective-permute-done | bytes 262176 | tf_op jit(solution)/shard_map/ppermute | solution.py:11
  83.7 1.2 %collective-permute-done.9 = f32[128,4,128]{2,0,1:T(8,128)} collective-permute-done((f32[128,4,128]{2,0,1:T(8,128)}, f32[128,4,128]{2,0,1:T(8,128)}, u32[]{:S(2)}, u32[]{:S(2)}) %collective-permute-start.9) | collective-permute-done | bytes 262176 | tf_op jit(solution)/shard_map/ppermute | solution.py:11
  84.9 0.0 collective-permute-done.8
  84.9 0.0 collective-permute-done.7
  84.9 1.5 %fusion.21 = f32[128,4,128]{2,0,1:T(8,128)S(1)} fusion(f32[128,4,128]{2,0,1:T(8,128)} %copy-done.1, f32[128,4,128]{2,0,1:T(8,128)} %copy-done.2, f32[128,4,128]{2,0,1:T(8,128)} %collective-permute-done.11, f32[128,4,128]{2,0,1:T(8,128)} %collective-permute-done.10, f32[128,4,128]{2,0,1:T(8,128)} %collective-permute-done.9, ...), kind=kLoop, calls=%fused_computation.39 | loop fusion | flops 524288 | bytes 4194304 | tf_op jit(solution)/shard_map/add | solution.py:73
  86.4 0.8 copy.69
  87.2 0.8 copy.70
  (20 shorter events, 0.2 us)
Async XLA Ops:
  0.6 29.6 %copy-start = (bf16[128,8,128]{2,1,0:T(8,128)(2,1)S(1)}, bf16[128,8,128]{2,1,0:T(8,128)(2,1)}, u32[]{:S(2)}) copy-start(bf16[128,8,128]{2,1,0:T(8,128)(2,1)} %param.6) | copy-start | bytes 786436
  2.4 8.7 %collective-permute-start = (bf16[528,128]{1,0:T(8,128)(2,1)S(1)}, bf16[528,128]{1,0:T(8,128)(2,1)S(1)}, u32[]{:S(2)}, u32[]{:S(2)}) collective-permute-start(bf16[528,128]{1,0:T(8,128)(2,1)S(1)} %maximum_maximum_fusion), channel_id=1, source_target_pairs={{0,2},{2,4},{4,6},{6,8},{8,10},{10,12},{12,14},{14,0},{1,3},{3,5},... | collective-permute-start | bytes 405512 | tf_op jit(solution)/shard_map/ppermute | solution.py:11
  2.6 9.9 %collective-permute-start.1 = (bf16[528,128]{1,0:T(8,128)(2,1)S(1)}, bf16[528,128]{1,0:T(8,128)(2,1)S(1)}, u32[]{:S(2)}, u32[]{:S(2)}) collective-permute-start(bf16[528,128]{1,0:T(8,128)(2,1)S(1)} %maximum_maximum_fusion), channel_id=1, source_target_pairs={{0,4},{2,6},{4,8},{6,10},{8,12},{10,14},{12,0},{14,2},{1,5},{3,7},... | collective-permute-start | bytes 405512 | tf_op jit(solution)/shard_map/ppermute | solution.py:11
  4.2 8.9 %collective-permute-start.2 = (bf16[528,128]{1,0:T(8,128)(2,1)S(1)}, bf16[528,128]{1,0:T(8,128)(2,1)S(1)}, u32[]{:S(2)}, u32[]{:S(2)}) collective-permute-start(bf16[528,128]{1,0:T(8,128)(2,1)S(1)} %maximum_maximum_fusion), channel_id=1, source_target_pairs={{0,6},{2,8},{4,10},{6,12},{8,14},{10,0},{12,2},{14,4},{1,7},{3,9},... | collective-permute-start | bytes 405512 | tf_op jit(solution)/shard_map/ppermute | solution.py:11
  5.8 22.1 %collective-permute-start.3 = (bf16[528,128]{1,0:T(8,128)(2,1)S(1)}, bf16[528,128]{1,0:T(8,128)(2,1)S(1)}, u32[]{:S(2)}, u32[]{:S(2)}) collective-permute-start(bf16[528,128]{1,0:T(8,128)(2,1)S(1)} %maximum_maximum_fusion), channel_id=1, source_target_pairs={{0,8},{2,10},{4,12},{6,14},{8,0},{10,2},{12,4},{14,6},{1,9},{3,11}... | collective-permute-start | bytes 405512 | tf_op jit(solution)/shard_map/ppermute | solution.py:11
  7.0 22.1 %collective-permute-start.4 = (bf16[528,128]{1,0:T(8,128)(2,1)S(1)}, bf16[528,128]{1,0:T(8,128)(2,1)S(1)}, u32[]{:S(2)}, u32[]{:S(2)}) collective-permute-start(bf16[528,128]{1,0:T(8,128)(2,1)S(1)} %maximum_maximum_fusion), channel_id=1, source_target_pairs={{0,10},{2,12},{4,14},{6,0},{8,2},{10,4},{12,6},{14,8},{1,11},{3,13... | collective-permute-start | bytes 405512 | tf_op jit(solution)/shard_map/ppermute | solution.py:11
  11.1 18.0 %collective-permute-start.5 = (bf16[528,128]{1,0:T(8,128)(2,1)S(1)}, bf16[528,128]{1,0:T(8,128)(2,1)S(1)}, u32[]{:S(2)}, u32[]{:S(2)}) collective-permute-start(bf16[528,128]{1,0:T(8,128)(2,1)S(1)} %maximum_maximum_fusion), channel_id=1, source_target_pairs={{0,12},{2,14},{4,0},{6,2},{8,4},{10,6},{12,8},{14,10},{1,13},{3,15... | collective-permute-start | bytes 405512 | tf_op jit(solution)/shard_map/ppermute | solution.py:11
  12.5 16.6 %collective-permute-start.6 = (bf16[528,128]{1,0:T(8,128)(2,1)S(1)}, bf16[528,128]{1,0:T(8,128)(2,1)S(1)}, u32[]{:S(2)}, u32[]{:S(2)}) collective-permute-start(bf16[528,128]{1,0:T(8,128)(2,1)S(1)} %maximum_maximum_fusion), channel_id=1, source_target_pairs={{0,14},{2,0},{4,2},{6,4},{8,6},{10,8},{12,10},{14,12},{1,15},{3,1}... | collective-permute-start | bytes 405512 | tf_op jit(solution)/shard_map/ppermute | solution.py:11
  31.1 1.0 %copy-start.3 = (bf16[128,8,128]{2,1,0:T(8,128)(2,1)S(1)}, bf16[128,8,128]{2,1,0:T(8,128)(2,1)}, u32[]{:S(2)}) copy-start(bf16[128,8,128]{2,1,0:T(8,128)(2,1)} %param.10) | copy-start | bytes 786436
  36.5 8.3 %collective-permute-start.13 = (f32[128,4,128]{2,0,1:T(8,128)S(1)}, f32[128,4,128]{2,0,1:T(8,128)S(1)}, u32[]{:S(2)}, u32[]{:S(2)}) collective-permute-start(f32[128,4,128]{2,0,1:T(8,128)S(1)} %get-tuple-element.23), channel_id=1, source_target_pairs={{0,2},{2,4},{4,6},{6,8},{8,10},{10,12},{12,14},{14,0},{1,3},{3,5},... | collective-permute-start | bytes 786440 | tf_op jit(solution)/shard_map/ppermute | solution.py:11
  36.5 12.5 %collective-permute-start.12 = (f32[128,4,128]{2,0,1:T(8,128)S(1)}, f32[128,4,128]{2,0,1:T(8,128)S(1)}, u32[]{:S(2)}, u32[]{:S(2)}) collective-permute-start(f32[128,4,128]{2,0,1:T(8,128)S(1)} %get-tuple-element.24), channel_id=1, source_target_pairs={{0,4},{2,6},{4,8},{6,10},{8,12},{10,14},{12,0},{14,2},{1,5},{3,7},... | collective-permute-start | bytes 786440 | tf_op jit(solution)/shard_map/ppermute | solution.py:11
  37.5 17.2 %collective-permute-start.11 = (f32[128,4,128]{2,0,1:T(8,128)}, f32[128,4,128]{2,0,1:T(8,128)}, u32[]{:S(2)}, u32[]{:S(2)}) collective-permute-start(f32[128,4,128]{2,0,1:T(8,128)} %get-tuple-element.22), channel_id=1, source_target_pairs={{0,6},{2,8},{4,10},{6,12},{8,14},{10,0},{12,2},{14,4},{1,7},{3,9},... | collective-permute-start | bytes 786440 | tf_op jit(solution)/shard_map/ppermute | solution.py:11
  39.9 43.7 %collective-permute-start.10 = (f32[128,4,128]{2,0,1:T(8,128)}, f32[128,4,128]{2,0,1:T(8,128)}, u32[]{:S(2)}, u32[]{:S(2)}) collective-permute-start(f32[128,4,128]{2,0,1:T(8,128)} %get-tuple-element.21), channel_id=1, source_target_pairs={{0,8},{2,10},{4,12},{6,14},{8,0},{10,2},{12,4},{14,6},{1,9},{3,11}... | collective-permute-start | bytes 786440 | tf_op jit(solution)/shard_map/ppermute | solution.py:11
  40.9 44.0 %collective-permute-start.9 = (f32[128,4,128]{2,0,1:T(8,128)}, f32[128,4,128]{2,0,1:T(8,128)}, u32[]{:S(2)}, u32[]{:S(2)}) collective-permute-start(f32[128,4,128]{2,0,1:T(8,128)} %get-tuple-element.20), channel_id=1, source_target_pairs={{0,10},{2,12},{4,14},{6,0},{8,2},{10,4},{12,6},{14,8},{1,11},{3,13... | collective-permute-start | bytes 786440 | tf_op jit(solution)/shard_map/ppermute | solution.py:11
  44.9 4.1 %copy-start.1 = (f32[128,4,128]{2,0,1:T(8,128)}, f32[128,4,128]{2,0,1:T(8,128)S(1)}, u32[]{:S(2)}) copy-start(f32[128,4,128]{2,0,1:T(8,128)S(1)} %collective-permute-done.13) | copy-start | bytes 786436
  44.9 40.0 %collective-permute-start.8 = (f32[128,4,128]{2,0,1:T(8,128)}, f32[128,4,128]{2,0,1:T(8,128)}, u32[]{:S(2)}, u32[]{:S(2)}) collective-permute-start(f32[128,4,128]{2,0,1:T(8,128)} %get-tuple-element.19), channel_id=1, source_target_pairs={{0,12},{2,14},{4,0},{6,2},{8,4},{10,6},{12,8},{14,10},{1,13},{3,15... | collective-permute-start | bytes 786440 | tf_op jit(solution)/shard_map/ppermute | solution.py:11
  49.0 0.7 copy-start.2
  49.7 35.2 %collective-permute-start.7 = (f32[128,4,128]{2,0,1:T(8,128)}, f32[128,4,128]{2,0,1:T(8,128)}, u32[]{:S(2)}, u32[]{:S(2)}) collective-permute-start(f32[128,4,128]{2,0,1:T(8,128)} %get-tuple-element.18), channel_id=1, source_target_pairs={{0,14},{2,0},{4,2},{6,4},{8,6},{10,8},{12,10},{14,12},{1,15},{3,1}... | collective-permute-start | bytes 786440 | tf_op jit(solution)/shard_map/ppermute | solution.py:11

commit v3 on v2

--- a/solution.py
+++ b/solution.py
@@ -70,7 +70,7 @@
     )
     owned = parts[0]
     for s in range(1, cycle_size):
-        owned = owned + passed_along(parts[s], "ctx", -s)
+        owned = owned + passed_along(parts[s].astype(jnp.bfloat16), "ctx", -s).astype(jnp.float32)
     return (
         query_grad.reshape(tok_rows, q_heads, head_width),
         owned[:, :kv_heads],

time: 88.3 us -> 66.5 us (0.75)
  the two profiles are of different devices: /device:TPU:30 before, /device:TPU:15 now
where the time goes in v3:
time: 66.5 us; the launch traced here: 66.2 us
  waiting for transfers between devices  36.3 us (55%)
  starting transfers between devices  13.4 us (20%)
  other arithmetic  6.14 us (9%)
  matrix products  4.64 us (7%)
  local copies, waits for them, and re-layouts  4.09 us (6%)
  between operations  1.55 us (2%)
    ppermute x14, waiting for transfers between devices, passed_along(): lax.ppermute(value, axis, [(i, (i + by) % peers) for i in range(peers)])  36.3 us
    ppermute x14, starting transfers between devices, passed_along(): lax.ppermute(value, axis, [(i, (i + by) % peers) for i in range(peers)])  13.4 us
    unnamed x17, local copies, waits for them, and re-layouts  2.65 us
    dot_general x1, matrix products, on_device(): jnp.einsum('tgrd,ugd->grtu', grouped_grad, all_values, preferred_element_...  1.56 us
    add x1, other arithmetic, on_device(): owned + passed_along(parts[s].astype(jnp.bfloat16), 'ctx', -s).astype(jnp...  1.37 us
  transfers between devices with their start and end apart: 14, of which 10 were waited for; matrix products, arithmetic and copies ran while one was open for 6% of the time, Pallas kernels for 0%

profile of v3, /device:TPU:15, one launch (start us, length us, event | category | flops | bytes accessed | tf_op | source)
XLA Modules:
  0.0 66.2 jit_solution(3208445466005143708)
XLA Ops:
  0.6 0.0 copy-start
  1.4 1.0 %maximum_maximum_fusion = bf16[528,128]{1,0:T(8,128)(2,1)S(1)} fusion(bf16[256,128]{1,0:T(8,128)(2,1)} %bitcast.84, bf16[256,128]{1,0:T(8,128)(2,1)} %bitcast.86, bf16[528]{0:T(1024)(128)(2,1)S(1)} %pad.4.clone), kind=kLoop, calls=%fused_computation.35 | loop fusion | flops 405504 | bytes 267296 | tf_op jit(solution)/shard_map/concatenate | solution.py:23
  2.4 1.3 %collective-permute-start = (bf16[528,128]{1,0:T(8,128)(2,1)S(1)}, bf16[528,128]{1,0:T(8,128)(2,1)S(1)}, u32[]{:S(2)}, u32[]{:S(2)}) collective-permute-start(bf16[528,128]{1,0:T(8,128)(2,1)S(1)} %maximum_maximum_fusion), channel_id=1, source_target_pairs={{0,2},{2,4},{4,6},{6,8},{8,10},{10,12},{12,14},{14,0},{1,3},{3,5},... | collective-permute-start | bytes 405512 | tf_op jit(solution)/shard_map/ppermute | solution.py:11
  3.7 1.3 %collective-permute-start.1 = (bf16[528,128]{1,0:T(8,128)(2,1)S(1)}, bf16[528,128]{1,0:T(8,128)(2,1)S(1)}, u32[]{:S(2)}, u32[]{:S(2)}) collective-permute-start(bf16[528,128]{1,0:T(8,128)(2,1)S(1)} %maximum_maximum_fusion), channel_id=1, source_target_pairs={{0,4},{2,6},{4,8},{6,10},{8,12},{10,14},{12,0},{14,2},{1,5},{3,7},... | collective-permute-start | bytes 405512 | tf_op jit(solution)/shard_map/ppermute | solution.py:11
  5.0 1.0 %collective-permute-start.2 = (bf16[528,128]{1,0:T(8,128)(2,1)S(1)}, bf16[528,128]{1,0:T(8,128)(2,1)S(1)}, u32[]{:S(2)}, u32[]{:S(2)}) collective-permute-start(bf16[528,128]{1,0:T(8,128)(2,1)S(1)} %maximum_maximum_fusion), channel_id=1, source_target_pairs={{0,6},{2,8},{4,10},{6,12},{8,14},{10,0},{12,2},{14,4},{1,7},{3,9},... | collective-permute-start | bytes 405512 | tf_op jit(solution)/shard_map/ppermute | solution.py:11
  5.9 1.3 %collective-permute-start.3 = (bf16[528,128]{1,0:T(8,128)(2,1)S(1)}, bf16[528,128]{1,0:T(8,128)(2,1)S(1)}, u32[]{:S(2)}, u32[]{:S(2)}) collective-permute-start(bf16[528,128]{1,0:T(8,128)(2,1)S(1)} %maximum_maximum_fusion), channel_id=1, source_target_pairs={{0,8},{2,10},{4,12},{6,14},{8,0},{10,2},{12,4},{14,6},{1,9},{3,11}... | collective-permute-start | bytes 405512 | tf_op jit(solution)/shard_map/ppermute | solution.py:11
  7.3 1.0 %collective-permute-start.4 = (bf16[528,128]{1,0:T(8,128)(2,1)S(1)}, bf16[528,128]{1,0:T(8,128)(2,1)S(1)}, u32[]{:S(2)}, u32[]{:S(2)}) collective-permute-start(bf16[528,128]{1,0:T(8,128)(2,1)S(1)} %maximum_maximum_fusion), channel_id=1, source_target_pairs={{0,10},{2,12},{4,14},{6,0},{8,2},{10,4},{12,6},{14,8},{1,11},{3,13... | collective-permute-start | bytes 405512 | tf_op jit(solution)/shard_map/ppermute | solution.py:11
  8.3 1.0 %bitcast_dynamic-update-slice_fusion.7 = bf16[8,528,128]{2,1,0:T(8,128)(2,1)S(1)} fusion(bf16[528]{0:T(1024)(128)(2,1)S(1)} %pad.4.clone, bf16[256,128]{1,0:T(8,128)(2,1)} %bitcast.85, bf16[256,128]{1,0:T(8,128)(2,1)} %bitcast.87), kind=kLoop, calls=%fused_computation.43 | loop fusion | flops 405503 | bytes 267296
  9.3 1.2 %multiply_reduce_fusion = f32[128,8]{1,0:T(8,128)S(1)} fusion(bf16[128,8,128]{2,1,0:T(8,128)(2,1)} %param.9, bf16[128,8,128]{2,1,0:T(8,128)(2,1)} %param.10), kind=kLoop, calls=%fused_computation.20 | loop fusion | flops 523264 | bytes 528384 | tf_op jit(solution)/shard_map/reduce_sum | solution.py:43
  10.6 0.0 collective-permute-done
  10.6 1.3 %collective-permute-start.5 = (bf16[528,128]{1,0:T(8,128)(2,1)S(1)}, bf16[528,128]{1,0:T(8,128)(2,1)S(1)}, u32[]{:S(2)}, u32[]{:S(2)}) collective-permute-start(bf16[528,128]{1,0:T(8,128)(2,1)S(1)} %maximum_maximum_fusion), channel_id=1, source_target_pairs={{0,12},{2,14},{4,0},{6,2},{8,4},{10,6},{12,8},{14,10},{1,13},{3,15... | collective-permute-start | bytes 405512 | tf_op jit(solution)/shard_map/ppermute | solution.py:11
  11.9 0.0 collective-permute-done.1
  11.9 1.5 %collective-permute-start.6 = (bf16[528,128]{1,0:T(8,128)(2,1)S(1)}, bf16[528,128]{1,0:T(8,128)(2,1)S(1)}, u32[]{:S(2)}, u32[]{:S(2)}) collective-permute-start(bf16[528,128]{1,0:T(8,128)(2,1)S(1)} %maximum_maximum_fusion), channel_id=1, source_target_pairs={{0,14},{2,0},{4,2},{6,4},{8,6},{10,8},{12,10},{14,12},{1,15},{3,1}... | collective-permute-start | bytes 405512 | tf_op jit(solution)/shard_map/ppermute | solution.py:11
  13.4 9.9 %collective-permute-done.2 = bf16[528,128]{1,0:T(8,128)(2,1)S(1)} collective-permute-done((bf16[528,128]{1,0:T(8,128)(2,1)S(1)}, bf16[528,128]{1,0:T(8,128)(2,1)S(1)}, u32[]{:S(2)}, u32[]{:S(2)}) %collective-permute-start.2) | collective-permute-done | bytes 135200 | tf_op jit(solution)/shard_map/ppermute | solution.py:11
  23.3 2.9 %collective-permute-done.3 = bf16[528,128]{1,0:T(8,128)(2,1)S(1)} collective-permute-done((bf16[528,128]{1,0:T(8,128)(2,1)S(1)}, bf16[528,128]{1,0:T(8,128)(2,1)S(1)}, u32[]{:S(2)}, u32[]{:S(2)}) %collective-permute-start.3) | collective-permute-done | bytes 135200 | tf_op jit(solution)/shard_map/ppermute | solution.py:11
  26.2 0.0 collective-permute-done.4
  26.3 2.8 %collective-permute-done.5 = bf16[528,128]{1,0:T(8,128)(2,1)S(1)} collective-permute-done((bf16[528,128]{1,0:T(8,128)(2,1)S(1)}, bf16[528,128]{1,0:T(8,128)(2,1)S(1)}, u32[]{:S(2)}, u32[]{:S(2)}) %collective-permute-start.5) | collective-permute-done | bytes 135200 | tf_op jit(solution)/shard_map/ppermute | solution.py:11
  29.1 1.2 %collective-permute-done.6 = bf16[528,128]{1,0:T(8,128)(2,1)S(1)} collective-permute-done((bf16[528,128]{1,0:T(8,128)(2,1)S(1)}, bf16[528,128]{1,0:T(8,128)(2,1)S(1)}, u32[]{:S(2)}, u32[]{:S(2)}) %collective-permute-start.6) | collective-permute-done | bytes 135200 | tf_op jit(solution)/shard_map/ppermute | solution.py:11
  30.3 0.1 fusion.33
  30.4 0.2 fusion.29
  30.7 0.4 copy.73
  31.1 0.1 add_bitcast_fusion
  31.2 0.2 broadcast_compare_fusion
  31.4 0.0 copy-start.1
  31.4 0.9 %fusion.3 = (f32[2,4,128]{2,1,0:T(4,128)S(1)}, f32[2,1024,128,4]{2,1,3,0:T(8,128)S(1)}) fusion(pred[128,1024]{0,1:T(8,128)(4,1)S(1)} %broadcast_compare_fusion, bf16[1024,2,128,1]{0,2,3,1:T(8,128)(2,1)S(1)} %copy.73, bf16[128,2,4,128]{3,2,1,0:T(4,128)(2,1)S(1)} %bitcast.77), kind=kOutput, calls=%fused_computation.7 | convolution fusion | flops 271580160 | bytes 5115904 | tf_op jit(solution)/shard_map/tgrd,ugd->grtu/dot_general | solution.py:47
  32.3 0.9 %exponential_reduce_fusion = f32[2,4,128]{2,1,0:T(4,128)S(1)} fusion(f32[2,1024,128,4]{2,1,3,0:T(8,128)S(1)} %get-tuple-element.30, f32[2,4,128]{2,1,0:T(4,128)S(1)} %get-tuple-element.29, pred[128,1024]{0,1:T(8,128)(4,1)S(1)} %broadcast_compare_fusion), kind=kLoop, calls=%fused_computation.5 | loop fusion | flops 4193280 | bytes 4333568 | tf_op jit(solution)/shard_map/reduce_sum | solution.py:52
  33.2 1.0 %fusion.9 = f32[1024,2,128]{2,0,1:T(8,128)S(1)} fusion(f32[2,1024,128,4]{2,1,3,0:T(8,128)S(1)} %get-tuple-element.30, f32[2,4,128]{2,1,0:T(4,128)S(1)} %bitcast.91, pred[128,1024]{0,1:T(8,128)(4,1)S(1)} %broadcast_compare_fusion, bf16[128,2,4,128]{3,2,1,0:T(4,128)(2,1)S(1)} %bitcast.82), kind=kOutput, calls=%fused_computation.16 | convolution fusion | flops 273678336 | bytes 5640192 | tf_op jit(solution)/shard_map/grtu,tgrd->ugd/dot_general | solution.py:65
  34.2 1.6 %fusion.1 = bf16[2,4,128,1024]{2,3,1,0:T(8,128)(2,1)S(1)} fusion(f32[2,1024,128,4]{2,1,3,0:T(8,128)S(1)} %get-tuple-element.30, f32[2,4,128]{2,1,0:T(4,128)S(1)} %bitcast.90, f32[2,4,128]{2,1,0:T(4,128)S(1)} %bitcast.92, pred[128,1024]{0,1:T(8,128)(4,1)S(1)} %broadcast_compare_fusion, bf16[1024,2,128,1]{2,1,0,3:T(2,128)(2,1)S(1)} %bitcast.81, ...), kind=kOutput, calls=%fused_computation.2 | convolution fusion | flops 275775488 | bytes 7217152 | tf_op jit(solution)/shard_map/tgrd,ugd->grtu/dot_general | solution.py:55
  35.8 0.7 %fusion.12 = f32[1024,2,128]{2,0,1:T(8,128)S(1)} fusion(bf16[2,4,128,1024]{2,3,1,0:T(8,128)(2,1)S(1)} %fusion.1, bf16[128,2,4,128]{3,2,1,0:T(4,128)(2,1)S(1)} %bitcast.78), kind=kOutput, calls=%fused_computation.17 | convolution fusion | flops 268697600 | bytes 3407872 | tf_op jit(solution)/shard_map/grtu,tgrd->ugd/dot_general | solution.py:62
  36.5 0.1 fusion.4
  36.6 0.8 %fusion.34 = (bf16[128,4,128]{2,0,1:T(8,128)(2,1)S(1)}, bf16[128,4,128]{2,0,1:T(8,128)(2,1)S(1)}, bf16[128,4,128]{2,0,1:T(8,128)(2,1)S(1)}, bf16[128,4,128]{2,0,...) fusion(bf16[1024,4,128]{2,0,1:T(8,128)(2,1)S(1)} %fusion.4), kind=kLoop, calls=%fused_computation.55 | loop fusion | bytes 1835008 | tf_op jit(solution)/shard_map/slice | solution.py:73
  37.5 0.9 %collective-permute-start.11 = (bf16[128,4,128]{2,0,1:T(8,128)(2,1)}, bf16[128,4,128]{2,0,1:T(8,128)(2,1)}, u32[]{:S(2)}, u32[]{:S(2)}) collective-permute-start(bf16[128,4,128]{2,0,1:T(8,128)(2,1)} %get-tuple-element.23), channel_id=1, source_target_pairs={{0,6},{2,8},{4,10},{6,12},{8,14},{10,0},{12,2},{14,4},{1,7},{3,9},... | collective-permute-start | bytes 393224 | tf_op jit(solution)/shard_map/ppermute | solution.py:11
  38.4 2.7 %collective-permute-start.10 = (bf16[128,4,128]{2,0,1:T(8,128)(2,1)}, bf16[128,4,128]{2,0,1:T(8,128)(2,1)}, u32[]{:S(2)}, u32[]{:S(2)}) collective-permute-start(bf16[128,4,128]{2,0,1:T(8,128)(2,1)} %get-tuple-element.24), channel_id=1, source_target_pairs={{0,8},{2,10},{4,12},{6,14},{8,0},{10,2},{12,4},{14,6},{1,9},{3,11}... | collective-permute-start | bytes 393224 | tf_op jit(solution)/shard_map/ppermute | solution.py:11
  41.0 0.0 collective-permute-start.9
  41.0 1.0 %collective-permute-done.13 = bf16[128,4,128]{2,0,1:T(8,128)(2,1)S(1)} collective-permute-done((bf16[128,4,128]{2,0,1:T(8,128)(2,1)S(1)}, bf16[128,4,128]{2,0,1:T(8,128)(2,1)S(1)}, u32[]{:S(2)}, u32[]{:S(2)}) %collective-permute-start.13) | collective-permute-done | bytes 131104 | tf_op jit(solution)/shard_map/ppermute | solution.py:11
  42.0 1.1 %collective-permute-start.8 = (bf16[128,4,128]{2,0,1:T(8,128)(2,1)}, bf16[128,4,128]{2,0,1:T(8,128)(2,1)}, u32[]{:S(2)}, u32[]{:S(2)}) collective-permute-start(bf16[128,4,128]{2,0,1:T(8,128)(2,1)} %get-tuple-element.26), channel_id=1, source_target_pairs={{0,12},{2,14},{4,0},{6,2},{8,4},{10,6},{12,8},{14,10},{1,13},{3,15... | collective-permute-start | bytes 393224 | tf_op jit(solution)/shard_map/ppermute | solution.py:11
  43.1 0.4 collective-permute-done.12
  43.5 0.2 collective-permute-start.7
  43.7 0.5 convolution_multiply_fusion
  44.2 1.0 %copy.68 = f32[128,8,128]{2,1,0:T(8,128)} copy(f32[128,8,128]{0,2,1:T(8,128)S(1)} %bitcast.80) | data formatting | bytes 1048576
  45.1 12.0 %collective-permute-done.11 = bf16[128,4,128]{2,0,1:T(8,128)(2,1)} collective-permute-done((bf16[128,4,128]{2,0,1:T(8,128)(2,1)}, bf16[128,4,128]{2,0,1:T(8,128)(2,1)}, u32[]{:S(2)}, u32[]{:S(2)}) %collective-permute-start.11) | collective-permute-done | bytes 131104 | tf_op jit(solution)/shard_map/ppermute | solution.py:11
  57.1 2.8 %collective-permute-done.10 = bf16[128,4,128]{2,0,1:T(8,128)(2,1)} collective-permute-done((bf16[128,4,128]{2,0,1:T(8,128)(2,1)}, bf16[128,4,128]{2,0,1:T(8,128)(2,1)}, u32[]{:S(2)}, u32[]{:S(2)}) %collective-permute-start.10) | collective-permute-done | bytes 131104 | tf_op jit(solution)/shard_map/ppermute | solution.py:11
  59.9 0.0 collective-permute-done.9
  59.9 1.0 %collective-permute-done.8 = bf16[128,4,128]{2,0,1:T(8,128)(2,1)} collective-permute-done((bf16[128,4,128]{2,0,1:T(8,128)(2,1)}, bf16[128,4,128]{2,0,1:T(8,128)(2,1)}, u32[]{:S(2)}, u32[]{:S(2)}) %collective-permute-start.8) | collective-permute-done | bytes 131104 | tf_op jit(solution)/shard_map/ppermute | solution.py:11
  60.9 2.4 %collective-permute-done.7 = bf16[128,4,128]{2,0,1:T(8,128)(2,1)} collective-permute-done((bf16[128,4,128]{2,0,1:T(8,128)(2,1)S(1)}, bf16[128,4,128]{2,0,1:T(8,128)(2,1)}, u32[]{:S(2)}, u32[]{:S(2)}) %collective-permute-start.7) | collective-permute-done | bytes 131104 | tf_op jit(solution)/shard_map/ppermute | solution.py:11
  63.3 1.4 %fusion.21 = f32[128,4,128]{2,0,1:T(8,128)S(1)} fusion(f32[1024,2,128]{2,0,1:T(8,128)S(1)} %fusion.12, f32[1024,2,128]{2,0,1:T(8,128)S(1)} %fusion.9, bf16[128,4,128]{2,0,1:T(8,128)(2,1)} %copy-done.2, bf16[128,4,128]{2,0,1:T(8,128)(2,1)} %copy-done.3, bf16[128,4,128]{2,0,1:T(8,128)(2,1)} %collective-permute-done.11, ...), kind=kLoop, calls=%fused_computation.28 | loop fusion | flops 983040 | bytes 3276800 | tf_op jit(solution)/shard_map/add | solution.py:73
  64.7 0.8 %copy.69 = f32[128,2,128]{2,1,0:T(2,128)} copy(f32[128,2,128]{2,0,1:T(8,128)S(1)} %get-tuple-element.28) | data formatting | bytes 262144
  65.4 0.8 %copy.70 = f32[128,2,128]{2,1,0:T(2,128)} copy(f32[128,2,128]{2,0,1:T(8,128)S(1)} %get-tuple-element.27) | data formatting | bytes 262144
  (21 shorter events, 0.2 us)
Async XLA Ops:
  0.6 30.8 %copy-start = (bf16[128,8,128]{2,1,0:T(8,128)(2,1)S(1)}, bf16[128,8,128]{2,1,0:T(8,128)(2,1)}, u32[]{:S(2)}) copy-start(bf16[128,8,128]{2,1,0:T(8,128)(2,1)} %param.6) | copy-start | bytes 786436
  2.4 8.2 %collective-permute-start = (bf16[528,128]{1,0:T(8,128)(2,1)S(1)}, bf16[528,128]{1,0:T(8,128)(2,1)S(1)}, u32[]{:S(2)}, u32[]{:S(2)}) collective-permute-start(bf16[528,128]{1,0:T(8,128)(2,1)S(1)} %maximum_maximum_fusion), channel_id=1, source_target_pairs={{0,2},{2,4},{4,6},{6,8},{8,10},{10,12},{12,14},{14,0},{1,3},{3,5},... | collective-permute-start | bytes 405512 | tf_op jit(solution)/shard_map/ppermute | solution.py:11
  3.7 8.2 %collective-permute-start.1 = (bf16[528,128]{1,0:T(8,128)(2,1)S(1)}, bf16[528,128]{1,0:T(8,128)(2,1)S(1)}, u32[]{:S(2)}, u32[]{:S(2)}) collective-permute-start(bf16[528,128]{1,0:T(8,128)(2,1)S(1)} %maximum_maximum_fusion), channel_id=1, source_target_pairs={{0,4},{2,6},{4,8},{6,10},{8,12},{10,14},{12,0},{14,2},{1,5},{3,7},... | collective-permute-start | bytes 405512 | tf_op jit(solution)/shard_map/ppermute | solution.py:11
  5.0 18.3 %collective-permute-start.2 = (bf16[528,128]{1,0:T(8,128)(2,1)S(1)}, bf16[528,128]{1,0:T(8,128)(2,1)S(1)}, u32[]{:S(2)}, u32[]{:S(2)}) collective-permute-start(bf16[528,128]{1,0:T(8,128)(2,1)S(1)} %maximum_maximum_fusion), channel_id=1, source_target_pairs={{0,6},{2,8},{4,10},{6,12},{8,14},{10,0},{12,2},{14,4},{1,7},{3,9},... | collective-permute-start | bytes 405512 | tf_op jit(solution)/shard_map/ppermute | solution.py:11
  5.9 20.3 %collective-permute-start.3 = (bf16[528,128]{1,0:T(8,128)(2,1)S(1)}, bf16[528,128]{1,0:T(8,128)(2,1)S(1)}, u32[]{:S(2)}, u32[]{:S(2)}) collective-permute-start(bf16[528,128]{1,0:T(8,128)(2,1)S(1)} %maximum_maximum_fusion), channel_id=1, source_target_pairs={{0,8},{2,10},{4,12},{6,14},{8,0},{10,2},{12,4},{14,6},{1,9},{3,11}... | collective-permute-start | bytes 405512 | tf_op jit(solution)/shard_map/ppermute | solution.py:11
  7.3 18.9 %collective-permute-start.4 = (bf16[528,128]{1,0:T(8,128)(2,1)S(1)}, bf16[528,128]{1,0:T(8,128)(2,1)S(1)}, u32[]{:S(2)}, u32[]{:S(2)}) collective-permute-start(bf16[528,128]{1,0:T(8,128)(2,1)S(1)} %maximum_maximum_fusion), channel_id=1, source_target_pairs={{0,10},{2,12},{4,14},{6,0},{8,2},{10,4},{12,6},{14,8},{1,11},{3,13... | collective-permute-start | bytes 405512 | tf_op jit(solution)/shard_map/ppermute | solution.py:11
  10.6 18.5 %collective-permute-start.5 = (bf16[528,128]{1,0:T(8,128)(2,1)S(1)}, bf16[528,128]{1,0:T(8,128)(2,1)S(1)}, u32[]{:S(2)}, u32[]{:S(2)}) collective-permute-start(bf16[528,128]{1,0:T(8,128)(2,1)S(1)} %maximum_maximum_fusion), channel_id=1, source_target_pairs={{0,12},{2,14},{4,0},{6,2},{8,4},{10,6},{12,8},{14,10},{1,13},{3,15... | collective-permute-start | bytes 405512 | tf_op jit(solution)/shard_map/ppermute | solution.py:11
  11.9 18.4 %collective-permute-start.6 = (bf16[528,128]{1,0:T(8,128)(2,1)S(1)}, bf16[528,128]{1,0:T(8,128)(2,1)S(1)}, u32[]{:S(2)}, u32[]{:S(2)}) collective-permute-start(bf16[528,128]{1,0:T(8,128)(2,1)S(1)} %maximum_maximum_fusion), channel_id=1, source_target_pairs={{0,14},{2,0},{4,2},{6,4},{8,6},{10,8},{12,10},{14,12},{1,15},{3,1}... | collective-permute-start | bytes 405512 | tf_op jit(solution)/shard_map/ppermute | solution.py:11
  31.4 1.8 %copy-start.1 = (bf16[128,8,128]{2,1,0:T(8,128)(2,1)S(1)}, bf16[128,8,128]{2,1,0:T(8,128)(2,1)}, u32[]{:S(2)}) copy-start(bf16[128,8,128]{2,1,0:T(8,128)(2,1)} %param.10) | copy-start | bytes 786436
  37.5 4.6 %collective-permute-start.13 = (bf16[128,4,128]{2,0,1:T(8,128)(2,1)S(1)}, bf16[128,4,128]{2,0,1:T(8,128)(2,1)S(1)}, u32[]{:S(2)}, u32[]{:S(2)}) collective-permute-start(bf16[128,4,128]{2,0,1:T(8,128)(2,1)S(1)} %get-tuple-element.21), channel_id=1, source_target_pairs={{0,2},{2,4},{4,6},{6,8},{8,10},{10,12},{12,14},{14,0},{1,3},{3,5},... | collective-permute-start | bytes 393224 | tf_op jit(solution)/shard_map/ppermute | solution.py:11
  37.5 6.0 %collective-permute-start.12 = (bf16[128,4,128]{2,0,1:T(8,128)(2,1)S(1)}, bf16[128,4,128]{2,0,1:T(8,128)(2,1)S(1)}, u32[]{:S(2)}, u32[]{:S(2)}) collective-permute-start(bf16[128,4,128]{2,0,1:T(8,128)(2,1)S(1)} %get-tuple-element.22), channel_id=1, source_target_pairs={{0,4},{2,6},{4,8},{6,10},{8,12},{10,14},{12,0},{14,2},{1,5},{3,7},... | collective-permute-start | bytes 393224 | tf_op jit(solution)/shard_map/ppermute | solution.py:11
  37.5 19.6 %collective-permute-start.11 = (bf16[128,4,128]{2,0,1:T(8,128)(2,1)}, bf16[128,4,128]{2,0,1:T(8,128)(2,1)}, u32[]{:S(2)}, u32[]{:S(2)}) collective-permute-start(bf16[128,4,128]{2,0,1:T(8,128)(2,1)} %get-tuple-element.23), channel_id=1, source_target_pairs={{0,6},{2,8},{4,10},{6,12},{8,14},{10,0},{12,2},{14,4},{1,7},{3,9},... | collective-permute-start | bytes 393224 | tf_op jit(solution)/shard_map/ppermute | solution.py:11
  38.4 21.6 %collective-permute-start.10 = (bf16[128,4,128]{2,0,1:T(8,128)(2,1)}, bf16[128,4,128]{2,0,1:T(8,128)(2,1)}, u32[]{:S(2)}, u32[]{:S(2)}) collective-permute-start(bf16[128,4,128]{2,0,1:T(8,128)(2,1)} %get-tuple-element.24), channel_id=1, source_target_pairs={{0,8},{2,10},{4,12},{6,14},{8,0},{10,2},{12,4},{14,6},{1,9},{3,11}... | collective-permute-start | bytes 393224 | tf_op jit(solution)/shard_map/ppermute | solution.py:11
  41.0 18.9 %collective-permute-start.9 = (bf16[128,4,128]{2,0,1:T(8,128)(2,1)}, bf16[128,4,128]{2,0,1:T(8,128)(2,1)}, u32[]{:S(2)}, u32[]{:S(2)}) collective-permute-start(bf16[128,4,128]{2,0,1:T(8,128)(2,1)} %get-tuple-element.25), channel_id=1, source_target_pairs={{0,10},{2,12},{4,14},{6,0},{8,2},{10,4},{12,6},{14,8},{1,11},{3,13... | collective-permute-start | bytes 393224 | tf_op jit(solution)/shard_map/ppermute | solution.py:11
  42.0 2.1 %copy-start.2 = (bf16[128,4,128]{2,0,1:T(8,128)(2,1)}, bf16[128,4,128]{2,0,1:T(8,128)(2,1)S(1)}, u32[]{:S(2)}) copy-start(bf16[128,4,128]{2,0,1:T(8,128)(2,1)S(1)} %collective-permute-done.13) | copy-start | bytes 393220
  42.0 18.9 %collective-permute-start.8 = (bf16[128,4,128]{2,0,1:T(8,128)(2,1)}, bf16[128,4,128]{2,0,1:T(8,128)(2,1)}, u32[]{:S(2)}, u32[]{:S(2)}) collective-permute-start(bf16[128,4,128]{2,0,1:T(8,128)(2,1)} %get-tuple-element.26), channel_id=1, source_target_pairs={{0,12},{2,14},{4,0},{6,2},{8,4},{10,6},{12,8},{14,10},{1,13},{3,15... | collective-permute-start | bytes 393224 | tf_op jit(solution)/shard_map/ppermute | solution.py:11
  43.5 0.7 copy-start.3
  43.5 19.8 %collective-permute-start.7 = (bf16[128,4,128]{2,0,1:T(8,128)(2,1)S(1)}, bf16[128,4,128]{2,0,1:T(8,128)(2,1)}, u32[]{:S(2)}, u32[]{:S(2)}) collective-permute-start(bf16[128,4,128]{2,0,1:T(8,128)(2,1)S(1)} %get-tuple-element.20), channel_id=1, source_target_pairs={{0,14},{2,0},{4,2},{6,4},{8,6},{10,8},{12,10},{14,12},{1,15},{3,1}... | collective-permute-start | bytes 393224 | tf_op jit(solution)/shard_map/ppermute | solution.py:11

commit v4 on v3

v4 whole, which is shorter than its diff:
```python
import functools

import jax
import jax.numpy as jnp
from jax import lax
from jax.experimental import pallas as pl
from jax.experimental.pallas import tpu as pltpu
from jax.sharding import PartitionSpec as P

OFFSET_ROWS = 16
CHUNK_BLOCKS = 8
MASKED = -1e30


def passed_along(value, axis, by):
    peers = lax.axis_size(axis)
    return lax.ppermute(value, axis, [(i, (i + by) % peers) for i in range(peers)])


def backward_kernel(
    offs_ref, own_ref, q_ref, do_ref, fo_ref, kv_ref, dq_ref, own_part_ref, parts_ref,
    *, kv_heads, chunk_blocks
):
    q_heads, tok_rows, head_width = q_ref.shape
    blocks = kv_ref.shape[0]
    heads_per_group = q_heads // kv_heads
    rows = heads_per_group * tok_rows
    chunk_keys = chunk_blocks * tok_rows
    shift = tok_rows.bit_length() - 1
    scale = head_width ** (-0.5)
    f32 = jnp.float32
    row_pos = own_ref[0] * tok_rows + (
        lax.broadcasted_iota(jnp.int32, (rows, 1), 0) & (tok_rows - 1)
    )
    lane = lax.broadcasted_iota(jnp.int32, (1, chunk_keys), 1)
    lane_block = lax.shift_right_logical(lane, shift)
    lane_row = lane & (tok_rows - 1)

    def chunk_keys_of(c, g):
        k = kv_ref[c * chunk_blocks : (c + 1) * chunk_blocks, g * tok_rows : (g + 1) * tok_rows, :]
        return k.reshape(chunk_keys, head_width)

    def chunk_values_of(c, g):
        base = kv_heads * tok_rows + g * tok_rows
        v = kv_ref[c * chunk_blocks : (c + 1) * chunk_blocks, base : base + tok_rows, :]
        return v.reshape(chunk_keys, head_width)

    def chunk_scores(q, k, c):
        s = lax.dot_general(q, k, (((1,), (1,)), ((), ())), preferred_element_type=f32) * scale
        key_off = jnp.zeros((1, chunk_keys), jnp.int32)
        for b in range(chunk_blocks):
            key_off = jnp.where(lane_block == b, offs_ref[c * chunk_blocks + b], key_off)
        visible = (key_off * tok_rows + lane_row) <= row_pos
        return jnp.where(visible, s, MASKED), visible

    for g in range(kv_heads):
        heads = slice(g * heads_per_group, (g + 1) * heads_per_group)
        q = q_ref[heads].reshape(rows, head_width)
        do = do_ref[heads].reshape(rows, head_width)
        fo = fo_ref[heads].reshape(rows, head_width)
        delta = jnp.sum(do.astype(f32) * fo.astype(f32), axis=1, keepdims=True)

        run_max = jnp.full((rows, 1), MASKED, f32)
        run_total = jnp.zeros((rows, 1), f32)
        for c in range(blocks // chunk_blocks):
            s, _ = chunk_scores(q, chunk_keys_of(c, g), c)
            new_max = jnp.maximum(run_max, jnp.max(s, axis=1, keepdims=True))
            run_total = run_total * jnp.exp(run_max - new_max) + jnp.sum(
                jnp.exp(s - new_max), axis=1, keepdims=True
            )
            run_max = new_max
        log_total = run_max + jnp.log(run_total)

        dq = jnp.zeros((rows, head_width), f32)
        for c in range(blocks // chunk_blocks):
            k = chunk_keys_of(c, g)
            v = chunk_values_of(c, g)
            s, visible = chunk_scores(q, k, c)
            probs = jnp.where(visible, jnp.exp(s - log_total), 0.0)
            prob_grad = lax.dot_general(
                do, v, (((1,), (1,)), ((), ())), preferred_element_type=f32
            )
            score_grad = (probs * (prob_grad - delta)).astype(jnp.bfloat16)
            dq = dq + jnp.dot(score_grad, k, preferred_element_type=f32)
            dk = scale * lax.dot_general(
                score_grad, q, (((0,), (0,)), ((), ())), preferred_element_type=f32
            )
            dv = lax.dot_general(
                probs.astype(jnp.bfloat16), do, (((0,), (0,)), ((), ())), preferred_element_type=f32
            )
            for b in range(chunk_blocks):
                block = c * chunk_blocks + b
                piece = slice(b * tok_rows, (b + 1) * tok_rows)
                if block == 0:
                    own_part_ref[g] = dk[piece]
                    own_part_ref[kv_heads + g] = dv[piece]
                else:
                    parts_ref[block - 1, g] = dk[piece].astype(jnp.bfloat16)
                    parts_ref[block - 1, kv_heads + g] = dv[piece].astype(jnp.bfloat16)
        dq_ref[heads] = (scale * dq).reshape(heads_per_group, tok_rows, head_width)


def local_backward(offsets, own_offset, q_t, do_t, fo_t, gathered, kv_heads):
    q_heads, tok_rows, head_width = q_t.shape
    blocks = gathered.shape[0]
    chunk_blocks = min(CHUNK_BLOCKS, blocks)
    rows = q_heads * tok_rows
    keys = blocks * tok_rows
    smem = pl.BlockSpec(memory_space=pltpu.SMEM)
    vmem = pl.BlockSpec(memory_space=pltpu.VMEM)
    return pl.pallas_call(
        functools.partial(backward_kernel, kv_heads=kv_heads, chunk_blocks=chunk_blocks),
        out_shape=(
            jax.ShapeDtypeStruct((q_heads, tok_rows, head_width), jnp.float32),
            jax.ShapeDtypeStruct((2 * kv_heads, tok_rows, head_width), jnp.float32),
            jax.ShapeDtypeStruct((blocks - 1, 2 * kv_heads, tok_rows, head_width), jnp.bfloat16),
        ),
        in_specs=[smem, smem, vmem, vmem, vmem, vmem],
        out_specs=(vmem, vmem, vmem),
        compiler_params=pltpu.CompilerParams(vmem_limit_bytes=48 * 1024 * 1024),
        cost_estimate=pl.CostEstimate(
            flops=12 * rows * keys * head_width,
            transcendentals=2 * rows * keys,
            bytes_accessed=gathered.size * 2 + 3 * q_t.size * 2 + 6 * q_t.size,
        ),
    )(offsets, own_offset, q_t, do_t, fo_t, gathered)


def on_device(query_vectors, key_vectors, value_rows, forward_out, out_grad, block_offsets):
    tok_rows, q_heads, head_width = query_vectors.shape
    kv_heads = key_vectors.shape[1]
    cycle_size = lax.axis_size("ctx")
    kv_rows = tok_rows * kv_heads

    offset_rows = jnp.full((OFFSET_ROWS, head_width), block_offsets[0], jnp.float32).astype(jnp.bfloat16)
    slab = jnp.concatenate(
        [
            key_vectors.transpose(1, 0, 2).reshape(kv_rows, head_width),
            value_rows.transpose(1, 0, 2).reshape(kv_rows, head_width),
            offset_rows,
        ],
        axis=0,
    )
    gathered = jnp.stack([slab] + [passed_along(slab, "ctx", s) for s in range(1, cycle_size)])
    all_offsets = gathered[:, 2 * kv_rows, 0].astype(jnp.float32).astype(jnp.int32)

    dq_t, own_part, parts = local_backward(
        all_offsets,
        block_offsets,
        query_vectors.transpose(1, 0, 2),
        out_grad.transpose(1, 0, 2),
        forward_out.transpose(1, 0, 2),
        gathered,
        kv_heads,
    )
    arrived = [passed_along(parts[s - 1], "ctx", -s) for s in range(1, cycle_size)]
    key_grad = own_part[:kv_heads]
    value_grad = own_part[kv_heads:]
    for piece in arrived:
        key_grad = key_grad + piece[:kv_heads].astype(jnp.float32)
        value_grad = value_grad + piece[kv_heads:].astype(jnp.float32)
    return (
        dq_t.transpose(1, 0, 2),
        key_grad.transpose(1, 0, 2),
        value_grad.transpose(1, 0, 2),
    )


def solution(mesh):
    in_specs = (
        P(("groups", "ctx"), "heads", None),
        P(("groups", "ctx"), "heads", None),
        P(("groups", "ctx"), "heads", None),
        P(("groups", "ctx"), "heads", None),
        P(("groups", "ctx"), "heads", None),
        P(("groups", "ctx")),
    )
    out_specs = (
        P(("groups", "ctx"), "heads", None),
        P(("groups", "ctx"), "heads", None),
        P(("groups", "ctx"), "heads", None),
    )
    return jax.shard_map(
        on_device, mesh=mesh, in_specs=in_specs, out_specs=out_specs, check_vma=False
    )
```

time: 66.5 us -> 66.3 us (level)
  the two profiles are of different devices: /device:TPU:15 before, /device:TPU:0 now
where the time goes in v4:
time: 66.3 us; the launch traced here: 66.1 us
  starting transfers between devices  30.2 us (46%)
  waiting for transfers between devices  23 us (35%)
  local copies, waits for them, and re-layouts  5.63 us (8%)
  Pallas kernels  5.12 us (8%)
  between operations  1.53 us (2%)
    ppermute x14, starting transfers between devices, passed_along(): lax.ppermute(value, axis, [(i, (i + by) % peers) for i in range(peers)])  30.2 us
    ppermute x14, waiting for transfers between devices, passed_along(): lax.ppermute(value, axis, [(i, (i + by) % peers) for i in range(peers)])  23 us
    pallas_call x1, Pallas kernels, local_backward(): pl.pallas_call(functools.partial(backward_kernel, kv_heads=kv_heads, chun...  5.12 us
    unnamed x14, local copies, waits for them, and re-layouts  3.72 us
  transfers between devices with their start and end apart: 14, of which 5 were waited for; matrix products, arithmetic and copies ran while one was open for 4% of the time, Pallas kernels for 0%

profile of v4, /device:TPU:0, one launch (start us, length us, event | category | flops | bytes accessed | tf_op | source)
XLA Modules:
  0.0 66.1 jit_solution(12748356008433118889)
XLA Ops:
  0.6 0.0 copy-start.1
  0.6 0.0 copy-start
  1.4 0.9 %copy.17 = bf16[2,128,128]{2,1,0:T(8,128)(2,1)S(1)} copy(bf16[2,128,128]{2,0,1:T(2,128)(2,1)} %bitcast.53) | data formatting | bytes 131072 | tf_op jit(solution)/shard_map/transpose | solution.py:138
  2.2 0.9 %copy.18 = bf16[2,128,128]{2,1,0:T(8,128)(2,1)S(1)} copy(bf16[2,128,128]{2,0,1:T(2,128)(2,1)} %bitcast.54) | data formatting | bytes 131072 | tf_op jit(solution)/shard_map/transpose | solution.py:139
  3.1 0.1 maximum_maximum_fusion
  3.2 3.0 %collective-permute-start = (bf16[528,128]{1,0:T(8,128)(2,1)S(1)}, bf16[528,128]{1,0:T(8,128)(2,1)S(1)}, u32[]{:S(2)}, u32[]{:S(2)}) collective-permute-start(bf16[528,128]{1,0:T(8,128)(2,1)S(1)} %maximum_maximum_fusion), channel_id=1, source_target_pairs={{0,2},{2,4},{4,6},{6,8},{8,10},{10,12},{12,14},{14,0},{1,3},{3,5},... | collective-permute-start | bytes 405512 | tf_op jit(solution)/shard_map/ppermute | solution.py:17
  6.3 1.6 %collective-permute-start.1 = (bf16[528,128]{1,0:T(8,128)(2,1)S(1)}, bf16[528,128]{1,0:T(8,128)(2,1)S(1)}, u32[]{:S(2)}, u32[]{:S(2)}) collective-permute-start(bf16[528,128]{1,0:T(8,128)(2,1)S(1)} %maximum_maximum_fusion), channel_id=1, source_target_pairs={{0,4},{2,6},{4,8},{6,10},{8,12},{10,14},{12,0},{14,2},{1,5},{3,7},... | collective-permute-start | bytes 405512 | tf_op jit(solution)/shard_map/ppermute | solution.py:17
  7.8 2.5 %collective-permute-start.2 = (bf16[528,128]{1,0:T(8,128)(2,1)S(1)}, bf16[528,128]{1,0:T(8,128)(2,1)S(1)}, u32[]{:S(2)}, u32[]{:S(2)}) collective-permute-start(bf16[528,128]{1,0:T(8,128)(2,1)S(1)} %maximum_maximum_fusion), channel_id=1, source_target_pairs={{0,6},{2,8},{4,10},{6,12},{8,14},{10,0},{12,2},{14,4},{1,7},{3,9},... | collective-permute-start | bytes 405512 | tf_op jit(solution)/shard_map/ppermute | solution.py:17
  10.4 1.2 %collective-permute-start.3 = (bf16[528,128]{1,0:T(8,128)(2,1)S(1)}, bf16[528,128]{1,0:T(8,128)(2,1)S(1)}, u32[]{:S(2)}, u32[]{:S(2)}) collective-permute-start(bf16[528,128]{1,0:T(8,128)(2,1)S(1)} %maximum_maximum_fusion), channel_id=1, source_target_pairs={{0,8},{2,10},{4,12},{6,14},{8,0},{10,2},{12,4},{14,6},{1,9},{3,11}... | collective-permute-start | bytes 405512 | tf_op jit(solution)/shard_map/ppermute | solution.py:17
  11.6 2.6 %collective-permute-start.4 = (bf16[528,128]{1,0:T(8,128)(2,1)S(1)}, bf16[528,128]{1,0:T(8,128)(2,1)S(1)}, u32[]{:S(2)}, u32[]{:S(2)}) collective-permute-start(bf16[528,128]{1,0:T(8,128)(2,1)S(1)} %maximum_maximum_fusion), channel_id=1, source_target_pairs={{0,10},{2,12},{4,14},{6,0},{8,2},{10,4},{12,6},{14,8},{1,11},{3,13... | collective-permute-start | bytes 405512 | tf_op jit(solution)/shard_map/ppermute | solution.py:17
  14.2 1.0 %copy.28 = bf16[128,8,128]{2,0,1:T(8,128)(2,1)S(1)} copy(bf16[128,8,128]{2,1,0:T(8,128)(2,1)} %param.6) | data formatting | bytes 524288 | tf_op args[0]
  15.2 0.0 copy-done.1
  15.2 0.0 copy-done
  15.3 0.1 copy_bitcast_fusion
  15.4 0.1 bitcast_dynamic-update-slice_fusion.7
  15.5 0.0 collective-permute-done
  15.5 1.4 %collective-permute-start.5 = (bf16[528,128]{1,0:T(8,128)(2,1)S(1)}, bf16[528,128]{1,0:T(8,128)(2,1)S(1)}, u32[]{:S(2)}, u32[]{:S(2)}) collective-permute-start(bf16[528,128]{1,0:T(8,128)(2,1)S(1)} %maximum_maximum_fusion), channel_id=1, source_target_pairs={{0,12},{2,14},{4,0},{6,2},{8,4},{10,6},{12,8},{14,10},{1,13},{3,15... | collective-permute-start | bytes 405512 | tf_op jit(solution)/shard_map/ppermute | solution.py:17
  16.9 0.0 collective-permute-done.1
  16.9 1.5 %collective-permute-start.6 = (bf16[528,128]{1,0:T(8,128)(2,1)S(1)}, bf16[528,128]{1,0:T(8,128)(2,1)S(1)}, u32[]{:S(2)}, u32[]{:S(2)}) collective-permute-start(bf16[528,128]{1,0:T(8,128)(2,1)S(1)} %maximum_maximum_fusion), channel_id=1, source_target_pairs={{0,14},{2,0},{4,2},{6,4},{8,6},{10,8},{12,10},{14,12},{1,15},{3,1}... | collective-permute-start | bytes 405512 | tf_op jit(solution)/shard_map/ppermute | solution.py:17
  18.4 6.2 %collective-permute-done.2 = bf16[528,128]{1,0:T(8,128)(2,1)S(1)} collective-permute-done((bf16[528,128]{1,0:T(8,128)(2,1)S(1)}, bf16[528,128]{1,0:T(8,128)(2,1)S(1)}, u32[]{:S(2)}, u32[]{:S(2)}) %collective-permute-start.2) | collective-permute-done | bytes 135200 | tf_op jit(solution)/shard_map/ppermute | solution.py:17
  24.6 0.3 collective-permute-done.3
  25.0 0.0 collective-permute-done.4
  25.0 0.0 collective-permute-done.5
  25.0 0.0 collective-permute-done.6
  25.1 0.2 fusion.1.offs_ref
  25.3 5.1 %shard_map.85 = (f32[8,128,128]{2,1,0:T(8,128)S(1)}, f32[4,128,128]{2,1,0:T(8,128)S(1)}, bf16[7,4,128,128]{3,2,1,0:T(8,128)(2,1)S(1)}) custom-call(s32[8]{0:T(128)S(1)} %fusion.1.offs_ref, s32[1]{0:T(128)S(6)} %copy.36.own_ref, bf16[8,128,128]{2,1,0:T(8,128)(2,1)S(1)} %bitcast.48, bf16[8,128,128]{2,1,0:T(8,128)(2,1)S(1)} %get-tuple-element.25.do_ref, ...), custom_call_target="tpu_custom_call" | custom-call | flops 1610612736 | bytes 2654208 | tf_op jit(solution)/shard_map/pallas_call | solution.py:111
  30.4 0.1 slice_bitcast_fusion.6
  30.5 8.0 %collective-permute-start.10 = (bf16[4,128,128]{2,1,0:T(8,128)(2,1)S(1)}, bf16[4,128,128]{2,1,0:T(8,128)(2,1)S(1)}, u32[]{:S(2)}, u32[]{:S(2)}) collective-permute-start(bf16[4,128,128]{2,1,0:T(8,128)(2,1)S(1)} %get-tuple-element.21), channel_id=1, source_target_pairs={{0,8},{2,10},{4,12},{6,14},{8,0},{10,2},{12,4},{14,6},{1,9},{3,11}... | collective-permute-start | bytes 393224 | tf_op jit(solution)/shard_map/ppermute | solution.py:17
  38.6 3.6 %collective-permute-start.11 = (bf16[4,128,128]{2,1,0:T(8,128)(2,1)S(1)}, bf16[4,128,128]{2,1,0:T(8,128)(2,1)S(1)}, u32[]{:S(2)}, u32[]{:S(2)}) collective-permute-start(bf16[4,128,128]{2,1,0:T(8,128)(2,1)S(1)} %get-tuple-element.20), channel_id=1, source_target_pairs={{0,6},{2,8},{4,10},{6,12},{8,14},{10,0},{12,2},{14,4},{1,7},{3,9},... | collective-permute-start | bytes 393224 | tf_op jit(solution)/shard_map/ppermute | solution.py:17
  42.1 0.0 collective-permute-start.12
  42.1 0.6 collective-permute-start.13
  42.7 4.2 %collective-permute-start.7 = (bf16[4,128,128]{2,1,0:T(8,128)(2,1)S(1)}, bf16[4,128,128]{2,1,0:T(8,128)(2,1)S(1)}, u32[]{:S(2)}, u32[]{:S(2)}) collective-permute-start(bf16[4,128,128]{2,1,0:T(8,128)(2,1)S(1)} %get-tuple-element.17), channel_id=1, source_target_pairs={{0,14},{2,0},{4,2},{6,4},{8,6},{10,8},{12,10},{14,12},{1,15},{3,1}... | collective-permute-start | bytes 393224 | tf_op jit(solution)/shard_map/ppermute | solution.py:17
  46.9 4.2 %collective-permute-done.10 = bf16[4,128,128]{2,1,0:T(8,128)(2,1)S(1)} collective-permute-done((bf16[4,128,128]{2,1,0:T(8,128)(2,1)S(1)}, bf16[4,128,128]{2,1,0:T(8,128)(2,1)S(1)}, u32[]{:S(2)}, u32[]{:S(2)}) %collective-permute-start.10) | collective-permute-done | bytes 131104 | tf_op jit(solution)/shard_map/ppermute | solution.py:17
  51.1 0.0 collective-permute-start.8
  51.1 7.5 %collective-permute-done.11 = bf16[4,128,128]{2,1,0:T(8,128)(2,1)S(1)} collective-permute-done((bf16[4,128,128]{2,1,0:T(8,128)(2,1)S(1)}, bf16[4,128,128]{2,1,0:T(8,128)(2,1)S(1)}, u32[]{:S(2)}, u32[]{:S(2)}) %collective-permute-start.11) | collective-permute-done | bytes 131104 | tf_op jit(solution)/shard_map/ppermute | solution.py:17
  58.6 0.0 collective-permute-start.9
  58.6 1.1 %copy.22 = f32[128,8,128]{2,1,0:T(8,128)} copy(f32[128,8,128]{2,0,1:T(8,128)S(1)} %bitcast.47) | data formatting | bytes 1048576
  59.7 0.0 collective-permute-done.12
  59.7 0.0 collective-permute-done.13
  59.7 0.0 collective-permute-done.7
  59.7 0.0 collective-permute-done.8
  59.7 4.7 %collective-permute-done.9 = bf16[4,128,128]{2,1,0:T(8,128)(2,1)S(1)} collective-permute-done((bf16[4,128,128]{2,1,0:T(8,128)(2,1)S(1)}, bf16[4,128,128]{2,1,0:T(8,128)(2,1)S(1)}, u32[]{:S(2)}, u32[]{:S(2)}) %collective-permute-start.9) | collective-permute-done | bytes 131104 | tf_op jit(solution)/shard_map/ppermute | solution.py:17
  64.4 0.1 add_bitcast_fusion
  64.6 0.8 %copy.23 = f32[128,2,128]{2,1,0:T(2,128)} copy(f32[128,2,128]{2,0,1:T(8,128)S(1)} %get-tuple-element.16) | data formatting | bytes 262144
  65.3 0.8 %copy.24 = f32[128,2,128]{2,1,0:T(2,128)} copy(f32[128,2,128]{2,0,1:T(8,128)S(1)} %get-tuple-element.15) | data formatting | bytes 262144
  (9 shorter events, 0.1 us)
Async XLA Ops:
  0.6 14.6 %copy-start.1 = (bf16[128,8,128]{2,1,0:T(8,128)(2,1)S(1)}, bf16[128,8,128]{2,1,0:T(8,128)(2,1)}, u32[]{:S(2)}) copy-start(bf16[128,8,128]{2,1,0:T(8,128)(2,1)} %param.10) | copy-start | bytes 786436
  0.6 14.6 %copy-start = (bf16[128,8,128]{2,1,0:T(8,128)(2,1)S(1)}, bf16[128,8,128]{2,1,0:T(8,128)(2,1)}, u32[]{:S(2)}) copy-start(bf16[128,8,128]{2,1,0:T(8,128)(2,1)} %param.9) | copy-start | bytes 786436
  3.2 12.3 %collective-permute-start = (bf16[528,128]{1,0:T(8,128)(2,1)S(1)}, bf16[528,128]{1,0:T(8,128)(2,1)S(1)}, u32[]{:S(2)}, u32[]{:S(2)}) collective-permute-start(bf16[528,128]{1,0:T(8,128)(2,1)S(1)} %maximum_maximum_fusion), channel_id=1, source_target_pairs={{0,2},{2,4},{4,6},{6,8},{8,10},{10,12},{12,14},{14,0},{1,3},{3,5},... | collective-permute-start | bytes 405512 | tf_op jit(solution)/shard_map/ppermute | solution.py:17
  6.3 10.7 %collective-permute-start.1 = (bf16[528,128]{1,0:T(8,128)(2,1)S(1)}, bf16[528,128]{1,0:T(8,128)(2,1)S(1)}, u32[]{:S(2)}, u32[]{:S(2)}) collective-permute-start(bf16[528,128]{1,0:T(8,128)(2,1)S(1)} %maximum_maximum_fusion), channel_id=1, source_target_pairs={{0,4},{2,6},{4,8},{6,10},{8,12},{10,14},{12,0},{14,2},{1,5},{3,7},... | collective-permute-start | bytes 405512 | tf_op jit(solution)/shard_map/ppermute | solution.py:17
  7.8 16.8 %collective-permute-start.2 = (bf16[528,128]{1,0:T(8,128)(2,1)S(1)}, bf16[528,128]{1,0:T(8,128)(2,1)S(1)}, u32[]{:S(2)}, u32[]{:S(2)}) collective-permute-start(bf16[528,128]{1,0:T(8,128)(2,1)S(1)} %maximum_maximum_fusion), channel_id=1, source_target_pairs={{0,6},{2,8},{4,10},{6,12},{8,14},{10,0},{12,2},{14,4},{1,7},{3,9},... | collective-permute-start | bytes 405512 | tf_op jit(solution)/shard_map/ppermute | solution.py:17
  10.4 14.6 %collective-permute-start.3 = (bf16[528,128]{1,0:T(8,128)(2,1)S(1)}, bf16[528,128]{1,0:T(8,128)(2,1)S(1)}, u32[]{:S(2)}, u32[]{:S(2)}) collective-permute-start(bf16[528,128]{1,0:T(8,128)(2,1)S(1)} %maximum_maximum_fusion), channel_id=1, source_target_pairs={{0,8},{2,10},{4,12},{6,14},{8,0},{10,2},{12,4},{14,6},{1,9},{3,11}... | collective-permute-start | bytes 405512 | tf_op jit(solution)/shard_map/ppermute | solution.py:17
  11.6 13.4 %collective-permute-start.4 = (bf16[528,128]{1,0:T(8,128)(2,1)S(1)}, bf16[528,128]{1,0:T(8,128)(2,1)S(1)}, u32[]{:S(2)}, u32[]{:S(2)}) collective-permute-start(bf16[528,128]{1,0:T(8,128)(2,1)S(1)} %maximum_maximum_fusion), channel_id=1, source_target_pairs={{0,10},{2,12},{4,14},{6,0},{8,2},{10,4},{12,6},{14,8},{1,11},{3,13... | collective-permute-start | bytes 405512 | tf_op jit(solution)/shard_map/ppermute | solution.py:17
  15.5 9.5 %collective-permute-start.5 = (bf16[528,128]{1,0:T(8,128)(2,1)S(1)}, bf16[528,128]{1,0:T(8,128)(2,1)S(1)}, u32[]{:S(2)}, u32[]{:S(2)}) collective-permute-start(bf16[528,128]{1,0:T(8,128)(2,1)S(1)} %maximum_maximum_fusion), channel_id=1, source_target_pairs={{0,12},{2,14},{4,0},{6,2},{8,4},{10,6},{12,8},{14,10},{1,13},{3,15... | collective-permute-start | bytes 405512 | tf_op jit(solution)/shard_map/ppermute | solution.py:17
  16.9 8.1 %collective-permute-start.6 = (bf16[528,128]{1,0:T(8,128)(2,1)S(1)}, bf16[528,128]{1,0:T(8,128)(2,1)S(1)}, u32[]{:S(2)}, u32[]{:S(2)}) collective-permute-start(bf16[528,128]{1,0:T(8,128)(2,1)S(1)} %maximum_maximum_fusion), channel_id=1, source_target_pairs={{0,14},{2,0},{4,2},{6,4},{8,6},{10,8},{12,10},{14,12},{1,15},{3,1}... | collective-permute-start | bytes 405512 | tf_op jit(solution)/shard_map/ppermute | solution.py:17
  30.5 20.6 %collective-permute-start.10 = (bf16[4,128,128]{2,1,0:T(8,128)(2,1)S(1)}, bf16[4,128,128]{2,1,0:T(8,128)(2,1)S(1)}, u32[]{:S(2)}, u32[]{:S(2)}) collective-permute-start(bf16[4,128,128]{2,1,0:T(8,128)(2,1)S(1)} %get-tuple-element.21), channel_id=1, source_target_pairs={{0,8},{2,10},{4,12},{6,14},{8,0},{10,2},{12,4},{14,6},{1,9},{3,11}... | collective-permute-start | bytes 393224 | tf_op jit(solution)/shard_map/ppermute | solution.py:17
  38.6 20.0 %collective-permute-start.11 = (bf16[4,128,128]{2,1,0:T(8,128)(2,1)S(1)}, bf16[4,128,128]{2,1,0:T(8,128)(2,1)S(1)}, u32[]{:S(2)}, u32[]{:S(2)}) collective-permute-start(bf16[4,128,128]{2,1,0:T(8,128)(2,1)S(1)} %get-tuple-element.20), channel_id=1, source_target_pairs={{0,6},{2,8},{4,10},{6,12},{8,14},{10,0},{12,2},{14,4},{1,7},{3,9},... | collective-permute-start | bytes 393224 | tf_op jit(solution)/shard_map/ppermute | solution.py:17
  42.1 17.5 %collective-permute-start.12 = (bf16[4,128,128]{2,1,0:T(8,128)(2,1)S(1)}, bf16[4,128,128]{2,1,0:T(8,128)(2,1)S(1)}, u32[]{:S(2)}, u32[]{:S(2)}) collective-permute-start(bf16[4,128,128]{2,1,0:T(8,128)(2,1)S(1)} %get-tuple-element.19), channel_id=1, source_target_pairs={{0,4},{2,6},{4,8},{6,10},{8,12},{10,14},{12,0},{14,2},{1,5},{3,7},... | collective-permute-start | bytes 393224 | tf_op jit(solution)/shard_map/ppermute | solution.py:17
  42.1 17.5 %collective-permute-start.13 = (bf16[4,128,128]{2,1,0:T(8,128)(2,1)S(1)}, bf16[4,128,128]{2,1,0:T(8,128)(2,1)S(1)}, u32[]{:S(2)}, u32[]{:S(2)}) collective-permute-start(bf16[4,128,128]{2,1,0:T(8,128)(2,1)S(1)} %get-tuple-element.18), channel_id=1, source_target_pairs={{0,2},{2,4},{4,6},{6,8},{8,10},{10,12},{12,14},{14,0},{1,3},{3,5},... | collective-permute-start | bytes 393224 | tf_op jit(solution)/shard_map/ppermute | solution.py:17
  42.7 17.0 %collective-permute-start.7 = (bf16[4,128,128]{2,1,0:T(8,128)(2,1)S(1)}, bf16[4,128,128]{2,1,0:T(8,128)(2,1)S(1)}, u32[]{:S(2)}, u32[]{:S(2)}) collective-permute-start(bf16[4,128,128]{2,1,0:T(8,128)(2,1)S(1)} %get-tuple-element.17), channel_id=1, source_target_pairs={{0,14},{2,0},{4,2},{6,4},{8,6},{10,8},{12,10},{14,12},{1,15},{3,1}... | collective-permute-start | bytes 393224 | tf_op jit(solution)/shard_map/ppermute | solution.py:17
  51.1 8.6 %collective-permute-start.8 = (bf16[4,128,128]{2,1,0:T(8,128)(2,1)S(1)}, bf16[4,128,128]{2,1,0:T(8,128)(2,1)S(1)}, u32[]{:S(2)}, u32[]{:S(2)}) collective-permute-start(bf16[4,128,128]{2,1,0:T(8,128)(2,1)S(1)} %get-tuple-element.23), channel_id=1, source_target_pairs={{0,12},{2,14},{4,0},{6,2},{8,4},{10,6},{12,8},{14,10},{1,13},{3,15... | collective-permute-start | bytes 393224 | tf_op jit(solution)/shard_map/ppermute | solution.py:17
  58.6 5.9 %collective-permute-start.9 = (bf16[4,128,128]{2,1,0:T(8,128)(2,1)S(1)}, bf16[4,128,128]{2,1,0:T(8,128)(2,1)S(1)}, u32[]{:S(2)}, u32[]{:S(2)}) collective-permute-start(bf16[4,128,128]{2,1,0:T(8,128)(2,1)S(1)} %get-tuple-element.22), channel_id=1, source_target_pairs={{0,10},{2,12},{4,14},{6,0},{8,2},{10,4},{12,6},{14,8},{1,11},{3,13... | collective-permute-start | bytes 393224 | tf_op jit(solution)/shard_map/ppermute | solution.py:17

commit v5 on v4

--- a/solution.py
+++ b/solution.py
@@ -153,12 +153,12 @@
         gathered,
         kv_heads,
     )
-    arrived = [passed_along(parts[s - 1], "ctx", -s) for s in range(1, cycle_size)]
-    key_grad = own_part[:kv_heads]
-    value_grad = own_part[kv_heads:]
-    for piece in arrived:
-        key_grad = key_grad + piece[:kv_heads].astype(jnp.float32)
-        value_grad = value_grad + piece[kv_heads:].astype(jnp.float32)
+    me = lax.axis_index("ctx")
+    outgoing = jnp.concatenate([jnp.zeros_like(parts[:1]), parts], axis=0)
+    outgoing = jnp.take(outgoing, (me - jnp.arange(cycle_size)) % cycle_size, axis=0)
+    arrived = lax.all_to_all(outgoing, "ctx", 0, 0, tiled=True).astype(jnp.float32)
+    key_grad = own_part[:kv_heads] + jnp.sum(arrived[:, :kv_heads], axis=0)
+    value_grad = own_part[kv_heads:] + jnp.sum(arrived[:, kv_heads:], axis=0)
     return (
         dq_t.transpose(1, 0, 2),
         key_grad.transpose(1, 0, 2),

time: 66.3 us -> 81.4 us (1.23)
  waiting for transfers between devices: 23 us -> 41.9 us
  starting transfers between devices: 30.2 us -> 24 us
  other arithmetic: 0.64 us -> 2.05 us
  local copies, waits for them, and re-layouts: 5.63 us -> 6.51 us
    all_to_all x0 -> x1, waiting for transfers between devices: none -> 23.1 us  [on_device(): lax.all_to_all(outgoing, 'ctx', 0, 0, tiled=True).astype(jnp.float32)]
    ppermute x14 -> x7, starting transfers between devices: 30.2 us -> 14 us  [passed_along(): lax.ppermute(value, axis, [(i, (i + by) % peers) for i in range(peers)])]
    all_to_all x0 -> x1, starting transfers between devices: none -> 10 us  [on_device(): lax.all_to_all(outgoing, 'ctx', 0, 0, tiled=True).astype(jnp.float32)]
    ppermute x14 -> x7, waiting for transfers between devices: 23 us -> 18.8 us  [passed_along(): lax.ppermute(value, axis, [(i, (i + by) % peers) for i in range(peers)])]
    select_n x0 -> x2, other arithmetic: none -> 1.15 us  [on_device(): jnp.take(outgoing, (me - jnp.arange(cycle_size)) % cycle_size, axis=0)]
    transpose x1, local copies, waits for them, and re-layouts: 0.09 us -> 1.12 us  [on_device(): forward_out.transpose(1, 0, 2)]
    unnamed x14 -> x12, local copies, waits for them, and re-layouts: 3.72 us -> 2.77 us
  transfers between devices with their start and end apart: 14 -> 8, of which waited for: 5 -> 4; matrix products, arithmetic and copies ran while one was open for 4% -> 3% of each run, Pallas kernels for 0% -> 0%
where the time goes in v5:
time: 81.4 us; the launch traced here: 81.1 us
  waiting for transfers between devices  41.9 us (51%)
  starting transfers between devices  24 us (29%)
  local copies, waits for them, and re-layouts  6.51 us (8%)
  Pallas kernels  5.1 us (6%)
  other arithmetic  2.05 us (3%)
  between operations  1.53 us (2%)
    all_to_all x1, waiting for transfers between devices, on_device(): lax.all_to_all(outgoing, 'ctx', 0, 0, tiled=True).astype(jnp.float32)  23.1 us
    ppermute x7, waiting for transfers between devices, passed_along(): lax.ppermute(value, axis, [(i, (i + by) % peers) for i in range(peers)])  18.8 us
    ppermute x7, starting transfers between devices, passed_along(): lax.ppermute(value, axis, [(i, (i + by) % peers) for i in range(peers)])  14 us
    all_to_all x1, starting transfers between devices, on_device(): lax.all_to_all(outgoing, 'ctx', 0, 0, tiled=True).astype(jnp.float32)  10 us
    pallas_call x1, Pallas kernels, local_backward(): pl.pallas_call(functools.partial(backward_kernel, kv_heads=kv_heads, chun...  5.1 us
    unnamed x12, local copies, waits for them, and re-layouts  2.77 us
  transfers between devices with their start and end apart: 8, of which 4 were waited for; matrix products, arithmetic and copies ran while one was open for 3% of the time, Pallas kernels for 0%

profile of v5, /device:TPU:0, one launch (start us, length us, event | category | flops | bytes accessed | tf_op | source)
XLA Modules:
  0.0 81.1 jit_solution(931349421090374380)
XLA Ops:
  0.6 0.0 copy-start
  1.3 0.9 %copy.17 = bf16[2,128,128]{2,1,0:T(8,128)(2,1)S(1)} copy(bf16[2,128,128]{2,0,1:T(2,128)(2,1)} %bitcast.41) | data formatting | bytes 131072 | tf_op jit(solution)/shard_map/transpose | solution.py:138
  2.2 0.9 %copy.18 = bf16[2,128,128]{2,1,0:T(8,128)(2,1)S(1)} copy(bf16[2,128,128]{2,0,1:T(2,128)(2,1)} %bitcast.42) | data formatting | bytes 131072 | tf_op jit(solution)/shard_map/transpose | solution.py:139
  3.1 0.1 maximum_maximum_fusion
  3.2 5.1 %collective-permute-start.5 = (bf16[528,128]{1,0:T(8,128)(2,1)S(1)}, bf16[528,128]{1,0:T(8,128)(2,1)S(1)}, u32[]{:S(2)}, u32[]{:S(2)}) collective-permute-start(bf16[528,128]{1,0:T(8,128)(2,1)S(1)} %maximum_maximum_fusion), channel_id=1, source_target_pairs={{0,12},{2,14},{4,0},{6,2},{8,4},{10,6},{12,8},{14,10},{1,13},{3,15... | collective-permute-start | bytes 405512 | tf_op jit(solution)/shard_map/ppermute | solution.py:17
  8.3 0.4 collective-permute-start.4
  8.7 3.5 %collective-permute-start.3 = (bf16[528,128]{1,0:T(8,128)(2,1)S(1)}, bf16[528,128]{1,0:T(8,128)(2,1)S(1)}, u32[]{:S(2)}, u32[]{:S(2)}) collective-permute-start(bf16[528,128]{1,0:T(8,128)(2,1)S(1)} %maximum_maximum_fusion), channel_id=1, source_target_pairs={{0,8},{2,10},{4,12},{6,14},{8,0},{10,2},{12,4},{14,6},{1,9},{3,11}... | collective-permute-start | bytes 405512 | tf_op jit(solution)/shard_map/ppermute | solution.py:17
  12.2 0.0 collective-permute-start.2
  12.2 1.5 %collective-permute-start = (bf16[528,128]{1,0:T(8,128)(2,1)S(1)}, bf16[528,128]{1,0:T(8,128)(2,1)S(1)}, u32[]{:S(2)}, u32[]{:S(2)}) collective-permute-start(bf16[528,128]{1,0:T(8,128)(2,1)S(1)} %maximum_maximum_fusion), channel_id=1, source_target_pairs={{0,2},{2,4},{4,6},{6,8},{8,10},{10,12},{12,14},{14,0},{1,3},{3,5},... | collective-permute-start | bytes 405512 | tf_op jit(solution)/shard_map/ppermute | solution.py:17
  13.7 0.1 bitcast_dynamic-update-slice_fusion.7
  13.8 1.1 %copy_bitcast_fusion = (bf16[8,128,128]{2,1,0:T(8,128)(2,1)S(1)}, bf16[8,128,128]{2,1,0:T(8,128)(2,1)S(1)}) fusion(bf16[128,8,128]{2,1,0:T(8,128)(2,1)} %param.9, bf16[128,8,128]{2,1,0:T(8,128)(2,1)} %param.10), kind=kLoop, calls=%fused_computation.4 | loop fusion | bytes 1048576 | tf_op jit(solution)/shard_map/transpose | solution.py:152
  15.0 0.0 copy-done
  15.0 9.7 %collective-permute-done = bf16[528,128]{1,0:T(8,128)(2,1)S(1)} collective-permute-done((bf16[528,128]{1,0:T(8,128)(2,1)S(1)}, bf16[528,128]{1,0:T(8,128)(2,1)S(1)}, u32[]{:S(2)}, u32[]{:S(2)}) %collective-permute-start) | collective-permute-done | bytes 135200 | tf_op jit(solution)/shard_map/ppermute | solution.py:17
  24.7 1.5 %collective-permute-start.1 = (bf16[528,128]{1,0:T(8,128)(2,1)S(1)}, bf16[528,128]{1,0:T(8,128)(2,1)S(1)}, u32[]{:S(2)}, u32[]{:S(2)}) collective-permute-start(bf16[528,128]{1,0:T(8,128)(2,1)S(1)} %maximum_maximum_fusion), channel_id=1, source_target_pairs={{0,4},{2,6},{4,8},{6,10},{8,12},{10,14},{12,0},{14,2},{1,5},{3,7},... | collective-permute-start | bytes 405512 | tf_op jit(solution)/shard_map/ppermute | solution.py:17
  26.3 5.3 %collective-permute-done.1 = bf16[528,128]{1,0:T(8,128)(2,1)S(1)} collective-permute-done((bf16[528,128]{1,0:T(8,128)(2,1)S(1)}, bf16[528,128]{1,0:T(8,128)(2,1)S(1)}, u32[]{:S(2)}, u32[]{:S(2)}) %collective-permute-start.1) | collective-permute-done | bytes 135200 | tf_op jit(solution)/shard_map/ppermute | solution.py:17
  31.5 2.0 %collective-permute-start.6 = (bf16[528,128]{1,0:T(8,128)(2,1)S(1)}, bf16[528,128]{1,0:T(8,128)(2,1)S(1)}, u32[]{:S(2)}, u32[]{:S(2)}) collective-permute-start(bf16[528,128]{1,0:T(8,128)(2,1)S(1)} %maximum_maximum_fusion), channel_id=1, source_target_pairs={{0,14},{2,0},{4,2},{6,4},{8,6},{10,8},{12,10},{14,12},{1,15},{3,1}... | collective-permute-start | bytes 405512 | tf_op jit(solution)/shard_map/ppermute | solution.py:17
  33.5 0.0 collective-permute-done.2
  33.6 0.0 collective-permute-done.3
  33.6 0.0 collective-permute-done.4
  33.6 0.0 collective-permute-done.5
  33.7 3.9 %collective-permute-done.6 = bf16[528,128]{1,0:T(8,128)(2,1)S(1)} collective-permute-done((bf16[528,128]{1,0:T(8,128)(2,1)S(1)}, bf16[528,128]{1,0:T(8,128)(2,1)S(1)}, u32[]{:S(2)}, u32[]{:S(2)}) %collective-permute-start.6) | collective-permute-done | bytes 135200 | tf_op jit(solution)/shard_map/ppermute | solution.py:17
  37.6 0.2 fusion.1.offs_ref
  37.8 5.1 %shard_map.85 = (f32[8,128,128]{2,1,0:T(8,128)S(1)}, f32[4,128,128]{2,1,0:T(8,128)S(1)}, bf16[7,4,128,128]{3,2,1,0:T(8,128)(2,1)S(1)}) custom-call(s32[8]{0:T(128)S(1)} %fusion.1.offs_ref, s32[1]{0:T(128)S(6)} %copy.36.own_ref, bf16[8,128,128]{2,1,0:T(8,128)(2,1)S(1)} %bitcast.36, bf16[8,128,128]{2,1,0:T(8,128)(2,1)S(1)} %get-tuple-element.20.do_ref, ...), custom_call_target="tpu_custom_call" | custom-call | flops 1610612736 | bytes 2654208 | tf_op jit(solution)/shard_map/pallas_call | solution.py:111
  42.9 0.1 concatenate.7
  43.1 0.8 gather_fusion
  43.8 1.1 %broadcast_select_fusion = bf16[8,4,128,128]{3,2,1,0:T(8,128)(2,1)} fusion(bf16[8,4,128,128]{3,2,1,0:T(8,128)(2,1)S(1)} %gather_fusion, pred[8]{0:T(512)(128)(4,1)S(1)} %compare_and_fusion), kind=kLoop, calls=%fused_computation.3 | loop fusion | flops 524288 | bytes 2097160 | tf_op jit(solution)/shard_map/jit(_take)/select_n | solution.py:158
  45.0 10.0 %all-to-all-start = ((bf16[8,4,128,128]{3,2,1,0:T(8,128)(2,1)}), bf16[8,4,128,128]{3,2,1,0:T(8,128)(2,1)S(1)}, u32[]{:S(2)}, u32[]{:S(2)}) async-start(bf16[8,4,128,128]{3,2,1,0:T(8,128)(2,1)} %broadcast_select_fusion), calls=%async_computation | async-start | bytes 2097152 | tf_op jit(solution)/shard_map/all_to_all | solution.py:159
  55.0 1.1 %copy.22 = f32[128,8,128]{2,1,0:T(8,128)} copy(f32[128,8,128]{2,0,1:T(8,128)S(1)} %bitcast.35) | data formatting | bytes 1048576
  56.1 23.1 %all-to-all-done = bf16[8,4,128,128]{3,2,1,0:T(8,128)(2,1)S(1)} async-done(((bf16[8,4,128,128]{3,2,1,0:T(8,128)(2,1)}), bf16[8,4,128,128]{3,2,1,0:T(8,128)(2,1)S(1)}, u32[]{:S(2)}, u32[]{:S(2)}) %all-to-all-start) | async-done | bytes 1048608 | tf_op jit(solution)/shard_map/all_to_all | solution.py:159
  79.2 0.2 convert_element_type.29
  79.4 0.1 slice_reduce_fusion
  79.6 0.8 copy.24
  80.3 0.8 copy.23
  (14 shorter events, 0.2 us)
Async XLA Ops:
  0.6 14.3 %copy-start = (bf16[128,8,128]{2,1,0:T(8,128)(2,1)S(1)}, bf16[128,8,128]{2,1,0:T(8,128)(2,1)}, u32[]{:S(2)}) copy-start(bf16[128,8,128]{2,1,0:T(8,128)(2,1)} %param.6) | copy-start | bytes 786436
  3.2 30.4 %collective-permute-start.5 = (bf16[528,128]{1,0:T(8,128)(2,1)S(1)}, bf16[528,128]{1,0:T(8,128)(2,1)S(1)}, u32[]{:S(2)}, u32[]{:S(2)}) collective-permute-start(bf16[528,128]{1,0:T(8,128)(2,1)S(1)} %maximum_maximum_fusion), channel_id=1, source_target_pairs={{0,12},{2,14},{4,0},{6,2},{8,4},{10,6},{12,8},{14,10},{1,13},{3,15... | collective-permute-start | bytes 405512 | tf_op jit(solution)/shard_map/ppermute | solution.py:17
  8.3 25.3 %collective-permute-start.4 = (bf16[528,128]{1,0:T(8,128)(2,1)S(1)}, bf16[528,128]{1,0:T(8,128)(2,1)S(1)}, u32[]{:S(2)}, u32[]{:S(2)}) collective-permute-start(bf16[528,128]{1,0:T(8,128)(2,1)S(1)} %maximum_maximum_fusion), channel_id=1, source_target_pairs={{0,10},{2,12},{4,14},{6,0},{8,2},{10,4},{12,6},{14,8},{1,11},{3,13... | collective-permute-start | bytes 405512 | tf_op jit(solution)/shard_map/ppermute | solution.py:17
  8.7 24.9 %collective-permute-start.3 = (bf16[528,128]{1,0:T(8,128)(2,1)S(1)}, bf16[528,128]{1,0:T(8,128)(2,1)S(1)}, u32[]{:S(2)}, u32[]{:S(2)}) collective-permute-start(bf16[528,128]{1,0:T(8,128)(2,1)S(1)} %maximum_maximum_fusion), channel_id=1, source_target_pairs={{0,8},{2,10},{4,12},{6,14},{8,0},{10,2},{12,4},{14,6},{1,9},{3,11}... | collective-permute-start | bytes 405512 | tf_op jit(solution)/shard_map/ppermute | solution.py:17
  12.2 21.3 %collective-permute-start.2 = (bf16[528,128]{1,0:T(8,128)(2,1)S(1)}, bf16[528,128]{1,0:T(8,128)(2,1)S(1)}, u32[]{:S(2)}, u32[]{:S(2)}) collective-permute-start(bf16[528,128]{1,0:T(8,128)(2,1)S(1)} %maximum_maximum_fusion), channel_id=1, source_target_pairs={{0,6},{2,8},{4,10},{6,12},{8,14},{10,0},{12,2},{14,4},{1,7},{3,9},... | collective-permute-start | bytes 405512 | tf_op jit(solution)/shard_map/ppermute | solution.py:17
  12.2 12.5 %collective-permute-start = (bf16[528,128]{1,0:T(8,128)(2,1)S(1)}, bf16[528,128]{1,0:T(8,128)(2,1)S(1)}, u32[]{:S(2)}, u32[]{:S(2)}) collective-permute-start(bf16[528,128]{1,0:T(8,128)(2,1)S(1)} %maximum_maximum_fusion), channel_id=1, source_target_pairs={{0,2},{2,4},{4,6},{6,8},{8,10},{10,12},{12,14},{14,0},{1,3},{3,5},... | collective-permute-start | bytes 405512 | tf_op jit(solution)/shard_map/ppermute | solution.py:17
  24.7 6.8 %collective-permute-start.1 = (bf16[528,128]{1,0:T(8,128)(2,1)S(1)}, bf16[528,128]{1,0:T(8,128)(2,1)S(1)}, u32[]{:S(2)}, u32[]{:S(2)}) collective-permute-start(bf16[528,128]{1,0:T(8,128)(2,1)S(1)} %maximum_maximum_fusion), channel_id=1, source_target_pairs={{0,4},{2,6},{4,8},{6,10},{8,12},{10,14},{12,0},{14,2},{1,5},{3,7},... | collective-permute-start | bytes 405512 | tf_op jit(solution)/shard_map/ppermute | solution.py:17
  31.5 6.1 %collective-permute-start.6 = (bf16[528,128]{1,0:T(8,128)(2,1)S(1)}, bf16[528,128]{1,0:T(8,128)(2,1)S(1)}, u32[]{:S(2)}, u32[]{:S(2)}) collective-permute-start(bf16[528,128]{1,0:T(8,128)(2,1)S(1)} %maximum_maximum_fusion), channel_id=1, source_target_pairs={{0,14},{2,0},{4,2},{6,4},{8,6},{10,8},{12,10},{14,12},{1,15},{3,1}... | collective-permute-start | bytes 405512 | tf_op jit(solution)/shard_map/ppermute | solution.py:17
  45.0 34.2 %all-to-all-start = ((bf16[8,4,128,128]{3,2,1,0:T(8,128)(2,1)}), bf16[8,4,128,128]{3,2,1,0:T(8,128)(2,1)S(1)}, u32[]{:S(2)}, u32[]{:S(2)}) async-start(bf16[8,4,128,128]{3,2,1,0:T(8,128)(2,1)} %broadcast_select_fusion), calls=%async_computation | async-start | bytes 2097152 | tf_op jit(solution)/shard_map/all_to_all | solution.py:159

commit v6 on v5

--- a/solution.py
+++ b/solution.py
@@ -12,14 +12,18 @@
 MASKED = -1e30
 
 
-def passed_along(value, axis, by):
-    peers = lax.axis_size(axis)
-    return lax.ppermute(value, axis, [(i, (i + by) % peers) for i in range(peers)])
+def mate_pairs(peers, by):
+    half = peers // 2
+    return [(i, half * (i // half) + (i % half + by) % half) for i in range(peers)]
+
+
+def mirror_pairs(peers):
+    return [(i, (i + peers // 2) % peers) for i in range(peers)]
 
 
 def backward_kernel(
-    offs_ref, own_ref, q_ref, do_ref, fo_ref, kv_ref, dq_ref, own_part_ref, parts_ref,
-    *, kv_heads, chunk_blocks
+    offs_ref, own_ref, q_ref, do_ref, fo_ref, kv_ref, dq_ref, own_part_ref, mirror_part_ref,
+    parts_ref, *, kv_heads, chunk_blocks
 ):
     q_heads, tok_rows, head_width = q_ref.shape
     blocks = kv_ref.shape[0]
@@ -97,6 +101,9 @@
                 else:
                     parts_ref[block - 1, g] = dk[piece].astype(jnp.bfloat16)
                     parts_ref[block - 1, kv_heads + g] = dv[piece].astype(jnp.bfloat16)
+                if block == blocks // 2:
+                    mirror_part_ref[g] = dk[piece]
+                    mirror_part_ref[kv_heads + g] = dv[piece]
         dq_ref[heads] = (scale * dq).reshape(heads_per_group, tok_rows, head_width)
 
 
@@ -113,10 +120,11 @@
         out_shape=(
             jax.ShapeDtypeStruct((q_heads, tok_rows, head_width), jnp.float32),
             jax.ShapeDtypeStruct((2 * kv_heads, tok_rows, head_width), jnp.float32),
+            jax.ShapeDtypeStruct((2 * kv_heads, tok_rows, head_width), jnp.float32),
             jax.ShapeDtypeStruct((blocks - 1, 2 * kv_heads, tok_rows, head_width), jnp.bfloat16),
         ),
         in_specs=[smem, smem, vmem, vmem, vmem, vmem],
-        out_specs=(vmem, vmem, vmem),
+        out_specs=(vmem, vmem, vmem, vmem),
         compiler_params=pltpu.CompilerParams(vmem_limit_bytes=48 * 1024 * 1024),
         cost_estimate=pl.CostEstimate(
             flops=12 * rows * keys * head_width,
@@ -133,18 +141,18 @@
     kv_rows = tok_rows * kv_heads
 
     offset_rows = jnp.full((OFFSET_ROWS, head_width), block_offsets[0], jnp.float32).astype(jnp.bfloat16)
-    slab = jnp.concatenate(
-        [
-            key_vectors.transpose(1, 0, 2).reshape(kv_rows, head_width),
-            value_rows.transpose(1, 0, 2).reshape(kv_rows, head_width),
-            offset_rows,
-        ],
-        axis=0,
-    )
-    gathered = jnp.stack([slab] + [passed_along(slab, "ctx", s) for s in range(1, cycle_size)])
+    paired = jnp.concatenate([key_vectors, value_rows], axis=1).transpose(1, 0, 2)
+    slab = jnp.concatenate([paired.reshape(2 * kv_rows, head_width), offset_rows], axis=0)
+    half = cycle_size // 2
+    from_mates = [lax.ppermute(slab, "ctx", mate_pairs(cycle_size, k)) for k in range(1, half)]
+    from_mirror = lax.ppermute(slab, "ctx", mirror_pairs(cycle_size))
+    handed_on = [
+        lax.ppermute(from_mirror, "ctx", mate_pairs(cycle_size, k)) for k in range(1, half)
+    ]
+    gathered = jnp.stack([slab] + from_mates + [from_mirror] + handed_on)
     all_offsets = gathered[:, 2 * kv_rows, 0].astype(jnp.float32).astype(jnp.int32)
 
-    dq_t, own_part, parts = local_backward(
+    dq_t, own_part, mirror_part, parts = local_backward(
         all_offsets,
         block_offsets,
         query_vectors.transpose(1, 0, 2),
@@ -153,17 +161,18 @@
         gathered,
         kv_heads,
     )
-    me = lax.axis_index("ctx")
-    outgoing = jnp.concatenate([jnp.zeros_like(parts[:1]), parts], axis=0)
-    outgoing = jnp.take(outgoing, (me - jnp.arange(cycle_size)) % cycle_size, axis=0)
-    arrived = lax.all_to_all(outgoing, "ctx", 0, 0, tiled=True).astype(jnp.float32)
-    key_grad = own_part[:kv_heads] + jnp.sum(arrived[:, :kv_heads], axis=0)
-    value_grad = own_part[kv_heads:] + jnp.sum(arrived[:, kv_heads:], axis=0)
-    return (
-        dq_t.transpose(1, 0, 2),
-        key_grad.transpose(1, 0, 2),
-        value_grad.transpose(1, 0, 2),
-    )
+    own_total = own_part
+    mirror_total = mirror_part
+    for k in range(1, half):
+        pair = jnp.stack([parts[k - 1], parts[half + k - 1]])
+        arrived = lax.ppermute(pair, "ctx", mate_pairs(cycle_size, half - k)).astype(jnp.float32)
+        own_total = own_total + arrived[0]
+        mirror_total = mirror_total + arrived[1]
+    crossed = lax.ppermute(mirror_total.astype(jnp.bfloat16), "ctx", mirror_pairs(cycle_size))
+    total = own_total + crossed.astype(jnp.float32)
+    key_grad = total[:kv_heads].transpose(1, 0, 2)
+    value_grad = total[kv_heads:].transpose(1, 0, 2)
+    return (dq_t.transpose(1, 0, 2), key_grad, value_grad)
 
 
 def solution(mesh):

time: 81.4 us -> 53.2 us (0.65)
  waiting for transfers between devices: 41.9 us -> 20.7 us
  starting transfers between devices: 24 us -> 20.1 us
  local copies, waits for them, and re-layouts: 6.51 us -> 4.04 us
    all_to_all x1 -> x0, waiting for transfers between devices: 23.1 us -> none  [on_device(): lax.all_to_all(outgoing, 'ctx', 0, 0, tiled=True).astype(jnp.float32)]
    all_to_all x1 -> x0, starting transfers between devices: 10 us -> none  [on_device(): lax.all_to_all(outgoing, 'ctx', 0, 0, tiled=True).astype(jnp.float32)]
    ppermute x7 -> x11, starting transfers between devices: 14 us -> 20.1 us  [the longest x3 6.42 us: on_device(): lax.ppermute(from_mirror, 'ctx', mate_pairs(cycle_size, k))]
    ppermute x7 -> x11, waiting for transfers between devices: 18.8 us -> 20.7 us  [the longest x3 9.62 us: on_device(): lax.ppermute(pair, 'ctx', mate_pairs(cycle_size, half - k))]
    transpose x2, local copies, waits for them, and re-layouts: 1.7 us -> 0.04 us  [the longest x1 0.02 us: on_device(): jnp.concatenate([key_vectors, value_rows], axis=1).transpose(1, 0, 2)]
    select_n x2 -> x0, other arithmetic: 1.15 us -> none  [on_device(): jnp.take(outgoing, (me - jnp.arange(cycle_size)) % cycle_size, axis=0)]
    transpose x1, other arithmetic: 0.03 us -> 1.01 us  [on_device(): jnp.concatenate([key_vectors, value_rows], axis=1).transpose(1, 0, 2)]
    unnamed x12 -> x13, local copies, waits for them, and re-layouts: 2.77 us -> 2.78 us
  transfers between devices with their start and end apart: 8 -> 11, of which waited for: 4 -> 8; matrix products, arithmetic and copies ran while one was open for 3% -> 5% of each run, Pallas kernels for 0% -> 0%
where the time goes in v6:
time: 53.2 us; the launch traced here: 53 us
  waiting for transfers between devices  20.7 us (39%)
  starting transfers between devices  20.1 us (38%)
  Pallas kernels  5.12 us (10%)
  local copies, waits for them, and re-layouts  4.04 us (8%)
  other arithmetic  1.55 us (3%)
  between operations  1.52 us (3%)
    ppermute x3, waiting for transfers between devices, on_device(): lax.ppermute(pair, 'ctx', mate_pairs(cycle_size, half - k))  9.62 us
    ppermute x3, starting transfers between devices, on_device(): lax.ppermute(from_mirror, 'ctx', mate_pairs(cycle_size, k))  6.42 us
    ppermute x3, starting transfers between devices, on_device(): lax.ppermute(slab, 'ctx', mate_pairs(cycle_size, k))  6 us
    ppermute x1, waiting for transfers between devices, on_device(): lax.ppermute(mirror_total.astype(jnp.bfloat16), 'ctx', mirror_pairs(cycle...  5.46 us
    pallas_call x1, Pallas kernels, local_backward(): pl.pallas_call(functools.partial(backward_kernel, kv_heads=kv_heads, chun...  5.12 us
    ppermute x3, starting transfers between devices, on_device(): lax.ppermute(pair, 'ctx', mate_pairs(cycle_size, half - k))  4.28 us
    ppermute x1, waiting for transfers between devices, on_device(): from_mirror = lax.ppermute(slab, 'ctx', mirror_pairs(cycle_size))  3.16 us
    unnamed x13, local copies, waits for them, and re-layouts  2.78 us
  transfers between devices with their start and end apart: 11, of which 8 were waited for; matrix products, arithmetic and copies ran while one was open for 5% of the time, Pallas kernels for 0%

profile of v6, /device:TPU:0, one launch (start us, length us, event | category | flops | bytes accessed | tf_op | source)
XLA Modules:
  0.0 53.0 jit_solution(9954453284364510789)
XLA Ops:
  0.6 0.0 copy-start
  1.3 1.0 %maximum_bitcast_fusion = bf16[4,128,128]{2,0,1:T(4,128)(2,1)S(1)} fusion(bf16[128,2,128]{2,1,0:T(2,128)(2,1)} %param.8, bf16[128,2,128]{2,1,0:T(2,128)(2,1)} %param.7), kind=kLoop, calls=%fused_computation.30 | loop fusion | flops 262144 | bytes 262144 | tf_op jit(solution)/shard_map/transpose | solution.py:144
  2.4 3.0 %collective-permute-start = (bf16[528,128]{1,0:T(8,128)(2,1)S(1)}, bf16[528,128]{1,0:T(8,128)(2,1)S(1)}, u32[]{:S(2)}, u32[]{:S(2)}) collective-permute-start(bf16[528,128]{1,0:T(8,128)(2,1)S(1)} %concatenate.7), channel_id=1, source_target_pairs={{0,2},{2,4},{4,6},{6,0},{8,10},{10,12},{12,14},{14,8},{1,3},{3,5},... | collective-permute-start | bytes 405512 | tf_op jit(solution)/shard_map/ppermute | solution.py:147
  5.4 1.6 %collective-permute-start.1 = (bf16[528,128]{1,0:T(8,128)(2,1)S(1)}, bf16[528,128]{1,0:T(8,128)(2,1)S(1)}, u32[]{:S(2)}, u32[]{:S(2)}) collective-permute-start(bf16[528,128]{1,0:T(8,128)(2,1)S(1)} %concatenate.7), channel_id=1, source_target_pairs={{0,4},{2,6},{4,0},{6,2},{8,12},{10,14},{12,8},{14,10},{1,5},{3,7},... | collective-permute-start | bytes 405512 | tf_op jit(solution)/shard_map/ppermute | solution.py:147
  7.0 1.4 %collective-permute-start.2 = (bf16[528,128]{1,0:T(8,128)(2,1)S(1)}, bf16[528,128]{1,0:T(8,128)(2,1)S(1)}, u32[]{:S(2)}, u32[]{:S(2)}) collective-permute-start(bf16[528,128]{1,0:T(8,128)(2,1)S(1)} %concatenate.7), channel_id=1, source_target_pairs={{0,6},{2,0},{4,2},{6,4},{8,14},{10,8},{12,10},{14,12},{1,7},{3,1},... | collective-permute-start | bytes 405512 | tf_op jit(solution)/shard_map/ppermute | solution.py:147
  8.4 2.6 %collective-permute-start.3 = (bf16[528,128]{1,0:T(8,128)(2,1)S(1)}, bf16[528,128]{1,0:T(8,128)(2,1)S(1)}, u32[]{:S(2)}, u32[]{:S(2)}) collective-permute-start(bf16[528,128]{1,0:T(8,128)(2,1)S(1)} %concatenate.7), channel_id=1, source_target_pairs={{0,8},{2,10},{4,12},{6,14},{8,0},{10,2},{12,4},{14,6},{1,9},{3,11}... | collective-permute-start | bytes 405512 | tf_op jit(solution)/shard_map/ppermute | solution.py:148
  11.0 1.1 %copy_bitcast_fusion = (bf16[8,128,128]{2,1,0:T(8,128)(2,1)S(1)}, bf16[8,128,128]{2,1,0:T(8,128)(2,1)S(1)}) fusion(bf16[128,8,128]{2,1,0:T(8,128)(2,1)} %param.9, bf16[128,8,128]{2,1,0:T(8,128)(2,1)} %param.10), kind=kLoop, calls=%fused_computation.17 | loop fusion | bytes 1048576 | tf_op jit(solution)/shard_map/transpose | solution.py:160
  12.1 0.0 copy-done
  12.2 3.2 %collective-permute-done.3 = bf16[528,128]{1,0:T(8,128)(2,1)S(1)} collective-permute-done((bf16[528,128]{1,0:T(8,128)(2,1)S(1)}, bf16[528,128]{1,0:T(8,128)(2,1)S(1)}, u32[]{:S(2)}, u32[]{:S(2)}) %collective-permute-start.3) | collective-permute-done | bytes 135200 | tf_op jit(solution)/shard_map/ppermute | solution.py:148
  15.4 0.3 collective-permute-start.4
  15.6 3.5 %collective-permute-start.5 = (bf16[528,128]{1,0:T(8,128)(2,1)S(1)}, bf16[528,128]{1,0:T(8,128)(2,1)S(1)}, u32[]{:S(2)}, u32[]{:S(2)}) collective-permute-start(bf16[528,128]{1,0:T(8,128)(2,1)S(1)} %collective-permute-done.3), channel_id=1, source_target_pairs={{0,4},{2,6},{4,0},{6,2},{8,12},{10,14},{12,8},{14,10},{1,5},{3,7},... | collective-permute-start | bytes 405512 | tf_op jit(solution)/shard_map/ppermute | solution.py:150
  19.1 0.0 collective-permute-done
  19.1 2.7 %collective-permute-start.6 = (bf16[528,128]{1,0:T(8,128)(2,1)S(1)}, bf16[528,128]{1,0:T(8,128)(2,1)S(1)}, u32[]{:S(2)}, u32[]{:S(2)}) collective-permute-start(bf16[528,128]{1,0:T(8,128)(2,1)S(1)} %collective-permute-done.3), channel_id=1, source_target_pairs={{0,6},{2,0},{4,2},{6,4},{8,14},{10,8},{12,10},{14,12},{1,7},{3,1},... | collective-permute-start | bytes 405512 | tf_op jit(solution)/shard_map/ppermute | solution.py:150
  21.8 0.0 collective-permute-done.1
  21.8 0.0 collective-permute-done.2
  21.9 0.8 %collective-permute-done.4 = bf16[528,128]{1,0:T(8,128)(2,1)S(1)} collective-permute-done((bf16[528,128]{1,0:T(8,128)(2,1)S(1)}, bf16[528,128]{1,0:T(8,128)(2,1)S(1)}, u32[]{:S(2)}, u32[]{:S(2)}) %collective-permute-start.4) | collective-permute-done | bytes 135200 | tf_op jit(solution)/shard_map/ppermute | solution.py:150
  22.7 0.6 %collective-permute-done.5 = bf16[528,128]{1,0:T(8,128)(2,1)S(1)} collective-permute-done((bf16[528,128]{1,0:T(8,128)(2,1)S(1)}, bf16[528,128]{1,0:T(8,128)(2,1)S(1)}, u32[]{:S(2)}, u32[]{:S(2)}) %collective-permute-start.5) | collective-permute-done | bytes 135200 | tf_op jit(solution)/shard_map/ppermute | solution.py:150
  23.3 1.1 %collective-permute-done.6 = bf16[528,128]{1,0:T(8,128)(2,1)S(1)} collective-permute-done((bf16[528,128]{1,0:T(8,128)(2,1)S(1)}, bf16[528,128]{1,0:T(8,128)(2,1)S(1)}, u32[]{:S(2)}, u32[]{:S(2)}) %collective-permute-start.6) | collective-permute-done | bytes 135200 | tf_op jit(solution)/shard_map/ppermute | solution.py:150
  24.4 0.2 fusion.9.offs_ref
  24.6 5.1 %shard_map.85 = (f32[8,128,128]{2,1,0:T(8,128)S(1)}, f32[4,128,128]{2,1,0:T(8,128)S(1)}, f32[4,128,128]{2,1,0:T(8,128)S(1)}, bf16[7,4,128,128]{3,2,1,0:T(8,128)(2,1)S(1)}) custom-call(s32[8]{0:T(128)S(1)} %fusion.9.offs_ref, s32[1]{0:T(128)S(6)} %copy.34.own_ref, bf16[8,128,128]{2,1,0:T(8,128)(2,1)S(1)} %bitcast.69, ...), custom_call_target="tpu_custom_call" | custom-call | flops 1610612736 | bytes 2654208 | tf_op jit(solution)/shard_map/pallas_call | solution.py:118
  29.8 0.1 fusion.10
  29.9 3.3 %collective-permute-start.7 = (bf16[2,4,128,128]{3,2,1,0:T(8,128)(2,1)S(1)}, bf16[2,4,128,128]{3,2,1,0:T(8,128)(2,1)S(1)}, u32[]{:S(2)}, u32[]{:S(2)}) collective-permute-start(bf16[2,4,128,128]{3,2,1,0:T(8,128)(2,1)S(1)} %pad_maximum_fusion), channel_id=1, source_target_pairs={{0,6},{2,0},{4,2},{6,4},{8,14},{10,8},{12,10},{14,12},{1,7},{3,1},... | collective-permute-start | bytes 786440 | tf_op jit(solution)/shard_map/ppermute | solution.py:168
  33.3 0.1 collective-permute-start.8
  33.4 0.9 %collective-permute-start.9 = (bf16[2,4,128,128]{3,2,1,0:T(8,128)(2,1)S(1)}, bf16[2,4,128,128]{3,2,1,0:T(8,128)(2,1)S(1)}, u32[]{:S(2)}, u32[]{:S(2)}) collective-permute-start(bf16[2,4,128,128]{3,2,1,0:T(8,128)(2,1)S(1)} %pad_maximum_fusion.2), channel_id=1, source_target_pairs={{0,2},{2,4},{4,6},{6,0},{8,10},{10,12},{12,14},{14,8},{1,3},{3,5},... | collective-permute-start | bytes 786440 | tf_op jit(solution)/shard_map/ppermute | solution.py:168
  34.2 5.3 %collective-permute-done.7 = bf16[2,4,128,128]{3,2,1,0:T(8,128)(2,1)S(1)} collective-permute-done((bf16[2,4,128,128]{3,2,1,0:T(8,128)(2,1)S(1)}, bf16[2,4,128,128]{3,2,1,0:T(8,128)(2,1)S(1)}, u32[]{:S(2)}, u32[]{:S(2)}) %collective-permute-start.7) | collective-permute-done | bytes 262176 | tf_op jit(solution)/shard_map/ppermute | solution.py:168
  39.5 3.7 %collective-permute-done.8 = bf16[2,4,128,128]{3,2,1,0:T(8,128)(2,1)S(1)} collective-permute-done((bf16[2,4,128,128]{3,2,1,0:T(8,128)(2,1)S(1)}, bf16[2,4,128,128]{3,2,1,0:T(8,128)(2,1)S(1)}, u32[]{:S(2)}, u32[]{:S(2)}) %collective-permute-start.8) | collective-permute-done | bytes 262176 | tf_op jit(solution)/shard_map/ppermute | solution.py:168
  43.3 0.6 %collective-permute-done.9 = bf16[2,4,128,128]{3,2,1,0:T(8,128)(2,1)S(1)} collective-permute-done((bf16[2,4,128,128]{3,2,1,0:T(8,128)(2,1)S(1)}, bf16[2,4,128,128]{3,2,1,0:T(8,128)(2,1)S(1)}, u32[]{:S(2)}, u32[]{:S(2)}) %collective-permute-start.9) | collective-permute-done | bytes 262176 | tf_op jit(solution)/shard_map/ppermute | solution.py:168
  44.0 0.1 fusion.1
  44.0 0.8 %collective-permute-start.10 = (bf16[4,128,128]{2,1,0:T(8,128)(2,1)S(1)}, bf16[4,128,128]{2,1,0:T(8,128)(2,1)S(1)}, u32[]{:S(2)}, u32[]{:S(2)}) collective-permute-start(bf16[4,128,128]{2,1,0:T(8,128)(2,1)S(1)} %fusion.1), channel_id=1, source_target_pairs={{0,8},{2,10},{4,12},{6,14},{8,0},{10,2},{12,4},{14,6},{1,9},{3,11}... | collective-permute-start | bytes 393224 | tf_op jit(solution)/shard_map/ppermute | solution.py:171
  44.8 1.1 %copy.20 = f32[128,8,128]{2,1,0:T(8,128)} copy(f32[128,8,128]{2,0,1:T(8,128)S(1)} %bitcast.68) | data formatting | bytes 1048576
  45.9 5.5 %collective-permute-done.10 = bf16[4,128,128]{2,1,0:T(8,128)(2,1)S(1)} collective-permute-done((bf16[4,128,128]{2,1,0:T(8,128)(2,1)S(1)}, bf16[4,128,128]{2,1,0:T(8,128)(2,1)S(1)}, u32[]{:S(2)}, u32[]{:S(2)}) %collective-permute-start.10) | collective-permute-done | bytes 131104 | tf_op jit(solution)/shard_map/ppermute | solution.py:171
  51.4 0.1 fusion.5
  51.5 0.8 %copy.21 = f32[128,2,128]{2,1,0:T(2,128)} copy(f32[128,2,128]{2,0,1:T(8,128)S(1)} %get-tuple-element.24) | data formatting | bytes 262144
  52.2 0.8 %copy.22 = f32[128,2,128]{2,1,0:T(2,128)} copy(f32[128,2,128]{2,0,1:T(8,128)S(1)} %get-tuple-element.23) | data formatting | bytes 262144
  (18 shorter events, 0.4 us)
Async XLA Ops:
  0.6 11.5 %copy-start = (bf16[128,8,128]{2,1,0:T(8,128)(2,1)S(1)}, bf16[128,8,128]{2,1,0:T(8,128)(2,1)}, u32[]{:S(2)}) copy-start(bf16[128,8,128]{2,1,0:T(8,128)(2,1)} %param.6) | copy-start | bytes 786436
  2.4 16.7 %collective-permute-start = (bf16[528,128]{1,0:T(8,128)(2,1)S(1)}, bf16[528,128]{1,0:T(8,128)(2,1)S(1)}, u32[]{:S(2)}, u32[]{:S(2)}) collective-permute-start(bf16[528,128]{1,0:T(8,128)(2,1)S(1)} %concatenate.7), channel_id=1, source_target_pairs={{0,2},{2,4},{4,6},{6,0},{8,10},{10,12},{12,14},{14,8},{1,3},{3,5},... | collective-permute-start | bytes 405512 | tf_op jit(solution)/shard_map/ppermute | solution.py:147
  5.4 16.4 %collective-permute-start.1 = (bf16[528,128]{1,0:T(8,128)(2,1)S(1)}, bf16[528,128]{1,0:T(8,128)(2,1)S(1)}, u32[]{:S(2)}, u32[]{:S(2)}) collective-permute-start(bf16[528,128]{1,0:T(8,128)(2,1)S(1)} %concatenate.7), channel_id=1, source_target_pairs={{0,4},{2,6},{4,0},{6,2},{8,12},{10,14},{12,8},{14,10},{1,5},{3,7},... | collective-permute-start | bytes 405512 | tf_op jit(solution)/shard_map/ppermute | solution.py:147
  7.0 14.8 %collective-permute-start.2 = (bf16[528,128]{1,0:T(8,128)(2,1)S(1)}, bf16[528,128]{1,0:T(8,128)(2,1)S(1)}, u32[]{:S(2)}, u32[]{:S(2)}) collective-permute-start(bf16[528,128]{1,0:T(8,128)(2,1)S(1)} %concatenate.7), channel_id=1, source_target_pairs={{0,6},{2,0},{4,2},{6,4},{8,14},{10,8},{12,10},{14,12},{1,7},{3,1},... | collective-permute-start | bytes 405512 | tf_op jit(solution)/shard_map/ppermute | solution.py:147
  8.4 7.0 %collective-permute-start.3 = (bf16[528,128]{1,0:T(8,128)(2,1)S(1)}, bf16[528,128]{1,0:T(8,128)(2,1)S(1)}, u32[]{:S(2)}, u32[]{:S(2)}) collective-permute-start(bf16[528,128]{1,0:T(8,128)(2,1)S(1)} %concatenate.7), channel_id=1, source_target_pairs={{0,8},{2,10},{4,12},{6,14},{8,0},{10,2},{12,4},{14,6},{1,9},{3,11}... | collective-permute-start | bytes 405512 | tf_op jit(solution)/shard_map/ppermute | solution.py:148
  15.4 7.3 %collective-permute-start.4 = (bf16[528,128]{1,0:T(8,128)(2,1)S(1)}, bf16[528,128]{1,0:T(8,128)(2,1)S(1)}, u32[]{:S(2)}, u32[]{:S(2)}) collective-permute-start(bf16[528,128]{1,0:T(8,128)(2,1)S(1)} %collective-permute-done.3), channel_id=1, source_target_pairs={{0,2},{2,4},{4,6},{6,0},{8,10},{10,12},{12,14},{14,8},{1,3},{3,5},... | collective-permute-start | bytes 405512 | tf_op jit(solution)/shard_map/ppermute | solution.py:150
  15.6 7.7 %collective-permute-start.5 = (bf16[528,128]{1,0:T(8,128)(2,1)S(1)}, bf16[528,128]{1,0:T(8,128)(2,1)S(1)}, u32[]{:S(2)}, u32[]{:S(2)}) collective-permute-start(bf16[528,128]{1,0:T(8,128)(2,1)S(1)} %collective-permute-done.3), channel_id=1, source_target_pairs={{0,4},{2,6},{4,0},{6,2},{8,12},{10,14},{12,8},{14,10},{1,5},{3,7},... | collective-permute-start | bytes 405512 | tf_op jit(solution)/shard_map/ppermute | solution.py:150
  19.1 5.3 %collective-permute-start.6 = (bf16[528,128]{1,0:T(8,128)(2,1)S(1)}, bf16[528,128]{1,0:T(8,128)(2,1)S(1)}, u32[]{:S(2)}, u32[]{:S(2)}) collective-permute-start(bf16[528,128]{1,0:T(8,128)(2,1)S(1)} %collective-permute-done.3), channel_id=1, source_target_pairs={{0,6},{2,0},{4,2},{6,4},{8,14},{10,8},{12,10},{14,12},{1,7},{3,1},... | collective-permute-start | bytes 405512 | tf_op jit(solution)/shard_map/ppermute | solution.py:150
  29.9 9.6 %collective-permute-start.7 = (bf16[2,4,128,128]{3,2,1,0:T(8,128)(2,1)S(1)}, bf16[2,4,128,128]{3,2,1,0:T(8,128)(2,1)S(1)}, u32[]{:S(2)}, u32[]{:S(2)}) collective-permute-start(bf16[2,4,128,128]{3,2,1,0:T(8,128)(2,1)S(1)} %pad_maximum_fusion), channel_id=1, source_target_pairs={{0,6},{2,0},{4,2},{6,4},{8,14},{10,8},{12,10},{14,12},{1,7},{3,1},... | collective-permute-start | bytes 786440 | tf_op jit(solution)/shard_map/ppermute | solution.py:168
  33.3 10.0 %collective-permute-start.8 = (bf16[2,4,128,128]{3,2,1,0:T(8,128)(2,1)S(1)}, bf16[2,4,128,128]{3,2,1,0:T(8,128)(2,1)S(1)}, u32[]{:S(2)}, u32[]{:S(2)}) collective-permute-start(bf16[2,4,128,128]{3,2,1,0:T(8,128)(2,1)S(1)} %pad_maximum_fusion.1), channel_id=1, source_target_pairs={{0,4},{2,6},{4,0},{6,2},{8,12},{10,14},{12,8},{14,10},{1,5},{3,7},... | collective-permute-start | bytes 786440 | tf_op jit(solution)/shard_map/ppermute | solution.py:168
  33.4 10.6 %collective-permute-start.9 = (bf16[2,4,128,128]{3,2,1,0:T(8,128)(2,1)S(1)}, bf16[2,4,128,128]{3,2,1,0:T(8,128)(2,1)S(1)}, u32[]{:S(2)}, u32[]{:S(2)}) collective-permute-start(bf16[2,4,128,128]{3,2,1,0:T(8,128)(2,1)S(1)} %pad_maximum_fusion.2), channel_id=1, source_target_pairs={{0,2},{2,4},{4,6},{6,0},{8,10},{10,12},{12,14},{14,8},{1,3},{3,5},... | collective-permute-start | bytes 786440 | tf_op jit(solution)/shard_map/ppermute | solution.py:168
  44.0 7.3 %collective-permute-start.10 = (bf16[4,128,128]{2,1,0:T(8,128)(2,1)S(1)}, bf16[4,128,128]{2,1,0:T(8,128)(2,1)S(1)}, u32[]{:S(2)}, u32[]{:S(2)}) collective-permute-start(bf16[4,128,128]{2,1,0:T(8,128)(2,1)S(1)} %fusion.1), channel_id=1, source_target_pairs={{0,8},{2,10},{4,12},{6,14},{8,0},{10,2},{12,4},{14,6},{1,9},{3,11}... | collective-permute-start | bytes 393224 | tf_op jit(solution)/shard_map/ppermute | solution.py:171

commit v7 on v6

--- a/solution.py
+++ b/solution.py
@@ -144,12 +144,14 @@
     paired = jnp.concatenate([key_vectors, value_rows], axis=1).transpose(1, 0, 2)
     slab = jnp.concatenate([paired.reshape(2 * kv_rows, head_width), offset_rows], axis=0)
     half = cycle_size // 2
-    from_mates = [lax.ppermute(slab, "ctx", mate_pairs(cycle_size, k)) for k in range(1, half)]
     from_mirror = lax.ppermute(slab, "ctx", mirror_pairs(cycle_size))
-    handed_on = [
-        lax.ppermute(from_mirror, "ctx", mate_pairs(cycle_size, k)) for k in range(1, half)
+    bundle = jnp.stack([slab, from_mirror])
+    from_mates = [
+        lax.ppermute(bundle, "ctx", mate_pairs(cycle_size, k)) for k in range(1, half)
     ]
-    gathered = jnp.stack([slab] + from_mates + [from_mirror] + handed_on)
+    gathered = jnp.stack(
+        [slab] + [got[0] for got in from_mates] + [from_mirror] + [got[1] for got in from_mates]
+    )
     all_offsets = gathered[:, 2 * kv_rows, 0].astype(jnp.float32).astype(jnp.int32)
 
     dq_t, own_part, mirror_part, parts = local_backward(

time: 53.2 us -> 58.7 us (1.10)
  waiting for transfers between devices: 20.7 us -> 32.4 us
  starting transfers between devices: 20.1 us -> 14.8 us
  local copies, waits for them, and re-layouts: 4.04 us -> 3.03 us
    ppermute x6 -> x3, starting transfers between devices: 12.4 us -> 3.82 us  [on_device(): lax.ppermute(bundle, 'ctx', mate_pairs(cycle_size, k))]
    ppermute x6 -> x3, waiting for transfers between devices: 2.45 us -> 10.4 us  [on_device(): lax.ppermute(bundle, 'ctx', mate_pairs(cycle_size, k))]
    ppermute x1, waiting for transfers between devices: 3.16 us -> 6.48 us  [on_device(): from_mirror = lax.ppermute(slab, 'ctx', mirror_pairs(cycle_size))]
    ppermute x1, starting transfers between devices: 0.77 us -> 3.22 us  [on_device(): lax.ppermute(mirror_total.astype(jnp.bfloat16), 'ctx', mirror_pairs(cycle...]
    ppermute x3, waiting for transfers between devices: 9.62 us -> 11.4 us  [on_device(): lax.ppermute(pair, 'ctx', mate_pairs(cycle_size, half - k))]
    ppermute x1, starting transfers between devices: 2.59 us -> 4.1 us  [on_device(): from_mirror = lax.ppermute(slab, 'ctx', mirror_pairs(cycle_size))]
    ppermute x1, waiting for transfers between devices: 5.46 us -> 4.21 us  [on_device(): lax.ppermute(mirror_total.astype(jnp.bfloat16), 'ctx', mirror_pairs(cycle...]
    transpose x1, local copies, waits for them, and re-layouts: 1.12 us -> 0.09 us  [on_device(): forward_out.transpose(1, 0, 2)]
  transfers between devices with their start and end apart: 11 -> 8, of which waited for: 8 -> 8; matrix products, arithmetic and copies ran while one was open for 5% -> 2% of each run, Pallas kernels for 0% -> 0%
where the time goes in v7:
time: 58.7 us; the launch traced here: 58.5 us
  waiting for transfers between devices  32.4 us (55%)
  starting transfers between devices  14.8 us (25%)
  Pallas kernels  5.12 us (9%)
  local copies, waits for them, and re-layouts  3.03 us (5%)
  other arithmetic  1.58 us (3%)
  between operations  1.52 us (3%)
    ppermute x3, waiting for transfers between devices, on_device(): lax.ppermute(pair, 'ctx', mate_pairs(cycle_size, half - k))  11.4 us
    ppermute x3, waiting for transfers between devices, on_device(): lax.ppermute(bundle, 'ctx', mate_pairs(cycle_size, k))  10.4 us
    ppermute x1, waiting for transfers between devices, on_device(): from_mirror = lax.ppermute(slab, 'ctx', mirror_pairs(cycle_size))  6.48 us
    pallas_call x1, Pallas kernels, local_backward(): pl.pallas_call(functools.partial(backward_kernel, kv_heads=kv_heads, chun...  5.12 us
    ppermute x1, waiting for transfers between devices, on_device(): lax.ppermute(mirror_total.astype(jnp.bfloat16), 'ctx', mirror_pairs(cycle...  4.21 us
    ppermute x1, starting transfers between devices, on_device(): from_mirror = lax.ppermute(slab, 'ctx', mirror_pairs(cycle_size))  4.1 us
    ppermute x3, starting transfers between devices, on_device(): lax.ppermute(bundle, 'ctx', mate_pairs(cycle_size, k))  3.82 us
    ppermute x3, starting transfers between devices, on_device(): lax.ppermute(pair, 'ctx', mate_pairs(cycle_size, half - k))  3.66 us
  transfers between devices with their start and end apart: 8, of which 8 were waited for; matrix products, arithmetic and copies ran while one was open for 2% of the time, Pallas kernels for 0%

profile of v7, /device:TPU:0, one launch (start us, length us, event | category | flops | bytes accessed | tf_op | source)
XLA Modules:
  0.0 58.5 jit_solution(2754341156211258487)
XLA Ops:
  0.6 0.0 copy-start.2
  0.6 0.0 copy-start.1
  1.4 1.0 %maximum_bitcast_fusion = bf16[4,128,128]{2,0,1:T(4,128)(2,1)S(1)} fusion(bf16[128,2,128]{2,1,0:T(2,128)(2,1)} %param.8, bf16[128,2,128]{2,1,0:T(2,128)(2,1)} %param.7), kind=kLoop, calls=%fused_computation.29 | loop fusion | flops 262144 | bytes 262144 | tf_op jit(solution)/shard_map/transpose | solution.py:144
  2.4 0.0 copy-start
  2.4 4.1 %collective-permute-start = (bf16[528,128]{1,0:T(8,128)(2,1)S(1)}, bf16[528,128]{1,0:T(8,128)(2,1)S(1)}, u32[]{:S(2)}, u32[]{:S(2)}) collective-permute-start(bf16[528,128]{1,0:T(8,128)(2,1)S(1)} %get-tuple-element.26), channel_id=1, source_target_pairs={{0,8},{2,10},{4,12},{6,14},{8,0},{10,2},{12,4},{14,6},{1,9},{3,11}... | collective-permute-start | bytes 405512 | tf_op jit(solution)/shard_map/ppermute | solution.py:147
  6.5 6.5 %collective-permute-done = bf16[528,128]{1,0:T(8,128)(2,1)S(1)} collective-permute-done((bf16[528,128]{1,0:T(8,128)(2,1)S(1)}, bf16[528,128]{1,0:T(8,128)(2,1)S(1)}, u32[]{:S(2)}, u32[]{:S(2)}) %collective-permute-start) | collective-permute-done | bytes 135200 | tf_op jit(solution)/shard_map/ppermute | solution.py:147
  13.1 1.6 %collective-permute-start.1 = (bf16[2,528,128]{2,1,0:T(8,128)(2,1)S(1)}, bf16[2,528,128]{2,1,0:T(8,128)(2,1)S(1)}, u32[]{:S(2)}, u32[]{:S(2)}) collective-permute-start(bf16[2,528,128]{2,1,0:T(8,128)(2,1)S(1)} %pad_maximum_fusion), channel_id=1, source_target_pairs={{0,2},{2,4},{4,6},{6,0},{8,10},{10,12},{12,14},{14,8},{1,3},{3,5},... | collective-permute-start | bytes 811016 | tf_op jit(solution)/shard_map/ppermute | solution.py:150
  14.7 0.0 copy-done.2
  14.7 0.0 copy-done.1
  14.7 0.1 copy_bitcast_fusion
  14.8 0.7 %collective-permute-start.2 = (bf16[2,528,128]{2,1,0:T(8,128)(2,1)S(1)}, bf16[2,528,128]{2,1,0:T(8,128)(2,1)S(1)}, u32[]{:S(2)}, u32[]{:S(2)}) collective-permute-start(bf16[2,528,128]{2,1,0:T(8,128)(2,1)S(1)} %pad_maximum_fusion), channel_id=1, source_target_pairs={{0,4},{2,6},{4,0},{6,2},{8,12},{10,14},{12,8},{14,10},{1,5},{3,7},... | collective-permute-start | bytes 811016 | tf_op jit(solution)/shard_map/ppermute | solution.py:150
  15.5 0.0 copy-done
  15.6 1.5 %collective-permute-start.3 = (bf16[2,528,128]{2,1,0:T(8,128)(2,1)S(1)}, bf16[2,528,128]{2,1,0:T(8,128)(2,1)S(1)}, u32[]{:S(2)}, u32[]{:S(2)}) collective-permute-start(bf16[2,528,128]{2,1,0:T(8,128)(2,1)S(1)} %pad_maximum_fusion), channel_id=1, source_target_pairs={{0,6},{2,0},{4,2},{6,4},{8,14},{10,8},{12,10},{14,12},{1,7},{3,1},... | collective-permute-start | bytes 811016 | tf_op jit(solution)/shard_map/ppermute | solution.py:150
  17.0 6.4 %collective-permute-done.1 = bf16[2,528,128]{2,1,0:T(8,128)(2,1)S(1)} collective-permute-done((bf16[2,528,128]{2,1,0:T(8,128)(2,1)S(1)}, bf16[2,528,128]{2,1,0:T(8,128)(2,1)S(1)}, u32[]{:S(2)}, u32[]{:S(2)}) %collective-permute-start.1) | collective-permute-done | bytes 270368 | tf_op jit(solution)/shard_map/ppermute | solution.py:150
  23.5 0.8 %collective-permute-done.2 = bf16[2,528,128]{2,1,0:T(8,128)(2,1)S(1)} collective-permute-done((bf16[2,528,128]{2,1,0:T(8,128)(2,1)S(1)}, bf16[2,528,128]{2,1,0:T(8,128)(2,1)S(1)}, u32[]{:S(2)}, u32[]{:S(2)}) %collective-permute-start.2) | collective-permute-done | bytes 270368 | tf_op jit(solution)/shard_map/ppermute | solution.py:150
  24.3 3.2 %collective-permute-done.3 = bf16[2,528,128]{2,1,0:T(8,128)(2,1)S(1)} collective-permute-done((bf16[2,528,128]{2,1,0:T(8,128)(2,1)S(1)}, bf16[2,528,128]{2,1,0:T(8,128)(2,1)S(1)}, u32[]{:S(2)}, u32[]{:S(2)}) %collective-permute-start.3) | collective-permute-done | bytes 270368 | tf_op jit(solution)/shard_map/ppermute | solution.py:150
  27.6 0.2 fusion.9.offs_ref
  27.8 5.1 %shard_map.85 = (f32[8,128,128]{2,1,0:T(8,128)S(1)}, f32[4,128,128]{2,1,0:T(8,128)S(1)}, f32[4,128,128]{2,1,0:T(8,128)S(1)}, bf16[7,4,128,128]{3,2,1,0:T(8,128)(2,1)S(1)}) custom-call(s32[8]{0:T(128)S(1)} %fusion.9.offs_ref, s32[1]{0:T(128)S(6)} %copy.34.own_ref, bf16[8,128,128]{2,1,0:T(8,128)(2,1)S(1)} %bitcast.58, ...), custom_call_target="tpu_custom_call" | custom-call | flops 1610612736 | bytes 2654208 | tf_op jit(solution)/shard_map/pallas_call | solution.py:118
  33.0 0.1 fusion.10
  33.1 2.9 %collective-permute-start.4 = (bf16[2,4,128,128]{3,2,1,0:T(8,128)(2,1)S(1)}, bf16[2,4,128,128]{3,2,1,0:T(8,128)(2,1)S(1)}, u32[]{:S(2)}, u32[]{:S(2)}) collective-permute-start(bf16[2,4,128,128]{3,2,1,0:T(8,128)(2,1)S(1)} %pad_maximum_fusion.1), channel_id=1, source_target_pairs={{0,6},{2,0},{4,2},{6,4},{8,14},{10,8},{12,10},{14,12},{1,7},{3,1},... | collective-permute-start | bytes 786440 | tf_op jit(solution)/shard_map/ppermute | solution.py:170
  36.0 0.4 collective-permute-start.5
  36.4 0.4 collective-permute-start.6
  36.8 6.0 %collective-permute-done.4 = bf16[2,4,128,128]{3,2,1,0:T(8,128)(2,1)S(1)} collective-permute-done((bf16[2,4,128,128]{3,2,1,0:T(8,128)(2,1)S(1)}, bf16[2,4,128,128]{3,2,1,0:T(8,128)(2,1)S(1)}, u32[]{:S(2)}, u32[]{:S(2)}) %collective-permute-start.4) | collective-permute-done | bytes 262176 | tf_op jit(solution)/shard_map/ppermute | solution.py:170
  42.8 3.9 %collective-permute-done.5 = bf16[2,4,128,128]{3,2,1,0:T(8,128)(2,1)S(1)} collective-permute-done((bf16[2,4,128,128]{3,2,1,0:T(8,128)(2,1)S(1)}, bf16[2,4,128,128]{3,2,1,0:T(8,128)(2,1)S(1)}, u32[]{:S(2)}, u32[]{:S(2)}) %collective-permute-start.5) | collective-permute-done | bytes 262176 | tf_op jit(solution)/shard_map/ppermute | solution.py:170
  46.7 1.5 %collective-permute-done.6 = bf16[2,4,128,128]{3,2,1,0:T(8,128)(2,1)S(1)} collective-permute-done((bf16[2,4,128,128]{3,2,1,0:T(8,128)(2,1)S(1)}, bf16[2,4,128,128]{3,2,1,0:T(8,128)(2,1)S(1)}, u32[]{:S(2)}, u32[]{:S(2)}) %collective-permute-start.6) | collective-permute-done | bytes 262176 | tf_op jit(solution)/shard_map/ppermute | solution.py:170
  48.3 0.1 fusion.1
  48.4 3.2 %collective-permute-start.7 = (bf16[4,128,128]{2,1,0:T(8,128)(2,1)S(1)}, bf16[4,128,128]{2,1,0:T(8,128)(2,1)S(1)}, u32[]{:S(2)}, u32[]{:S(2)}) collective-permute-start(bf16[4,128,128]{2,1,0:T(8,128)(2,1)S(1)} %fusion.1), channel_id=1, source_target_pairs={{0,8},{2,10},{4,12},{6,14},{8,0},{10,2},{12,4},{14,6},{1,9},{3,11}... | collective-permute-start | bytes 393224 | tf_op jit(solution)/shard_map/ppermute | solution.py:173
  51.6 1.1 %copy.20 = f32[128,8,128]{2,1,0:T(8,128)} copy(f32[128,8,128]{2,0,1:T(8,128)S(1)} %bitcast.57) | data formatting | bytes 1048576
  52.7 4.2 %collective-permute-done.7 = bf16[4,128,128]{2,1,0:T(8,128)(2,1)S(1)} collective-permute-done((bf16[4,128,128]{2,1,0:T(8,128)(2,1)S(1)}, bf16[4,128,128]{2,1,0:T(8,128)(2,1)S(1)}, u32[]{:S(2)}, u32[]{:S(2)}) %collective-permute-start.7) | collective-permute-done | bytes 131104 | tf_op jit(solution)/shard_map/ppermute | solution.py:173
  56.9 0.1 fusion.5
  57.0 0.8 %copy.21 = f32[128,2,128]{2,1,0:T(2,128)} copy(f32[128,2,128]{2,0,1:T(8,128)S(1)} %get-tuple-element.24) | data formatting | bytes 262144
  57.7 0.8 %copy.22 = f32[128,2,128]{2,1,0:T(2,128)} copy(f32[128,2,128]{2,0,1:T(8,128)S(1)} %get-tuple-element.23) | data formatting | bytes 262144
  (19 shorter events, 0.5 us)
Async XLA Ops:
  0.6 14.1 %copy-start.2 = (bf16[128,8,128]{2,1,0:T(8,128)(2,1)S(1)}, bf16[128,8,128]{2,1,0:T(8,128)(2,1)}, u32[]{:S(2)}) copy-start(bf16[128,8,128]{2,1,0:T(8,128)(2,1)} %param.10) | copy-start | bytes 786436
  0.6 14.0 %copy-start.1 = (bf16[128,8,128]{2,1,0:T(8,128)(2,1)S(1)}, bf16[128,8,128]{2,1,0:T(8,128)(2,1)}, u32[]{:S(2)}) copy-start(bf16[128,8,128]{2,1,0:T(8,128)(2,1)} %param.9) | copy-start | bytes 786436
  2.4 13.1 %copy-start = (bf16[128,8,128]{2,1,0:T(8,128)(2,1)S(1)}, bf16[128,8,128]{2,1,0:T(8,128)(2,1)}, u32[]{:S(2)}) copy-start(bf16[128,8,128]{2,1,0:T(8,128)(2,1)} %param.6) | copy-start | bytes 786436
  2.4 10.6 %collective-permute-start = (bf16[528,128]{1,0:T(8,128)(2,1)S(1)}, bf16[528,128]{1,0:T(8,128)(2,1)S(1)}, u32[]{:S(2)}, u32[]{:S(2)}) collective-permute-start(bf16[528,128]{1,0:T(8,128)(2,1)S(1)} %get-tuple-element.26), channel_id=1, source_target_pairs={{0,8},{2,10},{4,12},{6,14},{8,0},{10,2},{12,4},{14,6},{1,9},{3,11}... | collective-permute-start | bytes 405512 | tf_op jit(solution)/shard_map/ppermute | solution.py:147
  13.1 10.4 %collective-permute-start.1 = (bf16[2,528,128]{2,1,0:T(8,128)(2,1)S(1)}, bf16[2,528,128]{2,1,0:T(8,128)(2,1)S(1)}, u32[]{:S(2)}, u32[]{:S(2)}) collective-permute-start(bf16[2,528,128]{2,1,0:T(8,128)(2,1)S(1)} %pad_maximum_fusion), channel_id=1, source_target_pairs={{0,2},{2,4},{4,6},{6,0},{8,10},{10,12},{12,14},{14,8},{1,3},{3,5},... | collective-permute-start | bytes 811016 | tf_op jit(solution)/shard_map/ppermute | solution.py:150
  14.8 9.5 %collective-permute-start.2 = (bf16[2,528,128]{2,1,0:T(8,128)(2,1)S(1)}, bf16[2,528,128]{2,1,0:T(8,128)(2,1)S(1)}, u32[]{:S(2)}, u32[]{:S(2)}) collective-permute-start(bf16[2,528,128]{2,1,0:T(8,128)(2,1)S(1)} %pad_maximum_fusion), channel_id=1, source_target_pairs={{0,4},{2,6},{4,0},{6,2},{8,12},{10,14},{12,8},{14,10},{1,5},{3,7},... | collective-permute-start | bytes 811016 | tf_op jit(solution)/shard_map/ppermute | solution.py:150
  15.6 11.9 %collective-permute-start.3 = (bf16[2,528,128]{2,1,0:T(8,128)(2,1)S(1)}, bf16[2,528,128]{2,1,0:T(8,128)(2,1)S(1)}, u32[]{:S(2)}, u32[]{:S(2)}) collective-permute-start(bf16[2,528,128]{2,1,0:T(8,128)(2,1)S(1)} %pad_maximum_fusion), channel_id=1, source_target_pairs={{0,6},{2,0},{4,2},{6,4},{8,14},{10,8},{12,10},{14,12},{1,7},{3,1},... | collective-permute-start | bytes 811016 | tf_op jit(solution)/shard_map/ppermute | solution.py:150
  33.1 9.7 %collective-permute-start.4 = (bf16[2,4,128,128]{3,2,1,0:T(8,128)(2,1)S(1)}, bf16[2,4,128,128]{3,2,1,0:T(8,128)(2,1)S(1)}, u32[]{:S(2)}, u32[]{:S(2)}) collective-permute-start(bf16[2,4,128,128]{3,2,1,0:T(8,128)(2,1)S(1)} %pad_maximum_fusion.1), channel_id=1, source_target_pairs={{0,6},{2,0},{4,2},{6,4},{8,14},{10,8},{12,10},{14,12},{1,7},{3,1},... | collective-permute-start | bytes 786440 | tf_op jit(solution)/shard_map/ppermute | solution.py:170
  36.0 10.7 %collective-permute-start.5 = (bf16[2,4,128,128]{3,2,1,0:T(8,128)(2,1)S(1)}, bf16[2,4,128,128]{3,2,1,0:T(8,128)(2,1)S(1)}, u32[]{:S(2)}, u32[]{:S(2)}) collective-permute-start(bf16[2,4,128,128]{3,2,1,0:T(8,128)(2,1)S(1)} %pad_maximum_fusion.2), channel_id=1, source_target_pairs={{0,4},{2,6},{4,0},{6,2},{8,12},{10,14},{12,8},{14,10},{1,5},{3,7},... | collective-permute-start | bytes 786440 | tf_op jit(solution)/shard_map/ppermute | solution.py:170
  36.4 11.8 %collective-permute-start.6 = (bf16[2,4,128,128]{3,2,1,0:T(8,128)(2,1)S(1)}, bf16[2,4,128,128]{3,2,1,0:T(8,128)(2,1)S(1)}, u32[]{:S(2)}, u32[]{:S(2)}) collective-permute-start(bf16[2,4,128,128]{3,2,1,0:T(8,128)(2,1)S(1)} %pad_maximum_fusion.3), channel_id=1, source_target_pairs={{0,2},{2,4},{4,6},{6,0},{8,10},{10,12},{12,14},{14,8},{1,3},{3,5},... | collective-permute-start | bytes 786440 | tf_op jit(solution)/shard_map/ppermute | solution.py:170
  48.4 8.5 %collective-permute-start.7 = (bf16[4,128,128]{2,1,0:T(8,128)(2,1)S(1)}, bf16[4,128,128]{2,1,0:T(8,128)(2,1)S(1)}, u32[]{:S(2)}, u32[]{:S(2)}) collective-permute-start(bf16[4,128,128]{2,1,0:T(8,128)(2,1)S(1)} %fusion.1), channel_id=1, source_target_pairs={{0,8},{2,10},{4,12},{6,14},{8,0},{10,2},{12,4},{14,6},{1,9},{3,11}... | collective-permute-start | bytes 393224 | tf_op jit(solution)/shard_map/ppermute | solution.py:173

commit v8 on v6

--- a/solution.py
+++ b/solution.py
@@ -66,8 +66,9 @@
 
         run_max = jnp.full((rows, 1), MASKED, f32)
         run_total = jnp.zeros((rows, 1), f32)
+        single = blocks == chunk_blocks
         for c in range(blocks // chunk_blocks):
-            s, _ = chunk_scores(q, chunk_keys_of(c, g), c)
+            s, visible = chunk_scores(q, chunk_keys_of(c, g), c)
             new_max = jnp.maximum(run_max, jnp.max(s, axis=1, keepdims=True))
             run_total = run_total * jnp.exp(run_max - new_max) + jnp.sum(
                 jnp.exp(s - new_max), axis=1, keepdims=True
@@ -79,7 +80,8 @@
         for c in range(blocks // chunk_blocks):
             k = chunk_keys_of(c, g)
             v = chunk_values_of(c, g)
-            s, visible = chunk_scores(q, k, c)
+            if not single:
+                s, visible = chunk_scores(q, k, c)
             probs = jnp.where(visible, jnp.exp(s - log_total), 0.0)
             prob_grad = lax.dot_general(
                 do, v, (((1,), (1,)), ((), ())), preferred_element_type=f32

time: 53.2 us -> 53.2 us (level)
  no operation moved by 1% of the time
where the time goes in v8:
time: 53.2 us; the launch traced here: 53 us
  waiting for transfers between devices  20.7 us (39%)
  starting transfers between devices  20.1 us (38%)
  Pallas kernels  5.12 us (10%)
  local copies, waits for them, and re-layouts  4.04 us (8%)
  other arithmetic  1.55 us (3%)
  between operations  1.52 us (3%)
    ppermute x3, waiting for transfers between devices, on_device(): lax.ppermute(pair, 'ctx', mate_pairs(cycle_size, half - k))  9.62 us
    ppermute x3, starting transfers between devices, on_device(): lax.ppermute(from_mirror, 'ctx', mate_pairs(cycle_size, k))  6.42 us
    ppermute x3, starting transfers between devices, on_device(): lax.ppermute(slab, 'ctx', mate_pairs(cycle_size, k))  6 us
    ppermute x1, waiting for transfers between devices, on_device(): lax.ppermute(mirror_total.astype(jnp.bfloat16), 'ctx', mirror_pairs(cycle...  5.46 us
    pallas_call x1, Pallas kernels, local_backward(): pl.pallas_call(functools.partial(backward_kernel, kv_heads=kv_heads, chun...  5.12 us
    ppermute x3, starting transfers between devices, on_device(): lax.ppermute(pair, 'ctx', mate_pairs(cycle_size, half - k))  4.28 us
    ppermute x1, waiting for transfers between devices, on_device(): from_mirror = lax.ppermute(slab, 'ctx', mirror_pairs(cycle_size))  3.16 us
    unnamed x13, local copies, waits for them, and re-layouts  2.78 us
  transfers between devices with their start and end apart: 11, of which 8 were waited for; matrix products, arithmetic and copies ran while one was open for 5% of the time, Pallas kernels for 0%

profile of v8, /device:TPU:0, one launch (start us, length us, event | category | flops | bytes accessed | tf_op | source)
XLA Modules:
  0.0 53.0 jit_solution(9954453284364510789)
XLA Ops:
  0.6 0.0 copy-start
  1.3 1.0 %maximum_bitcast_fusion = bf16[4,128,128]{2,0,1:T(4,128)(2,1)S(1)} fusion(bf16[128,2,128]{2,1,0:T(2,128)(2,1)} %param.8, bf16[128,2,128]{2,1,0:T(2,128)(2,1)} %param.7), kind=kLoop, calls=%fused_computation.30 | loop fusion | flops 262144 | bytes 262144 | tf_op jit(solution)/shard_map/transpose | solution.py:146
  2.4 3.0 %collective-permute-start = (bf16[528,128]{1,0:T(8,128)(2,1)S(1)}, bf16[528,128]{1,0:T(8,128)(2,1)S(1)}, u32[]{:S(2)}, u32[]{:S(2)}) collective-permute-start(bf16[528,128]{1,0:T(8,128)(2,1)S(1)} %concatenate.7), channel_id=1, source_target_pairs={{0,2},{2,4},{4,6},{6,0},{8,10},{10,12},{12,14},{14,8},{1,3},{3,5},... | collective-permute-start | bytes 405512 | tf_op jit(solution)/shard_map/ppermute | solution.py:149
  5.4 1.6 %collective-permute-start.1 = (bf16[528,128]{1,0:T(8,128)(2,1)S(1)}, bf16[528,128]{1,0:T(8,128)(2,1)S(1)}, u32[]{:S(2)}, u32[]{:S(2)}) collective-permute-start(bf16[528,128]{1,0:T(8,128)(2,1)S(1)} %concatenate.7), channel_id=1, source_target_pairs={{0,4},{2,6},{4,0},{6,2},{8,12},{10,14},{12,8},{14,10},{1,5},{3,7},... | collective-permute-start | bytes 405512 | tf_op jit(solution)/shard_map/ppermute | solution.py:149
  7.0 1.4 %collective-permute-start.2 = (bf16[528,128]{1,0:T(8,128)(2,1)S(1)}, bf16[528,128]{1,0:T(8,128)(2,1)S(1)}, u32[]{:S(2)}, u32[]{:S(2)}) collective-permute-start(bf16[528,128]{1,0:T(8,128)(2,1)S(1)} %concatenate.7), channel_id=1, source_target_pairs={{0,6},{2,0},{4,2},{6,4},{8,14},{10,8},{12,10},{14,12},{1,7},{3,1},... | collective-permute-start | bytes 405512 | tf_op jit(solution)/shard_map/ppermute | solution.py:149
  8.4 2.6 %collective-permute-start.3 = (bf16[528,128]{1,0:T(8,128)(2,1)S(1)}, bf16[528,128]{1,0:T(8,128)(2,1)S(1)}, u32[]{:S(2)}, u32[]{:S(2)}) collective-permute-start(bf16[528,128]{1,0:T(8,128)(2,1)S(1)} %concatenate.7), channel_id=1, source_target_pairs={{0,8},{2,10},{4,12},{6,14},{8,0},{10,2},{12,4},{14,6},{1,9},{3,11}... | collective-permute-start | bytes 405512 | tf_op jit(solution)/shard_map/ppermute | solution.py:150
  11.0 1.1 %copy_bitcast_fusion = (bf16[8,128,128]{2,1,0:T(8,128)(2,1)S(1)}, bf16[8,128,128]{2,1,0:T(8,128)(2,1)S(1)}) fusion(bf16[128,8,128]{2,1,0:T(8,128)(2,1)} %param.9, bf16[128,8,128]{2,1,0:T(8,128)(2,1)} %param.10), kind=kLoop, calls=%fused_computation.17 | loop fusion | bytes 1048576 | tf_op jit(solution)/shard_map/transpose | solution.py:162
  12.1 0.0 copy-done
  12.2 3.2 %collective-permute-done.3 = bf16[528,128]{1,0:T(8,128)(2,1)S(1)} collective-permute-done((bf16[528,128]{1,0:T(8,128)(2,1)S(1)}, bf16[528,128]{1,0:T(8,128)(2,1)S(1)}, u32[]{:S(2)}, u32[]{:S(2)}) %collective-permute-start.3) | collective-permute-done | bytes 135200 | tf_op jit(solution)/shard_map/ppermute | solution.py:150
  15.4 0.3 collective-permute-start.4
  15.6 3.5 %collective-permute-start.5 = (bf16[528,128]{1,0:T(8,128)(2,1)S(1)}, bf16[528,128]{1,0:T(8,128)(2,1)S(1)}, u32[]{:S(2)}, u32[]{:S(2)}) collective-permute-start(bf16[528,128]{1,0:T(8,128)(2,1)S(1)} %collective-permute-done.3), channel_id=1, source_target_pairs={{0,4},{2,6},{4,0},{6,2},{8,12},{10,14},{12,8},{14,10},{1,5},{3,7},... | collective-permute-start | bytes 405512 | tf_op jit(solution)/shard_map/ppermute | solution.py:152
  19.1 0.0 collective-permute-done
  19.1 2.7 %collective-permute-start.6 = (bf16[528,128]{1,0:T(8,128)(2,1)S(1)}, bf16[528,128]{1,0:T(8,128)(2,1)S(1)}, u32[]{:S(2)}, u32[]{:S(2)}) collective-permute-start(bf16[528,128]{1,0:T(8,128)(2,1)S(1)} %collective-permute-done.3), channel_id=1, source_target_pairs={{0,6},{2,0},{4,2},{6,4},{8,14},{10,8},{12,10},{14,12},{1,7},{3,1},... | collective-permute-start | bytes 405512 | tf_op jit(solution)/shard_map/ppermute | solution.py:152
  21.8 0.0 collective-permute-done.1
  21.8 0.0 collective-permute-done.2
  21.9 0.8 %collective-permute-done.4 = bf16[528,128]{1,0:T(8,128)(2,1)S(1)} collective-permute-done((bf16[528,128]{1,0:T(8,128)(2,1)S(1)}, bf16[528,128]{1,0:T(8,128)(2,1)S(1)}, u32[]{:S(2)}, u32[]{:S(2)}) %collective-permute-start.4) | collective-permute-done | bytes 135200 | tf_op jit(solution)/shard_map/ppermute | solution.py:152
  22.7 0.6 %collective-permute-done.5 = bf16[528,128]{1,0:T(8,128)(2,1)S(1)} collective-permute-done((bf16[528,128]{1,0:T(8,128)(2,1)S(1)}, bf16[528,128]{1,0:T(8,128)(2,1)S(1)}, u32[]{:S(2)}, u32[]{:S(2)}) %collective-permute-start.5) | collective-permute-done | bytes 135200 | tf_op jit(solution)/shard_map/ppermute | solution.py:152
  23.3 1.1 %collective-permute-done.6 = bf16[528,128]{1,0:T(8,128)(2,1)S(1)} collective-permute-done((bf16[528,128]{1,0:T(8,128)(2,1)S(1)}, bf16[528,128]{1,0:T(8,128)(2,1)S(1)}, u32[]{:S(2)}, u32[]{:S(2)}) %collective-permute-start.6) | collective-permute-done | bytes 135200 | tf_op jit(solution)/shard_map/ppermute | solution.py:152
  24.4 0.2 fusion.9.offs_ref
  24.6 5.1 %shard_map.85 = (f32[8,128,128]{2,1,0:T(8,128)S(1)}, f32[4,128,128]{2,1,0:T(8,128)S(1)}, f32[4,128,128]{2,1,0:T(8,128)S(1)}, bf16[7,4,128,128]{3,2,1,0:T(8,128)(2,1)S(1)}) custom-call(s32[8]{0:T(128)S(1)} %fusion.9.offs_ref, s32[1]{0:T(128)S(6)} %copy.34.own_ref, bf16[8,128,128]{2,1,0:T(8,128)(2,1)S(1)} %bitcast.69, ...), custom_call_target="tpu_custom_call" | custom-call | flops 1610612736 | bytes 2654208 | tf_op jit(solution)/shard_map/pallas_call | solution.py:120
  29.8 0.1 fusion.10
  29.9 3.3 %collective-permute-start.7 = (bf16[2,4,128,128]{3,2,1,0:T(8,128)(2,1)S(1)}, bf16[2,4,128,128]{3,2,1,0:T(8,128)(2,1)S(1)}, u32[]{:S(2)}, u32[]{:S(2)}) collective-permute-start(bf16[2,4,128,128]{3,2,1,0:T(8,128)(2,1)S(1)} %pad_maximum_fusion), channel_id=1, source_target_pairs={{0,6},{2,0},{4,2},{6,4},{8,14},{10,8},{12,10},{14,12},{1,7},{3,1},... | collective-permute-start | bytes 786440 | tf_op jit(solution)/shard_map/ppermute | solution.py:170
  33.3 0.1 collective-permute-start.8
  33.4 0.9 %collective-permute-start.9 = (bf16[2,4,128,128]{3,2,1,0:T(8,128)(2,1)S(1)}, bf16[2,4,128,128]{3,2,1,0:T(8,128)(2,1)S(1)}, u32[]{:S(2)}, u32[]{:S(2)}) collective-permute-start(bf16[2,4,128,128]{3,2,1,0:T(8,128)(2,1)S(1)} %pad_maximum_fusion.2), channel_id=1, source_target_pairs={{0,2},{2,4},{4,6},{6,0},{8,10},{10,12},{12,14},{14,8},{1,3},{3,5},... | collective-permute-start | bytes 786440 | tf_op jit(solution)/shard_map/ppermute | solution.py:170
  34.2 5.3 %collective-permute-done.7 = bf16[2,4,128,128]{3,2,1,0:T(8,128)(2,1)S(1)} collective-permute-done((bf16[2,4,128,128]{3,2,1,0:T(8,128)(2,1)S(1)}, bf16[2,4,128,128]{3,2,1,0:T(8,128)(2,1)S(1)}, u32[]{:S(2)}, u32[]{:S(2)}) %collective-permute-start.7) | collective-permute-done | bytes 262176 | tf_op jit(solution)/shard_map/ppermute | solution.py:170
  39.5 3.7 %collective-permute-done.8 = bf16[2,4,128,128]{3,2,1,0:T(8,128)(2,1)S(1)} collective-permute-done((bf16[2,4,128,128]{3,2,1,0:T(8,128)(2,1)S(1)}, bf16[2,4,128,128]{3,2,1,0:T(8,128)(2,1)S(1)}, u32[]{:S(2)}, u32[]{:S(2)}) %collective-permute-start.8) | collective-permute-done | bytes 262176 | tf_op jit(solution)/shard_map/ppermute | solution.py:170
  43.3 0.6 %collective-permute-done.9 = bf16[2,4,128,128]{3,2,1,0:T(8,128)(2,1)S(1)} collective-permute-done((bf16[2,4,128,128]{3,2,1,0:T(8,128)(2,1)S(1)}, bf16[2,4,128,128]{3,2,1,0:T(8,128)(2,1)S(1)}, u32[]{:S(2)}, u32[]{:S(2)}) %collective-permute-start.9) | collective-permute-done | bytes 262176 | tf_op jit(solution)/shard_map/ppermute | solution.py:170
  44.0 0.1 fusion.1
  44.0 0.8 %collective-permute-start.10 = (bf16[4,128,128]{2,1,0:T(8,128)(2,1)S(1)}, bf16[4,128,128]{2,1,0:T(8,128)(2,1)S(1)}, u32[]{:S(2)}, u32[]{:S(2)}) collective-permute-start(bf16[4,128,128]{2,1,0:T(8,128)(2,1)S(1)} %fusion.1), channel_id=1, source_target_pairs={{0,8},{2,10},{4,12},{6,14},{8,0},{10,2},{12,4},{14,6},{1,9},{3,11}... | collective-permute-start | bytes 393224 | tf_op jit(solution)/shard_map/ppermute | solution.py:173
  44.8 1.1 %copy.20 = f32[128,8,128]{2,1,0:T(8,128)} copy(f32[128,8,128]{2,0,1:T(8,128)S(1)} %bitcast.68) | data formatting | bytes 1048576
  45.9 5.5 %collective-permute-done.10 = bf16[4,128,128]{2,1,0:T(8,128)(2,1)S(1)} collective-permute-done((bf16[4,128,128]{2,1,0:T(8,128)(2,1)S(1)}, bf16[4,128,128]{2,1,0:T(8,128)(2,1)S(1)}, u32[]{:S(2)}, u32[]{:S(2)}) %collective-permute-start.10) | collective-permute-done | bytes 131104 | tf_op jit(solution)/shard_map/ppermute | solution.py:173
  51.4 0.1 fusion.5
  51.5 0.8 %copy.21 = f32[128,2,128]{2,1,0:T(2,128)} copy(f32[128,2,128]{2,0,1:T(8,128)S(1)} %get-tuple-element.24) | data formatting | bytes 262144
  52.2 0.8 %copy.22 = f32[128,2,128]{2,1,0:T(2,128)} copy(f32[128,2,128]{2,0,1:T(8,128)S(1)} %get-tuple-element.23) | data formatting | bytes 262144
  (18 shorter events, 0.4 us)
Async XLA Ops:
  0.6 11.5 %copy-start = (bf16[128,8,128]{2,1,0:T(8,128)(2,1)S(1)}, bf16[128,8,128]{2,1,0:T(8,128)(2,1)}, u32[]{:S(2)}) copy-start(bf16[128,8,128]{2,1,0:T(8,128)(2,1)} %param.6) | copy-start | bytes 786436
  2.4 16.7 %collective-permute-start = (bf16[528,128]{1,0:T(8,128)(2,1)S(1)}, bf16[528,128]{1,0:T(8,128)(2,1)S(1)}, u32[]{:S(2)}, u32[]{:S(2)}) collective-permute-start(bf16[528,128]{1,0:T(8,128)(2,1)S(1)} %concatenate.7), channel_id=1, source_target_pairs={{0,2},{2,4},{4,6},{6,0},{8,10},{10,12},{12,14},{14,8},{1,3},{3,5},... | collective-permute-start | bytes 405512 | tf_op jit(solution)/shard_map/ppermute | solution.py:149
  5.4 16.4 %collective-permute-start.1 = (bf16[528,128]{1,0:T(8,128)(2,1)S(1)}, bf16[528,128]{1,0:T(8,128)(2,1)S(1)}, u32[]{:S(2)}, u32[]{:S(2)}) collective-permute-start(bf16[528,128]{1,0:T(8,128)(2,1)S(1)} %concatenate.7), channel_id=1, source_target_pairs={{0,4},{2,6},{4,0},{6,2},{8,12},{10,14},{12,8},{14,10},{1,5},{3,7},... | collective-permute-start | bytes 405512 | tf_op jit(solution)/shard_map/ppermute | solution.py:149
  7.0 14.8 %collective-permute-start.2 = (bf16[528,128]{1,0:T(8,128)(2,1)S(1)}, bf16[528,128]{1,0:T(8,128)(2,1)S(1)}, u32[]{:S(2)}, u32[]{:S(2)}) collective-permute-start(bf16[528,128]{1,0:T(8,128)(2,1)S(1)} %concatenate.7), channel_id=1, source_target_pairs={{0,6},{2,0},{4,2},{6,4},{8,14},{10,8},{12,10},{14,12},{1,7},{3,1},... | collective-permute-start | bytes 405512 | tf_op jit(solution)/shard_map/ppermute | solution.py:149
  8.4 7.0 %collective-permute-start.3 = (bf16[528,128]{1,0:T(8,128)(2,1)S(1)}, bf16[528,128]{1,0:T(8,128)(2,1)S(1)}, u32[]{:S(2)}, u32[]{:S(2)}) collective-permute-start(bf16[528,128]{1,0:T(8,128)(2,1)S(1)} %concatenate.7), channel_id=1, source_target_pairs={{0,8},{2,10},{4,12},{6,14},{8,0},{10,2},{12,4},{14,6},{1,9},{3,11}... | collective-permute-start | bytes 405512 | tf_op jit(solution)/shard_map/ppermute | solution.py:150
  15.4 7.3 %collective-permute-start.4 = (bf16[528,128]{1,0:T(8,128)(2,1)S(1)}, bf16[528,128]{1,0:T(8,128)(2,1)S(1)}, u32[]{:S(2)}, u32[]{:S(2)}) collective-permute-start(bf16[528,128]{1,0:T(8,128)(2,1)S(1)} %collective-permute-done.3), channel_id=1, source_target_pairs={{0,2},{2,4},{4,6},{6,0},{8,10},{10,12},{12,14},{14,8},{1,3},{3,5},... | collective-permute-start | bytes 405512 | tf_op jit(solution)/shard_map/ppermute | solution.py:152
  15.6 7.7 %collective-permute-start.5 = (bf16[528,128]{1,0:T(8,128)(2,1)S(1)}, bf16[528,128]{1,0:T(8,128)(2,1)S(1)}, u32[]{:S(2)}, u32[]{:S(2)}) collective-permute-start(bf16[528,128]{1,0:T(8,128)(2,1)S(1)} %collective-permute-done.3), channel_id=1, source_target_pairs={{0,4},{2,6},{4,0},{6,2},{8,12},{10,14},{12,8},{14,10},{1,5},{3,7},... | collective-permute-start | bytes 405512 | tf_op jit(solution)/shard_map/ppermute | solution.py:152
  19.1 5.3 %collective-permute-start.6 = (bf16[528,128]{1,0:T(8,128)(2,1)S(1)}, bf16[528,128]{1,0:T(8,128)(2,1)S(1)}, u32[]{:S(2)}, u32[]{:S(2)}) collective-permute-start(bf16[528,128]{1,0:T(8,128)(2,1)S(1)} %collective-permute-done.3), channel_id=1, source_target_pairs={{0,6},{2,0},{4,2},{6,4},{8,14},{10,8},{12,10},{14,12},{1,7},{3,1},... | collective-permute-start | bytes 405512 | tf_op jit(solution)/shard_map/ppermute | solution.py:152
  29.9 9.6 %collective-permute-start.7 = (bf16[2,4,128,128]{3,2,1,0:T(8,128)(2,1)S(1)}, bf16[2,4,128,128]{3,2,1,0:T(8,128)(2,1)S(1)}, u32[]{:S(2)}, u32[]{:S(2)}) collective-permute-start(bf16[2,4,128,128]{3,2,1,0:T(8,128)(2,1)S(1)} %pad_maximum_fusion), channel_id=1, source_target_pairs={{0,6},{2,0},{4,2},{6,4},{8,14},{10,8},{12,10},{14,12},{1,7},{3,1},... | collective-permute-start | bytes 786440 | tf_op jit(solution)/shard_map/ppermute | solution.py:170
  33.3 10.0 %collective-permute-start.8 = (bf16[2,4,128,128]{3,2,1,0:T(8,128)(2,1)S(1)}, bf16[2,4,128,128]{3,2,1,0:T(8,128)(2,1)S(1)}, u32[]{:S(2)}, u32[]{:S(2)}) collective-permute-start(bf16[2,4,128,128]{3,2,1,0:T(8,128)(2,1)S(1)} %pad_maximum_fusion.1), channel_id=1, source_target_pairs={{0,4},{2,6},{4,0},{6,2},{8,12},{10,14},{12,8},{14,10},{1,5},{3,7},... | collective-permute-start | bytes 786440 | tf_op jit(solution)/shard_map/ppermute | solution.py:170
  33.4 10.6 %collective-permute-start.9 = (bf16[2,4,128,128]{3,2,1,0:T(8,128)(2,1)S(1)}, bf16[2,4,128,128]{3,2,1,0:T(8,128)(2,1)S(1)}, u32[]{:S(2)}, u32[]{:S(2)}) collective-permute-start(bf16[2,4,128,128]{3,2,1,0:T(8,128)(2,1)S(1)} %pad_maximum_fusion.2), channel_id=1, source_target_pairs={{0,2},{2,4},{4,6},{6,0},{8,10},{10,12},{12,14},{14,8},{1,3},{3,5},... | collective-permute-start | bytes 786440 | tf_op jit(solution)/shard_map/ppermute | solution.py:170
  44.0 7.3 %collective-permute-start.10 = (bf16[4,128,128]{2,1,0:T(8,128)(2,1)S(1)}, bf16[4,128,128]{2,1,0:T(8,128)(2,1)S(1)}, u32[]{:S(2)}, u32[]{:S(2)}) collective-permute-start(bf16[4,128,128]{2,1,0:T(8,128)(2,1)S(1)} %fusion.1), channel_id=1, source_target_pairs={{0,8},{2,10},{4,12},{6,14},{8,0},{10,2},{12,4},{14,6},{1,9},{3,11}... | collective-permute-start | bytes 393224 | tf_op jit(solution)/shard_map/ppermute | solution.py:173

commit v9 on v8

--- a/solution.py
+++ b/solution.py
@@ -70,8 +70,9 @@
         for c in range(blocks // chunk_blocks):
             s, visible = chunk_scores(q, chunk_keys_of(c, g), c)
             new_max = jnp.maximum(run_max, jnp.max(s, axis=1, keepdims=True))
+            lifted = jnp.exp(s - new_max)
             run_total = run_total * jnp.exp(run_max - new_max) + jnp.sum(
-                jnp.exp(s - new_max), axis=1, keepdims=True
+                lifted, axis=1, keepdims=True
             )
             run_max = new_max
         log_total = run_max + jnp.log(run_total)
@@ -80,20 +81,22 @@
         for c in range(blocks // chunk_blocks):
             k = chunk_keys_of(c, g)
             v = chunk_values_of(c, g)
-            if not single:
+            if single:
+                probs = lifted * (1.0 / run_total)
+            else:
                 s, visible = chunk_scores(q, k, c)
-            probs = jnp.where(visible, jnp.exp(s - log_total), 0.0)
+                probs = jnp.exp(s - log_total)
             prob_grad = lax.dot_general(
                 do, v, (((1,), (1,)), ((), ())), preferred_element_type=f32
             )
             score_grad = (probs * (prob_grad - delta)).astype(jnp.bfloat16)
             dq = dq + jnp.dot(score_grad, k, preferred_element_type=f32)
             dk = scale * lax.dot_general(
-                score_grad, q, (((0,), (0,)), ((), ())), preferred_element_type=f32
-            )
+                q, score_grad, (((0,), (0,)), ((), ())), preferred_element_type=f32
+            ).T
             dv = lax.dot_general(
-                probs.astype(jnp.bfloat16), do, (((0,), (0,)), ((), ())), preferred_element_type=f32
-            )
+                do, probs.astype(jnp.bfloat16), (((0,), (0,)), ((), ())), preferred_element_type=f32
+            ).T
             for b in range(chunk_blocks):
                 block = c * chunk_blocks + b
                 piece = slice(b * tok_rows, (b + 1) * tok_rows)

time: 53.2 us -> 52.2 us (0.981)
  Pallas kernels: 5.12 us -> 4.1 us
    pallas_call x1, Pallas kernels: 5.12 us -> 4.1 us  [local_backward(): pl.pallas_call(functools.partial(backward_kernel, kv_heads=kv_heads, chun...]
where the time goes in v9:
time: 52.2 us; the launch traced here: 52 us
  waiting for transfers between devices  20.7 us (40%)
  starting transfers between devices  20.1 us (39%)
  Pallas kernels  4.1 us (8%)
  local copies, waits for them, and re-layouts  4.04 us (8%)
  other arithmetic  1.55 us (3%)
  between operations  1.52 us (3%)
    ppermute x3, waiting for transfers between devices, on_device(): lax.ppermute(pair, 'ctx', mate_pairs(cycle_size, half - k))  9.62 us
    ppermute x3, starting transfers between devices, on_device(): lax.ppermute(from_mirror, 'ctx', mate_pairs(cycle_size, k))  6.42 us
    ppermute x3, starting transfers between devices, on_device(): lax.ppermute(slab, 'ctx', mate_pairs(cycle_size, k))  6 us
    ppermute x1, waiting for transfers between devices, on_device(): lax.ppermute(mirror_total.astype(jnp.bfloat16), 'ctx', mirror_pairs(cycle...  5.47 us
    ppermute x3, starting transfers between devices, on_device(): lax.ppermute(pair, 'ctx', mate_pairs(cycle_size, half - k))  4.28 us
    pallas_call x1, Pallas kernels, local_backward(): pl.pallas_call(functools.partial(backward_kernel, kv_heads=kv_heads, chun...  4.1 us
    ppermute x1, waiting for transfers between devices, on_device(): from_mirror = lax.ppermute(slab, 'ctx', mirror_pairs(cycle_size))  3.16 us
    unnamed x13, local copies, waits for them, and re-layouts  2.78 us
  transfers between devices with their start and end apart: 11, of which 8 were waited for; matrix products, arithmetic and copies ran while one was open for 5% of the time, Pallas kernels for 0%

profile of v9, /device:TPU:0, one launch (start us, length us, event | category | flops | bytes accessed | tf_op | source)
XLA Modules:
  0.0 52.0 jit_solution(1671115250781940532)
XLA Ops:
  0.6 0.0 copy-start
  1.3 1.0 %maximum_bitcast_fusion = bf16[4,128,128]{2,0,1:T(4,128)(2,1)S(1)} fusion(bf16[128,2,128]{2,1,0:T(2,128)(2,1)} %param.8, bf16[128,2,128]{2,1,0:T(2,128)(2,1)} %param.7), kind=kLoop, calls=%fused_computation.30 | loop fusion | flops 262144 | bytes 262144 | tf_op jit(solution)/shard_map/transpose | solution.py:149
  2.4 3.0 %collective-permute-start = (bf16[528,128]{1,0:T(8,128)(2,1)S(1)}, bf16[528,128]{1,0:T(8,128)(2,1)S(1)}, u32[]{:S(2)}, u32[]{:S(2)}) collective-permute-start(bf16[528,128]{1,0:T(8,128)(2,1)S(1)} %concatenate.7), channel_id=1, source_target_pairs={{0,2},{2,4},{4,6},{6,0},{8,10},{10,12},{12,14},{14,8},{1,3},{3,5},... | collective-permute-start | bytes 405512 | tf_op jit(solution)/shard_map/ppermute | solution.py:152
  5.4 1.6 %collective-permute-start.1 = (bf16[528,128]{1,0:T(8,128)(2,1)S(1)}, bf16[528,128]{1,0:T(8,128)(2,1)S(1)}, u32[]{:S(2)}, u32[]{:S(2)}) collective-permute-start(bf16[528,128]{1,0:T(8,128)(2,1)S(1)} %concatenate.7), channel_id=1, source_target_pairs={{0,4},{2,6},{4,0},{6,2},{8,12},{10,14},{12,8},{14,10},{1,5},{3,7},... | collective-permute-start | bytes 405512 | tf_op jit(solution)/shard_map/ppermute | solution.py:152
  7.0 1.4 %collective-permute-start.2 = (bf16[528,128]{1,0:T(8,128)(2,1)S(1)}, bf16[528,128]{1,0:T(8,128)(2,1)S(1)}, u32[]{:S(2)}, u32[]{:S(2)}) collective-permute-start(bf16[528,128]{1,0:T(8,128)(2,1)S(1)} %concatenate.7), channel_id=1, source_target_pairs={{0,6},{2,0},{4,2},{6,4},{8,14},{10,8},{12,10},{14,12},{1,7},{3,1},... | collective-permute-start | bytes 405512 | tf_op jit(solution)/shard_map/ppermute | solution.py:152
  8.4 2.6 %collective-permute-start.3 = (bf16[528,128]{1,0:T(8,128)(2,1)S(1)}, bf16[528,128]{1,0:T(8,128)(2,1)S(1)}, u32[]{:S(2)}, u32[]{:S(2)}) collective-permute-start(bf16[528,128]{1,0:T(8,128)(2,1)S(1)} %concatenate.7), channel_id=1, source_target_pairs={{0,8},{2,10},{4,12},{6,14},{8,0},{10,2},{12,4},{14,6},{1,9},{3,11}... | collective-permute-start | bytes 405512 | tf_op jit(solution)/shard_map/ppermute | solution.py:153
  11.0 1.1 %copy_bitcast_fusion = (bf16[8,128,128]{2,1,0:T(8,128)(2,1)S(1)}, bf16[8,128,128]{2,1,0:T(8,128)(2,1)S(1)}) fusion(bf16[128,8,128]{2,1,0:T(8,128)(2,1)} %param.9, bf16[128,8,128]{2,1,0:T(8,128)(2,1)} %param.10), kind=kLoop, calls=%fused_computation.17 | loop fusion | bytes 1048576 | tf_op jit(solution)/shard_map/transpose | solution.py:165
  12.1 0.0 copy-done
  12.2 3.2 %collective-permute-done.3 = bf16[528,128]{1,0:T(8,128)(2,1)S(1)} collective-permute-done((bf16[528,128]{1,0:T(8,128)(2,1)S(1)}, bf16[528,128]{1,0:T(8,128)(2,1)S(1)}, u32[]{:S(2)}, u32[]{:S(2)}) %collective-permute-start.3) | collective-permute-done | bytes 135200 | tf_op jit(solution)/shard_map/ppermute | solution.py:153
  15.4 0.3 collective-permute-start.4
  15.6 3.5 %collective-permute-start.5 = (bf16[528,128]{1,0:T(8,128)(2,1)S(1)}, bf16[528,128]{1,0:T(8,128)(2,1)S(1)}, u32[]{:S(2)}, u32[]{:S(2)}) collective-permute-start(bf16[528,128]{1,0:T(8,128)(2,1)S(1)} %collective-permute-done.3), channel_id=1, source_target_pairs={{0,4},{2,6},{4,0},{6,2},{8,12},{10,14},{12,8},{14,10},{1,5},{3,7},... | collective-permute-start | bytes 405512 | tf_op jit(solution)/shard_map/ppermute | solution.py:155
  19.1 0.0 collective-permute-done
  19.1 2.7 %collective-permute-start.6 = (bf16[528,128]{1,0:T(8,128)(2,1)S(1)}, bf16[528,128]{1,0:T(8,128)(2,1)S(1)}, u32[]{:S(2)}, u32[]{:S(2)}) collective-permute-start(bf16[528,128]{1,0:T(8,128)(2,1)S(1)} %collective-permute-done.3), channel_id=1, source_target_pairs={{0,6},{2,0},{4,2},{6,4},{8,14},{10,8},{12,10},{14,12},{1,7},{3,1},... | collective-permute-start | bytes 405512 | tf_op jit(solution)/shard_map/ppermute | solution.py:155
  21.8 0.0 collective-permute-done.1
  21.8 0.0 collective-permute-done.2
  21.9 0.8 %collective-permute-done.4 = bf16[528,128]{1,0:T(8,128)(2,1)S(1)} collective-permute-done((bf16[528,128]{1,0:T(8,128)(2,1)S(1)}, bf16[528,128]{1,0:T(8,128)(2,1)S(1)}, u32[]{:S(2)}, u32[]{:S(2)}) %collective-permute-start.4) | collective-permute-done | bytes 135200 | tf_op jit(solution)/shard_map/ppermute | solution.py:155
  22.7 0.6 %collective-permute-done.5 = bf16[528,128]{1,0:T(8,128)(2,1)S(1)} collective-permute-done((bf16[528,128]{1,0:T(8,128)(2,1)S(1)}, bf16[528,128]{1,0:T(8,128)(2,1)S(1)}, u32[]{:S(2)}, u32[]{:S(2)}) %collective-permute-start.5) | collective-permute-done | bytes 135200 | tf_op jit(solution)/shard_map/ppermute | solution.py:155
  23.3 1.1 %collective-permute-done.6 = bf16[528,128]{1,0:T(8,128)(2,1)S(1)} collective-permute-done((bf16[528,128]{1,0:T(8,128)(2,1)S(1)}, bf16[528,128]{1,0:T(8,128)(2,1)S(1)}, u32[]{:S(2)}, u32[]{:S(2)}) %collective-permute-start.6) | collective-permute-done | bytes 135200 | tf_op jit(solution)/shard_map/ppermute | solution.py:155
  24.4 0.2 fusion.9.offs_ref
  24.6 4.1 %shard_map.85 = (f32[8,128,128]{2,1,0:T(8,128)S(1)}, f32[4,128,128]{2,1,0:T(8,128)S(1)}, f32[4,128,128]{2,1,0:T(8,128)S(1)}, bf16[7,4,128,128]{3,2,1,0:T(8,128)(2,1)S(1)}) custom-call(s32[8]{0:T(128)S(1)} %fusion.9.offs_ref, s32[1]{0:T(128)S(6)} %copy.34.own_ref, bf16[8,128,128]{2,1,0:T(8,128)(2,1)S(1)} %bitcast.69, ...), custom_call_target="tpu_custom_call" | custom-call | flops 1610612736 | bytes 2654208 | tf_op jit(solution)/shard_map/pallas_call | solution.py:123
  28.8 0.1 fusion.10
  28.9 3.3 %collective-permute-start.7 = (bf16[2,4,128,128]{3,2,1,0:T(8,128)(2,1)S(1)}, bf16[2,4,128,128]{3,2,1,0:T(8,128)(2,1)S(1)}, u32[]{:S(2)}, u32[]{:S(2)}) collective-permute-start(bf16[2,4,128,128]{3,2,1,0:T(8,128)(2,1)S(1)} %pad_maximum_fusion), channel_id=1, source_target_pairs={{0,6},{2,0},{4,2},{6,4},{8,14},{10,8},{12,10},{14,12},{1,7},{3,1},... | collective-permute-start | bytes 786440 | tf_op jit(solution)/shard_map/ppermute | solution.py:173
  32.2 0.1 collective-permute-start.8
  32.4 0.9 %collective-permute-start.9 = (bf16[2,4,128,128]{3,2,1,0:T(8,128)(2,1)S(1)}, bf16[2,4,128,128]{3,2,1,0:T(8,128)(2,1)S(1)}, u32[]{:S(2)}, u32[]{:S(2)}) collective-permute-start(bf16[2,4,128,128]{3,2,1,0:T(8,128)(2,1)S(1)} %pad_maximum_fusion.2), channel_id=1, source_target_pairs={{0,2},{2,4},{4,6},{6,0},{8,10},{10,12},{12,14},{14,8},{1,3},{3,5},... | collective-permute-start | bytes 786440 | tf_op jit(solution)/shard_map/ppermute | solution.py:173
  33.2 5.3 %collective-permute-done.7 = bf16[2,4,128,128]{3,2,1,0:T(8,128)(2,1)S(1)} collective-permute-done((bf16[2,4,128,128]{3,2,1,0:T(8,128)(2,1)S(1)}, bf16[2,4,128,128]{3,2,1,0:T(8,128)(2,1)S(1)}, u32[]{:S(2)}, u32[]{:S(2)}) %collective-permute-start.7) | collective-permute-done | bytes 262176 | tf_op jit(solution)/shard_map/ppermute | solution.py:173
  38.5 3.7 %collective-permute-done.8 = bf16[2,4,128,128]{3,2,1,0:T(8,128)(2,1)S(1)} collective-permute-done((bf16[2,4,128,128]{3,2,1,0:T(8,128)(2,1)S(1)}, bf16[2,4,128,128]{3,2,1,0:T(8,128)(2,1)S(1)}, u32[]{:S(2)}, u32[]{:S(2)}) %collective-permute-start.8) | collective-permute-done | bytes 262176 | tf_op jit(solution)/shard_map/ppermute | solution.py:173
  42.3 0.6 %collective-permute-done.9 = bf16[2,4,128,128]{3,2,1,0:T(8,128)(2,1)S(1)} collective-permute-done((bf16[2,4,128,128]{3,2,1,0:T(8,128)(2,1)S(1)}, bf16[2,4,128,128]{3,2,1,0:T(8,128)(2,1)S(1)}, u32[]{:S(2)}, u32[]{:S(2)}) %collective-permute-start.9) | collective-permute-done | bytes 262176 | tf_op jit(solution)/shard_map/ppermute | solution.py:173
  43.0 0.1 fusion.1
  43.0 0.8 %collective-permute-start.10 = (bf16[4,128,128]{2,1,0:T(8,128)(2,1)S(1)}, bf16[4,128,128]{2,1,0:T(8,128)(2,1)S(1)}, u32[]{:S(2)}, u32[]{:S(2)}) collective-permute-start(bf16[4,128,128]{2,1,0:T(8,128)(2,1)S(1)} %fusion.1), channel_id=1, source_target_pairs={{0,8},{2,10},{4,12},{6,14},{8,0},{10,2},{12,4},{14,6},{1,9},{3,11}... | collective-permute-start | bytes 393224 | tf_op jit(solution)/shard_map/ppermute | solution.py:176
  43.8 1.1 %copy.20 = f32[128,8,128]{2,1,0:T(8,128)} copy(f32[128,8,128]{2,0,1:T(8,128)S(1)} %bitcast.68) | data formatting | bytes 1048576
  44.9 5.5 %collective-permute-done.10 = bf16[4,128,128]{2,1,0:T(8,128)(2,1)S(1)} collective-permute-done((bf16[4,128,128]{2,1,0:T(8,128)(2,1)S(1)}, bf16[4,128,128]{2,1,0:T(8,128)(2,1)S(1)}, u32[]{:S(2)}, u32[]{:S(2)}) %collective-permute-start.10) | collective-permute-done | bytes 131104 | tf_op jit(solution)/shard_map/ppermute | solution.py:176
  50.4 0.1 fusion.5
  50.4 0.8 %copy.21 = f32[128,2,128]{2,1,0:T(2,128)} copy(f32[128,2,128]{2,0,1:T(8,128)S(1)} %get-tuple-element.24) | data formatting | bytes 262144
  51.2 0.8 %copy.22 = f32[128,2,128]{2,1,0:T(2,128)} copy(f32[128,2,128]{2,0,1:T(8,128)S(1)} %get-tuple-element.23) | data formatting | bytes 262144
  (18 shorter events, 0.4 us)
Async XLA Ops:
  0.6 11.5 %copy-start = (bf16[128,8,128]{2,1,0:T(8,128)(2,1)S(1)}, bf16[128,8,128]{2,1,0:T(8,128)(2,1)}, u32[]{:S(2)}) copy-start(bf16[128,8,128]{2,1,0:T(8,128)(2,1)} %param.6) | copy-start | bytes 786436
  2.4 16.7 %collective-permute-start = (bf16[528,128]{1,0:T(8,128)(2,1)S(1)}, bf16[528,128]{1,0:T(8,128)(2,1)S(1)}, u32[]{:S(2)}, u32[]{:S(2)}) collective-permute-start(bf16[528,128]{1,0:T(8,128)(2,1)S(1)} %concatenate.7), channel_id=1, source_target_pairs={{0,2},{2,4},{4,6},{6,0},{8,10},{10,12},{12,14},{14,8},{1,3},{3,5},... | collective-permute-start | bytes 405512 | tf_op jit(solution)/shard_map/ppermute | solution.py:152
  5.4 16.4 %collective-permute-start.1 = (bf16[528,128]{1,0:T(8,128)(2,1)S(1)}, bf16[528,128]{1,0:T(8,128)(2,1)S(1)}, u32[]{:S(2)}, u32[]{:S(2)}) collective-permute-start(bf16[528,128]{1,0:T(8,128)(2,1)S(1)} %concatenate.7), channel_id=1, source_target_pairs={{0,4},{2,6},{4,0},{6,2},{8,12},{10,14},{12,8},{14,10},{1,5},{3,7},... | collective-permute-start | bytes 405512 | tf_op jit(solution)/shard_map/ppermute | solution.py:152
  7.0 14.8 %collective-permute-start.2 = (bf16[528,128]{1,0:T(8,128)(2,1)S(1)}, bf16[528,128]{1,0:T(8,128)(2,1)S(1)}, u32[]{:S(2)}, u32[]{:S(2)}) collective-permute-start(bf16[528,128]{1,0:T(8,128)(2,1)S(1)} %concatenate.7), channel_id=1, source_target_pairs={{0,6},{2,0},{4,2},{6,4},{8,14},{10,8},{12,10},{14,12},{1,7},{3,1},... | collective-permute-start | bytes 405512 | tf_op jit(solution)/shard_map/ppermute | solution.py:152
  8.4 7.0 %collective-permute-start.3 = (bf16[528,128]{1,0:T(8,128)(2,1)S(1)}, bf16[528,128]{1,0:T(8,128)(2,1)S(1)}, u32[]{:S(2)}, u32[]{:S(2)}) collective-permute-start(bf16[528,128]{1,0:T(8,128)(2,1)S(1)} %concatenate.7), channel_id=1, source_target_pairs={{0,8},{2,10},{4,12},{6,14},{8,0},{10,2},{12,4},{14,6},{1,9},{3,11}... | collective-permute-start | bytes 405512 | tf_op jit(solution)/shard_map/ppermute | solution.py:153
  15.4 7.3 %collective-permute-start.4 = (bf16[528,128]{1,0:T(8,128)(2,1)S(1)}, bf16[528,128]{1,0:T(8,128)(2,1)S(1)}, u32[]{:S(2)}, u32[]{:S(2)}) collective-permute-start(bf16[528,128]{1,0:T(8,128)(2,1)S(1)} %collective-permute-done.3), channel_id=1, source_target_pairs={{0,2},{2,4},{4,6},{6,0},{8,10},{10,12},{12,14},{14,8},{1,3},{3,5},... | collective-permute-start | bytes 405512 | tf_op jit(solution)/shard_map/ppermute | solution.py:155
  15.6 7.7 %collective-permute-start.5 = (bf16[528,128]{1,0:T(8,128)(2,1)S(1)}, bf16[528,128]{1,0:T(8,128)(2,1)S(1)}, u32[]{:S(2)}, u32[]{:S(2)}) collective-permute-start(bf16[528,128]{1,0:T(8,128)(2,1)S(1)} %collective-permute-done.3), channel_id=1, source_target_pairs={{0,4},{2,6},{4,0},{6,2},{8,12},{10,14},{12,8},{14,10},{1,5},{3,7},... | collective-permute-start | bytes 405512 | tf_op jit(solution)/shard_map/ppermute | solution.py:155
  19.1 5.3 %collective-permute-start.6 = (bf16[528,128]{1,0:T(8,128)(2,1)S(1)}, bf16[528,128]{1,0:T(8,128)(2,1)S(1)}, u32[]{:S(2)}, u32[]{:S(2)}) collective-permute-start(bf16[528,128]{1,0:T(8,128)(2,1)S(1)} %collective-permute-done.3), channel_id=1, source_target_pairs={{0,6},{2,0},{4,2},{6,4},{8,14},{10,8},{12,10},{14,12},{1,7},{3,1},... | collective-permute-start | bytes 405512 | tf_op jit(solution)/shard_map/ppermute | solution.py:155
  28.9 9.6 %collective-permute-start.7 = (bf16[2,4,128,128]{3,2,1,0:T(8,128)(2,1)S(1)}, bf16[2,4,128,128]{3,2,1,0:T(8,128)(2,1)S(1)}, u32[]{:S(2)}, u32[]{:S(2)}) collective-permute-start(bf16[2,4,128,128]{3,2,1,0:T(8,128)(2,1)S(1)} %pad_maximum_fusion), channel_id=1, source_target_pairs={{0,6},{2,0},{4,2},{6,4},{8,14},{10,8},{12,10},{14,12},{1,7},{3,1},... | collective-permute-start | bytes 786440 | tf_op jit(solution)/shard_map/ppermute | solution.py:173
  32.2 10.0 %collective-permute-start.8 = (bf16[2,4,128,128]{3,2,1,0:T(8,128)(2,1)S(1)}, bf16[2,4,128,128]{3,2,1,0:T(8,128)(2,1)S(1)}, u32[]{:S(2)}, u32[]{:S(2)}) collective-permute-start(bf16[2,4,128,128]{3,2,1,0:T(8,128)(2,1)S(1)} %pad_maximum_fusion.1), channel_id=1, source_target_pairs={{0,4},{2,6},{4,0},{6,2},{8,12},{10,14},{12,8},{14,10},{1,5},{3,7},... | collective-permute-start | bytes 786440 | tf_op jit(solution)/shard_map/ppermute | solution.py:173
  32.4 10.6 %collective-permute-start.9 = (bf16[2,4,128,128]{3,2,1,0:T(8,128)(2,1)S(1)}, bf16[2,4,128,128]{3,2,1,0:T(8,128)(2,1)S(1)}, u32[]{:S(2)}, u32[]{:S(2)}) collective-permute-start(bf16[2,4,128,128]{3,2,1,0:T(8,128)(2,1)S(1)} %pad_maximum_fusion.2), channel_id=1, source_target_pairs={{0,2},{2,4},{4,6},{6,0},{8,10},{10,12},{12,14},{14,8},{1,3},{3,5},... | collective-permute-start | bytes 786440 | tf_op jit(solution)/shard_map/ppermute | solution.py:173
  43.0 7.3 %collective-permute-start.10 = (bf16[4,128,128]{2,1,0:T(8,128)(2,1)S(1)}, bf16[4,128,128]{2,1,0:T(8,128)(2,1)S(1)}, u32[]{:S(2)}, u32[]{:S(2)}) collective-permute-start(bf16[4,128,128]{2,1,0:T(8,128)(2,1)S(1)} %fusion.1), channel_id=1, source_target_pairs={{0,8},{2,10},{4,12},{6,14},{8,0},{10,2},{12,4},{14,6},{1,9},{3,11}... | collective-permute-start | bytes 393224 | tf_op jit(solution)/shard_map/ppermute | solution.py:176

commit v10 on v9

--- a/solution.py
+++ b/solution.py
@@ -14,7 +14,8 @@
 
 def mate_pairs(peers, by):
     half = peers // 2
-    return [(i, half * (i // half) + (i % half + by) % half) for i in range(peers)]
+    assert half & (half - 1) == 0
+    return [(i, half * (i // half) + ((i % half) ^ by)) for i in range(peers)]
 
 
 def mirror_pairs(peers):
@@ -149,12 +150,21 @@
     paired = jnp.concatenate([key_vectors, value_rows], axis=1).transpose(1, 0, 2)
     slab = jnp.concatenate([paired.reshape(2 * kv_rows, head_width), offset_rows], axis=0)
     half = cycle_size // 2
-    from_mates = [lax.ppermute(slab, "ctx", mate_pairs(cycle_size, k)) for k in range(1, half)]
     from_mirror = lax.ppermute(slab, "ctx", mirror_pairs(cycle_size))
-    handed_on = [
-        lax.ppermute(from_mirror, "ctx", mate_pairs(cycle_size, k)) for k in range(1, half)
-    ]
-    gathered = jnp.stack([slab] + from_mates + [from_mirror] + handed_on)
+    if half == 4:
+        from_x1 = lax.ppermute(slab, "ctx", mate_pairs(cycle_size, 1))
+        from_x2 = lax.ppermute(slab, "ctx", mate_pairs(cycle_size, 2))
+        pair = lax.ppermute(jnp.stack([from_mirror, from_x2]), "ctx", mate_pairs(cycle_size, 1))
+        mirror_of_x2 = lax.ppermute(from_mirror, "ctx", mate_pairs(cycle_size, 2))
+        mirror_of_x3 = lax.ppermute(from_mirror, "ctx", mate_pairs(cycle_size, 3))
+        blocks = [slab, from_x1, from_x2, pair[1], from_mirror, pair[0], mirror_of_x2, mirror_of_x3]
+    else:
+        from_mates = [lax.ppermute(slab, "ctx", mate_pairs(cycle_size, k)) for k in range(1, half)]
+        handed_on = [
+            lax.ppermute(from_mirror, "ctx", mate_pairs(cycle_size, k)) for k in range(1, half)
+        ]
+        blocks = [slab] + from_mates + [from_mirror] + handed_on
+    gathered = jnp.stack(blocks)
     all_offsets = gathered[:, 2 * kv_rows, 0].astype(jnp.float32).astype(jnp.int32)
 
     dq_t, own_part, mirror_part, parts = local_backward(
@@ -170,7 +180,7 @@
     mirror_total = mirror_part
     for k in range(1, half):
         pair = jnp.stack([parts[k - 1], parts[half + k - 1]])
-        arrived = lax.ppermute(pair, "ctx", mate_pairs(cycle_size, half - k)).astype(jnp.float32)
+        arrived = lax.ppermute(pair, "ctx", mate_pairs(cycle_size, k)).astype(jnp.float32)
         own_total = own_total + arrived[0]
         mirror_total = mirror_total + arrived[1]
     crossed = lax.ppermute(mirror_total.astype(jnp.bfloat16), "ctx", mirror_pairs(cycle_size))

time: 52.2 us -> 52.4 us (level)
  waiting for transfers between devices: 20.7 us -> 21.3 us
    ppermute x9 -> x8, starting transfers between devices: 16.7 us -> 10.3 us  [the longest x3 3.68 us: on_device(): lax.ppermute(pair, 'ctx', mate_pairs(cycle_size, k)).astype(jnp.float32)]
    ppermute x1, starting transfers between devices: 0.77 us -> 5.2 us  [on_device(): lax.ppermute(mirror_total.astype(jnp.bfloat16), 'ctx', mirror_pairs(cycle...]
    ppermute x9 -> x8, waiting for transfers between devices: 12.1 us -> 15.4 us  [the longest x3 8.62 us: on_device(): lax.ppermute(pair, 'ctx', mate_pairs(cycle_size, k)).astype(jnp.float32)]
    ppermute x1, waiting for transfers between devices: 5.47 us -> 3.62 us  [on_device(): lax.ppermute(mirror_total.astype(jnp.bfloat16), 'ctx', mirror_pairs(cycle...]
    ppermute x1, starting transfers between devices: 2.59 us -> 4.1 us  [on_device(): from_mirror = lax.ppermute(slab, 'ctx', mirror_pairs(cycle_size))]
    ppermute x1, waiting for transfers between devices: 3.16 us -> 2.29 us  [on_device(): from_mirror = lax.ppermute(slab, 'ctx', mirror_pairs(cycle_size))]
  transfers between devices with their start and end apart: 11 -> 10, of which waited for: 8 -> 6; matrix products, arithmetic and copies ran while one was open for 5% -> 5% of each run, Pallas kernels for 0% -> 0%
where the time goes in v10:
time: 52.4 us; the launch traced here: 52.2 us
  waiting for transfers between devices  21.3 us (41%)
  starting transfers between devices  19.6 us (37%)
  Pallas kernels  4.1 us (8%)
  local copies, waits for them, and re-layouts  4.05 us (8%)
  other arithmetic  1.58 us (3%)
  between operations  1.53 us (3%)
    ppermute x3, waiting for transfers between devices, on_device(): lax.ppermute(pair, 'ctx', mate_pairs(cycle_size, k)).astype(jnp.float32)  8.62 us
    ppermute x1, waiting for transfers between devices, on_device(): lax.ppermute(jnp.stack([from_mirror, from_x2]), 'ctx', mate_pairs(cycle_s...  6.57 us
    ppermute x1, starting transfers between devices, on_device(): lax.ppermute(mirror_total.astype(jnp.bfloat16), 'ctx', mirror_pairs(cycle...  5.2 us
    pallas_call x1, Pallas kernels, local_backward(): pl.pallas_call(functools.partial(backward_kernel, kv_heads=kv_heads, chun...  4.1 us
    ppermute x1, starting transfers between devices, on_device(): from_mirror = lax.ppermute(slab, 'ctx', mirror_pairs(cycle_size))  4.1 us
    ppermute x3, starting transfers between devices, on_device(): lax.ppermute(pair, 'ctx', mate_pairs(cycle_size, k)).astype(jnp.float32)  3.68 us
    ppermute x1, waiting for transfers between devices, on_device(): lax.ppermute(mirror_total.astype(jnp.bfloat16), 'ctx', mirror_pairs(cycle...  3.62 us
    unnamed x13, local copies, waits for them, and re-layouts  2.78 us
  transfers between devices with their start and end apart: 10, of which 6 were waited for; matrix products, arithmetic and copies ran while one was open for 5% of the time, Pallas kernels for 0%

profile of v10, /device:TPU:0, one launch (start us, length us, event | category | flops | bytes accessed | tf_op | source)
XLA Modules:
  0.0 52.2 jit_solution(4954630058237603571)
XLA Ops:
  0.6 0.0 copy-start
  1.3 1.0 %maximum_bitcast_fusion = bf16[4,128,128]{2,0,1:T(4,128)(2,1)S(1)} fusion(bf16[128,2,128]{2,1,0:T(2,128)(2,1)} %param.8, bf16[128,2,128]{2,1,0:T(2,128)(2,1)} %param.7), kind=kLoop, calls=%fused_computation.29 | loop fusion | flops 262144 | bytes 262144 | tf_op jit(solution)/shard_map/transpose | solution.py:150
  2.4 4.1 %collective-permute-start.2 = (bf16[528,128]{1,0:T(8,128)(2,1)S(1)}, bf16[528,128]{1,0:T(8,128)(2,1)S(1)}, u32[]{:S(2)}, u32[]{:S(2)}) collective-permute-start(bf16[528,128]{1,0:T(8,128)(2,1)S(1)} %concatenate.7), channel_id=1, source_target_pairs={{0,8},{2,10},{4,12},{6,14},{8,0},{10,2},{12,4},{14,6},{1,9},{3,11}... | collective-permute-start | bytes 405512 | tf_op jit(solution)/shard_map/ppermute | solution.py:153
  6.5 1.6 %collective-permute-start.1 = (bf16[528,128]{1,0:T(8,128)(2,1)S(1)}, bf16[528,128]{1,0:T(8,128)(2,1)S(1)}, u32[]{:S(2)}, u32[]{:S(2)}) collective-permute-start(bf16[528,128]{1,0:T(8,128)(2,1)S(1)} %concatenate.7), channel_id=1, source_target_pairs={{0,4},{2,6},{4,0},{6,2},{8,12},{10,14},{12,8},{14,10},{1,5},{3,7},... | collective-permute-start | bytes 405512 | tf_op jit(solution)/shard_map/ppermute | solution.py:156
  8.1 1.5 %collective-permute-start = (bf16[528,128]{1,0:T(8,128)(2,1)S(1)}, bf16[528,128]{1,0:T(8,128)(2,1)S(1)}, u32[]{:S(2)}, u32[]{:S(2)}) collective-permute-start(bf16[528,128]{1,0:T(8,128)(2,1)S(1)} %concatenate.7), channel_id=1, source_target_pairs={{0,2},{2,0},{4,6},{6,4},{8,10},{10,8},{12,14},{14,12},{1,3},{3,1},... | collective-permute-start | bytes 405512 | tf_op jit(solution)/shard_map/ppermute | solution.py:155
  9.6 1.1 %copy_bitcast_fusion = (bf16[8,128,128]{2,1,0:T(8,128)(2,1)S(1)}, bf16[8,128,128]{2,1,0:T(8,128)(2,1)S(1)}) fusion(bf16[128,8,128]{2,1,0:T(8,128)(2,1)} %param.9, bf16[128,8,128]{2,1,0:T(8,128)(2,1)} %param.10), kind=kLoop, calls=%fused_computation.18 | loop fusion | bytes 1048576 | tf_op jit(solution)/shard_map/transpose | solution.py:175
  10.7 0.0 copy-done
  10.8 2.3 %collective-permute-done.2 = bf16[528,128]{1,0:T(8,128)(2,1)S(1)} collective-permute-done((bf16[528,128]{1,0:T(8,128)(2,1)S(1)}, bf16[528,128]{1,0:T(8,128)(2,1)S(1)}, u32[]{:S(2)}, u32[]{:S(2)}) %collective-permute-start.2) | collective-permute-done | bytes 135200 | tf_op jit(solution)/shard_map/ppermute | solution.py:153
  13.1 0.2 collective-permute-done.1
  13.3 1.6 %collective-permute-start.3 = (bf16[2,528,128]{2,1,0:T(8,128)(2,1)S(1)}, bf16[2,528,128]{2,1,0:T(8,128)(2,1)S(1)}, u32[]{:S(2)}, u32[]{:S(2)}) collective-permute-start(bf16[2,528,128]{2,1,0:T(8,128)(2,1)S(1)} %pad_maximum_fusion), channel_id=1, source_target_pairs={{0,2},{2,0},{4,6},{6,4},{8,10},{10,8},{12,14},{14,12},{1,3},{3,1},... | collective-permute-start | bytes 811016 | tf_op jit(solution)/shard_map/ppermute | solution.py:157
  14.9 1.4 %collective-permute-start.4 = (bf16[528,128]{1,0:T(8,128)(2,1)S(1)}, bf16[528,128]{1,0:T(8,128)(2,1)S(1)}, u32[]{:S(2)}, u32[]{:S(2)}) collective-permute-start(bf16[528,128]{1,0:T(8,128)(2,1)S(1)} %collective-permute-done.2), channel_id=1, source_target_pairs={{0,4},{2,6},{4,0},{6,2},{8,12},{10,14},{12,8},{14,10},{1,5},{3,7},... | collective-permute-start | bytes 405512 | tf_op jit(solution)/shard_map/ppermute | solution.py:158
  16.4 0.5 collective-permute-start.5
  16.9 0.0 collective-permute-done
  16.9 6.6 %collective-permute-done.3 = bf16[2,528,128]{2,1,0:T(8,128)(2,1)S(1)} collective-permute-done((bf16[2,528,128]{2,1,0:T(8,128)(2,1)S(1)}, bf16[2,528,128]{2,1,0:T(8,128)(2,1)S(1)}, u32[]{:S(2)}, u32[]{:S(2)}) %collective-permute-start.3) | collective-permute-done | bytes 270368 | tf_op jit(solution)/shard_map/ppermute | solution.py:157
  23.6 0.0 collective-permute-done.4
  23.6 0.0 collective-permute-done.5
  23.6 0.2 fusion.9.offs_ref
  23.9 4.1 %shard_map.85 = (f32[8,128,128]{2,1,0:T(8,128)S(1)}, f32[4,128,128]{2,1,0:T(8,128)S(1)}, f32[4,128,128]{2,1,0:T(8,128)S(1)}, bf16[7,4,128,128]{3,2,1,0:T(8,128)(2,1)S(1)}) custom-call(s32[8]{0:T(128)S(1)} %fusion.9.offs_ref, s32[1]{0:T(128)S(6)} %copy.34.own_ref, bf16[8,128,128]{2,1,0:T(8,128)(2,1)S(1)} %bitcast.65, ...), custom_call_target="tpu_custom_call" | custom-call | flops 1610612736 | bytes 2654208 | tf_op jit(solution)/shard_map/pallas_call | solution.py:124
  28.0 0.1 fusion.10
  28.1 1.1 %collective-permute-start.6 = (bf16[2,4,128,128]{3,2,1,0:T(8,128)(2,1)S(1)}, bf16[2,4,128,128]{3,2,1,0:T(8,128)(2,1)S(1)}, u32[]{:S(2)}, u32[]{:S(2)}) collective-permute-start(bf16[2,4,128,128]{3,2,1,0:T(8,128)(2,1)S(1)} %pad_maximum_fusion.1), channel_id=1, source_target_pairs={{0,2},{2,0},{4,6},{6,4},{8,10},{10,8},{12,14},{14,12},{1,3},{3,1},... | collective-permute-start | bytes 786440 | tf_op jit(solution)/shard_map/ppermute | solution.py:183
  29.2 2.2 %collective-permute-start.7 = (bf16[2,4,128,128]{3,2,1,0:T(8,128)(2,1)S(1)}, bf16[2,4,128,128]{3,2,1,0:T(8,128)(2,1)S(1)}, u32[]{:S(2)}, u32[]{:S(2)}) collective-permute-start(bf16[2,4,128,128]{3,2,1,0:T(8,128)(2,1)S(1)} %pad_maximum_fusion.2), channel_id=1, source_target_pairs={{0,4},{2,6},{4,0},{6,2},{8,12},{10,14},{12,8},{14,10},{1,5},{3,7},... | collective-permute-start | bytes 786440 | tf_op jit(solution)/shard_map/ppermute | solution.py:183
  31.4 0.4 collective-permute-start.8
  31.8 5.5 %collective-permute-done.6 = bf16[2,4,128,128]{3,2,1,0:T(8,128)(2,1)S(1)} collective-permute-done((bf16[2,4,128,128]{3,2,1,0:T(8,128)(2,1)S(1)}, bf16[2,4,128,128]{3,2,1,0:T(8,128)(2,1)S(1)}, u32[]{:S(2)}, u32[]{:S(2)}) %collective-permute-start.6) | collective-permute-done | bytes 262176 | tf_op jit(solution)/shard_map/ppermute | solution.py:183
  37.4 0.0 collective-permute-done.7
  37.4 3.1 %collective-permute-done.8 = bf16[2,4,128,128]{3,2,1,0:T(8,128)(2,1)S(1)} collective-permute-done((bf16[2,4,128,128]{3,2,1,0:T(8,128)(2,1)S(1)}, bf16[2,4,128,128]{3,2,1,0:T(8,128)(2,1)S(1)}, u32[]{:S(2)}, u32[]{:S(2)}) %collective-permute-start.8) | collective-permute-done | bytes 262176 | tf_op jit(solution)/shard_map/ppermute | solution.py:183
  40.6 0.1 fusion.1
  40.7 5.2 %collective-permute-start.9 = (bf16[4,128,128]{2,1,0:T(8,128)(2,1)S(1)}, bf16[4,128,128]{2,1,0:T(8,128)(2,1)S(1)}, u32[]{:S(2)}, u32[]{:S(2)}) collective-permute-start(bf16[4,128,128]{2,1,0:T(8,128)(2,1)S(1)} %fusion.1), channel_id=1, source_target_pairs={{0,8},{2,10},{4,12},{6,14},{8,0},{10,2},{12,4},{14,6},{1,9},{3,11}... | collective-permute-start | bytes 393224 | tf_op jit(solution)/shard_map/ppermute | solution.py:186
  45.9 1.1 %copy.20 = f32[128,8,128]{2,1,0:T(8,128)} copy(f32[128,8,128]{2,0,1:T(8,128)S(1)} %bitcast.64) | data formatting | bytes 1048576
  47.0 3.6 %collective-permute-done.9 = bf16[4,128,128]{2,1,0:T(8,128)(2,1)S(1)} collective-permute-done((bf16[4,128,128]{2,1,0:T(8,128)(2,1)S(1)}, bf16[4,128,128]{2,1,0:T(8,128)(2,1)S(1)}, u32[]{:S(2)}, u32[]{:S(2)}) %collective-permute-start.9) | collective-permute-done | bytes 131104 | tf_op jit(solution)/shard_map/ppermute | solution.py:186
  50.6 0.1 fusion.5
  50.7 0.8 %copy.21 = f32[128,2,128]{2,1,0:T(2,128)} copy(f32[128,2,128]{2,0,1:T(8,128)S(1)} %get-tuple-element.24) | data formatting | bytes 262144
  51.4 0.8 %copy.22 = f32[128,2,128]{2,1,0:T(2,128)} copy(f32[128,2,128]{2,0,1:T(8,128)S(1)} %get-tuple-element.23) | data formatting | bytes 262144
  (19 shorter events, 0.4 us)
Async XLA Ops:
  0.6 10.1 %copy-start = (bf16[128,8,128]{2,1,0:T(8,128)(2,1)S(1)}, bf16[128,8,128]{2,1,0:T(8,128)(2,1)}, u32[]{:S(2)}) copy-start(bf16[128,8,128]{2,1,0:T(8,128)(2,1)} %param.6) | copy-start | bytes 786436
  2.4 10.7 %collective-permute-start.2 = (bf16[528,128]{1,0:T(8,128)(2,1)S(1)}, bf16[528,128]{1,0:T(8,128)(2,1)S(1)}, u32[]{:S(2)}, u32[]{:S(2)}) collective-permute-start(bf16[528,128]{1,0:T(8,128)(2,1)S(1)} %concatenate.7), channel_id=1, source_target_pairs={{0,8},{2,10},{4,12},{6,14},{8,0},{10,2},{12,4},{14,6},{1,9},{3,11}... | collective-permute-start | bytes 405512 | tf_op jit(solution)/shard_map/ppermute | solution.py:153
  6.5 6.8 %collective-permute-start.1 = (bf16[528,128]{1,0:T(8,128)(2,1)S(1)}, bf16[528,128]{1,0:T(8,128)(2,1)S(1)}, u32[]{:S(2)}, u32[]{:S(2)}) collective-permute-start(bf16[528,128]{1,0:T(8,128)(2,1)S(1)} %concatenate.7), channel_id=1, source_target_pairs={{0,4},{2,6},{4,0},{6,2},{8,12},{10,14},{12,8},{14,10},{1,5},{3,7},... | collective-permute-start | bytes 405512 | tf_op jit(solution)/shard_map/ppermute | solution.py:156
  8.1 8.8 %collective-permute-start = (bf16[528,128]{1,0:T(8,128)(2,1)S(1)}, bf16[528,128]{1,0:T(8,128)(2,1)S(1)}, u32[]{:S(2)}, u32[]{:S(2)}) collective-permute-start(bf16[528,128]{1,0:T(8,128)(2,1)S(1)} %concatenate.7), channel_id=1, source_target_pairs={{0,2},{2,0},{4,6},{6,4},{8,10},{10,8},{12,14},{14,12},{1,3},{3,1},... | collective-permute-start | bytes 405512 | tf_op jit(solution)/shard_map/ppermute | solution.py:155
  13.3 10.2 %collective-permute-start.3 = (bf16[2,528,128]{2,1,0:T(8,128)(2,1)S(1)}, bf16[2,528,128]{2,1,0:T(8,128)(2,1)S(1)}, u32[]{:S(2)}, u32[]{:S(2)}) collective-permute-start(bf16[2,528,128]{2,1,0:T(8,128)(2,1)S(1)} %pad_maximum_fusion), channel_id=1, source_target_pairs={{0,2},{2,0},{4,6},{6,4},{8,10},{10,8},{12,14},{14,12},{1,3},{3,1},... | collective-permute-start | bytes 811016 | tf_op jit(solution)/shard_map/ppermute | solution.py:157
  14.9 8.6 %collective-permute-start.4 = (bf16[528,128]{1,0:T(8,128)(2,1)S(1)}, bf16[528,128]{1,0:T(8,128)(2,1)S(1)}, u32[]{:S(2)}, u32[]{:S(2)}) collective-permute-start(bf16[528,128]{1,0:T(8,128)(2,1)S(1)} %collective-permute-done.2), channel_id=1, source_target_pairs={{0,4},{2,6},{4,0},{6,2},{8,12},{10,14},{12,8},{14,10},{1,5},{3,7},... | collective-permute-start | bytes 405512 | tf_op jit(solution)/shard_map/ppermute | solution.py:158
  16.4 7.3 %collective-permute-start.5 = (bf16[528,128]{1,0:T(8,128)(2,1)S(1)}, bf16[528,128]{1,0:T(8,128)(2,1)S(1)}, u32[]{:S(2)}, u32[]{:S(2)}) collective-permute-start(bf16[528,128]{1,0:T(8,128)(2,1)S(1)} %collective-permute-done.2), channel_id=1, source_target_pairs={{0,6},{2,4},{4,2},{6,0},{8,14},{10,12},{12,10},{14,8},{1,7},{3,5},... | collective-permute-start | bytes 405512 | tf_op jit(solution)/shard_map/ppermute | solution.py:159
  28.1 9.2 %collective-permute-start.6 = (bf16[2,4,128,128]{3,2,1,0:T(8,128)(2,1)S(1)}, bf16[2,4,128,128]{3,2,1,0:T(8,128)(2,1)S(1)}, u32[]{:S(2)}, u32[]{:S(2)}) collective-permute-start(bf16[2,4,128,128]{3,2,1,0:T(8,128)(2,1)S(1)} %pad_maximum_fusion.1), channel_id=1, source_target_pairs={{0,2},{2,0},{4,6},{6,4},{8,10},{10,8},{12,14},{14,12},{1,3},{3,1},... | collective-permute-start | bytes 786440 | tf_op jit(solution)/shard_map/ppermute | solution.py:183
  29.2 8.2 %collective-permute-start.7 = (bf16[2,4,128,128]{3,2,1,0:T(8,128)(2,1)S(1)}, bf16[2,4,128,128]{3,2,1,0:T(8,128)(2,1)S(1)}, u32[]{:S(2)}, u32[]{:S(2)}) collective-permute-start(bf16[2,4,128,128]{3,2,1,0:T(8,128)(2,1)S(1)} %pad_maximum_fusion.2), channel_id=1, source_target_pairs={{0,4},{2,6},{4,0},{6,2},{8,12},{10,14},{12,8},{14,10},{1,5},{3,7},... | collective-permute-start | bytes 786440 | tf_op jit(solution)/shard_map/ppermute | solution.py:183
  31.4 9.1 %collective-permute-start.8 = (bf16[2,4,128,128]{3,2,1,0:T(8,128)(2,1)S(1)}, bf16[2,4,128,128]{3,2,1,0:T(8,128)(2,1)S(1)}, u32[]{:S(2)}, u32[]{:S(2)}) collective-permute-start(bf16[2,4,128,128]{3,2,1,0:T(8,128)(2,1)S(1)} %pad_maximum_fusion.3), channel_id=1, source_target_pairs={{0,6},{2,4},{4,2},{6,0},{8,14},{10,12},{12,10},{14,8},{1,7},{3,5},... | collective-permute-start | bytes 786440 | tf_op jit(solution)/shard_map/ppermute | solution.py:183
  40.7 9.9 %collective-permute-start.9 = (bf16[4,128,128]{2,1,0:T(8,128)(2,1)S(1)}, bf16[4,128,128]{2,1,0:T(8,128)(2,1)S(1)}, u32[]{:S(2)}, u32[]{:S(2)}) collective-permute-start(bf16[4,128,128]{2,1,0:T(8,128)(2,1)S(1)} %fusion.1), channel_id=1, source_target_pairs={{0,8},{2,10},{4,12},{6,14},{8,0},{10,2},{12,4},{14,6},{1,9},{3,11}... | collective-permute-start | bytes 393224 | tf_op jit(solution)/shard_map/ppermute | solution.py:186

commit v11 on v9

--- a/solution.py
+++ b/solution.py
@@ -139,6 +139,29 @@
     )(offsets, own_offset, q_t, do_t, fo_t, gathered)
 
 
+def finish_kernel(own_ref, crossed_ref, key_ref, value_ref):
+    kv_heads = key_ref.shape[1]
+    for j in range(2 * kv_heads):
+        total = own_ref[j] + crossed_ref[j].astype(jnp.float32)
+        out = key_ref if j < kv_heads else value_ref
+        out[:, j % kv_heads, :] = total
+
+
+def finish_sums(own_total, crossed, kv_heads):
+    rows, tok_rows, head_width = own_total.shape
+    vmem = pl.BlockSpec(memory_space=pltpu.VMEM)
+    shape = jax.ShapeDtypeStruct((tok_rows, kv_heads, head_width), jnp.float32)
+    return pl.pallas_call(
+        finish_kernel,
+        out_shape=(shape, shape),
+        in_specs=[vmem, vmem],
+        out_specs=(vmem, vmem),
+        cost_estimate=pl.CostEstimate(
+            flops=own_total.size, transcendentals=0, bytes_accessed=own_total.size * 10
+        ),
+    )(own_total, crossed)
+
+
 def on_device(query_vectors, key_vectors, value_rows, forward_out, out_grad, block_offsets):
     tok_rows, q_heads, head_width = query_vectors.shape
     kv_heads = key_vectors.shape[1]
@@ -174,9 +197,7 @@
         own_total = own_total + arrived[0]
         mirror_total = mirror_total + arrived[1]
     crossed = lax.ppermute(mirror_total.astype(jnp.bfloat16), "ctx", mirror_pairs(cycle_size))
-    total = own_total + crossed.astype(jnp.float32)
-    key_grad = total[:kv_heads].transpose(1, 0, 2)
-    value_grad = total[kv_heads:].transpose(1, 0, 2)
+    key_grad, value_grad = finish_sums(own_total, crossed, kv_heads)
     return (dq_t.transpose(1, 0, 2), key_grad, value_grad)
 
 

time: 52.2 us -> 53.7 us (1.029)
  Pallas kernels: 4.1 us -> 5.9 us
  local copies, waits for them, and re-layouts: 4.04 us -> 3.16 us
  other arithmetic: 1.55 us -> 2.27 us
    pallas_call x0 -> x1, Pallas kernels: none -> 1.79 us  [finish_sums(): pl.pallas_call(finish_kernel, out_shape=(shape, shape), in_specs=[vmem, v...]
    unnamed x13, local copies, waits for them, and re-layouts: 2.78 us -> 1.92 us
    convert_element_type x1, other arithmetic: 0.06 us -> 0.84 us  [on_device(): mirror_total.astype(jnp.bfloat16)]
where the time goes in v11:
time: 53.7 us; the launch traced here: 53.5 us
  waiting for transfers between devices  20.7 us (39%)
  starting transfers between devices  20 us (37%)
  Pallas kernels  5.9 us (11%)
  local copies, waits for them, and re-layouts  3.16 us (6%)
  other arithmetic  2.27 us (4%)
  between operations  1.5 us (3%)
    ppermute x3, waiting for transfers between devices, on_device(): lax.ppermute(pair, 'ctx', mate_pairs(cycle_size, half - k))  9.61 us
    ppermute x3, starting transfers between devices, on_device(): lax.ppermute(from_mirror, 'ctx', mate_pairs(cycle_size, k))  6.42 us
    ppermute x3, starting transfers between devices, on_device(): lax.ppermute(slab, 'ctx', mate_pairs(cycle_size, k))  6 us
    ppermute x1, waiting for transfers between devices, on_device(): lax.ppermute(mirror_total.astype(jnp.bfloat16), 'ctx', mirror_pairs(cycle...  5.47 us
    ppermute x3, starting transfers between devices, on_device(): lax.ppermute(pair, 'ctx', mate_pairs(cycle_size, half - k))  4.28 us
    pallas_call x1, Pallas kernels, local_backward(): pl.pallas_call(functools.partial(backward_kernel, kv_heads=kv_heads, chun...  4.1 us
    ppermute x1, waiting for transfers between devices, on_device(): from_mirror = lax.ppermute(slab, 'ctx', mirror_pairs(cycle_size))  3.16 us
    ppermute x1, starting transfers between devices, on_device(): from_mirror = lax.ppermute(slab, 'ctx', mirror_pairs(cycle_size))  2.59 us
  transfers between devices with their start and end apart: 11, of which 8 were waited for; matrix products, arithmetic and copies ran while one was open for 5% of the time, Pallas kernels for 0%

profile of v11, /device:TPU:0, one launch (start us, length us, event | category | flops | bytes accessed | tf_op | source)
XLA Modules:
  0.0 53.5 jit_solution(8183541089075999084)
XLA Ops:
  0.6 0.0 copy-start
  1.3 1.0 %maximum_bitcast_fusion = bf16[4,128,128]{2,0,1:T(4,128)(2,1)S(1)} fusion(bf16[128,2,128]{2,1,0:T(2,128)(2,1)} %param.8, bf16[128,2,128]{2,1,0:T(2,128)(2,1)} %param.7), kind=kLoop, calls=%fused_computation.27 | loop fusion | flops 262144 | bytes 262144 | tf_op jit(solution)/shard_map/transpose | solution.py:172
  2.4 3.0 %collective-permute-start = (bf16[528,128]{1,0:T(8,128)(2,1)S(1)}, bf16[528,128]{1,0:T(8,128)(2,1)S(1)}, u32[]{:S(2)}, u32[]{:S(2)}) collective-permute-start(bf16[528,128]{1,0:T(8,128)(2,1)S(1)} %concatenate.7), channel_id=1, source_target_pairs={{0,2},{2,4},{4,6},{6,0},{8,10},{10,12},{12,14},{14,8},{1,3},{3,5},... | collective-permute-start | bytes 405512 | tf_op jit(solution)/shard_map/ppermute | solution.py:175
  5.4 1.6 %collective-permute-start.1 = (bf16[528,128]{1,0:T(8,128)(2,1)S(1)}, bf16[528,128]{1,0:T(8,128)(2,1)S(1)}, u32[]{:S(2)}, u32[]{:S(2)}) collective-permute-start(bf16[528,128]{1,0:T(8,128)(2,1)S(1)} %concatenate.7), channel_id=1, source_target_pairs={{0,4},{2,6},{4,0},{6,2},{8,12},{10,14},{12,8},{14,10},{1,5},{3,7},... | collective-permute-start | bytes 405512 | tf_op jit(solution)/shard_map/ppermute | solution.py:175
  7.0 1.4 %collective-permute-start.2 = (bf16[528,128]{1,0:T(8,128)(2,1)S(1)}, bf16[528,128]{1,0:T(8,128)(2,1)S(1)}, u32[]{:S(2)}, u32[]{:S(2)}) collective-permute-start(bf16[528,128]{1,0:T(8,128)(2,1)S(1)} %concatenate.7), channel_id=1, source_target_pairs={{0,6},{2,0},{4,2},{6,4},{8,14},{10,8},{12,10},{14,12},{1,7},{3,1},... | collective-permute-start | bytes 405512 | tf_op jit(solution)/shard_map/ppermute | solution.py:175
  8.4 2.6 %collective-permute-start.3 = (bf16[528,128]{1,0:T(8,128)(2,1)S(1)}, bf16[528,128]{1,0:T(8,128)(2,1)S(1)}, u32[]{:S(2)}, u32[]{:S(2)}) collective-permute-start(bf16[528,128]{1,0:T(8,128)(2,1)S(1)} %concatenate.7), channel_id=1, source_target_pairs={{0,8},{2,10},{4,12},{6,14},{8,0},{10,2},{12,4},{14,6},{1,9},{3,11}... | collective-permute-start | bytes 405512 | tf_op jit(solution)/shard_map/ppermute | solution.py:176
  11.0 1.1 %copy_bitcast_fusion = (bf16[8,128,128]{2,1,0:T(8,128)(2,1)S(1)}, bf16[8,128,128]{2,1,0:T(8,128)(2,1)S(1)}) fusion(bf16[128,8,128]{2,1,0:T(8,128)(2,1)} %param.9, bf16[128,8,128]{2,1,0:T(8,128)(2,1)} %param.10), kind=kLoop, calls=%fused_computation.16 | loop fusion | bytes 1048576 | tf_op jit(solution)/shard_map/transpose | solution.py:188
  12.1 0.0 copy-done
  12.2 3.2 %collective-permute-done.3 = bf16[528,128]{1,0:T(8,128)(2,1)S(1)} collective-permute-done((bf16[528,128]{1,0:T(8,128)(2,1)S(1)}, bf16[528,128]{1,0:T(8,128)(2,1)S(1)}, u32[]{:S(2)}, u32[]{:S(2)}) %collective-permute-start.3) | collective-permute-done | bytes 135200 | tf_op jit(solution)/shard_map/ppermute | solution.py:176
  15.4 0.3 collective-permute-start.4
  15.6 3.5 %collective-permute-start.5 = (bf16[528,128]{1,0:T(8,128)(2,1)S(1)}, bf16[528,128]{1,0:T(8,128)(2,1)S(1)}, u32[]{:S(2)}, u32[]{:S(2)}) collective-permute-start(bf16[528,128]{1,0:T(8,128)(2,1)S(1)} %collective-permute-done.3), channel_id=1, source_target_pairs={{0,4},{2,6},{4,0},{6,2},{8,12},{10,14},{12,8},{14,10},{1,5},{3,7},... | collective-permute-start | bytes 405512 | tf_op jit(solution)/shard_map/ppermute | solution.py:178
  19.1 0.0 collective-permute-done
  19.1 2.7 %collective-permute-start.6 = (bf16[528,128]{1,0:T(8,128)(2,1)S(1)}, bf16[528,128]{1,0:T(8,128)(2,1)S(1)}, u32[]{:S(2)}, u32[]{:S(2)}) collective-permute-start(bf16[528,128]{1,0:T(8,128)(2,1)S(1)} %collective-permute-done.3), channel_id=1, source_target_pairs={{0,6},{2,0},{4,2},{6,4},{8,14},{10,8},{12,10},{14,12},{1,7},{3,1},... | collective-permute-start | bytes 405512 | tf_op jit(solution)/shard_map/ppermute | solution.py:178
  21.8 0.0 collective-permute-done.1
  21.8 0.0 collective-permute-done.2
  21.9 0.8 %collective-permute-done.4 = bf16[528,128]{1,0:T(8,128)(2,1)S(1)} collective-permute-done((bf16[528,128]{1,0:T(8,128)(2,1)S(1)}, bf16[528,128]{1,0:T(8,128)(2,1)S(1)}, u32[]{:S(2)}, u32[]{:S(2)}) %collective-permute-start.4) | collective-permute-done | bytes 135200 | tf_op jit(solution)/shard_map/ppermute | solution.py:178
  22.7 0.6 %collective-permute-done.5 = bf16[528,128]{1,0:T(8,128)(2,1)S(1)} collective-permute-done((bf16[528,128]{1,0:T(8,128)(2,1)S(1)}, bf16[528,128]{1,0:T(8,128)(2,1)S(1)}, u32[]{:S(2)}, u32[]{:S(2)}) %collective-permute-start.5) | collective-permute-done | bytes 135200 | tf_op jit(solution)/shard_map/ppermute | solution.py:178
  23.3 1.1 %collective-permute-done.6 = bf16[528,128]{1,0:T(8,128)(2,1)S(1)} collective-permute-done((bf16[528,128]{1,0:T(8,128)(2,1)S(1)}, bf16[528,128]{1,0:T(8,128)(2,1)S(1)}, u32[]{:S(2)}, u32[]{:S(2)}) %collective-permute-start.6) | collective-permute-done | bytes 135200 | tf_op jit(solution)/shard_map/ppermute | solution.py:178
  24.4 0.2 fusion.8.offs_ref
  24.6 4.1 %shard_map.85 = (f32[8,128,128]{2,1,0:T(8,128)S(1)}, f32[4,128,128]{2,1,0:T(8,128)S(1)}, f32[4,128,128]{2,1,0:T(8,128)S(1)}, bf16[7,4,128,128]{3,2,1,0:T(8,128)(2,1)S(1)}) custom-call(s32[8]{0:T(128)S(1)} %fusion.8.offs_ref, s32[1]{0:T(128)S(6)} %copy.30.own_ref, bf16[8,128,128]{2,1,0:T(8,128)(2,1)S(1)} %bitcast.63, ...), custom_call_target="tpu_custom_call" | custom-call | flops 1610612736 | bytes 2654208 | tf_op jit(solution)/shard_map/pallas_call | solution.py:123
  28.8 0.1 fusion.9
  28.9 3.3 %collective-permute-start.7 = (bf16[2,4,128,128]{3,2,1,0:T(8,128)(2,1)S(1)}, bf16[2,4,128,128]{3,2,1,0:T(8,128)(2,1)S(1)}, u32[]{:S(2)}, u32[]{:S(2)}) collective-permute-start(bf16[2,4,128,128]{3,2,1,0:T(8,128)(2,1)S(1)} %pad_maximum_fusion), channel_id=1, source_target_pairs={{0,6},{2,0},{4,2},{6,4},{8,14},{10,8},{12,10},{14,12},{1,7},{3,1},... | collective-permute-start | bytes 786440 | tf_op jit(solution)/shard_map/ppermute | solution.py:196
  32.2 0.1 collective-permute-start.8
  32.4 0.9 %collective-permute-start.9 = (bf16[2,4,128,128]{3,2,1,0:T(8,128)(2,1)S(1)}, bf16[2,4,128,128]{3,2,1,0:T(8,128)(2,1)S(1)}, u32[]{:S(2)}, u32[]{:S(2)}) collective-permute-start(bf16[2,4,128,128]{3,2,1,0:T(8,128)(2,1)S(1)} %pad_maximum_fusion.2), channel_id=1, source_target_pairs={{0,2},{2,4},{4,6},{6,0},{8,10},{10,12},{12,14},{14,8},{1,3},{3,5},... | collective-permute-start | bytes 786440 | tf_op jit(solution)/shard_map/ppermute | solution.py:196
  33.2 5.3 %collective-permute-done.7 = bf16[2,4,128,128]{3,2,1,0:T(8,128)(2,1)S(1)} collective-permute-done((bf16[2,4,128,128]{3,2,1,0:T(8,128)(2,1)S(1)}, bf16[2,4,128,128]{3,2,1,0:T(8,128)(2,1)S(1)}, u32[]{:S(2)}, u32[]{:S(2)}) %collective-permute-start.7) | collective-permute-done | bytes 262176 | tf_op jit(solution)/shard_map/ppermute | solution.py:196
  38.5 3.7 %collective-permute-done.8 = bf16[2,4,128,128]{3,2,1,0:T(8,128)(2,1)S(1)} collective-permute-done((bf16[2,4,128,128]{3,2,1,0:T(8,128)(2,1)S(1)}, bf16[2,4,128,128]{3,2,1,0:T(8,128)(2,1)S(1)}, u32[]{:S(2)}, u32[]{:S(2)}) %collective-permute-start.8) | collective-permute-done | bytes 262176 | tf_op jit(solution)/shard_map/ppermute | solution.py:196
  42.3 0.6 %collective-permute-done.9 = bf16[2,4,128,128]{3,2,1,0:T(8,128)(2,1)S(1)} collective-permute-done((bf16[2,4,128,128]{3,2,1,0:T(8,128)(2,1)S(1)}, bf16[2,4,128,128]{3,2,1,0:T(8,128)(2,1)S(1)}, u32[]{:S(2)}, u32[]{:S(2)}) %collective-permute-start.9) | collective-permute-done | bytes 262176 | tf_op jit(solution)/shard_map/ppermute | solution.py:196
  43.0 0.8 %fusion.1 = (bf16[4,128,128]{2,1,0:T(8,128)(2,1)S(1)}, f32[4,128,128]{2,1,0:T(8,128)}) fusion(f32[2,4,128,128]{3,2,1,0:T(8,128)S(1)} %convert_element_type.40, f32[2,4,128,128]{3,2,1,0:T(8,128)S(1)} %convert_element_type.39, f32[4,128,128]{2,1,0:T(8,128)S(1)} %get-tuple-element.12, f32[2,4,128,128]{3,2,1,0:T(8,128)S(1)} %convert_element_type.38, ...), kind=kLoop, calls=%fused_computation.2 | loop fusion | flops 458752 | bytes 2490368 | tf_op jit(solution)/shard_map/convert_element_type | solution.py:199
  43.8 0.7 %collective-permute-start.10 = (bf16[4,128,128]{2,1,0:T(8,128)(2,1)S(1)}, bf16[4,128,128]{2,1,0:T(8,128)(2,1)S(1)}, u32[]{:S(2)}, u32[]{:S(2)}) collective-permute-start(bf16[4,128,128]{2,1,0:T(8,128)(2,1)S(1)} %get-tuple-element.21), channel_id=1, source_target_pairs={{0,8},{2,10},{4,12},{6,14},{8,0},{10,2},{12,4},{14,6},{1,9},{3,11}... | collective-permute-start | bytes 393224 | tf_op jit(solution)/shard_map/ppermute | solution.py:199
  44.5 1.1 %copy.18 = f32[128,8,128]{2,1,0:T(8,128)} copy(f32[128,8,128]{2,0,1:T(8,128)S(1)} %bitcast.62) | data formatting | bytes 1048576
  45.6 5.5 %collective-permute-done.10.crossed_ref = bf16[4,128,128]{2,1,0:T(8,128)(2,1)S(1)} collective-permute-done((bf16[4,128,128]{2,1,0:T(8,128)(2,1)S(1)}, bf16[4,128,128]{2,1,0:T(8,128)(2,1)S(1)}, u32[]{:S(2)}, u32[]{:S(2)}) %collective-permute-start.10) | collective-permute-done | bytes 131104 | tf_op jit(solution)/shard_map/ppermute | solution.py:199
  51.1 0.0 copy-start.1
  51.1 0.6 %copy-done.1 = bf16[4,128,128]{2,1,0:T(8,128)(2,1)} copy-done((bf16[4,128,128]{2,1,0:T(8,128)(2,1)}, bf16[4,128,128]{2,1,0:T(8,128)(2,1)S(1)}, u32[]{:S(2)}) %copy-start.1) | copy-done | bytes 131096
  51.7 1.8 %shard_map.86 = (f32[128,2,128]{2,1,0:T(2,128)}, f32[128,2,128]{2,1,0:T(2,128)}) custom-call(f32[4,128,128]{2,1,0:T(8,128)} %get-tuple-element.22.own_ref, bf16[4,128,128]{2,1,0:T(8,128)(2,1)} %copy-done.1), custom_call_target="tpu_custom_call" | custom-call | flops 65536 | bytes 655360 | tf_op jit(solution)/shard_map/pallas_call | solution.py:154
  (17 shorter events, 0.4 us)
Async XLA Ops:
  0.6 11.5 %copy-start = (bf16[128,8,128]{2,1,0:T(8,128)(2,1)S(1)}, bf16[128,8,128]{2,1,0:T(8,128)(2,1)}, u32[]{:S(2)}) copy-start(bf16[128,8,128]{2,1,0:T(8,128)(2,1)} %param.6) | copy-start | bytes 786436
  2.4 16.7 %collective-permute-start = (bf16[528,128]{1,0:T(8,128)(2,1)S(1)}, bf16[528,128]{1,0:T(8,128)(2,1)S(1)}, u32[]{:S(2)}, u32[]{:S(2)}) collective-permute-start(bf16[528,128]{1,0:T(8,128)(2,1)S(1)} %concatenate.7), channel_id=1, source_target_pairs={{0,2},{2,4},{4,6},{6,0},{8,10},{10,12},{12,14},{14,8},{1,3},{3,5},... | collective-permute-start | bytes 405512 | tf_op jit(solution)/shard_map/ppermute | solution.py:175
  5.4 16.4 %collective-permute-start.1 = (bf16[528,128]{1,0:T(8,128)(2,1)S(1)}, bf16[528,128]{1,0:T(8,128)(2,1)S(1)}, u32[]{:S(2)}, u32[]{:S(2)}) collective-permute-start(bf16[528,128]{1,0:T(8,128)(2,1)S(1)} %concatenate.7), channel_id=1, source_target_pairs={{0,4},{2,6},{4,0},{6,2},{8,12},{10,14},{12,8},{14,10},{1,5},{3,7},... | collective-permute-start | bytes 405512 | tf_op jit(solution)/shard_map/ppermute | solution.py:175
  7.0 14.8 %collective-permute-start.2 = (bf16[528,128]{1,0:T(8,128)(2,1)S(1)}, bf16[528,128]{1,0:T(8,128)(2,1)S(1)}, u32[]{:S(2)}, u32[]{:S(2)}) collective-permute-start(bf16[528,128]{1,0:T(8,128)(2,1)S(1)} %concatenate.7), channel_id=1, source_target_pairs={{0,6},{2,0},{4,2},{6,4},{8,14},{10,8},{12,10},{14,12},{1,7},{3,1},... | collective-permute-start | bytes 405512 | tf_op jit(solution)/shard_map/ppermute | solution.py:175
  8.4 7.0 %collective-permute-start.3 = (bf16[528,128]{1,0:T(8,128)(2,1)S(1)}, bf16[528,128]{1,0:T(8,128)(2,1)S(1)}, u32[]{:S(2)}, u32[]{:S(2)}) collective-permute-start(bf16[528,128]{1,0:T(8,128)(2,1)S(1)} %concatenate.7), channel_id=1, source_target_pairs={{0,8},{2,10},{4,12},{6,14},{8,0},{10,2},{12,4},{14,6},{1,9},{3,11}... | collective-permute-start | bytes 405512 | tf_op jit(solution)/shard_map/ppermute | solution.py:176
  15.4 7.3 %collective-permute-start.4 = (bf16[528,128]{1,0:T(8,128)(2,1)S(1)}, bf16[528,128]{1,0:T(8,128)(2,1)S(1)}, u32[]{:S(2)}, u32[]{:S(2)}) collective-permute-start(bf16[528,128]{1,0:T(8,128)(2,1)S(1)} %collective-permute-done.3), channel_id=1, source_target_pairs={{0,2},{2,4},{4,6},{6,0},{8,10},{10,12},{12,14},{14,8},{1,3},{3,5},... | collective-permute-start | bytes 405512 | tf_op jit(solution)/shard_map/ppermute | solution.py:178
  15.6 7.7 %collective-permute-start.5 = (bf16[528,128]{1,0:T(8,128)(2,1)S(1)}, bf16[528,128]{1,0:T(8,128)(2,1)S(1)}, u32[]{:S(2)}, u32[]{:S(2)}) collective-permute-start(bf16[528,128]{1,0:T(8,128)(2,1)S(1)} %collective-permute-done.3), channel_id=1, source_target_pairs={{0,4},{2,6},{4,0},{6,2},{8,12},{10,14},{12,8},{14,10},{1,5},{3,7},... | collective-permute-start | bytes 405512 | tf_op jit(solution)/shard_map/ppermute | solution.py:178
  19.1 5.3 %collective-permute-start.6 = (bf16[528,128]{1,0:T(8,128)(2,1)S(1)}, bf16[528,128]{1,0:T(8,128)(2,1)S(1)}, u32[]{:S(2)}, u32[]{:S(2)}) collective-permute-start(bf16[528,128]{1,0:T(8,128)(2,1)S(1)} %collective-permute-done.3), channel_id=1, source_target_pairs={{0,6},{2,0},{4,2},{6,4},{8,14},{10,8},{12,10},{14,12},{1,7},{3,1},... | collective-permute-start | bytes 405512 | tf_op jit(solution)/shard_map/ppermute | solution.py:178
  28.9 9.6 %collective-permute-start.7 = (bf16[2,4,128,128]{3,2,1,0:T(8,128)(2,1)S(1)}, bf16[2,4,128,128]{3,2,1,0:T(8,128)(2,1)S(1)}, u32[]{:S(2)}, u32[]{:S(2)}) collective-permute-start(bf16[2,4,128,128]{3,2,1,0:T(8,128)(2,1)S(1)} %pad_maximum_fusion), channel_id=1, source_target_pairs={{0,6},{2,0},{4,2},{6,4},{8,14},{10,8},{12,10},{14,12},{1,7},{3,1},... | collective-permute-start | bytes 786440 | tf_op jit(solution)/shard_map/ppermute | solution.py:196
  32.2 10.0 %collective-permute-start.8 = (bf16[2,4,128,128]{3,2,1,0:T(8,128)(2,1)S(1)}, bf16[2,4,128,128]{3,2,1,0:T(8,128)(2,1)S(1)}, u32[]{:S(2)}, u32[]{:S(2)}) collective-permute-start(bf16[2,4,128,128]{3,2,1,0:T(8,128)(2,1)S(1)} %pad_maximum_fusion.1), channel_id=1, source_target_pairs={{0,4},{2,6},{4,0},{6,2},{8,12},{10,14},{12,8},{14,10},{1,5},{3,7},... | collective-permute-start | bytes 786440 | tf_op jit(solution)/shard_map/ppermute | solution.py:196
  32.4 10.6 %collective-permute-start.9 = (bf16[2,4,128,128]{3,2,1,0:T(8,128)(2,1)S(1)}, bf16[2,4,128,128]{3,2,1,0:T(8,128)(2,1)S(1)}, u32[]{:S(2)}, u32[]{:S(2)}) collective-permute-start(bf16[2,4,128,128]{3,2,1,0:T(8,128)(2,1)S(1)} %pad_maximum_fusion.2), channel_id=1, source_target_pairs={{0,2},{2,4},{4,6},{6,0},{8,10},{10,12},{12,14},{14,8},{1,3},{3,5},... | collective-permute-start | bytes 786440 | tf_op jit(solution)/shard_map/ppermute | solution.py:196
  43.8 7.3 %collective-permute-start.10 = (bf16[4,128,128]{2,1,0:T(8,128)(2,1)S(1)}, bf16[4,128,128]{2,1,0:T(8,128)(2,1)S(1)}, u32[]{:S(2)}, u32[]{:S(2)}) collective-permute-start(bf16[4,128,128]{2,1,0:T(8,128)(2,1)S(1)} %get-tuple-element.21), channel_id=1, source_target_pairs={{0,8},{2,10},{4,12},{6,14},{8,0},{10,2},{12,4},{14,6},{1,9},{3,11}... | collective-permute-start | bytes 393224 | tf_op jit(solution)/shard_map/ppermute | solution.py:199
  51.1 0.7 %copy-start.1 = (bf16[4,128,128]{2,1,0:T(8,128)(2,1)}, bf16[4,128,128]{2,1,0:T(8,128)(2,1)S(1)}, u32[]{:S(2)}) copy-start(bf16[4,128,128]{2,1,0:T(8,128)(2,1)S(1)} %collective-permute-done.10.crossed_ref) | copy-start | bytes 393220

commit v12 on v10

--- a/solution.py
+++ b/solution.py
@@ -152,12 +152,15 @@
     half = cycle_size // 2
     from_mirror = lax.ppermute(slab, "ctx", mirror_pairs(cycle_size))
     if half == 4:
+        across_pairs = [(i, half * (j // half) + ((j % half) ^ 1)) for i, j in mirror_pairs(cycle_size)]
+        from_mirror_x1 = lax.ppermute(slab, "ctx", across_pairs)
         from_x1 = lax.ppermute(slab, "ctx", mate_pairs(cycle_size, 1))
         from_x2 = lax.ppermute(slab, "ctx", mate_pairs(cycle_size, 2))
-        pair = lax.ppermute(jnp.stack([from_mirror, from_x2]), "ctx", mate_pairs(cycle_size, 1))
-        mirror_of_x2 = lax.ppermute(from_mirror, "ctx", mate_pairs(cycle_size, 2))
-        mirror_of_x3 = lax.ppermute(from_mirror, "ctx", mate_pairs(cycle_size, 3))
-        blocks = [slab, from_x1, from_x2, pair[1], from_mirror, pair[0], mirror_of_x2, mirror_of_x3]
+        from_x3 = lax.ppermute(slab, "ctx", mate_pairs(cycle_size, 3))
+        pair = lax.ppermute(
+            jnp.stack([from_mirror, from_mirror_x1]), "ctx", mate_pairs(cycle_size, 2)
+        )
+        blocks = [slab, from_x1, from_x2, from_x3, from_mirror, from_mirror_x1, pair[0], pair[1]]
     else:
         from_mates = [lax.ppermute(slab, "ctx", mate_pairs(cycle_size, k)) for k in range(1, half)]
         handed_on = [

time: 52.4 us -> 57.3 us (1.094)
  waiting for transfers between devices: 21.3 us -> 30.7 us
  starting transfers between devices: 19.6 us -> 15.1 us
    ppermute x3, waiting for transfers between devices: 6.58 us -> 13.2 us  [the longest x1 7.13 us: on_device(): lax.ppermute(jnp.stack([from_mirror, from_mirror_x1]), 'ctx', mate_pairs(...]
    ppermute x1, starting transfers between devices: 5.2 us -> 2.51 us  [on_device(): lax.ppermute(mirror_total.astype(jnp.bfloat16), 'ctx', mirror_pairs(cycle...]
    ppermute x3, starting transfers between devices: 3.55 us -> 1.37 us  [the longest x1 1.29 us: on_device(): from_mirror_x1 = lax.ppermute(slab, 'ctx', across_pairs)]
    ppermute x1, waiting for transfers between devices: 2.29 us -> 4.39 us  [on_device(): from_mirror = lax.ppermute(slab, 'ctx', mirror_pairs(cycle_size))]
    ppermute x1, starting transfers between devices: 1.52 us -> 3.03 us  [on_device(): from_x1 = lax.ppermute(slab, 'ctx', mate_pairs(cycle_size, 1))]
    ppermute x1, starting transfers between devices: 4.1 us -> 2.98 us  [on_device(): from_mirror = lax.ppermute(slab, 'ctx', mirror_pairs(cycle_size))]
    ppermute x3, waiting for transfers between devices: 8.62 us -> 9.36 us  [on_device(): lax.ppermute(pair, 'ctx', mate_pairs(cycle_size, k)).astype(jnp.float32)]
    unnamed x13 -> x12, local copies, waits for them, and re-layouts: 2.78 us -> 2.77 us
  transfers between devices with their start and end apart: 10 -> 10, of which waited for: 6 -> 7; matrix products, arithmetic and copies ran while one was open for 5% -> 4% of each run, Pallas kernels for 0% -> 0%
where the time goes in v12:
time: 57.3 us; the launch traced here: 57.1 us
  waiting for transfers between devices  30.7 us (54%)
  starting transfers between devices  15.1 us (26%)
  Pallas kernels  4.1 us (7%)
  local copies, waits for them, and re-layouts  4.04 us (7%)
  other arithmetic  1.58 us (3%)
  between operations  1.54 us (3%)
    ppermute x3, waiting for transfers between devices, on_device(): lax.ppermute(pair, 'ctx', mate_pairs(cycle_size, k)).astype(jnp.float32)  9.36 us
    ppermute x1, waiting for transfers between devices, on_device(): lax.ppermute(jnp.stack([from_mirror, from_mirror_x1]), 'ctx', mate_pairs(...  7.13 us
    ppermute x1, waiting for transfers between devices, on_device(): from_mirror_x1 = lax.ppermute(slab, 'ctx', across_pairs)  6.09 us
    ppermute x1, waiting for transfers between devices, on_device(): from_mirror = lax.ppermute(slab, 'ctx', mirror_pairs(cycle_size))  4.39 us
    pallas_call x1, Pallas kernels, local_backward(): pl.pallas_call(functools.partial(backward_kernel, kv_heads=kv_heads, chun...  4.1 us
    ppermute x1, waiting for transfers between devices, on_device(): lax.ppermute(mirror_total.astype(jnp.bfloat16), 'ctx', mirror_pairs(cycle...  3.72 us
    ppermute x3, starting transfers between devices, on_device(): lax.ppermute(pair, 'ctx', mate_pairs(cycle_size, k)).astype(jnp.float32)  3.67 us
    ppermute x1, starting transfers between devices, on_device(): from_x1 = lax.ppermute(slab, 'ctx', mate_pairs(cycle_size, 1))  3.03 us
  transfers between devices with their start and end apart: 10, of which 7 were waited for; matrix products, arithmetic and copies ran while one was open for 4% of the time, Pallas kernels for 0%

profile of v12, /device:TPU:0, one launch (start us, length us, event | category | flops | bytes accessed | tf_op | source)
XLA Modules:
  0.0 57.1 jit_solution(1327220734659076984)
XLA Ops:
  0.6 0.0 copy-start
  1.3 1.0 %maximum_bitcast_fusion = bf16[4,128,128]{2,0,1:T(4,128)(2,1)S(1)} fusion(bf16[128,2,128]{2,1,0:T(2,128)(2,1)} %param.8, bf16[128,2,128]{2,1,0:T(2,128)(2,1)} %param.7), kind=kLoop, calls=%fused_computation.27 | loop fusion | flops 262144 | bytes 262144 | tf_op jit(solution)/shard_map/transpose | solution.py:150
  2.4 3.0 %collective-permute-start = (bf16[528,128]{1,0:T(8,128)(2,1)S(1)}, bf16[528,128]{1,0:T(8,128)(2,1)S(1)}, u32[]{:S(2)}, u32[]{:S(2)}) collective-permute-start(bf16[528,128]{1,0:T(8,128)(2,1)S(1)} %concatenate.7), channel_id=1, source_target_pairs={{0,2},{2,0},{4,6},{6,4},{8,10},{10,8},{12,14},{14,12},{1,3},{3,1},... | collective-permute-start | bytes 405512 | tf_op jit(solution)/shard_map/ppermute | solution.py:157
  5.4 1.6 %collective-permute-start.1 = (bf16[528,128]{1,0:T(8,128)(2,1)S(1)}, bf16[528,128]{1,0:T(8,128)(2,1)S(1)}, u32[]{:S(2)}, u32[]{:S(2)}) collective-permute-start(bf16[528,128]{1,0:T(8,128)(2,1)S(1)} %concatenate.7), channel_id=1, source_target_pairs={{0,4},{2,6},{4,0},{6,2},{8,12},{10,14},{12,8},{14,10},{1,5},{3,7},... | collective-permute-start | bytes 405512 | tf_op jit(solution)/shard_map/ppermute | solution.py:158
  7.0 0.0 collective-permute-start.2
  7.0 3.0 %collective-permute-start.3 = (bf16[528,128]{1,0:T(8,128)(2,1)S(1)}, bf16[528,128]{1,0:T(8,128)(2,1)S(1)}, u32[]{:S(2)}, u32[]{:S(2)}) collective-permute-start(bf16[528,128]{1,0:T(8,128)(2,1)S(1)} %concatenate.7), channel_id=1, source_target_pairs={{0,8},{2,10},{4,12},{6,14},{8,0},{10,2},{12,4},{14,6},{1,9},{3,11}... | collective-permute-start | bytes 405512 | tf_op jit(solution)/shard_map/ppermute | solution.py:153
  10.0 1.3 %collective-permute-start.4 = (bf16[528,128]{1,0:T(8,128)(2,1)S(1)}, bf16[528,128]{1,0:T(8,128)(2,1)S(1)}, u32[]{:S(2)}, u32[]{:S(2)}) collective-permute-start(bf16[528,128]{1,0:T(8,128)(2,1)S(1)} %concatenate.7), channel_id=1, source_target_pairs={{0,10},{2,8},{4,14},{6,12},{8,2},{10,0},{12,6},{14,4},{1,11},{3,9}... | collective-permute-start | bytes 405512 | tf_op jit(solution)/shard_map/ppermute | solution.py:156
  11.3 1.1 %copy_bitcast_fusion = (bf16[8,128,128]{2,1,0:T(8,128)(2,1)S(1)}, bf16[8,128,128]{2,1,0:T(8,128)(2,1)S(1)}) fusion(bf16[128,8,128]{2,1,0:T(8,128)(2,1)} %param.9, bf16[128,8,128]{2,1,0:T(8,128)(2,1)} %param.10), kind=kLoop, calls=%fused_computation.18 | loop fusion | bytes 1048576 | tf_op jit(solution)/shard_map/transpose | solution.py:178
  12.4 0.0 copy-done
  12.5 4.4 %collective-permute-done.3 = bf16[528,128]{1,0:T(8,128)(2,1)S(1)} collective-permute-done((bf16[528,128]{1,0:T(8,128)(2,1)S(1)}, bf16[528,128]{1,0:T(8,128)(2,1)S(1)}, u32[]{:S(2)}, u32[]{:S(2)}) %collective-permute-start.3) | collective-permute-done | bytes 135200 | tf_op jit(solution)/shard_map/ppermute | solution.py:153
  16.9 6.1 %collective-permute-done.4 = bf16[528,128]{1,0:T(8,128)(2,1)S(1)} collective-permute-done((bf16[528,128]{1,0:T(8,128)(2,1)S(1)}, bf16[528,128]{1,0:T(8,128)(2,1)S(1)}, u32[]{:S(2)}, u32[]{:S(2)}) %collective-permute-start.4) | collective-permute-done | bytes 135200 | tf_op jit(solution)/shard_map/ppermute | solution.py:156
  23.0 0.1 collective-permute-start.5
  23.1 0.0 collective-permute-done
  23.1 0.0 collective-permute-done.1
  23.2 0.0 collective-permute-done.2
  23.2 7.1 %collective-permute-done.5 = bf16[2,528,128]{2,1,0:T(8,128)(2,1)S(1)} collective-permute-done((bf16[2,528,128]{2,1,0:T(8,128)(2,1)S(1)}, bf16[2,528,128]{2,1,0:T(8,128)(2,1)S(1)}, u32[]{:S(2)}, u32[]{:S(2)}) %collective-permute-start.5) | collective-permute-done | bytes 270368 | tf_op jit(solution)/shard_map/ppermute | solution.py:160
  30.4 0.2 fusion.9.offs_ref
  30.7 4.1 %shard_map.85 = (f32[8,128,128]{2,1,0:T(8,128)S(1)}, f32[4,128,128]{2,1,0:T(8,128)S(1)}, f32[4,128,128]{2,1,0:T(8,128)S(1)}, bf16[7,4,128,128]{3,2,1,0:T(8,128)(2,1)S(1)}) custom-call(s32[8]{0:T(128)S(1)} %fusion.9.offs_ref, s32[1]{0:T(128)S(6)} %copy.33.own_ref, bf16[8,128,128]{2,1,0:T(8,128)(2,1)S(1)} %bitcast.65, ...), custom_call_target="tpu_custom_call" | custom-call | flops 1610612736 | bytes 2654208 | tf_op jit(solution)/shard_map/pallas_call | solution.py:124
  34.8 0.1 fusion.10
  34.9 0.1 collective-permute-start.6
  35.0 0.6 %collective-permute-start.7 = (bf16[2,4,128,128]{3,2,1,0:T(8,128)(2,1)S(1)}, bf16[2,4,128,128]{3,2,1,0:T(8,128)(2,1)S(1)}, u32[]{:S(2)}, u32[]{:S(2)}) collective-permute-start(bf16[2,4,128,128]{3,2,1,0:T(8,128)(2,1)S(1)} %pad_maximum_fusion.2), channel_id=1, source_target_pairs={{0,4},{2,6},{4,0},{6,2},{8,12},{10,14},{12,8},{14,10},{1,5},{3,7},... | collective-permute-start | bytes 786440 | tf_op jit(solution)/shard_map/ppermute | solution.py:186
  35.6 3.0 %collective-permute-start.8 = (bf16[2,4,128,128]{3,2,1,0:T(8,128)(2,1)S(1)}, bf16[2,4,128,128]{3,2,1,0:T(8,128)(2,1)S(1)}, u32[]{:S(2)}, u32[]{:S(2)}) collective-permute-start(bf16[2,4,128,128]{3,2,1,0:T(8,128)(2,1)S(1)} %pad_maximum_fusion.3), channel_id=1, source_target_pairs={{0,6},{2,4},{4,2},{6,0},{8,14},{10,12},{12,10},{14,8},{1,7},{3,5},... | collective-permute-start | bytes 786440 | tf_op jit(solution)/shard_map/ppermute | solution.py:186
  38.6 4.9 %collective-permute-done.6 = bf16[2,4,128,128]{3,2,1,0:T(8,128)(2,1)S(1)} collective-permute-done((bf16[2,4,128,128]{3,2,1,0:T(8,128)(2,1)S(1)}, bf16[2,4,128,128]{3,2,1,0:T(8,128)(2,1)S(1)}, u32[]{:S(2)}, u32[]{:S(2)}) %collective-permute-start.6) | collective-permute-done | bytes 262176 | tf_op jit(solution)/shard_map/ppermute | solution.py:186
  43.5 0.6 collective-permute-done.7
  44.1 3.9 %collective-permute-done.8 = bf16[2,4,128,128]{3,2,1,0:T(8,128)(2,1)S(1)} collective-permute-done((bf16[2,4,128,128]{3,2,1,0:T(8,128)(2,1)S(1)}, bf16[2,4,128,128]{3,2,1,0:T(8,128)(2,1)S(1)}, u32[]{:S(2)}, u32[]{:S(2)}) %collective-permute-start.8) | collective-permute-done | bytes 262176 | tf_op jit(solution)/shard_map/ppermute | solution.py:186
  48.1 0.1 fusion.1
  48.2 2.5 %collective-permute-start.9 = (bf16[4,128,128]{2,1,0:T(8,128)(2,1)S(1)}, bf16[4,128,128]{2,1,0:T(8,128)(2,1)S(1)}, u32[]{:S(2)}, u32[]{:S(2)}) collective-permute-start(bf16[4,128,128]{2,1,0:T(8,128)(2,1)S(1)} %fusion.1), channel_id=1, source_target_pairs={{0,8},{2,10},{4,12},{6,14},{8,0},{10,2},{12,4},{14,6},{1,9},{3,11}... | collective-permute-start | bytes 393224 | tf_op jit(solution)/shard_map/ppermute | solution.py:189
  50.7 1.1 %copy.20 = f32[128,8,128]{2,1,0:T(8,128)} copy(f32[128,8,128]{2,0,1:T(8,128)S(1)} %bitcast.64) | data formatting | bytes 1048576
  51.8 3.7 %collective-permute-done.9 = bf16[4,128,128]{2,1,0:T(8,128)(2,1)S(1)} collective-permute-done((bf16[4,128,128]{2,1,0:T(8,128)(2,1)S(1)}, bf16[4,128,128]{2,1,0:T(8,128)(2,1)S(1)}, u32[]{:S(2)}, u32[]{:S(2)}) %collective-permute-start.9) | collective-permute-done | bytes 131104 | tf_op jit(solution)/shard_map/ppermute | solution.py:189
  55.5 0.1 fusion.5
  55.6 0.8 %copy.21 = f32[128,2,128]{2,1,0:T(2,128)} copy(f32[128,2,128]{2,0,1:T(8,128)S(1)} %get-tuple-element.24) | data formatting | bytes 262144
  56.3 0.8 %copy.22 = f32[128,2,128]{2,1,0:T(2,128)} copy(f32[128,2,128]{2,0,1:T(8,128)S(1)} %get-tuple-element.23) | data formatting | bytes 262144
  (18 shorter events, 0.5 us)
Async XLA Ops:
  0.6 11.8 %copy-start = (bf16[128,8,128]{2,1,0:T(8,128)(2,1)S(1)}, bf16[128,8,128]{2,1,0:T(8,128)(2,1)}, u32[]{:S(2)}) copy-start(bf16[128,8,128]{2,1,0:T(8,128)(2,1)} %param.6) | copy-start | bytes 786436
  2.4 20.7 %collective-permute-start = (bf16[528,128]{1,0:T(8,128)(2,1)S(1)}, bf16[528,128]{1,0:T(8,128)(2,1)S(1)}, u32[]{:S(2)}, u32[]{:S(2)}) collective-permute-start(bf16[528,128]{1,0:T(8,128)(2,1)S(1)} %concatenate.7), channel_id=1, source_target_pairs={{0,2},{2,0},{4,6},{6,4},{8,10},{10,8},{12,14},{14,12},{1,3},{3,1},... | collective-permute-start | bytes 405512 | tf_op jit(solution)/shard_map/ppermute | solution.py:157
  5.4 17.7 %collective-permute-start.1 = (bf16[528,128]{1,0:T(8,128)(2,1)S(1)}, bf16[528,128]{1,0:T(8,128)(2,1)S(1)}, u32[]{:S(2)}, u32[]{:S(2)}) collective-permute-start(bf16[528,128]{1,0:T(8,128)(2,1)S(1)} %concatenate.7), channel_id=1, source_target_pairs={{0,4},{2,6},{4,0},{6,2},{8,12},{10,14},{12,8},{14,10},{1,5},{3,7},... | collective-permute-start | bytes 405512 | tf_op jit(solution)/shard_map/ppermute | solution.py:158
  7.0 16.1 %collective-permute-start.2 = (bf16[528,128]{1,0:T(8,128)(2,1)S(1)}, bf16[528,128]{1,0:T(8,128)(2,1)S(1)}, u32[]{:S(2)}, u32[]{:S(2)}) collective-permute-start(bf16[528,128]{1,0:T(8,128)(2,1)S(1)} %concatenate.7), channel_id=1, source_target_pairs={{0,6},{2,4},{4,2},{6,0},{8,14},{10,12},{12,10},{14,8},{1,7},{3,5},... | collective-permute-start | bytes 405512 | tf_op jit(solution)/shard_map/ppermute | solution.py:159
  7.0 9.9 %collective-permute-start.3 = (bf16[528,128]{1,0:T(8,128)(2,1)S(1)}, bf16[528,128]{1,0:T(8,128)(2,1)S(1)}, u32[]{:S(2)}, u32[]{:S(2)}) collective-permute-start(bf16[528,128]{1,0:T(8,128)(2,1)S(1)} %concatenate.7), channel_id=1, source_target_pairs={{0,8},{2,10},{4,12},{6,14},{8,0},{10,2},{12,4},{14,6},{1,9},{3,11}... | collective-permute-start | bytes 405512 | tf_op jit(solution)/shard_map/ppermute | solution.py:153
  10.0 13.0 %collective-permute-start.4 = (bf16[528,128]{1,0:T(8,128)(2,1)S(1)}, bf16[528,128]{1,0:T(8,128)(2,1)S(1)}, u32[]{:S(2)}, u32[]{:S(2)}) collective-permute-start(bf16[528,128]{1,0:T(8,128)(2,1)S(1)} %concatenate.7), channel_id=1, source_target_pairs={{0,10},{2,8},{4,14},{6,12},{8,2},{10,0},{12,6},{14,4},{1,11},{3,9}... | collective-permute-start | bytes 405512 | tf_op jit(solution)/shard_map/ppermute | solution.py:156
  23.0 7.4 %collective-permute-start.5 = (bf16[2,528,128]{2,1,0:T(8,128)(2,1)S(1)}, bf16[2,528,128]{2,1,0:T(8,128)(2,1)S(1)}, u32[]{:S(2)}, u32[]{:S(2)}) collective-permute-start(bf16[2,528,128]{2,1,0:T(8,128)(2,1)S(1)} %pad_maximum_fusion), channel_id=1, source_target_pairs={{0,4},{2,6},{4,0},{6,2},{8,12},{10,14},{12,8},{14,10},{1,5},{3,7},... | collective-permute-start | bytes 811016 | tf_op jit(solution)/shard_map/ppermute | solution.py:160
  34.9 8.6 %collective-permute-start.6 = (bf16[2,4,128,128]{3,2,1,0:T(8,128)(2,1)S(1)}, bf16[2,4,128,128]{3,2,1,0:T(8,128)(2,1)S(1)}, u32[]{:S(2)}, u32[]{:S(2)}) collective-permute-start(bf16[2,4,128,128]{3,2,1,0:T(8,128)(2,1)S(1)} %pad_maximum_fusion.1), channel_id=1, source_target_pairs={{0,2},{2,0},{4,6},{6,4},{8,10},{10,8},{12,14},{14,12},{1,3},{3,1},... | collective-permute-start | bytes 786440 | tf_op jit(solution)/shard_map/ppermute | solution.py:186
  35.0 9.1 %collective-permute-start.7 = (bf16[2,4,128,128]{3,2,1,0:T(8,128)(2,1)S(1)}, bf16[2,4,128,128]{3,2,1,0:T(8,128)(2,1)S(1)}, u32[]{:S(2)}, u32[]{:S(2)}) collective-permute-start(bf16[2,4,128,128]{3,2,1,0:T(8,128)(2,1)S(1)} %pad_maximum_fusion.2), channel_id=1, source_target_pairs={{0,4},{2,6},{4,0},{6,2},{8,12},{10,14},{12,8},{14,10},{1,5},{3,7},... | collective-permute-start | bytes 786440 | tf_op jit(solution)/shard_map/ppermute | solution.py:186
  35.6 12.4 %collective-permute-start.8 = (bf16[2,4,128,128]{3,2,1,0:T(8,128)(2,1)S(1)}, bf16[2,4,128,128]{3,2,1,0:T(8,128)(2,1)S(1)}, u32[]{:S(2)}, u32[]{:S(2)}) collective-permute-start(bf16[2,4,128,128]{3,2,1,0:T(8,128)(2,1)S(1)} %pad_maximum_fusion.3), channel_id=1, source_target_pairs={{0,6},{2,4},{4,2},{6,0},{8,14},{10,12},{12,10},{14,8},{1,7},{3,5},... | collective-permute-start | bytes 786440 | tf_op jit(solution)/shard_map/ppermute | solution.py:186
  48.2 7.3 %collective-permute-start.9 = (bf16[4,128,128]{2,1,0:T(8,128)(2,1)S(1)}, bf16[4,128,128]{2,1,0:T(8,128)(2,1)S(1)}, u32[]{:S(2)}, u32[]{:S(2)}) collective-permute-start(bf16[4,128,128]{2,1,0:T(8,128)(2,1)S(1)} %fusion.1), channel_id=1, source_target_pairs={{0,8},{2,10},{4,12},{6,14},{8,0},{10,2},{12,4},{14,6},{1,9},{3,11}... | collective-permute-start | bytes 393224 | tf_op jit(solution)/shard_map/ppermute | solution.py:189

commit v13 on v9

--- a/solution.py
+++ b/solution.py
@@ -166,13 +166,14 @@
         gathered,
         kv_heads,
     )
-    own_total = own_part
     mirror_total = mirror_part
     for k in range(1, half):
-        pair = jnp.stack([parts[k - 1], parts[half + k - 1]])
-        arrived = lax.ppermute(pair, "ctx", mate_pairs(cycle_size, half - k)).astype(jnp.float32)
-        own_total = own_total + arrived[0]
-        mirror_total = mirror_total + arrived[1]
+        arrived = lax.ppermute(parts[half + k - 1], "ctx", mate_pairs(cycle_size, half - k))
+        mirror_total = mirror_total + arrived.astype(jnp.float32)
+    own_total = own_part
+    for k in range(1, half):
+        arrived = lax.ppermute(parts[k - 1], "ctx", mate_pairs(cycle_size, half - k))
+        own_total = own_total + arrived.astype(jnp.float32)
     crossed = lax.ppermute(mirror_total.astype(jnp.bfloat16), "ctx", mirror_pairs(cycle_size))
     total = own_total + crossed.astype(jnp.float32)
     key_grad = total[:kv_heads].transpose(1, 0, 2)

time: 52.2 us -> 50.2 us (0.962)
  waiting for transfers between devices: 20.7 us -> 14.8 us
  starting transfers between devices: 20.1 us -> 24.2 us
    ppermute x3 -> x6, waiting for transfers between devices: 9.62 us -> 5.31 us  [the longest x3 3.66 us: on_device(): lax.ppermute(parts[half + k - 1], 'ctx', mate_pairs(cycle_size, half - k))]
    ppermute x3 -> x6, starting transfers between devices: 4.28 us -> 8.48 us  [the longest x3 4.29 us: on_device(): lax.ppermute(parts[k - 1], 'ctx', mate_pairs(cycle_size, half - k))]
    ppermute x1, waiting for transfers between devices: 5.47 us -> 3.85 us  [on_device(): lax.ppermute(mirror_total.astype(jnp.bfloat16), 'ctx', mirror_pairs(cycle...]
  transfers between devices with their start and end apart: 11 -> 14, of which waited for: 8 -> 9; matrix products, arithmetic and copies ran while one was open for 5% -> 5% of each run, Pallas kernels for 0% -> 0%
where the time goes in v13:
time: 50.2 us; the launch traced here: 50 us
  starting transfers between devices  24.2 us (48%)
  waiting for transfers between devices  14.8 us (29%)
  Pallas kernels  4.1 us (8%)
  local copies, waits for them, and re-layouts  4.04 us (8%)
  between operations  1.48 us (3%)
  other arithmetic  1.39 us (3%)
    ppermute x3, starting transfers between devices, on_device(): lax.ppermute(from_mirror, 'ctx', mate_pairs(cycle_size, k))  6.42 us
    ppermute x3, starting transfers between devices, on_device(): lax.ppermute(slab, 'ctx', mate_pairs(cycle_size, k))  6 us
    ppermute x3, starting transfers between devices, on_device(): lax.ppermute(parts[k - 1], 'ctx', mate_pairs(cycle_size, half - k))  4.29 us
    ppermute x3, starting transfers between devices, on_device(): lax.ppermute(parts[half + k - 1], 'ctx', mate_pairs(cycle_size, half - k))  4.19 us
    pallas_call x1, Pallas kernels, local_backward(): pl.pallas_call(functools.partial(backward_kernel, kv_heads=kv_heads, chun...  4.1 us
    ppermute x1, waiting for transfers between devices, on_device(): lax.ppermute(mirror_total.astype(jnp.bfloat16), 'ctx', mirror_pairs(cycle...  3.85 us
    ppermute x3, waiting for transfers between devices, on_device(): lax.ppermute(parts[half + k - 1], 'ctx', mate_pairs(cycle_size, half - k))  3.66 us
    ppermute x1, waiting for transfers between devices, on_device(): from_mirror = lax.ppermute(slab, 'ctx', mirror_pairs(cycle_size))  3.16 us
  transfers between devices with their start and end apart: 14, of which 9 were waited for; matrix products, arithmetic and copies ran while one was open for 5% of the time, Pallas kernels for 0%

profile of v13, /device:TPU:0, one launch (start us, length us, event | category | flops | bytes accessed | tf_op | source)
XLA Modules:
  0.0 50.0 jit_solution(2426789104535541432)
XLA Ops:
  0.6 0.0 copy-start
  1.3 1.0 %maximum_bitcast_fusion = bf16[4,128,128]{2,0,1:T(4,128)(2,1)S(1)} fusion(bf16[128,2,128]{2,1,0:T(2,128)(2,1)} %param.8, bf16[128,2,128]{2,1,0:T(2,128)(2,1)} %param.7), kind=kLoop, calls=%fused_computation.15 | loop fusion | flops 262144 | bytes 262144 | tf_op jit(solution)/shard_map/transpose | solution.py:149
  2.4 3.0 %collective-permute-start = (bf16[528,128]{1,0:T(8,128)(2,1)S(1)}, bf16[528,128]{1,0:T(8,128)(2,1)S(1)}, u32[]{:S(2)}, u32[]{:S(2)}) collective-permute-start(bf16[528,128]{1,0:T(8,128)(2,1)S(1)} %concatenate.7), channel_id=1, source_target_pairs={{0,2},{2,4},{4,6},{6,0},{8,10},{10,12},{12,14},{14,8},{1,3},{3,5},... | collective-permute-start | bytes 405512 | tf_op jit(solution)/shard_map/ppermute | solution.py:152
  5.4 1.6 %collective-permute-start.1 = (bf16[528,128]{1,0:T(8,128)(2,1)S(1)}, bf16[528,128]{1,0:T(8,128)(2,1)S(1)}, u32[]{:S(2)}, u32[]{:S(2)}) collective-permute-start(bf16[528,128]{1,0:T(8,128)(2,1)S(1)} %concatenate.7), channel_id=1, source_target_pairs={{0,4},{2,6},{4,0},{6,2},{8,12},{10,14},{12,8},{14,10},{1,5},{3,7},... | collective-permute-start | bytes 405512 | tf_op jit(solution)/shard_map/ppermute | solution.py:152
  7.0 1.4 %collective-permute-start.2 = (bf16[528,128]{1,0:T(8,128)(2,1)S(1)}, bf16[528,128]{1,0:T(8,128)(2,1)S(1)}, u32[]{:S(2)}, u32[]{:S(2)}) collective-permute-start(bf16[528,128]{1,0:T(8,128)(2,1)S(1)} %concatenate.7), channel_id=1, source_target_pairs={{0,6},{2,0},{4,2},{6,4},{8,14},{10,8},{12,10},{14,12},{1,7},{3,1},... | collective-permute-start | bytes 405512 | tf_op jit(solution)/shard_map/ppermute | solution.py:152
  8.4 2.6 %collective-permute-start.3 = (bf16[528,128]{1,0:T(8,128)(2,1)S(1)}, bf16[528,128]{1,0:T(8,128)(2,1)S(1)}, u32[]{:S(2)}, u32[]{:S(2)}) collective-permute-start(bf16[528,128]{1,0:T(8,128)(2,1)S(1)} %concatenate.7), channel_id=1, source_target_pairs={{0,8},{2,10},{4,12},{6,14},{8,0},{10,2},{12,4},{14,6},{1,9},{3,11}... | collective-permute-start | bytes 405512 | tf_op jit(solution)/shard_map/ppermute | solution.py:153
  11.0 1.1 %copy_bitcast_fusion = (bf16[8,128,128]{2,1,0:T(8,128)(2,1)S(1)}, bf16[8,128,128]{2,1,0:T(8,128)(2,1)S(1)}) fusion(bf16[128,8,128]{2,1,0:T(8,128)(2,1)} %param.9, bf16[128,8,128]{2,1,0:T(8,128)(2,1)} %param.10), kind=kLoop, calls=%fused_computation | loop fusion | bytes 1048576 | tf_op jit(solution)/shard_map/transpose | solution.py:165
  12.1 0.0 copy-done
  12.2 3.2 %collective-permute-done.3 = bf16[528,128]{1,0:T(8,128)(2,1)S(1)} collective-permute-done((bf16[528,128]{1,0:T(8,128)(2,1)S(1)}, bf16[528,128]{1,0:T(8,128)(2,1)S(1)}, u32[]{:S(2)}, u32[]{:S(2)}) %collective-permute-start.3) | collective-permute-done | bytes 135200 | tf_op jit(solution)/shard_map/ppermute | solution.py:153
  15.4 0.3 collective-permute-start.4
  15.6 3.5 %collective-permute-start.5 = (bf16[528,128]{1,0:T(8,128)(2,1)S(1)}, bf16[528,128]{1,0:T(8,128)(2,1)S(1)}, u32[]{:S(2)}, u32[]{:S(2)}) collective-permute-start(bf16[528,128]{1,0:T(8,128)(2,1)S(1)} %collective-permute-done.3), channel_id=1, source_target_pairs={{0,4},{2,6},{4,0},{6,2},{8,12},{10,14},{12,8},{14,10},{1,5},{3,7},... | collective-permute-start | bytes 405512 | tf_op jit(solution)/shard_map/ppermute | solution.py:155
  19.1 0.0 collective-permute-done
  19.1 2.7 %collective-permute-start.6 = (bf16[528,128]{1,0:T(8,128)(2,1)S(1)}, bf16[528,128]{1,0:T(8,128)(2,1)S(1)}, u32[]{:S(2)}, u32[]{:S(2)}) collective-permute-start(bf16[528,128]{1,0:T(8,128)(2,1)S(1)} %collective-permute-done.3), channel_id=1, source_target_pairs={{0,6},{2,0},{4,2},{6,4},{8,14},{10,8},{12,10},{14,12},{1,7},{3,1},... | collective-permute-start | bytes 405512 | tf_op jit(solution)/shard_map/ppermute | solution.py:155
  21.8 0.0 collective-permute-done.1
  21.8 0.0 collective-permute-done.2
  21.9 0.8 %collective-permute-done.4 = bf16[528,128]{1,0:T(8,128)(2,1)S(1)} collective-permute-done((bf16[528,128]{1,0:T(8,128)(2,1)S(1)}, bf16[528,128]{1,0:T(8,128)(2,1)S(1)}, u32[]{:S(2)}, u32[]{:S(2)}) %collective-permute-start.4) | collective-permute-done | bytes 135200 | tf_op jit(solution)/shard_map/ppermute | solution.py:155
  22.7 0.6 %collective-permute-done.5 = bf16[528,128]{1,0:T(8,128)(2,1)S(1)} collective-permute-done((bf16[528,128]{1,0:T(8,128)(2,1)S(1)}, bf16[528,128]{1,0:T(8,128)(2,1)S(1)}, u32[]{:S(2)}, u32[]{:S(2)}) %collective-permute-start.5) | collective-permute-done | bytes 135200 | tf_op jit(solution)/shard_map/ppermute | solution.py:155
  23.3 1.1 %collective-permute-done.6 = bf16[528,128]{1,0:T(8,128)(2,1)S(1)} collective-permute-done((bf16[528,128]{1,0:T(8,128)(2,1)S(1)}, bf16[528,128]{1,0:T(8,128)(2,1)S(1)}, u32[]{:S(2)}, u32[]{:S(2)}) %collective-permute-start.6) | collective-permute-done | bytes 135200 | tf_op jit(solution)/shard_map/ppermute | solution.py:155
  24.4 0.2 fusion.1.offs_ref
  24.6 4.1 %shard_map.85 = (f32[8,128,128]{2,1,0:T(8,128)S(1)}, f32[4,128,128]{2,1,0:T(8,128)S(1)}, f32[4,128,128]{2,1,0:T(8,128)S(1)}, bf16[7,4,128,128]{3,2,1,0:T(8,128)(2,1)S(1)}) custom-call(s32[8]{0:T(128)S(1)} %fusion.1.offs_ref, s32[1]{0:T(128)S(6)} %copy.34.own_ref, bf16[8,128,128]{2,1,0:T(8,128)(2,1)S(1)} %bitcast.45, ...), custom_call_target="tpu_custom_call" | custom-call | flops 1610612736 | bytes 2654208 | tf_op jit(solution)/shard_map/pallas_call | solution.py:123
  28.8 0.1 slice_bitcast_fusion.7
  28.8 3.3 %collective-permute-start.10 = (bf16[4,128,128]{2,1,0:T(8,128)(2,1)S(1)}, bf16[4,128,128]{2,1,0:T(8,128)(2,1)S(1)}, u32[]{:S(2)}, u32[]{:S(2)}) collective-permute-start(bf16[4,128,128]{2,1,0:T(8,128)(2,1)S(1)} %get-tuple-element.20), channel_id=1, source_target_pairs={{0,6},{2,0},{4,2},{6,4},{8,14},{10,8},{12,10},{14,12},{1,7},{3,1},... | collective-permute-start | bytes 393224 | tf_op jit(solution)/shard_map/ppermute | solution.py:171
  32.2 0.0 collective-permute-start.11
  32.2 0.8 %collective-permute-start.12 = (bf16[4,128,128]{2,1,0:T(8,128)(2,1)S(1)}, bf16[4,128,128]{2,1,0:T(8,128)(2,1)S(1)}, u32[]{:S(2)}, u32[]{:S(2)}) collective-permute-start(bf16[4,128,128]{2,1,0:T(8,128)(2,1)S(1)} %get-tuple-element.18), channel_id=1, source_target_pairs={{0,2},{2,4},{4,6},{6,0},{8,10},{10,12},{12,14},{14,8},{1,3},{3,5},... | collective-permute-start | bytes 393224 | tf_op jit(solution)/shard_map/ppermute | solution.py:171
  33.0 2.1 %collective-permute-start.7 = (bf16[4,128,128]{2,1,0:T(8,128)(2,1)S(1)}, bf16[4,128,128]{2,1,0:T(8,128)(2,1)S(1)}, u32[]{:S(2)}, u32[]{:S(2)}) collective-permute-start(bf16[4,128,128]{2,1,0:T(8,128)(2,1)S(1)} %get-tuple-element.17), channel_id=1, source_target_pairs={{0,6},{2,0},{4,2},{6,4},{8,14},{10,8},{12,10},{14,12},{1,7},{3,1},... | collective-permute-start | bytes 393224 | tf_op jit(solution)/shard_map/ppermute | solution.py:175
  35.1 2.0 %collective-permute-start.8 = (bf16[4,128,128]{2,1,0:T(8,128)(2,1)S(1)}, bf16[4,128,128]{2,1,0:T(8,128)(2,1)S(1)}, u32[]{:S(2)}, u32[]{:S(2)}) collective-permute-start(bf16[4,128,128]{2,1,0:T(8,128)(2,1)S(1)} %get-tuple-element.22), channel_id=1, source_target_pairs={{0,4},{2,6},{4,0},{6,2},{8,12},{10,14},{12,8},{14,10},{1,5},{3,7},... | collective-permute-start | bytes 393224 | tf_op jit(solution)/shard_map/ppermute | solution.py:175
  37.1 0.0 collective-permute-done.10
  37.1 0.2 collective-permute-start.9
  37.3 1.6 %collective-permute-done.11 = bf16[4,128,128]{2,1,0:T(8,128)(2,1)S(1)} collective-permute-done((bf16[4,128,128]{2,1,0:T(8,128)(2,1)S(1)}, bf16[4,128,128]{2,1,0:T(8,128)(2,1)S(1)}, u32[]{:S(2)}, u32[]{:S(2)}) %collective-permute-start.11) | collective-permute-done | bytes 131104 | tf_op jit(solution)/shard_map/ppermute | solution.py:171
  38.9 2.0 %collective-permute-done.12 = bf16[4,128,128]{2,1,0:T(8,128)(2,1)S(1)} collective-permute-done((bf16[4,128,128]{2,1,0:T(8,128)(2,1)S(1)}, bf16[4,128,128]{2,1,0:T(8,128)(2,1)S(1)}, u32[]{:S(2)}, u32[]{:S(2)}) %collective-permute-start.12) | collective-permute-done | bytes 131104 | tf_op jit(solution)/shard_map/ppermute | solution.py:171
  41.0 0.1 add_convert_fusion
  41.0 0.7 %collective-permute-start.13 = (bf16[4,128,128]{2,1,0:T(8,128)(2,1)S(1)}, bf16[4,128,128]{2,1,0:T(8,128)(2,1)S(1)}, u32[]{:S(2)}, u32[]{:S(2)}) collective-permute-start(bf16[4,128,128]{2,1,0:T(8,128)(2,1)S(1)} %add_convert_fusion), channel_id=1, source_target_pairs={{0,8},{2,10},{4,12},{6,14},{8,0},{10,2},{12,4},{14,6},{1,9},{3,11}... | collective-permute-start | bytes 393224 | tf_op jit(solution)/shard_map/ppermute | solution.py:177
  41.8 1.1 %copy.20 = f32[128,8,128]{2,1,0:T(8,128)} copy(f32[128,8,128]{2,0,1:T(8,128)S(1)} %bitcast.44) | data formatting | bytes 1048576
  42.9 0.0 collective-permute-done.7
  42.9 0.7 %collective-permute-done.8 = bf16[4,128,128]{2,1,0:T(8,128)(2,1)S(1)} collective-permute-done((bf16[4,128,128]{2,1,0:T(8,128)(2,1)S(1)}, bf16[4,128,128]{2,1,0:T(8,128)(2,1)S(1)}, u32[]{:S(2)}, u32[]{:S(2)}) %collective-permute-start.8) | collective-permute-done | bytes 131104 | tf_op jit(solution)/shard_map/ppermute | solution.py:175
  43.6 1.0 %collective-permute-done.9 = bf16[4,128,128]{2,1,0:T(8,128)(2,1)S(1)} collective-permute-done((bf16[4,128,128]{2,1,0:T(8,128)(2,1)S(1)}, bf16[4,128,128]{2,1,0:T(8,128)(2,1)S(1)}, u32[]{:S(2)}, u32[]{:S(2)}) %collective-permute-start.9) | collective-permute-done | bytes 131104 | tf_op jit(solution)/shard_map/ppermute | solution.py:175
  44.5 3.8 %collective-permute-done.13 = bf16[4,128,128]{2,1,0:T(8,128)(2,1)S(1)} collective-permute-done((bf16[4,128,128]{2,1,0:T(8,128)(2,1)S(1)}, bf16[4,128,128]{2,1,0:T(8,128)(2,1)S(1)}, u32[]{:S(2)}, u32[]{:S(2)}) %collective-permute-start.13) | collective-permute-done | bytes 131104 | tf_op jit(solution)/shard_map/ppermute | solution.py:177
  48.4 0.1 convert_add_fusion
  48.5 0.8 %copy.21 = f32[128,2,128]{2,1,0:T(2,128)} copy(f32[128,2,128]{2,0,1:T(8,128)S(1)} %get-tuple-element.24) | data formatting | bytes 262144
  49.2 0.8 %copy.22 = f32[128,2,128]{2,1,0:T(2,128)} copy(f32[128,2,128]{2,0,1:T(8,128)S(1)} %get-tuple-element.23) | data formatting | bytes 262144
  (12 shorter events, 0.2 us)
Async XLA Ops:
  0.6 11.5 %copy-start = (bf16[128,8,128]{2,1,0:T(8,128)(2,1)S(1)}, bf16[128,8,128]{2,1,0:T(8,128)(2,1)}, u32[]{:S(2)}) copy-start(bf16[128,8,128]{2,1,0:T(8,128)(2,1)} %param.6) | copy-start | bytes 786436
  2.4 16.7 %collective-permute-start = (bf16[528,128]{1,0:T(8,128)(2,1)S(1)}, bf16[528,128]{1,0:T(8,128)(2,1)S(1)}, u32[]{:S(2)}, u32[]{:S(2)}) collective-permute-start(bf16[528,128]{1,0:T(8,128)(2,1)S(1)} %concatenate.7), channel_id=1, source_target_pairs={{0,2},{2,4},{4,6},{6,0},{8,10},{10,12},{12,14},{14,8},{1,3},{3,5},... | collective-permute-start | bytes 405512 | tf_op jit(solution)/shard_map/ppermute | solution.py:152
  5.4 16.4 %collective-permute-start.1 = (bf16[528,128]{1,0:T(8,128)(2,1)S(1)}, bf16[528,128]{1,0:T(8,128)(2,1)S(1)}, u32[]{:S(2)}, u32[]{:S(2)}) collective-permute-start(bf16[528,128]{1,0:T(8,128)(2,1)S(1)} %concatenate.7), channel_id=1, source_target_pairs={{0,4},{2,6},{4,0},{6,2},{8,12},{10,14},{12,8},{14,10},{1,5},{3,7},... | collective-permute-start | bytes 405512 | tf_op jit(solution)/shard_map/ppermute | solution.py:152
  7.0 14.8 %collective-permute-start.2 = (bf16[528,128]{1,0:T(8,128)(2,1)S(1)}, bf16[528,128]{1,0:T(8,128)(2,1)S(1)}, u32[]{:S(2)}, u32[]{:S(2)}) collective-permute-start(bf16[528,128]{1,0:T(8,128)(2,1)S(1)} %concatenate.7), channel_id=1, source_target_pairs={{0,6},{2,0},{4,2},{6,4},{8,14},{10,8},{12,10},{14,12},{1,7},{3,1},... | collective-permute-start | bytes 405512 | tf_op jit(solution)/shard_map/ppermute | solution.py:152
  8.4 7.0 %collective-permute-start.3 = (bf16[528,128]{1,0:T(8,128)(2,1)S(1)}, bf16[528,128]{1,0:T(8,128)(2,1)S(1)}, u32[]{:S(2)}, u32[]{:S(2)}) collective-permute-start(bf16[528,128]{1,0:T(8,128)(2,1)S(1)} %concatenate.7), channel_id=1, source_target_pairs={{0,8},{2,10},{4,12},{6,14},{8,0},{10,2},{12,4},{14,6},{1,9},{3,11}... | collective-permute-start | bytes 405512 | tf_op jit(solution)/shard_map/ppermute | solution.py:153
  15.4 7.3 %collective-permute-start.4 = (bf16[528,128]{1,0:T(8,128)(2,1)S(1)}, bf16[528,128]{1,0:T(8,128)(2,1)S(1)}, u32[]{:S(2)}, u32[]{:S(2)}) collective-permute-start(bf16[528,128]{1,0:T(8,128)(2,1)S(1)} %collective-permute-done.3), channel_id=1, source_target_pairs={{0,2},{2,4},{4,6},{6,0},{8,10},{10,12},{12,14},{14,8},{1,3},{3,5},... | collective-permute-start | bytes 405512 | tf_op jit(solution)/shard_map/ppermute | solution.py:155
  15.6 7.7 %collective-permute-start.5 = (bf16[528,128]{1,0:T(8,128)(2,1)S(1)}, bf16[528,128]{1,0:T(8,128)(2,1)S(1)}, u32[]{:S(2)}, u32[]{:S(2)}) collective-permute-start(bf16[528,128]{1,0:T(8,128)(2,1)S(1)} %collective-permute-done.3), channel_id=1, source_target_pairs={{0,4},{2,6},{4,0},{6,2},{8,12},{10,14},{12,8},{14,10},{1,5},{3,7},... | collective-permute-start | bytes 405512 | tf_op jit(solution)/shard_map/ppermute | solution.py:155
  19.1 5.3 %collective-permute-start.6 = (bf16[528,128]{1,0:T(8,128)(2,1)S(1)}, bf16[528,128]{1,0:T(8,128)(2,1)S(1)}, u32[]{:S(2)}, u32[]{:S(2)}) collective-permute-start(bf16[528,128]{1,0:T(8,128)(2,1)S(1)} %collective-permute-done.3), channel_id=1, source_target_pairs={{0,6},{2,0},{4,2},{6,4},{8,14},{10,8},{12,10},{14,12},{1,7},{3,1},... | collective-permute-start | bytes 405512 | tf_op jit(solution)/shard_map/ppermute | solution.py:155
  28.8 8.3 %collective-permute-start.10 = (bf16[4,128,128]{2,1,0:T(8,128)(2,1)S(1)}, bf16[4,128,128]{2,1,0:T(8,128)(2,1)S(1)}, u32[]{:S(2)}, u32[]{:S(2)}) collective-permute-start(bf16[4,128,128]{2,1,0:T(8,128)(2,1)S(1)} %get-tuple-element.20), channel_id=1, source_target_pairs={{0,6},{2,0},{4,2},{6,4},{8,14},{10,8},{12,10},{14,12},{1,7},{3,1},... | collective-permute-start | bytes 393224 | tf_op jit(solution)/shard_map/ppermute | solution.py:171
  32.2 6.8 %collective-permute-start.11 = (bf16[4,128,128]{2,1,0:T(8,128)(2,1)S(1)}, bf16[4,128,128]{2,1,0:T(8,128)(2,1)S(1)}, u32[]{:S(2)}, u32[]{:S(2)}) collective-permute-start(bf16[4,128,128]{2,1,0:T(8,128)(2,1)S(1)} %get-tuple-element.19), channel_id=1, source_target_pairs={{0,4},{2,6},{4,0},{6,2},{8,12},{10,14},{12,8},{14,10},{1,5},{3,7},... | collective-permute-start | bytes 393224 | tf_op jit(solution)/shard_map/ppermute | solution.py:171
  32.2 8.8 %collective-permute-start.12 = (bf16[4,128,128]{2,1,0:T(8,128)(2,1)S(1)}, bf16[4,128,128]{2,1,0:T(8,128)(2,1)S(1)}, u32[]{:S(2)}, u32[]{:S(2)}) collective-permute-start(bf16[4,128,128]{2,1,0:T(8,128)(2,1)S(1)} %get-tuple-element.18), channel_id=1, source_target_pairs={{0,2},{2,4},{4,6},{6,0},{8,10},{10,12},{12,14},{14,8},{1,3},{3,5},... | collective-permute-start | bytes 393224 | tf_op jit(solution)/shard_map/ppermute | solution.py:171
  33.0 9.9 %collective-permute-start.7 = (bf16[4,128,128]{2,1,0:T(8,128)(2,1)S(1)}, bf16[4,128,128]{2,1,0:T(8,128)(2,1)S(1)}, u32[]{:S(2)}, u32[]{:S(2)}) collective-permute-start(bf16[4,128,128]{2,1,0:T(8,128)(2,1)S(1)} %get-tuple-element.17), channel_id=1, source_target_pairs={{0,6},{2,0},{4,2},{6,4},{8,14},{10,8},{12,10},{14,12},{1,7},{3,1},... | collective-permute-start | bytes 393224 | tf_op jit(solution)/shard_map/ppermute | solution.py:175
  35.1 8.5 %collective-permute-start.8 = (bf16[4,128,128]{2,1,0:T(8,128)(2,1)S(1)}, bf16[4,128,128]{2,1,0:T(8,128)(2,1)S(1)}, u32[]{:S(2)}, u32[]{:S(2)}) collective-permute-start(bf16[4,128,128]{2,1,0:T(8,128)(2,1)S(1)} %get-tuple-element.22), channel_id=1, source_target_pairs={{0,4},{2,6},{4,0},{6,2},{8,12},{10,14},{12,8},{14,10},{1,5},{3,7},... | collective-permute-start | bytes 393224 | tf_op jit(solution)/shard_map/ppermute | solution.py:175
  37.1 7.4 %collective-permute-start.9 = (bf16[4,128,128]{2,1,0:T(8,128)(2,1)S(1)}, bf16[4,128,128]{2,1,0:T(8,128)(2,1)S(1)}, u32[]{:S(2)}, u32[]{:S(2)}) collective-permute-start(bf16[4,128,128]{2,1,0:T(8,128)(2,1)S(1)} %get-tuple-element.21), channel_id=1, source_target_pairs={{0,2},{2,4},{4,6},{6,0},{8,10},{10,12},{12,14},{14,8},{1,3},{3,5},... | collective-permute-start | bytes 393224 | tf_op jit(solution)/shard_map/ppermute | solution.py:175
  41.0 7.3 %collective-permute-start.13 = (bf16[4,128,128]{2,1,0:T(8,128)(2,1)S(1)}, bf16[4,128,128]{2,1,0:T(8,128)(2,1)S(1)}, u32[]{:S(2)}, u32[]{:S(2)}) collective-permute-start(bf16[4,128,128]{2,1,0:T(8,128)(2,1)S(1)} %add_convert_fusion), channel_id=1, source_target_pairs={{0,8},{2,10},{4,12},{6,14},{8,0},{10,2},{12,4},{14,6},{1,9},{3,11}... | collective-permute-start | bytes 393224 | tf_op jit(solution)/shard_map/ppermute | solution.py:177

commit v14 on v10

--- a/solution.py
+++ b/solution.py
@@ -176,13 +176,14 @@
         gathered,
         kv_heads,
     )
-    own_total = own_part
     mirror_total = mirror_part
     for k in range(1, half):
-        pair = jnp.stack([parts[k - 1], parts[half + k - 1]])
-        arrived = lax.ppermute(pair, "ctx", mate_pairs(cycle_size, k)).astype(jnp.float32)
-        own_total = own_total + arrived[0]
-        mirror_total = mirror_total + arrived[1]
+        arrived = lax.ppermute(parts[half + k - 1], "ctx", mate_pairs(cycle_size, k))
+        mirror_total = mirror_total + arrived.astype(jnp.float32)
+    own_total = own_part
+    for k in range(1, half):
+        arrived = lax.ppermute(parts[k - 1], "ctx", mate_pairs(cycle_size, k))
+        own_total = own_total + arrived.astype(jnp.float32)
     crossed = lax.ppermute(mirror_total.astype(jnp.bfloat16), "ctx", mirror_pairs(cycle_size))
     total = own_total + crossed.astype(jnp.float32)
     key_grad = total[:kv_heads].transpose(1, 0, 2)

time: 52.4 us -> 49.8 us (0.950)
  waiting for transfers between devices: 21.3 us -> 13.8 us
  starting transfers between devices: 19.6 us -> 24.7 us
    ppermute x3 -> x6, waiting for transfers between devices: 8.62 us -> 1.52 us  [the longest x3 1.51 us: on_device(): lax.ppermute(parts[half + k - 1], 'ctx', mate_pairs(cycle_size, k))]
    ppermute x3 -> x6, starting transfers between devices: 3.68 us -> 8.92 us  [the longest x3 5.37 us: on_device(): arrived = lax.ppermute(parts[k - 1], 'ctx', mate_pairs(cycle_size, k))]
  transfers between devices with their start and end apart: 10 -> 13, of which waited for: 6 -> 6; matrix products, arithmetic and copies ran while one was open for 5% -> 5% of each run, Pallas kernels for 0% -> 0%
where the time goes in v14:
time: 49.8 us; the launch traced here: 49.6 us
  starting transfers between devices  24.7 us (50%)
  waiting for transfers between devices  13.8 us (28%)
  Pallas kernels  4.1 us (8%)
  local copies, waits for them, and re-layouts  4.05 us (8%)
  between operations  1.49 us (3%)
  other arithmetic  1.41 us (3%)
    ppermute x1, waiting for transfers between devices, on_device(): lax.ppermute(jnp.stack([from_mirror, from_x2]), 'ctx', mate_pairs(cycle_s...  6.57 us
    ppermute x3, starting transfers between devices, on_device(): arrived = lax.ppermute(parts[k - 1], 'ctx', mate_pairs(cycle_size, k))  5.37 us
    ppermute x1, starting transfers between devices, on_device(): lax.ppermute(mirror_total.astype(jnp.bfloat16), 'ctx', mirror_pairs(cycle...  5.03 us
    pallas_call x1, Pallas kernels, local_backward(): pl.pallas_call(functools.partial(backward_kernel, kv_heads=kv_heads, chun...  4.1 us
    ppermute x1, starting transfers between devices, on_device(): from_mirror = lax.ppermute(slab, 'ctx', mirror_pairs(cycle_size))  4.1 us
    ppermute x3, starting transfers between devices, on_device(): lax.ppermute(parts[half + k - 1], 'ctx', mate_pairs(cycle_size, k))  3.55 us
    ppermute x1, waiting for transfers between devices, on_device(): lax.ppermute(mirror_total.astype(jnp.bfloat16), 'ctx', mirror_pairs(cycle...  3.24 us
    unnamed x13, local copies, waits for them, and re-layouts  2.78 us
  transfers between devices with their start and end apart: 13, of which 6 were waited for; matrix products, arithmetic and copies ran while one was open for 5% of the time, Pallas kernels for 0%

profile of v14, /device:TPU:0, one launch (start us, length us, event | category | flops | bytes accessed | tf_op | source)
XLA Modules:
  0.0 49.6 jit_solution(10103618312853595389)
XLA Ops:
  0.6 0.0 copy-start
  1.3 1.0 %maximum_bitcast_fusion = bf16[4,128,128]{2,0,1:T(4,128)(2,1)S(1)} fusion(bf16[128,2,128]{2,1,0:T(2,128)(2,1)} %param.8, bf16[128,2,128]{2,1,0:T(2,128)(2,1)} %param.7), kind=kLoop, calls=%fused_computation.14 | loop fusion | flops 262144 | bytes 262144 | tf_op jit(solution)/shard_map/transpose | solution.py:150
  2.4 4.1 %collective-permute-start.2 = (bf16[528,128]{1,0:T(8,128)(2,1)S(1)}, bf16[528,128]{1,0:T(8,128)(2,1)S(1)}, u32[]{:S(2)}, u32[]{:S(2)}) collective-permute-start(bf16[528,128]{1,0:T(8,128)(2,1)S(1)} %concatenate.7), channel_id=1, source_target_pairs={{0,8},{2,10},{4,12},{6,14},{8,0},{10,2},{12,4},{14,6},{1,9},{3,11}... | collective-permute-start | bytes 405512 | tf_op jit(solution)/shard_map/ppermute | solution.py:153
  6.5 1.6 %collective-permute-start.1 = (bf16[528,128]{1,0:T(8,128)(2,1)S(1)}, bf16[528,128]{1,0:T(8,128)(2,1)S(1)}, u32[]{:S(2)}, u32[]{:S(2)}) collective-permute-start(bf16[528,128]{1,0:T(8,128)(2,1)S(1)} %concatenate.7), channel_id=1, source_target_pairs={{0,4},{2,6},{4,0},{6,2},{8,12},{10,14},{12,8},{14,10},{1,5},{3,7},... | collective-permute-start | bytes 405512 | tf_op jit(solution)/shard_map/ppermute | solution.py:156
  8.1 1.5 %collective-permute-start = (bf16[528,128]{1,0:T(8,128)(2,1)S(1)}, bf16[528,128]{1,0:T(8,128)(2,1)S(1)}, u32[]{:S(2)}, u32[]{:S(2)}) collective-permute-start(bf16[528,128]{1,0:T(8,128)(2,1)S(1)} %concatenate.7), channel_id=1, source_target_pairs={{0,2},{2,0},{4,6},{6,4},{8,10},{10,8},{12,14},{14,12},{1,3},{3,1},... | collective-permute-start | bytes 405512 | tf_op jit(solution)/shard_map/ppermute | solution.py:155
  9.6 1.1 %copy_bitcast_fusion = (bf16[8,128,128]{2,1,0:T(8,128)(2,1)S(1)}, bf16[8,128,128]{2,1,0:T(8,128)(2,1)S(1)}) fusion(bf16[128,8,128]{2,1,0:T(8,128)(2,1)} %param.9, bf16[128,8,128]{2,1,0:T(8,128)(2,1)} %param.10), kind=kLoop, calls=%fused_computation.1 | loop fusion | bytes 1048576 | tf_op jit(solution)/shard_map/transpose | solution.py:175
  10.7 0.0 copy-done
  10.8 2.3 %collective-permute-done.2 = bf16[528,128]{1,0:T(8,128)(2,1)S(1)} collective-permute-done((bf16[528,128]{1,0:T(8,128)(2,1)S(1)}, bf16[528,128]{1,0:T(8,128)(2,1)S(1)}, u32[]{:S(2)}, u32[]{:S(2)}) %collective-permute-start.2) | collective-permute-done | bytes 135200 | tf_op jit(solution)/shard_map/ppermute | solution.py:153
  13.1 0.2 collective-permute-done.1
  13.3 1.6 %collective-permute-start.3 = (bf16[2,528,128]{2,1,0:T(8,128)(2,1)S(1)}, bf16[2,528,128]{2,1,0:T(8,128)(2,1)S(1)}, u32[]{:S(2)}, u32[]{:S(2)}) collective-permute-start(bf16[2,528,128]{2,1,0:T(8,128)(2,1)S(1)} %pad_maximum_fusion), channel_id=1, source_target_pairs={{0,2},{2,0},{4,6},{6,4},{8,10},{10,8},{12,14},{14,12},{1,3},{3,1},... | collective-permute-start | bytes 811016 | tf_op jit(solution)/shard_map/ppermute | solution.py:157
  14.9 1.4 %collective-permute-start.4 = (bf16[528,128]{1,0:T(8,128)(2,1)S(1)}, bf16[528,128]{1,0:T(8,128)(2,1)S(1)}, u32[]{:S(2)}, u32[]{:S(2)}) collective-permute-start(bf16[528,128]{1,0:T(8,128)(2,1)S(1)} %collective-permute-done.2), channel_id=1, source_target_pairs={{0,4},{2,6},{4,0},{6,2},{8,12},{10,14},{12,8},{14,10},{1,5},{3,7},... | collective-permute-start | bytes 405512 | tf_op jit(solution)/shard_map/ppermute | solution.py:158
  16.4 0.5 %collective-permute-start.5 = (bf16[528,128]{1,0:T(8,128)(2,1)S(1)}, bf16[528,128]{1,0:T(8,128)(2,1)S(1)}, u32[]{:S(2)}, u32[]{:S(2)}) collective-permute-start(bf16[528,128]{1,0:T(8,128)(2,1)S(1)} %collective-permute-done.2), channel_id=1, source_target_pairs={{0,6},{2,4},{4,2},{6,0},{8,14},{10,12},{12,10},{14,8},{1,7},{3,5},... | collective-permute-start | bytes 405512 | tf_op jit(solution)/shard_map/ppermute | solution.py:159
  16.9 0.0 collective-permute-done
  16.9 6.6 %collective-permute-done.3 = bf16[2,528,128]{2,1,0:T(8,128)(2,1)S(1)} collective-permute-done((bf16[2,528,128]{2,1,0:T(8,128)(2,1)S(1)}, bf16[2,528,128]{2,1,0:T(8,128)(2,1)S(1)}, u32[]{:S(2)}, u32[]{:S(2)}) %collective-permute-start.3) | collective-permute-done | bytes 270368 | tf_op jit(solution)/shard_map/ppermute | solution.py:157
  23.6 0.0 collective-permute-done.4
  23.6 0.0 collective-permute-done.5
  23.6 0.2 fusion.1.offs_ref
  23.9 4.1 %shard_map.85 = (f32[8,128,128]{2,1,0:T(8,128)S(1)}, f32[4,128,128]{2,1,0:T(8,128)S(1)}, f32[4,128,128]{2,1,0:T(8,128)S(1)}, bf16[7,4,128,128]{3,2,1,0:T(8,128)(2,1)S(1)}) custom-call(s32[8]{0:T(128)S(1)} %fusion.1.offs_ref, s32[1]{0:T(128)S(6)} %copy.34.own_ref, bf16[8,128,128]{2,1,0:T(8,128)(2,1)S(1)} %bitcast.41, ...), custom_call_target="tpu_custom_call" | custom-call | flops 1610612736 | bytes 2654208 | tf_op jit(solution)/shard_map/pallas_call | solution.py:124
  28.0 0.1 slice_bitcast_fusion.7
  28.1 1.7 %collective-permute-start.10 = (bf16[4,128,128]{2,1,0:T(8,128)(2,1)S(1)}, bf16[4,128,128]{2,1,0:T(8,128)(2,1)S(1)}, u32[]{:S(2)}, u32[]{:S(2)}) collective-permute-start(bf16[4,128,128]{2,1,0:T(8,128)(2,1)S(1)} %get-tuple-element.19), channel_id=1, source_target_pairs={{0,4},{2,6},{4,0},{6,2},{8,12},{10,14},{12,8},{14,10},{1,5},{3,7},... | collective-permute-start | bytes 393224 | tf_op jit(solution)/shard_map/ppermute | solution.py:181
  29.7 1.0 %collective-permute-start.11 = (bf16[4,128,128]{2,1,0:T(8,128)(2,1)S(1)}, bf16[4,128,128]{2,1,0:T(8,128)(2,1)S(1)}, u32[]{:S(2)}, u32[]{:S(2)}) collective-permute-start(bf16[4,128,128]{2,1,0:T(8,128)(2,1)S(1)} %get-tuple-element.18), channel_id=1, source_target_pairs={{0,6},{2,4},{4,2},{6,0},{8,14},{10,12},{12,10},{14,8},{1,7},{3,5},... | collective-permute-start | bytes 393224 | tf_op jit(solution)/shard_map/ppermute | solution.py:181
  30.8 0.8 %collective-permute-start.9 = (bf16[4,128,128]{2,1,0:T(8,128)(2,1)S(1)}, bf16[4,128,128]{2,1,0:T(8,128)(2,1)S(1)}, u32[]{:S(2)}, u32[]{:S(2)}) collective-permute-start(bf16[4,128,128]{2,1,0:T(8,128)(2,1)S(1)} %get-tuple-element.20), channel_id=1, source_target_pairs={{0,2},{2,0},{4,6},{6,4},{8,10},{10,8},{12,14},{14,12},{1,3},{3,1},... | collective-permute-start | bytes 393224 | tf_op jit(solution)/shard_map/ppermute | solution.py:181
  31.6 1.2 %collective-permute-start.6 = (bf16[4,128,128]{2,1,0:T(8,128)(2,1)S(1)}, bf16[4,128,128]{2,1,0:T(8,128)(2,1)S(1)}, u32[]{:S(2)}, u32[]{:S(2)}) collective-permute-start(bf16[4,128,128]{2,1,0:T(8,128)(2,1)S(1)} %get-tuple-element.17), channel_id=1, source_target_pairs={{0,2},{2,0},{4,6},{6,4},{8,10},{10,8},{12,14},{14,12},{1,3},{3,1},... | collective-permute-start | bytes 393224 | tf_op jit(solution)/shard_map/ppermute | solution.py:185
  32.8 1.9 %collective-permute-start.7 = (bf16[4,128,128]{2,1,0:T(8,128)(2,1)S(1)}, bf16[4,128,128]{2,1,0:T(8,128)(2,1)S(1)}, u32[]{:S(2)}, u32[]{:S(2)}) collective-permute-start(bf16[4,128,128]{2,1,0:T(8,128)(2,1)S(1)} %get-tuple-element.22), channel_id=1, source_target_pairs={{0,4},{2,6},{4,0},{6,2},{8,12},{10,14},{12,8},{14,10},{1,5},{3,7},... | collective-permute-start | bytes 393224 | tf_op jit(solution)/shard_map/ppermute | solution.py:185
  34.8 0.0 collective-permute-done.10
  34.8 2.2 %collective-permute-start.8 = (bf16[4,128,128]{2,1,0:T(8,128)(2,1)S(1)}, bf16[4,128,128]{2,1,0:T(8,128)(2,1)S(1)}, u32[]{:S(2)}, u32[]{:S(2)}) collective-permute-start(bf16[4,128,128]{2,1,0:T(8,128)(2,1)S(1)} %get-tuple-element.21), channel_id=1, source_target_pairs={{0,6},{2,4},{4,2},{6,0},{8,14},{10,12},{12,10},{14,8},{1,7},{3,5},... | collective-permute-start | bytes 393224 | tf_op jit(solution)/shard_map/ppermute | solution.py:185
  37.0 0.5 %collective-permute-done.11 = bf16[4,128,128]{2,1,0:T(8,128)(2,1)S(1)} collective-permute-done((bf16[4,128,128]{2,1,0:T(8,128)(2,1)S(1)}, bf16[4,128,128]{2,1,0:T(8,128)(2,1)S(1)}, u32[]{:S(2)}, u32[]{:S(2)}) %collective-permute-start.11) | collective-permute-done | bytes 131104 | tf_op jit(solution)/shard_map/ppermute | solution.py:181
  37.5 1.0 %collective-permute-done.9 = bf16[4,128,128]{2,1,0:T(8,128)(2,1)S(1)} collective-permute-done((bf16[4,128,128]{2,1,0:T(8,128)(2,1)S(1)}, bf16[4,128,128]{2,1,0:T(8,128)(2,1)S(1)}, u32[]{:S(2)}, u32[]{:S(2)}) %collective-permute-start.9) | collective-permute-done | bytes 131104 | tf_op jit(solution)/shard_map/ppermute | solution.py:181
  38.5 0.1 add_convert_fusion
  38.6 5.0 %collective-permute-start.12 = (bf16[4,128,128]{2,1,0:T(8,128)(2,1)S(1)}, bf16[4,128,128]{2,1,0:T(8,128)(2,1)S(1)}, u32[]{:S(2)}, u32[]{:S(2)}) collective-permute-start(bf16[4,128,128]{2,1,0:T(8,128)(2,1)S(1)} %add_convert_fusion), channel_id=1, source_target_pairs={{0,8},{2,10},{4,12},{6,14},{8,0},{10,2},{12,4},{14,6},{1,9},{3,11}... | collective-permute-start | bytes 393224 | tf_op jit(solution)/shard_map/ppermute | solution.py:187
  43.6 1.1 %copy.20 = f32[128,8,128]{2,1,0:T(8,128)} copy(f32[128,8,128]{2,0,1:T(8,128)S(1)} %bitcast.40) | data formatting | bytes 1048576
  44.7 0.0 collective-permute-done.6
  44.7 0.0 collective-permute-done.7
  44.7 0.0 collective-permute-done.8
  44.7 3.2 %collective-permute-done.12 = bf16[4,128,128]{2,1,0:T(8,128)(2,1)S(1)} collective-permute-done((bf16[4,128,128]{2,1,0:T(8,128)(2,1)S(1)}, bf16[4,128,128]{2,1,0:T(8,128)(2,1)S(1)}, u32[]{:S(2)}, u32[]{:S(2)}) %collective-permute-start.12) | collective-permute-done | bytes 131104 | tf_op jit(solution)/shard_map/ppermute | solution.py:187
  48.0 0.1 convert_add_fusion
  48.1 0.8 %copy.21 = f32[128,2,128]{2,1,0:T(2,128)} copy(f32[128,2,128]{2,0,1:T(8,128)S(1)} %get-tuple-element.24) | data formatting | bytes 262144
  48.8 0.8 %copy.22 = f32[128,2,128]{2,1,0:T(2,128)} copy(f32[128,2,128]{2,0,1:T(8,128)S(1)} %get-tuple-element.23) | data formatting | bytes 262144
  (13 shorter events, 0.3 us)
Async XLA Ops:
  0.6 10.1 %copy-start = (bf16[128,8,128]{2,1,0:T(8,128)(2,1)S(1)}, bf16[128,8,128]{2,1,0:T(8,128)(2,1)}, u32[]{:S(2)}) copy-start(bf16[128,8,128]{2,1,0:T(8,128)(2,1)} %param.6) | copy-start | bytes 786436
  2.4 10.7 %collective-permute-start.2 = (bf16[528,128]{1,0:T(8,128)(2,1)S(1)}, bf16[528,128]{1,0:T(8,128)(2,1)S(1)}, u32[]{:S(2)}, u32[]{:S(2)}) collective-permute-start(bf16[528,128]{1,0:T(8,128)(2,1)S(1)} %concatenate.7), channel_id=1, source_target_pairs={{0,8},{2,10},{4,12},{6,14},{8,0},{10,2},{12,4},{14,6},{1,9},{3,11}... | collective-permute-start | bytes 405512 | tf_op jit(solution)/shard_map/ppermute | solution.py:153
  6.5 6.8 %collective-permute-start.1 = (bf16[528,128]{1,0:T(8,128)(2,1)S(1)}, bf16[528,128]{1,0:T(8,128)(2,1)S(1)}, u32[]{:S(2)}, u32[]{:S(2)}) collective-permute-start(bf16[528,128]{1,0:T(8,128)(2,1)S(1)} %concatenate.7), channel_id=1, source_target_pairs={{0,4},{2,6},{4,0},{6,2},{8,12},{10,14},{12,8},{14,10},{1,5},{3,7},... | collective-permute-start | bytes 405512 | tf_op jit(solution)/shard_map/ppermute | solution.py:156
  8.1 8.8 %collective-permute-start = (bf16[528,128]{1,0:T(8,128)(2,1)S(1)}, bf16[528,128]{1,0:T(8,128)(2,1)S(1)}, u32[]{:S(2)}, u32[]{:S(2)}) collective-permute-start(bf16[528,128]{1,0:T(8,128)(2,1)S(1)} %concatenate.7), channel_id=1, source_target_pairs={{0,2},{2,0},{4,6},{6,4},{8,10},{10,8},{12,14},{14,12},{1,3},{3,1},... | collective-permute-start | bytes 405512 | tf_op jit(solution)/shard_map/ppermute | solution.py:155
  13.3 10.2 %collective-permute-start.3 = (bf16[2,528,128]{2,1,0:T(8,128)(2,1)S(1)}, bf16[2,528,128]{2,1,0:T(8,128)(2,1)S(1)}, u32[]{:S(2)}, u32[]{:S(2)}) collective-permute-start(bf16[2,528,128]{2,1,0:T(8,128)(2,1)S(1)} %pad_maximum_fusion), channel_id=1, source_target_pairs={{0,2},{2,0},{4,6},{6,4},{8,10},{10,8},{12,14},{14,12},{1,3},{3,1},... | collective-permute-start | bytes 811016 | tf_op jit(solution)/shard_map/ppermute | solution.py:157
  14.9 8.6 %collective-permute-start.4 = (bf16[528,128]{1,0:T(8,128)(2,1)S(1)}, bf16[528,128]{1,0:T(8,128)(2,1)S(1)}, u32[]{:S(2)}, u32[]{:S(2)}) collective-permute-start(bf16[528,128]{1,0:T(8,128)(2,1)S(1)} %collective-permute-done.2), channel_id=1, source_target_pairs={{0,4},{2,6},{4,0},{6,2},{8,12},{10,14},{12,8},{14,10},{1,5},{3,7},... | collective-permute-start | bytes 405512 | tf_op jit(solution)/shard_map/ppermute | solution.py:158
  16.4 7.3 %collective-permute-start.5 = (bf16[528,128]{1,0:T(8,128)(2,1)S(1)}, bf16[528,128]{1,0:T(8,128)(2,1)S(1)}, u32[]{:S(2)}, u32[]{:S(2)}) collective-permute-start(bf16[528,128]{1,0:T(8,128)(2,1)S(1)} %collective-permute-done.2), channel_id=1, source_target_pairs={{0,6},{2,4},{4,2},{6,0},{8,14},{10,12},{12,10},{14,8},{1,7},{3,5},... | collective-permute-start | bytes 405512 | tf_op jit(solution)/shard_map/ppermute | solution.py:159
  28.1 6.7 %collective-permute-start.10 = (bf16[4,128,128]{2,1,0:T(8,128)(2,1)S(1)}, bf16[4,128,128]{2,1,0:T(8,128)(2,1)S(1)}, u32[]{:S(2)}, u32[]{:S(2)}) collective-permute-start(bf16[4,128,128]{2,1,0:T(8,128)(2,1)S(1)} %get-tuple-element.19), channel_id=1, source_target_pairs={{0,4},{2,6},{4,0},{6,2},{8,12},{10,14},{12,8},{14,10},{1,5},{3,7},... | collective-permute-start | bytes 393224 | tf_op jit(solution)/shard_map/ppermute | solution.py:181
  29.7 7.8 %collective-permute-start.11 = (bf16[4,128,128]{2,1,0:T(8,128)(2,1)S(1)}, bf16[4,128,128]{2,1,0:T(8,128)(2,1)S(1)}, u32[]{:S(2)}, u32[]{:S(2)}) collective-permute-start(bf16[4,128,128]{2,1,0:T(8,128)(2,1)S(1)} %get-tuple-element.18), channel_id=1, source_target_pairs={{0,6},{2,4},{4,2},{6,0},{8,14},{10,12},{12,10},{14,8},{1,7},{3,5},... | collective-permute-start | bytes 393224 | tf_op jit(solution)/shard_map/ppermute | solution.py:181
  30.8 7.7 %collective-permute-start.9 = (bf16[4,128,128]{2,1,0:T(8,128)(2,1)S(1)}, bf16[4,128,128]{2,1,0:T(8,128)(2,1)S(1)}, u32[]{:S(2)}, u32[]{:S(2)}) collective-permute-start(bf16[4,128,128]{2,1,0:T(8,128)(2,1)S(1)} %get-tuple-element.20), channel_id=1, source_target_pairs={{0,2},{2,0},{4,6},{6,4},{8,10},{10,8},{12,14},{14,12},{1,3},{3,1},... | collective-permute-start | bytes 393224 | tf_op jit(solution)/shard_map/ppermute | solution.py:181
  31.6 13.1 %collective-permute-start.6 = (bf16[4,128,128]{2,1,0:T(8,128)(2,1)S(1)}, bf16[4,128,128]{2,1,0:T(8,128)(2,1)S(1)}, u32[]{:S(2)}, u32[]{:S(2)}) collective-permute-start(bf16[4,128,128]{2,1,0:T(8,128)(2,1)S(1)} %get-tuple-element.17), channel_id=1, source_target_pairs={{0,2},{2,0},{4,6},{6,4},{8,10},{10,8},{12,14},{14,12},{1,3},{3,1},... | collective-permute-start | bytes 393224 | tf_op jit(solution)/shard_map/ppermute | solution.py:185
  32.8 11.9 %collective-permute-start.7 = (bf16[4,128,128]{2,1,0:T(8,128)(2,1)S(1)}, bf16[4,128,128]{2,1,0:T(8,128)(2,1)S(1)}, u32[]{:S(2)}, u32[]{:S(2)}) collective-permute-start(bf16[4,128,128]{2,1,0:T(8,128)(2,1)S(1)} %get-tuple-element.22), channel_id=1, source_target_pairs={{0,4},{2,6},{4,0},{6,2},{8,12},{10,14},{12,8},{14,10},{1,5},{3,7},... | collective-permute-start | bytes 393224 | tf_op jit(solution)/shard_map/ppermute | solution.py:185
  34.8 9.9 %collective-permute-start.8 = (bf16[4,128,128]{2,1,0:T(8,128)(2,1)S(1)}, bf16[4,128,128]{2,1,0:T(8,128)(2,1)S(1)}, u32[]{:S(2)}, u32[]{:S(2)}) collective-permute-start(bf16[4,128,128]{2,1,0:T(8,128)(2,1)S(1)} %get-tuple-element.21), channel_id=1, source_target_pairs={{0,6},{2,4},{4,2},{6,0},{8,14},{10,12},{12,10},{14,8},{1,7},{3,5},... | collective-permute-start | bytes 393224 | tf_op jit(solution)/shard_map/ppermute | solution.py:185
  38.6 9.4 %collective-permute-start.12 = (bf16[4,128,128]{2,1,0:T(8,128)(2,1)S(1)}, bf16[4,128,128]{2,1,0:T(8,128)(2,1)S(1)}, u32[]{:S(2)}, u32[]{:S(2)}) collective-permute-start(bf16[4,128,128]{2,1,0:T(8,128)(2,1)S(1)} %add_convert_fusion), channel_id=1, source_target_pairs={{0,8},{2,10},{4,12},{6,14},{8,0},{10,2},{12,4},{14,6},{1,9},{3,11}... | collective-permute-start | bytes 393224 | tf_op jit(solution)/shard_map/ppermute | solution.py:187

commit v15 on v14

--- a/solution.py
+++ b/solution.py
@@ -180,11 +180,12 @@
     for k in range(1, half):
         arrived = lax.ppermute(parts[half + k - 1], "ctx", mate_pairs(cycle_size, k))
         mirror_total = mirror_total + arrived.astype(jnp.float32)
+    parts, mirror_total = lax.optimization_barrier((parts, mirror_total))
+    crossed = lax.ppermute(mirror_total.astype(jnp.bfloat16), "ctx", mirror_pairs(cycle_size))
     own_total = own_part
     for k in range(1, half):
         arrived = lax.ppermute(parts[k - 1], "ctx", mate_pairs(cycle_size, k))
         own_total = own_total + arrived.astype(jnp.float32)
-    crossed = lax.ppermute(mirror_total.astype(jnp.bfloat16), "ctx", mirror_pairs(cycle_size))
     total = own_total + crossed.astype(jnp.float32)
     key_grad = total[:kv_heads].transpose(1, 0, 2)
     value_grad = total[kv_heads:].transpose(1, 0, 2)

time: 49.8 us -> 51.3 us (1.030)
  waiting for transfers between devices: 13.8 us -> 20.4 us
  starting transfers between devices: 24.7 us -> 19.7 us
    ppermute x3, waiting for transfers between devices: 1.51 us -> 7.01 us  [on_device(): lax.ppermute(parts[half + k - 1], 'ctx', mate_pairs(cycle_size, k))]
    ppermute x1, starting transfers between devices: 5.03 us -> 1.88 us  [on_device(): lax.ppermute(mirror_total.astype(jnp.bfloat16), 'ctx', mirror_pairs(cycle...]
    ppermute x3, waiting for transfers between devices: 0.01 us -> 2.15 us  [on_device(): arrived = lax.ppermute(parts[k - 1], 'ctx', mate_pairs(cycle_size, k))]
    ppermute x3, starting transfers between devices: 5.37 us -> 3.55 us  [on_device(): arrived = lax.ppermute(parts[k - 1], 'ctx', mate_pairs(cycle_size, k))]
    ppermute x1, waiting for transfers between devices: 3.24 us -> 2.14 us  [on_device(): lax.ppermute(mirror_total.astype(jnp.bfloat16), 'ctx', mirror_pairs(cycle...]
  transfers between devices with their start and end apart: 13 -> 13, of which waited for: 6 -> 9; matrix products, arithmetic and copies ran while one was open for 5% -> 5% of each run, Pallas kernels for 0% -> 0%
where the time goes in v15:
time: 51.3 us; the launch traced here: 51.1 us
  waiting for transfers between devices  20.4 us (40%)
  starting transfers between devices  19.7 us (38%)
  Pallas kernels  4.1 us (8%)
  local copies, waits for them, and re-layouts  4.03 us (8%)
  between operations  1.5 us (3%)
  other arithmetic  1.41 us (3%)
    ppermute x3, waiting for transfers between devices, on_device(): lax.ppermute(parts[half + k - 1], 'ctx', mate_pairs(cycle_size, k))  7.01 us
    ppermute x1, waiting for transfers between devices, on_device(): lax.ppermute(jnp.stack([from_mirror, from_x2]), 'ctx', mate_pairs(cycle_s...  6.57 us
    pallas_call x1, Pallas kernels, local_backward(): pl.pallas_call(functools.partial(backward_kernel, kv_heads=kv_heads, chun...  4.1 us
    ppermute x1, starting transfers between devices, on_device(): from_mirror = lax.ppermute(slab, 'ctx', mirror_pairs(cycle_size))  4.1 us
    ppermute x3, starting transfers between devices, on_device(): lax.ppermute(parts[half + k - 1], 'ctx', mate_pairs(cycle_size, k))  3.55 us
    ppermute x3, starting transfers between devices, on_device(): arrived = lax.ppermute(parts[k - 1], 'ctx', mate_pairs(cycle_size, k))  3.55 us
    unnamed x13, local copies, waits for them, and re-layouts  2.78 us
    ppermute x1, waiting for transfers between devices, on_device(): from_mirror = lax.ppermute(slab, 'ctx', mirror_pairs(cycle_size))  2.29 us
  transfers between devices with their start and end apart: 13, of which 9 were waited for; matrix products, arithmetic and copies ran while one was open for 5% of the time, Pallas kernels for 0%

profile of v15, /device:TPU:0, one launch (start us, length us, event | category | flops | bytes accessed | tf_op | source)
XLA Modules:
  0.0 51.1 jit_solution(3865327282415691134)
XLA Ops:
  0.6 0.0 copy-start
  1.3 1.0 %maximum_bitcast_fusion = bf16[4,128,128]{2,0,1:T(4,128)(2,1)S(1)} fusion(bf16[128,2,128]{2,1,0:T(2,128)(2,1)} %param.8, bf16[128,2,128]{2,1,0:T(2,128)(2,1)} %param.7), kind=kLoop, calls=%fused_computation.14 | loop fusion | flops 262144 | bytes 262144 | tf_op jit(solution)/shard_map/transpose | solution.py:150
  2.4 4.1 %collective-permute-start.2 = (bf16[528,128]{1,0:T(8,128)(2,1)S(1)}, bf16[528,128]{1,0:T(8,128)(2,1)S(1)}, u32[]{:S(2)}, u32[]{:S(2)}) collective-permute-start(bf16[528,128]{1,0:T(8,128)(2,1)S(1)} %concatenate.7), channel_id=1, source_target_pairs={{0,8},{2,10},{4,12},{6,14},{8,0},{10,2},{12,4},{14,6},{1,9},{3,11}... | collective-permute-start | bytes 405512 | tf_op jit(solution)/shard_map/ppermute | solution.py:153
  6.5 1.6 %collective-permute-start.1 = (bf16[528,128]{1,0:T(8,128)(2,1)S(1)}, bf16[528,128]{1,0:T(8,128)(2,1)S(1)}, u32[]{:S(2)}, u32[]{:S(2)}) collective-permute-start(bf16[528,128]{1,0:T(8,128)(2,1)S(1)} %concatenate.7), channel_id=1, source_target_pairs={{0,4},{2,6},{4,0},{6,2},{8,12},{10,14},{12,8},{14,10},{1,5},{3,7},... | collective-permute-start | bytes 405512 | tf_op jit(solution)/shard_map/ppermute | solution.py:156
  8.1 1.5 %collective-permute-start = (bf16[528,128]{1,0:T(8,128)(2,1)S(1)}, bf16[528,128]{1,0:T(8,128)(2,1)S(1)}, u32[]{:S(2)}, u32[]{:S(2)}) collective-permute-start(bf16[528,128]{1,0:T(8,128)(2,1)S(1)} %concatenate.7), channel_id=1, source_target_pairs={{0,2},{2,0},{4,6},{6,4},{8,10},{10,8},{12,14},{14,12},{1,3},{3,1},... | collective-permute-start | bytes 405512 | tf_op jit(solution)/shard_map/ppermute | solution.py:155
  9.6 1.1 %copy_bitcast_fusion = (bf16[8,128,128]{2,1,0:T(8,128)(2,1)S(1)}, bf16[8,128,128]{2,1,0:T(8,128)(2,1)S(1)}) fusion(bf16[128,8,128]{2,1,0:T(8,128)(2,1)} %param.9, bf16[128,8,128]{2,1,0:T(8,128)(2,1)} %param.10), kind=kLoop, calls=%fused_computation.1 | loop fusion | bytes 1048576 | tf_op jit(solution)/shard_map/transpose | solution.py:175
  10.7 0.0 copy-done
  10.8 2.3 %collective-permute-done.2 = bf16[528,128]{1,0:T(8,128)(2,1)S(1)} collective-permute-done((bf16[528,128]{1,0:T(8,128)(2,1)S(1)}, bf16[528,128]{1,0:T(8,128)(2,1)S(1)}, u32[]{:S(2)}, u32[]{:S(2)}) %collective-permute-start.2) | collective-permute-done | bytes 135200 | tf_op jit(solution)/shard_map/ppermute | solution.py:153
  13.1 0.2 collective-permute-done.1
  13.3 1.6 %collective-permute-start.3 = (bf16[2,528,128]{2,1,0:T(8,128)(2,1)S(1)}, bf16[2,528,128]{2,1,0:T(8,128)(2,1)S(1)}, u32[]{:S(2)}, u32[]{:S(2)}) collective-permute-start(bf16[2,528,128]{2,1,0:T(8,128)(2,1)S(1)} %pad_maximum_fusion), channel_id=1, source_target_pairs={{0,2},{2,0},{4,6},{6,4},{8,10},{10,8},{12,14},{14,12},{1,3},{3,1},... | collective-permute-start | bytes 811016 | tf_op jit(solution)/shard_map/ppermute | solution.py:157
  14.9 1.4 %collective-permute-start.4 = (bf16[528,128]{1,0:T(8,128)(2,1)S(1)}, bf16[528,128]{1,0:T(8,128)(2,1)S(1)}, u32[]{:S(2)}, u32[]{:S(2)}) collective-permute-start(bf16[528,128]{1,0:T(8,128)(2,1)S(1)} %collective-permute-done.2), channel_id=1, source_target_pairs={{0,4},{2,6},{4,0},{6,2},{8,12},{10,14},{12,8},{14,10},{1,5},{3,7},... | collective-permute-start | bytes 405512 | tf_op jit(solution)/shard_map/ppermute | solution.py:158
  16.4 0.5 collective-permute-start.5
  16.9 0.0 collective-permute-done
  16.9 6.6 %collective-permute-done.3 = bf16[2,528,128]{2,1,0:T(8,128)(2,1)S(1)} collective-permute-done((bf16[2,528,128]{2,1,0:T(8,128)(2,1)S(1)}, bf16[2,528,128]{2,1,0:T(8,128)(2,1)S(1)}, u32[]{:S(2)}, u32[]{:S(2)}) %collective-permute-start.3) | collective-permute-done | bytes 270368 | tf_op jit(solution)/shard_map/ppermute | solution.py:157
  23.6 0.0 collective-permute-done.4
  23.6 0.0 collective-permute-done.5
  23.6 0.2 fusion.1.offs_ref
  23.9 4.1 %shard_map.85 = (f32[8,128,128]{2,1,0:T(8,128)S(1)}, f32[4,128,128]{2,1,0:T(8,128)S(1)}, f32[4,128,128]{2,1,0:T(8,128)S(1)}, bf16[7,4,128,128]{3,2,1,0:T(8,128)(2,1)S(1)}) custom-call(s32[8]{0:T(128)S(1)} %fusion.1.offs_ref, s32[1]{0:T(128)S(6)} %copy.34.own_ref, bf16[8,128,128]{2,1,0:T(8,128)(2,1)S(1)} %bitcast.41, ...), custom_call_target="tpu_custom_call" | custom-call | flops 1610612736 | bytes 2654208 | tf_op jit(solution)/shard_map/pallas_call | solution.py:124
  28.0 1.1 %collective-permute-start.6 = (bf16[4,128,128]{2,1,0:T(8,128)(2,1)S(1)}, bf16[4,128,128]{2,1,0:T(8,128)(2,1)S(1)}, u32[]{:S(2)}, u32[]{:S(2)}) collective-permute-start(bf16[4,128,128]{2,1,0:T(8,128)(2,1)S(1)} %get-tuple-element.24), channel_id=1, source_target_pairs={{0,2},{2,0},{4,6},{6,4},{8,10},{10,8},{12,14},{14,12},{1,3},{3,1},... | collective-permute-start | bytes 393224 | tf_op jit(solution)/shard_map/ppermute | solution.py:181
  29.1 2.1 %collective-permute-start.7 = (bf16[4,128,128]{2,1,0:T(8,128)(2,1)S(1)}, bf16[4,128,128]{2,1,0:T(8,128)(2,1)S(1)}, u32[]{:S(2)}, u32[]{:S(2)}) collective-permute-start(bf16[4,128,128]{2,1,0:T(8,128)(2,1)S(1)} %get-tuple-element.26), channel_id=1, source_target_pairs={{0,4},{2,6},{4,0},{6,2},{8,12},{10,14},{12,8},{14,10},{1,5},{3,7},... | collective-permute-start | bytes 393224 | tf_op jit(solution)/shard_map/ppermute | solution.py:181
  31.2 0.4 collective-permute-start.8
  31.6 2.0 %collective-permute-done.6 = bf16[4,128,128]{2,1,0:T(8,128)(2,1)S(1)} collective-permute-done((bf16[4,128,128]{2,1,0:T(8,128)(2,1)S(1)}, bf16[4,128,128]{2,1,0:T(8,128)(2,1)S(1)}, u32[]{:S(2)}, u32[]{:S(2)}) %collective-permute-start.6) | collective-permute-done | bytes 131104 | tf_op jit(solution)/shard_map/ppermute | solution.py:181
  33.6 0.9 %collective-permute-done.7 = bf16[4,128,128]{2,1,0:T(8,128)(2,1)S(1)} collective-permute-done((bf16[4,128,128]{2,1,0:T(8,128)(2,1)S(1)}, bf16[4,128,128]{2,1,0:T(8,128)(2,1)S(1)}, u32[]{:S(2)}, u32[]{:S(2)}) %collective-permute-start.7) | collective-permute-done | bytes 131104 | tf_op jit(solution)/shard_map/ppermute | solution.py:181
  34.5 4.1 %collective-permute-done.8 = bf16[4,128,128]{2,1,0:T(8,128)(2,1)S(1)} collective-permute-done((bf16[4,128,128]{2,1,0:T(8,128)(2,1)S(1)}, bf16[4,128,128]{2,1,0:T(8,128)(2,1)S(1)}, u32[]{:S(2)}, u32[]{:S(2)}) %collective-permute-start.8) | collective-permute-done | bytes 131104 | tf_op jit(solution)/shard_map/ppermute | solution.py:181
  38.6 0.1 convert_add_fusion.1
  38.7 0.1 collective-permute-start.10
  38.8 2.2 %collective-permute-start.11 = (bf16[4,128,128]{2,1,0:T(8,128)(2,1)S(1)}, bf16[4,128,128]{2,1,0:T(8,128)(2,1)S(1)}, u32[]{:S(2)}, u32[]{:S(2)}) collective-permute-start(bf16[4,128,128]{2,1,0:T(8,128)(2,1)S(1)} %get-tuple-element.22), channel_id=1, source_target_pairs={{0,6},{2,4},{4,2},{6,0},{8,14},{10,12},{12,10},{14,8},{1,7},{3,5},... | collective-permute-start | bytes 393224 | tf_op jit(solution)/shard_map/ppermute | solution.py:187
  41.0 1.2 %collective-permute-start.9 = (bf16[4,128,128]{2,1,0:T(8,128)(2,1)S(1)}, bf16[4,128,128]{2,1,0:T(8,128)(2,1)S(1)}, u32[]{:S(2)}, u32[]{:S(2)}) collective-permute-start(bf16[4,128,128]{2,1,0:T(8,128)(2,1)S(1)} %get-tuple-element.21), channel_id=1, source_target_pairs={{0,2},{2,0},{4,6},{6,4},{8,10},{10,8},{12,14},{14,12},{1,3},{3,1},... | collective-permute-start | bytes 393224 | tf_op jit(solution)/shard_map/ppermute | solution.py:187
  42.2 1.9 %collective-permute-start.12 = (bf16[4,128,128]{2,1,0:T(8,128)(2,1)S(1)}, bf16[4,128,128]{2,1,0:T(8,128)(2,1)S(1)}, u32[]{:S(2)}, u32[]{:S(2)}) collective-permute-start(bf16[4,128,128]{2,1,0:T(8,128)(2,1)S(1)} %convert_add_fusion.1), channel_id=1, source_target_pairs={{0,8},{2,10},{4,12},{6,14},{8,0},{10,2},{12,4},{14,6},{1,9},{3,11}... | collective-permute-start | bytes 393224 | tf_op jit(solution)/shard_map/ppermute | solution.py:184
  44.1 1.1 %copy.20 = f32[128,8,128]{2,1,0:T(8,128)} copy(f32[128,8,128]{2,0,1:T(8,128)S(1)} %bitcast.40) | data formatting | bytes 1048576
  45.2 0.0 collective-permute-done.10
  45.2 1.6 %collective-permute-done.11 = bf16[4,128,128]{2,1,0:T(8,128)(2,1)S(1)} collective-permute-done((bf16[4,128,128]{2,1,0:T(8,128)(2,1)S(1)}, bf16[4,128,128]{2,1,0:T(8,128)(2,1)S(1)}, u32[]{:S(2)}, u32[]{:S(2)}) %collective-permute-start.11) | collective-permute-done | bytes 131104 | tf_op jit(solution)/shard_map/ppermute | solution.py:187
  46.8 0.6 %collective-permute-done.9 = bf16[4,128,128]{2,1,0:T(8,128)(2,1)S(1)} collective-permute-done((bf16[4,128,128]{2,1,0:T(8,128)(2,1)S(1)}, bf16[4,128,128]{2,1,0:T(8,128)(2,1)S(1)}, u32[]{:S(2)}, u32[]{:S(2)}) %collective-permute-start.9) | collective-permute-done | bytes 131104 | tf_op jit(solution)/shard_map/ppermute | solution.py:187
  47.4 2.1 %collective-permute-done.12 = bf16[4,128,128]{2,1,0:T(8,128)(2,1)S(1)} collective-permute-done((bf16[4,128,128]{2,1,0:T(8,128)(2,1)S(1)}, bf16[4,128,128]{2,1,0:T(8,128)(2,1)S(1)}, u32[]{:S(2)}, u32[]{:S(2)}) %collective-permute-start.12) | collective-permute-done | bytes 131104 | tf_op jit(solution)/shard_map/ppermute | solution.py:184
  49.5 0.1 convert_add_fusion
  49.6 0.8 %copy.21 = f32[128,2,128]{2,1,0:T(2,128)} copy(f32[128,2,128]{2,0,1:T(8,128)S(1)} %get-tuple-element.28) | data formatting | bytes 262144
  50.4 0.8 %copy.22 = f32[128,2,128]{2,1,0:T(2,128)} copy(f32[128,2,128]{2,0,1:T(8,128)S(1)} %get-tuple-element.27) | data formatting | bytes 262144
  (15 shorter events, 0.3 us)
Async XLA Ops:
  0.6 10.1 %copy-start = (bf16[128,8,128]{2,1,0:T(8,128)(2,1)S(1)}, bf16[128,8,128]{2,1,0:T(8,128)(2,1)}, u32[]{:S(2)}) copy-start(bf16[128,8,128]{2,1,0:T(8,128)(2,1)} %param.6) | copy-start | bytes 786436
  2.4 10.7 %collective-permute-start.2 = (bf16[528,128]{1,0:T(8,128)(2,1)S(1)}, bf16[528,128]{1,0:T(8,128)(2,1)S(1)}, u32[]{:S(2)}, u32[]{:S(2)}) collective-permute-start(bf16[528,128]{1,0:T(8,128)(2,1)S(1)} %concatenate.7), channel_id=1, source_target_pairs={{0,8},{2,10},{4,12},{6,14},{8,0},{10,2},{12,4},{14,6},{1,9},{3,11}... | collective-permute-start | bytes 405512 | tf_op jit(solution)/shard_map/ppermute | solution.py:153
  6.5 6.8 %collective-permute-start.1 = (bf16[528,128]{1,0:T(8,128)(2,1)S(1)}, bf16[528,128]{1,0:T(8,128)(2,1)S(1)}, u32[]{:S(2)}, u32[]{:S(2)}) collective-permute-start(bf16[528,128]{1,0:T(8,128)(2,1)S(1)} %concatenate.7), channel_id=1, source_target_pairs={{0,4},{2,6},{4,0},{6,2},{8,12},{10,14},{12,8},{14,10},{1,5},{3,7},... | collective-permute-start | bytes 405512 | tf_op jit(solution)/shard_map/ppermute | solution.py:156
  8.1 8.8 %collective-permute-start = (bf16[528,128]{1,0:T(8,128)(2,1)S(1)}, bf16[528,128]{1,0:T(8,128)(2,1)S(1)}, u32[]{:S(2)}, u32[]{:S(2)}) collective-permute-start(bf16[528,128]{1,0:T(8,128)(2,1)S(1)} %concatenate.7), channel_id=1, source_target_pairs={{0,2},{2,0},{4,6},{6,4},{8,10},{10,8},{12,14},{14,12},{1,3},{3,1},... | collective-permute-start | bytes 405512 | tf_op jit(solution)/shard_map/ppermute | solution.py:155
  13.3 10.2 %collective-permute-start.3 = (bf16[2,528,128]{2,1,0:T(8,128)(2,1)S(1)}, bf16[2,528,128]{2,1,0:T(8,128)(2,1)S(1)}, u32[]{:S(2)}, u32[]{:S(2)}) collective-permute-start(bf16[2,528,128]{2,1,0:T(8,128)(2,1)S(1)} %pad_maximum_fusion), channel_id=1, source_target_pairs={{0,2},{2,0},{4,6},{6,4},{8,10},{10,8},{12,14},{14,12},{1,3},{3,1},... | collective-permute-start | bytes 811016 | tf_op jit(solution)/shard_map/ppermute | solution.py:157
  14.9 8.6 %collective-permute-start.4 = (bf16[528,128]{1,0:T(8,128)(2,1)S(1)}, bf16[528,128]{1,0:T(8,128)(2,1)S(1)}, u32[]{:S(2)}, u32[]{:S(2)}) collective-permute-start(bf16[528,128]{1,0:T(8,128)(2,1)S(1)} %collective-permute-done.2), channel_id=1, source_target_pairs={{0,4},{2,6},{4,0},{6,2},{8,12},{10,14},{12,8},{14,10},{1,5},{3,7},... | collective-permute-start | bytes 405512 | tf_op jit(solution)/shard_map/ppermute | solution.py:158
  16.4 7.3 %collective-permute-start.5 = (bf16[528,128]{1,0:T(8,128)(2,1)S(1)}, bf16[528,128]{1,0:T(8,128)(2,1)S(1)}, u32[]{:S(2)}, u32[]{:S(2)}) collective-permute-start(bf16[528,128]{1,0:T(8,128)(2,1)S(1)} %collective-permute-done.2), channel_id=1, source_target_pairs={{0,6},{2,4},{4,2},{6,0},{8,14},{10,12},{12,10},{14,8},{1,7},{3,5},... | collective-permute-start | bytes 405512 | tf_op jit(solution)/shard_map/ppermute | solution.py:159
  28.0 5.6 %collective-permute-start.6 = (bf16[4,128,128]{2,1,0:T(8,128)(2,1)S(1)}, bf16[4,128,128]{2,1,0:T(8,128)(2,1)S(1)}, u32[]{:S(2)}, u32[]{:S(2)}) collective-permute-start(bf16[4,128,128]{2,1,0:T(8,128)(2,1)S(1)} %get-tuple-element.24), channel_id=1, source_target_pairs={{0,2},{2,0},{4,6},{6,4},{8,10},{10,8},{12,14},{14,12},{1,3},{3,1},... | collective-permute-start | bytes 393224 | tf_op jit(solution)/shard_map/ppermute | solution.py:181
  29.1 5.3 %collective-permute-start.7 = (bf16[4,128,128]{2,1,0:T(8,128)(2,1)S(1)}, bf16[4,128,128]{2,1,0:T(8,128)(2,1)S(1)}, u32[]{:S(2)}, u32[]{:S(2)}) collective-permute-start(bf16[4,128,128]{2,1,0:T(8,128)(2,1)S(1)} %get-tuple-element.26), channel_id=1, source_target_pairs={{0,4},{2,6},{4,0},{6,2},{8,12},{10,14},{12,8},{14,10},{1,5},{3,7},... | collective-permute-start | bytes 393224 | tf_op jit(solution)/shard_map/ppermute | solution.py:181
  31.2 7.4 %collective-permute-start.8 = (bf16[4,128,128]{2,1,0:T(8,128)(2,1)S(1)}, bf16[4,128,128]{2,1,0:T(8,128)(2,1)S(1)}, u32[]{:S(2)}, u32[]{:S(2)}) collective-permute-start(bf16[4,128,128]{2,1,0:T(8,128)(2,1)S(1)} %get-tuple-element.25), channel_id=1, source_target_pairs={{0,6},{2,4},{4,2},{6,0},{8,14},{10,12},{12,10},{14,8},{1,7},{3,5},... | collective-permute-start | bytes 393224 | tf_op jit(solution)/shard_map/ppermute | solution.py:181
  38.7 6.5 %collective-permute-start.10 = (bf16[4,128,128]{2,1,0:T(8,128)(2,1)S(1)}, bf16[4,128,128]{2,1,0:T(8,128)(2,1)S(1)}, u32[]{:S(2)}, u32[]{:S(2)}) collective-permute-start(bf16[4,128,128]{2,1,0:T(8,128)(2,1)S(1)} %get-tuple-element.23), channel_id=1, source_target_pairs={{0,4},{2,6},{4,0},{6,2},{8,12},{10,14},{12,8},{14,10},{1,5},{3,7},... | collective-permute-start | bytes 393224 | tf_op jit(solution)/shard_map/ppermute | solution.py:187
  38.8 8.0 %collective-permute-start.11 = (bf16[4,128,128]{2,1,0:T(8,128)(2,1)S(1)}, bf16[4,128,128]{2,1,0:T(8,128)(2,1)S(1)}, u32[]{:S(2)}, u32[]{:S(2)}) collective-permute-start(bf16[4,128,128]{2,1,0:T(8,128)(2,1)S(1)} %get-tuple-element.22), channel_id=1, source_target_pairs={{0,6},{2,4},{4,2},{6,0},{8,14},{10,12},{12,10},{14,8},{1,7},{3,5},... | collective-permute-start | bytes 393224 | tf_op jit(solution)/shard_map/ppermute | solution.py:187
  41.0 6.4 %collective-permute-start.9 = (bf16[4,128,128]{2,1,0:T(8,128)(2,1)S(1)}, bf16[4,128,128]{2,1,0:T(8,128)(2,1)S(1)}, u32[]{:S(2)}, u32[]{:S(2)}) collective-permute-start(bf16[4,128,128]{2,1,0:T(8,128)(2,1)S(1)} %get-tuple-element.21), channel_id=1, source_target_pairs={{0,2},{2,0},{4,6},{6,4},{8,10},{10,8},{12,14},{14,12},{1,3},{3,1},... | collective-permute-start | bytes 393224 | tf_op jit(solution)/shard_map/ppermute | solution.py:187
  42.2 7.3 %collective-permute-start.12 = (bf16[4,128,128]{2,1,0:T(8,128)(2,1)S(1)}, bf16[4,128,128]{2,1,0:T(8,128)(2,1)S(1)}, u32[]{:S(2)}, u32[]{:S(2)}) collective-permute-start(bf16[4,128,128]{2,1,0:T(8,128)(2,1)S(1)} %convert_add_fusion.1), channel_id=1, source_target_pairs={{0,8},{2,10},{4,12},{6,14},{8,0},{10,2},{12,4},{14,6},{1,9},{3,11}... | collective-permute-start | bytes 393224 | tf_op jit(solution)/shard_map/ppermute | solution.py:184

commit v16 on v14

--- a/solution.py
+++ b/solution.py
@@ -154,10 +154,11 @@
     if half == 4:
         from_x1 = lax.ppermute(slab, "ctx", mate_pairs(cycle_size, 1))
         from_x2 = lax.ppermute(slab, "ctx", mate_pairs(cycle_size, 2))
-        pair = lax.ppermute(jnp.stack([from_mirror, from_x2]), "ctx", mate_pairs(cycle_size, 1))
+        from_x3 = lax.ppermute(from_x2, "ctx", mate_pairs(cycle_size, 1))
+        mirror_of_x1 = lax.ppermute(from_mirror, "ctx", mate_pairs(cycle_size, 1))
         mirror_of_x2 = lax.ppermute(from_mirror, "ctx", mate_pairs(cycle_size, 2))
         mirror_of_x3 = lax.ppermute(from_mirror, "ctx", mate_pairs(cycle_size, 3))
-        blocks = [slab, from_x1, from_x2, pair[1], from_mirror, pair[0], mirror_of_x2, mirror_of_x3]
+        blocks = [slab, from_x1, from_x2, from_x3, from_mirror, mirror_of_x1, mirror_of_x2, mirror_of_x3]
     else:
         from_mates = [lax.ppermute(slab, "ctx", mate_pairs(cycle_size, k)) for k in range(1, half)]
         handed_on = [

time: 49.8 us -> 49.7 us (level)
  starting transfers between devices: 24.7 us -> 20.2 us
  waiting for transfers between devices: 13.8 us -> 18.3 us
    ppermute x1, starting transfers between devices: 5.03 us -> 1.67 us  [on_device(): lax.ppermute(mirror_total.astype(jnp.bfloat16), 'ctx', mirror_pairs(cycle...]
    ppermute x1, waiting for transfers between devices: 2.29 us -> 4.92 us  [on_device(): from_mirror = lax.ppermute(slab, 'ctx', mirror_pairs(cycle_size))]
    ppermute x1, starting transfers between devices: 0.51 us -> 2.74 us  [on_device(): mirror_of_x3 = lax.ppermute(from_mirror, 'ctx', mate_pairs(cycle_size, 3))]
    ppermute x3, waiting for transfers between devices: 1.51 us -> 3.42 us  [on_device(): lax.ppermute(parts[half + k - 1], 'ctx', mate_pairs(cycle_size, k))]
    ppermute x3, waiting for transfers between devices: 0.01 us -> 1.53 us  [on_device(): arrived = lax.ppermute(parts[k - 1], 'ctx', mate_pairs(cycle_size, k))]
    ppermute x3, starting transfers between devices: 5.37 us -> 3.85 us  [on_device(): arrived = lax.ppermute(parts[k - 1], 'ctx', mate_pairs(cycle_size, k))]
    ppermute x1, starting transfers between devices: 4.1 us -> 2.59 us  [on_device(): from_mirror = lax.ppermute(slab, 'ctx', mirror_pairs(cycle_size))]
    ppermute x1, starting transfers between devices: 1.52 us -> 3.03 us  [on_device(): from_x1 = lax.ppermute(slab, 'ctx', mate_pairs(cycle_size, 1))]
  transfers between devices with their start and end apart: 13 -> 14, of which waited for: 6 -> 7; matrix products, arithmetic and copies ran while one was open for 5% -> 5% of each run, Pallas kernels for 0% -> 0%
where the time goes in v16:
time: 49.7 us; the launch traced here: 49.5 us
  starting transfers between devices  20.2 us (41%)
  waiting for transfers between devices  18.3 us (37%)
  Pallas kernels  4.1 us (8%)
  local copies, waits for them, and re-layouts  4.05 us (8%)
  between operations  1.49 us (3%)
  other arithmetic  1.39 us (3%)
    ppermute x1, waiting for transfers between devices, on_device(): from_x3 = lax.ppermute(from_x2, 'ctx', mate_pairs(cycle_size, 1))  5.42 us
    ppermute x1, waiting for transfers between devices, on_device(): from_mirror = lax.ppermute(slab, 'ctx', mirror_pairs(cycle_size))  4.92 us
    pallas_call x1, Pallas kernels, local_backward(): pl.pallas_call(functools.partial(backward_kernel, kv_heads=kv_heads, chun...  4.1 us
    ppermute x3, starting transfers between devices, on_device(): arrived = lax.ppermute(parts[k - 1], 'ctx', mate_pairs(cycle_size, k))  3.85 us
    ppermute x3, starting transfers between devices, on_device(): lax.ppermute(parts[half + k - 1], 'ctx', mate_pairs(cycle_size, k))  3.55 us
    ppermute x3, waiting for transfers between devices, on_device(): lax.ppermute(parts[half + k - 1], 'ctx', mate_pairs(cycle_size, k))  3.42 us
    ppermute x1, starting transfers between devices, on_device(): from_x1 = lax.ppermute(slab, 'ctx', mate_pairs(cycle_size, 1))  3.03 us
    ppermute x1, waiting for transfers between devices, on_device(): lax.ppermute(mirror_total.astype(jnp.bfloat16), 'ctx', mirror_pairs(cycle...  3.03 us
  transfers between devices with their start and end apart: 14, of which 7 were waited for; matrix products, arithmetic and copies ran while one was open for 5% of the time, Pallas kernels for 0%

profile of v16, /device:TPU:0, one launch (start us, length us, event | category | flops | bytes accessed | tf_op | source)
XLA Modules:
  0.0 49.5 jit_solution(2441516472786804542)
XLA Ops:
  0.6 0.0 copy-start
  1.3 1.0 %maximum_bitcast_fusion = bf16[4,128,128]{2,0,1:T(4,128)(2,1)S(1)} fusion(bf16[128,2,128]{2,1,0:T(2,128)(2,1)} %param.8, bf16[128,2,128]{2,1,0:T(2,128)(2,1)} %param.7), kind=kLoop, calls=%fused_computation.15 | loop fusion | flops 262144 | bytes 262144 | tf_op jit(solution)/shard_map/transpose | solution.py:150
  2.4 3.0 %collective-permute-start = (bf16[528,128]{1,0:T(8,128)(2,1)S(1)}, bf16[528,128]{1,0:T(8,128)(2,1)S(1)}, u32[]{:S(2)}, u32[]{:S(2)}) collective-permute-start(bf16[528,128]{1,0:T(8,128)(2,1)S(1)} %concatenate.7), channel_id=1, source_target_pairs={{0,2},{2,0},{4,6},{6,4},{8,10},{10,8},{12,14},{14,12},{1,3},{3,1},... | collective-permute-start | bytes 405512 | tf_op jit(solution)/shard_map/ppermute | solution.py:155
  5.4 1.6 %collective-permute-start.1 = (bf16[528,128]{1,0:T(8,128)(2,1)S(1)}, bf16[528,128]{1,0:T(8,128)(2,1)S(1)}, u32[]{:S(2)}, u32[]{:S(2)}) collective-permute-start(bf16[528,128]{1,0:T(8,128)(2,1)S(1)} %concatenate.7), channel_id=1, source_target_pairs={{0,4},{2,6},{4,0},{6,2},{8,12},{10,14},{12,8},{14,10},{1,5},{3,7},... | collective-permute-start | bytes 405512 | tf_op jit(solution)/shard_map/ppermute | solution.py:156
  7.0 2.6 %collective-permute-start.3 = (bf16[528,128]{1,0:T(8,128)(2,1)S(1)}, bf16[528,128]{1,0:T(8,128)(2,1)S(1)}, u32[]{:S(2)}, u32[]{:S(2)}) collective-permute-start(bf16[528,128]{1,0:T(8,128)(2,1)S(1)} %concatenate.7), channel_id=1, source_target_pairs={{0,8},{2,10},{4,12},{6,14},{8,0},{10,2},{12,4},{14,6},{1,9},{3,11}... | collective-permute-start | bytes 405512 | tf_op jit(solution)/shard_map/ppermute | solution.py:153
  9.6 1.1 %copy_bitcast_fusion = (bf16[8,128,128]{2,1,0:T(8,128)(2,1)S(1)}, bf16[8,128,128]{2,1,0:T(8,128)(2,1)S(1)}) fusion(bf16[128,8,128]{2,1,0:T(8,128)(2,1)} %param.9, bf16[128,8,128]{2,1,0:T(8,128)(2,1)} %param.10), kind=kLoop, calls=%fused_computation | loop fusion | bytes 1048576 | tf_op jit(solution)/shard_map/transpose | solution.py:176
  10.7 0.0 copy-done
  10.8 4.9 %collective-permute-done.3 = bf16[528,128]{1,0:T(8,128)(2,1)S(1)} collective-permute-done((bf16[528,128]{1,0:T(8,128)(2,1)S(1)}, bf16[528,128]{1,0:T(8,128)(2,1)S(1)}, u32[]{:S(2)}, u32[]{:S(2)}) %collective-permute-start.3) | collective-permute-done | bytes 135200 | tf_op jit(solution)/shard_map/ppermute | solution.py:153
  15.7 0.4 collective-permute-start.4
  16.1 0.3 collective-permute-start.5
  16.5 2.7 %collective-permute-start.6 = (bf16[528,128]{1,0:T(8,128)(2,1)S(1)}, bf16[528,128]{1,0:T(8,128)(2,1)S(1)}, u32[]{:S(2)}, u32[]{:S(2)}) collective-permute-start(bf16[528,128]{1,0:T(8,128)(2,1)S(1)} %collective-permute-done.3), channel_id=1, source_target_pairs={{0,6},{2,4},{4,2},{6,0},{8,14},{10,12},{12,10},{14,8},{1,7},{3,5},... | collective-permute-start | bytes 405512 | tf_op jit(solution)/shard_map/ppermute | solution.py:160
  19.2 0.0 collective-permute-done.1
  19.2 0.4 collective-permute-start.2
  19.6 0.0 collective-permute-done
  19.7 5.4 %collective-permute-done.2 = bf16[528,128]{1,0:T(8,128)(2,1)S(1)} collective-permute-done((bf16[528,128]{1,0:T(8,128)(2,1)S(1)}, bf16[528,128]{1,0:T(8,128)(2,1)S(1)}, u32[]{:S(2)}, u32[]{:S(2)}) %collective-permute-start.2) | collective-permute-done | bytes 135200 | tf_op jit(solution)/shard_map/ppermute | solution.py:157
  25.1 0.0 collective-permute-done.4
  25.2 0.0 collective-permute-done.5
  25.2 0.0 collective-permute-done.6
  25.3 0.2 fusion.1.offs_ref
  25.5 4.1 %shard_map.85 = (f32[8,128,128]{2,1,0:T(8,128)S(1)}, f32[4,128,128]{2,1,0:T(8,128)S(1)}, f32[4,128,128]{2,1,0:T(8,128)S(1)}, bf16[7,4,128,128]{3,2,1,0:T(8,128)(2,1)S(1)}) custom-call(s32[8]{0:T(128)S(1)} %fusion.1.offs_ref, s32[1]{0:T(128)S(6)} %copy.34.own_ref, bf16[8,128,128]{2,1,0:T(8,128)(2,1)S(1)} %bitcast.45, ...), custom_call_target="tpu_custom_call" | custom-call | flops 1610612736 | bytes 2654208 | tf_op jit(solution)/shard_map/pallas_call | solution.py:124
  29.6 0.1 slice_bitcast_fusion.7
  29.7 0.6 %collective-permute-start.10 = (bf16[4,128,128]{2,1,0:T(8,128)(2,1)S(1)}, bf16[4,128,128]{2,1,0:T(8,128)(2,1)S(1)}, u32[]{:S(2)}, u32[]{:S(2)}) collective-permute-start(bf16[4,128,128]{2,1,0:T(8,128)(2,1)S(1)} %get-tuple-element.20), channel_id=1, source_target_pairs={{0,2},{2,0},{4,6},{6,4},{8,10},{10,8},{12,14},{14,12},{1,3},{3,1},... | collective-permute-start | bytes 393224 | tf_op jit(solution)/shard_map/ppermute | solution.py:182
  30.3 1.7 %collective-permute-start.11 = (bf16[4,128,128]{2,1,0:T(8,128)(2,1)S(1)}, bf16[4,128,128]{2,1,0:T(8,128)(2,1)S(1)}, u32[]{:S(2)}, u32[]{:S(2)}) collective-permute-start(bf16[4,128,128]{2,1,0:T(8,128)(2,1)S(1)} %get-tuple-element.19), channel_id=1, source_target_pairs={{0,4},{2,6},{4,0},{6,2},{8,12},{10,14},{12,8},{14,10},{1,5},{3,7},... | collective-permute-start | bytes 393224 | tf_op jit(solution)/shard_map/ppermute | solution.py:182
  31.9 1.3 %collective-permute-start.12 = (bf16[4,128,128]{2,1,0:T(8,128)(2,1)S(1)}, bf16[4,128,128]{2,1,0:T(8,128)(2,1)S(1)}, u32[]{:S(2)}, u32[]{:S(2)}) collective-permute-start(bf16[4,128,128]{2,1,0:T(8,128)(2,1)S(1)} %get-tuple-element.18), channel_id=1, source_target_pairs={{0,6},{2,4},{4,2},{6,0},{8,14},{10,12},{12,10},{14,8},{1,7},{3,5},... | collective-permute-start | bytes 393224 | tf_op jit(solution)/shard_map/ppermute | solution.py:182
  33.2 0.5 %collective-permute-start.7 = (bf16[4,128,128]{2,1,0:T(8,128)(2,1)S(1)}, bf16[4,128,128]{2,1,0:T(8,128)(2,1)S(1)}, u32[]{:S(2)}, u32[]{:S(2)}) collective-permute-start(bf16[4,128,128]{2,1,0:T(8,128)(2,1)S(1)} %get-tuple-element.17), channel_id=1, source_target_pairs={{0,2},{2,0},{4,6},{6,4},{8,10},{10,8},{12,14},{14,12},{1,3},{3,1},... | collective-permute-start | bytes 393224 | tf_op jit(solution)/shard_map/ppermute | solution.py:186
  33.8 1.7 %collective-permute-start.8 = (bf16[4,128,128]{2,1,0:T(8,128)(2,1)S(1)}, bf16[4,128,128]{2,1,0:T(8,128)(2,1)S(1)}, u32[]{:S(2)}, u32[]{:S(2)}) collective-permute-start(bf16[4,128,128]{2,1,0:T(8,128)(2,1)S(1)} %get-tuple-element.22), channel_id=1, source_target_pairs={{0,4},{2,6},{4,0},{6,2},{8,12},{10,14},{12,8},{14,10},{1,5},{3,7},... | collective-permute-start | bytes 393224 | tf_op jit(solution)/shard_map/ppermute | solution.py:186
  35.4 1.8 %collective-permute-done.10 = bf16[4,128,128]{2,1,0:T(8,128)(2,1)S(1)} collective-permute-done((bf16[4,128,128]{2,1,0:T(8,128)(2,1)S(1)}, bf16[4,128,128]{2,1,0:T(8,128)(2,1)S(1)}, u32[]{:S(2)}, u32[]{:S(2)}) %collective-permute-start.10) | collective-permute-done | bytes 131104 | tf_op jit(solution)/shard_map/ppermute | solution.py:182
  37.2 1.7 %collective-permute-start.9 = (bf16[4,128,128]{2,1,0:T(8,128)(2,1)S(1)}, bf16[4,128,128]{2,1,0:T(8,128)(2,1)S(1)}, u32[]{:S(2)}, u32[]{:S(2)}) collective-permute-start(bf16[4,128,128]{2,1,0:T(8,128)(2,1)S(1)} %get-tuple-element.21), channel_id=1, source_target_pairs={{0,6},{2,4},{4,2},{6,0},{8,14},{10,12},{12,10},{14,8},{1,7},{3,5},... | collective-permute-start | bytes 393224 | tf_op jit(solution)/shard_map/ppermute | solution.py:186
  38.9 0.0 collective-permute-done.11
  38.9 1.6 %collective-permute-done.12 = bf16[4,128,128]{2,1,0:T(8,128)(2,1)S(1)} collective-permute-done((bf16[4,128,128]{2,1,0:T(8,128)(2,1)S(1)}, bf16[4,128,128]{2,1,0:T(8,128)(2,1)S(1)}, u32[]{:S(2)}, u32[]{:S(2)}) %collective-permute-start.12) | collective-permute-done | bytes 131104 | tf_op jit(solution)/shard_map/ppermute | solution.py:182
  40.5 0.1 add_convert_fusion
  40.6 1.7 %collective-permute-start.13 = (bf16[4,128,128]{2,1,0:T(8,128)(2,1)S(1)}, bf16[4,128,128]{2,1,0:T(8,128)(2,1)S(1)}, u32[]{:S(2)}, u32[]{:S(2)}) collective-permute-start(bf16[4,128,128]{2,1,0:T(8,128)(2,1)S(1)} %add_convert_fusion), channel_id=1, source_target_pairs={{0,8},{2,10},{4,12},{6,14},{8,0},{10,2},{12,4},{14,6},{1,9},{3,11}... | collective-permute-start | bytes 393224 | tf_op jit(solution)/shard_map/ppermute | solution.py:188
  42.2 1.1 %copy.20 = f32[128,8,128]{2,1,0:T(8,128)} copy(f32[128,8,128]{2,0,1:T(8,128)S(1)} %bitcast.44) | data formatting | bytes 1048576
  43.3 0.0 collective-permute-done.7
  43.4 0.1 collective-permute-done.8
  43.4 1.4 %collective-permute-done.9 = bf16[4,128,128]{2,1,0:T(8,128)(2,1)S(1)} collective-permute-done((bf16[4,128,128]{2,1,0:T(8,128)(2,1)S(1)}, bf16[4,128,128]{2,1,0:T(8,128)(2,1)S(1)}, u32[]{:S(2)}, u32[]{:S(2)}) %collective-permute-start.9) | collective-permute-done | bytes 131104 | tf_op jit(solution)/shard_map/ppermute | solution.py:186
  44.9 3.0 %collective-permute-done.13 = bf16[4,128,128]{2,1,0:T(8,128)(2,1)S(1)} collective-permute-done((bf16[4,128,128]{2,1,0:T(8,128)(2,1)S(1)}, bf16[4,128,128]{2,1,0:T(8,128)(2,1)S(1)}, u32[]{:S(2)}, u32[]{:S(2)}) %collective-permute-start.13) | collective-permute-done | bytes 131104 | tf_op jit(solution)/shard_map/ppermute | solution.py:188
  47.9 0.1 convert_add_fusion
  48.0 0.8 %copy.21 = f32[128,2,128]{2,1,0:T(2,128)} copy(f32[128,2,128]{2,0,1:T(8,128)S(1)} %get-tuple-element.24) | data formatting | bytes 262144
  48.8 0.8 %copy.22 = f32[128,2,128]{2,1,0:T(2,128)} copy(f32[128,2,128]{2,0,1:T(8,128)S(1)} %get-tuple-element.23) | data formatting | bytes 262144
  (12 shorter events, 0.2 us)
Async XLA Ops:
  0.6 10.1 %copy-start = (bf16[128,8,128]{2,1,0:T(8,128)(2,1)S(1)}, bf16[128,8,128]{2,1,0:T(8,128)(2,1)}, u32[]{:S(2)}) copy-start(bf16[128,8,128]{2,1,0:T(8,128)(2,1)} %param.6) | copy-start | bytes 786436
  2.4 17.2 %collective-permute-start = (bf16[528,128]{1,0:T(8,128)(2,1)S(1)}, bf16[528,128]{1,0:T(8,128)(2,1)S(1)}, u32[]{:S(2)}, u32[]{:S(2)}) collective-permute-start(bf16[528,128]{1,0:T(8,128)(2,1)S(1)} %concatenate.7), channel_id=1, source_target_pairs={{0,2},{2,0},{4,6},{6,4},{8,10},{10,8},{12,14},{14,12},{1,3},{3,1},... | collective-permute-start | bytes 405512 | tf_op jit(solution)/shard_map/ppermute | solution.py:155
  5.4 13.8 %collective-permute-start.1 = (bf16[528,128]{1,0:T(8,128)(2,1)S(1)}, bf16[528,128]{1,0:T(8,128)(2,1)S(1)}, u32[]{:S(2)}, u32[]{:S(2)}) collective-permute-start(bf16[528,128]{1,0:T(8,128)(2,1)S(1)} %concatenate.7), channel_id=1, source_target_pairs={{0,4},{2,6},{4,0},{6,2},{8,12},{10,14},{12,8},{14,10},{1,5},{3,7},... | collective-permute-start | bytes 405512 | tf_op jit(solution)/shard_map/ppermute | solution.py:156
  7.0 8.7 %collective-permute-start.3 = (bf16[528,128]{1,0:T(8,128)(2,1)S(1)}, bf16[528,128]{1,0:T(8,128)(2,1)S(1)}, u32[]{:S(2)}, u32[]{:S(2)}) collective-permute-start(bf16[528,128]{1,0:T(8,128)(2,1)S(1)} %concatenate.7), channel_id=1, source_target_pairs={{0,8},{2,10},{4,12},{6,14},{8,0},{10,2},{12,4},{14,6},{1,9},{3,11}... | collective-permute-start | bytes 405512 | tf_op jit(solution)/shard_map/ppermute | solution.py:153
  15.7 9.4 %collective-permute-start.4 = (bf16[528,128]{1,0:T(8,128)(2,1)S(1)}, bf16[528,128]{1,0:T(8,128)(2,1)S(1)}, u32[]{:S(2)}, u32[]{:S(2)}) collective-permute-start(bf16[528,128]{1,0:T(8,128)(2,1)S(1)} %collective-permute-done.3), channel_id=1, source_target_pairs={{0,2},{2,0},{4,6},{6,4},{8,10},{10,8},{12,14},{14,12},{1,3},{3,1},... | collective-permute-start | bytes 405512 | tf_op jit(solution)/shard_map/ppermute | solution.py:158
  16.1 9.1 %collective-permute-start.5 = (bf16[528,128]{1,0:T(8,128)(2,1)S(1)}, bf16[528,128]{1,0:T(8,128)(2,1)S(1)}, u32[]{:S(2)}, u32[]{:S(2)}) collective-permute-start(bf16[528,128]{1,0:T(8,128)(2,1)S(1)} %collective-permute-done.3), channel_id=1, source_target_pairs={{0,4},{2,6},{4,0},{6,2},{8,12},{10,14},{12,8},{14,10},{1,5},{3,7},... | collective-permute-start | bytes 405512 | tf_op jit(solution)/shard_map/ppermute | solution.py:159
  16.5 8.8 %collective-permute-start.6 = (bf16[528,128]{1,0:T(8,128)(2,1)S(1)}, bf16[528,128]{1,0:T(8,128)(2,1)S(1)}, u32[]{:S(2)}, u32[]{:S(2)}) collective-permute-start(bf16[528,128]{1,0:T(8,128)(2,1)S(1)} %collective-permute-done.3), channel_id=1, source_target_pairs={{0,6},{2,4},{4,2},{6,0},{8,14},{10,12},{12,10},{14,8},{1,7},{3,5},... | collective-permute-start | bytes 405512 | tf_op jit(solution)/shard_map/ppermute | solution.py:160
  19.2 5.9 %collective-permute-start.2 = (bf16[528,128]{1,0:T(8,128)(2,1)S(1)}, bf16[528,128]{1,0:T(8,128)(2,1)S(1)}, u32[]{:S(2)}, u32[]{:S(2)}) collective-permute-start(bf16[528,128]{1,0:T(8,128)(2,1)S(1)} %collective-permute-done.1), channel_id=1, source_target_pairs={{0,2},{2,0},{4,6},{6,4},{8,10},{10,8},{12,14},{14,12},{1,3},{3,1},... | collective-permute-start | bytes 405512 | tf_op jit(solution)/shard_map/ppermute | solution.py:157
  29.7 7.5 %collective-permute-start.10 = (bf16[4,128,128]{2,1,0:T(8,128)(2,1)S(1)}, bf16[4,128,128]{2,1,0:T(8,128)(2,1)S(1)}, u32[]{:S(2)}, u32[]{:S(2)}) collective-permute-start(bf16[4,128,128]{2,1,0:T(8,128)(2,1)S(1)} %get-tuple-element.20), channel_id=1, source_target_pairs={{0,2},{2,0},{4,6},{6,4},{8,10},{10,8},{12,14},{14,12},{1,3},{3,1},... | collective-permute-start | bytes 393224 | tf_op jit(solution)/shard_map/ppermute | solution.py:182
  30.3 8.6 %collective-permute-start.11 = (bf16[4,128,128]{2,1,0:T(8,128)(2,1)S(1)}, bf16[4,128,128]{2,1,0:T(8,128)(2,1)S(1)}, u32[]{:S(2)}, u32[]{:S(2)}) collective-permute-start(bf16[4,128,128]{2,1,0:T(8,128)(2,1)S(1)} %get-tuple-element.19), channel_id=1, source_target_pairs={{0,4},{2,6},{4,0},{6,2},{8,12},{10,14},{12,8},{14,10},{1,5},{3,7},... | collective-permute-start | bytes 393224 | tf_op jit(solution)/shard_map/ppermute | solution.py:182
  31.9 8.6 %collective-permute-start.12 = (bf16[4,128,128]{2,1,0:T(8,128)(2,1)S(1)}, bf16[4,128,128]{2,1,0:T(8,128)(2,1)S(1)}, u32[]{:S(2)}, u32[]{:S(2)}) collective-permute-start(bf16[4,128,128]{2,1,0:T(8,128)(2,1)S(1)} %get-tuple-element.18), channel_id=1, source_target_pairs={{0,6},{2,4},{4,2},{6,0},{8,14},{10,12},{12,10},{14,8},{1,7},{3,5},... | collective-permute-start | bytes 393224 | tf_op jit(solution)/shard_map/ppermute | solution.py:182
  33.2 10.1 %collective-permute-start.7 = (bf16[4,128,128]{2,1,0:T(8,128)(2,1)S(1)}, bf16[4,128,128]{2,1,0:T(8,128)(2,1)S(1)}, u32[]{:S(2)}, u32[]{:S(2)}) collective-permute-start(bf16[4,128,128]{2,1,0:T(8,128)(2,1)S(1)} %get-tuple-element.17), channel_id=1, source_target_pairs={{0,2},{2,0},{4,6},{6,4},{8,10},{10,8},{12,14},{14,12},{1,3},{3,1},... | collective-permute-start | bytes 393224 | tf_op jit(solution)/shard_map/ppermute | solution.py:186
  33.8 9.7 %collective-permute-start.8 = (bf16[4,128,128]{2,1,0:T(8,128)(2,1)S(1)}, bf16[4,128,128]{2,1,0:T(8,128)(2,1)S(1)}, u32[]{:S(2)}, u32[]{:S(2)}) collective-permute-start(bf16[4,128,128]{2,1,0:T(8,128)(2,1)S(1)} %get-tuple-element.22), channel_id=1, source_target_pairs={{0,4},{2,6},{4,0},{6,2},{8,12},{10,14},{12,8},{14,10},{1,5},{3,7},... | collective-permute-start | bytes 393224 | tf_op jit(solution)/shard_map/ppermute | solution.py:186
  37.2 7.7 %collective-permute-start.9 = (bf16[4,128,128]{2,1,0:T(8,128)(2,1)S(1)}, bf16[4,128,128]{2,1,0:T(8,128)(2,1)S(1)}, u32[]{:S(2)}, u32[]{:S(2)}) collective-permute-start(bf16[4,128,128]{2,1,0:T(8,128)(2,1)S(1)} %get-tuple-element.21), channel_id=1, source_target_pairs={{0,6},{2,4},{4,2},{6,0},{8,14},{10,12},{12,10},{14,8},{1,7},{3,5},... | collective-permute-start | bytes 393224 | tf_op jit(solution)/shard_map/ppermute | solution.py:186
  40.6 7.3 %collective-permute-start.13 = (bf16[4,128,128]{2,1,0:T(8,128)(2,1)S(1)}, bf16[4,128,128]{2,1,0:T(8,128)(2,1)S(1)}, u32[]{:S(2)}, u32[]{:S(2)}) collective-permute-start(bf16[4,128,128]{2,1,0:T(8,128)(2,1)S(1)} %add_convert_fusion), channel_id=1, source_target_pairs={{0,8},{2,10},{4,12},{6,14},{8,0},{10,2},{12,4},{14,6},{1,9},{3,11}... | collective-permute-start | bytes 393224 | tf_op jit(solution)/shard_map/ppermute | solution.py:188

commit v17 on v16

--- a/solution.py
+++ b/solution.py
@@ -50,12 +50,17 @@
         v = kv_ref[c * chunk_blocks : (c + 1) * chunk_blocks, base : base + tok_rows, :]
         return v.reshape(chunk_keys, head_width)
 
-    def chunk_scores(q, k, c):
-        s = lax.dot_general(q, k, (((1,), (1,)), ((), ())), preferred_element_type=f32) * scale
+    def chunk_visible(c):
         key_off = jnp.zeros((1, chunk_keys), jnp.int32)
         for b in range(chunk_blocks):
             key_off = jnp.where(lane_block == b, offs_ref[c * chunk_blocks + b], key_off)
-        visible = (key_off * tok_rows + lane_row) <= row_pos
+        return (key_off * tok_rows + lane_row) <= row_pos
+
+    visibles = [chunk_visible(c) for c in range(blocks // chunk_blocks)]
+
+    def chunk_scores(q, k, c):
+        s = lax.dot_general(q, k, (((1,), (1,)), ((), ())), preferred_element_type=f32) * scale
+        visible = visibles[c]
         return jnp.where(visible, s, MASKED), visible
 
     for g in range(kv_heads):

time: 49.7 us -> 49.7 us (level)
  no operation moved by 1% of the time
where the time goes in v17:
time: 49.7 us; the launch traced here: 49.5 us
  starting transfers between devices  20.1 us (40%)
  waiting for transfers between devices  18.4 us (37%)
  Pallas kernels  4.11 us (8%)
  local copies, waits for them, and re-layouts  4.05 us (8%)
  between operations  1.49 us (3%)
  other arithmetic  1.39 us (3%)
    ppermute x1, waiting for transfers between devices, on_device(): from_x3 = lax.ppermute(from_x2, 'ctx', mate_pairs(cycle_size, 1))  5.42 us
    ppermute x1, waiting for transfers between devices, on_device(): from_mirror = lax.ppermute(slab, 'ctx', mirror_pairs(cycle_size))  4.92 us
    pallas_call x1, Pallas kernels, local_backward(): pl.pallas_call(functools.partial(backward_kernel, kv_heads=kv_heads, chun...  4.11 us
    ppermute x3, starting transfers between devices, on_device(): arrived = lax.ppermute(parts[k - 1], 'ctx', mate_pairs(cycle_size, k))  3.82 us
    ppermute x3, starting transfers between devices, on_device(): lax.ppermute(parts[half + k - 1], 'ctx', mate_pairs(cycle_size, k))  3.55 us
    ppermute x3, waiting for transfers between devices, on_device(): lax.ppermute(parts[half + k - 1], 'ctx', mate_pairs(cycle_size, k))  3.46 us
    ppermute x1, waiting for transfers between devices, on_device(): lax.ppermute(mirror_total.astype(jnp.bfloat16), 'ctx', mirror_pairs(cycle...  3.04 us
    ppermute x1, starting transfers between devices, on_device(): from_x1 = lax.ppermute(slab, 'ctx', mate_pairs(cycle_size, 1))  3.03 us
  transfers between devices with their start and end apart: 14, of which 7 were waited for; matrix products, arithmetic and copies ran while one was open for 5% of the time, Pallas kernels for 0%

profile of v17, /device:TPU:0, one launch (start us, length us, event | category | flops | bytes accessed | tf_op | source)
XLA Modules:
  0.0 49.5 jit_solution(9705421849865794266)
XLA Ops:
  0.6 0.0 copy-start
  1.3 1.0 %maximum_bitcast_fusion = bf16[4,128,128]{2,0,1:T(4,128)(2,1)S(1)} fusion(bf16[128,2,128]{2,1,0:T(2,128)(2,1)} %param.8, bf16[128,2,128]{2,1,0:T(2,128)(2,1)} %param.7), kind=kLoop, calls=%fused_computation.15 | loop fusion | flops 262144 | bytes 262144 | tf_op jit(solution)/shard_map/transpose | solution.py:155
  2.4 3.0 %collective-permute-start = (bf16[528,128]{1,0:T(8,128)(2,1)S(1)}, bf16[528,128]{1,0:T(8,128)(2,1)S(1)}, u32[]{:S(2)}, u32[]{:S(2)}) collective-permute-start(bf16[528,128]{1,0:T(8,128)(2,1)S(1)} %concatenate.7), channel_id=1, source_target_pairs={{0,2},{2,0},{4,6},{6,4},{8,10},{10,8},{12,14},{14,12},{1,3},{3,1},... | collective-permute-start | bytes 405512 | tf_op jit(solution)/shard_map/ppermute | solution.py:160
  5.4 1.6 %collective-permute-start.1 = (bf16[528,128]{1,0:T(8,128)(2,1)S(1)}, bf16[528,128]{1,0:T(8,128)(2,1)S(1)}, u32[]{:S(2)}, u32[]{:S(2)}) collective-permute-start(bf16[528,128]{1,0:T(8,128)(2,1)S(1)} %concatenate.7), channel_id=1, source_target_pairs={{0,4},{2,6},{4,0},{6,2},{8,12},{10,14},{12,8},{14,10},{1,5},{3,7},... | collective-permute-start | bytes 405512 | tf_op jit(solution)/shard_map/ppermute | solution.py:161
  7.0 2.6 %collective-permute-start.3 = (bf16[528,128]{1,0:T(8,128)(2,1)S(1)}, bf16[528,128]{1,0:T(8,128)(2,1)S(1)}, u32[]{:S(2)}, u32[]{:S(2)}) collective-permute-start(bf16[528,128]{1,0:T(8,128)(2,1)S(1)} %concatenate.7), channel_id=1, source_target_pairs={{0,8},{2,10},{4,12},{6,14},{8,0},{10,2},{12,4},{14,6},{1,9},{3,11}... | collective-permute-start | bytes 405512 | tf_op jit(solution)/shard_map/ppermute | solution.py:158
  9.6 1.1 %copy_bitcast_fusion = (bf16[8,128,128]{2,1,0:T(8,128)(2,1)S(1)}, bf16[8,128,128]{2,1,0:T(8,128)(2,1)S(1)}) fusion(bf16[128,8,128]{2,1,0:T(8,128)(2,1)} %param.9, bf16[128,8,128]{2,1,0:T(8,128)(2,1)} %param.10), kind=kLoop, calls=%fused_computation | loop fusion | bytes 1048576 | tf_op jit(solution)/shard_map/transpose | solution.py:181
  10.7 0.0 copy-done
  10.8 4.9 %collective-permute-done.3 = bf16[528,128]{1,0:T(8,128)(2,1)S(1)} collective-permute-done((bf16[528,128]{1,0:T(8,128)(2,1)S(1)}, bf16[528,128]{1,0:T(8,128)(2,1)S(1)}, u32[]{:S(2)}, u32[]{:S(2)}) %collective-permute-start.3) | collective-permute-done | bytes 135200 | tf_op jit(solution)/shard_map/ppermute | solution.py:158
  15.7 0.4 collective-permute-start.4
  16.1 0.3 collective-permute-start.5
  16.5 2.7 %collective-permute-start.6 = (bf16[528,128]{1,0:T(8,128)(2,1)S(1)}, bf16[528,128]{1,0:T(8,128)(2,1)S(1)}, u32[]{:S(2)}, u32[]{:S(2)}) collective-permute-start(bf16[528,128]{1,0:T(8,128)(2,1)S(1)} %collective-permute-done.3), channel_id=1, source_target_pairs={{0,6},{2,4},{4,2},{6,0},{8,14},{10,12},{12,10},{14,8},{1,7},{3,5},... | collective-permute-start | bytes 405512 | tf_op jit(solution)/shard_map/ppermute | solution.py:165
  19.2 0.0 collective-permute-done.1
  19.2 0.4 collective-permute-start.2
  19.6 0.0 collective-permute-done
  19.7 5.4 %collective-permute-done.2 = bf16[528,128]{1,0:T(8,128)(2,1)S(1)} collective-permute-done((bf16[528,128]{1,0:T(8,128)(2,1)S(1)}, bf16[528,128]{1,0:T(8,128)(2,1)S(1)}, u32[]{:S(2)}, u32[]{:S(2)}) %collective-permute-start.2) | collective-permute-done | bytes 135200 | tf_op jit(solution)/shard_map/ppermute | solution.py:162
  25.1 0.0 collective-permute-done.4
  25.2 0.0 collective-permute-done.5
  25.2 0.0 collective-permute-done.6
  25.3 0.2 fusion.1.offs_ref
  25.5 4.1 %shard_map.85 = (f32[8,128,128]{2,1,0:T(8,128)S(1)}, f32[4,128,128]{2,1,0:T(8,128)S(1)}, f32[4,128,128]{2,1,0:T(8,128)S(1)}, bf16[7,4,128,128]{3,2,1,0:T(8,128)(2,1)S(1)}) custom-call(s32[8]{0:T(128)S(1)} %fusion.1.offs_ref, s32[1]{0:T(128)S(6)} %copy.34.own_ref, bf16[8,128,128]{2,1,0:T(8,128)(2,1)S(1)} %bitcast.45, ...), custom_call_target="tpu_custom_call" | custom-call | flops 1610612736 | bytes 2654208 | tf_op jit(solution)/shard_map/pallas_call | solution.py:129
  29.6 0.1 slice_bitcast_fusion.7
  29.7 0.6 %collective-permute-start.10 = (bf16[4,128,128]{2,1,0:T(8,128)(2,1)S(1)}, bf16[4,128,128]{2,1,0:T(8,128)(2,1)S(1)}, u32[]{:S(2)}, u32[]{:S(2)}) collective-permute-start(bf16[4,128,128]{2,1,0:T(8,128)(2,1)S(1)} %get-tuple-element.20), channel_id=1, source_target_pairs={{0,2},{2,0},{4,6},{6,4},{8,10},{10,8},{12,14},{14,12},{1,3},{3,1},... | collective-permute-start | bytes 393224 | tf_op jit(solution)/shard_map/ppermute | solution.py:187
  30.3 1.7 %collective-permute-start.11 = (bf16[4,128,128]{2,1,0:T(8,128)(2,1)S(1)}, bf16[4,128,128]{2,1,0:T(8,128)(2,1)S(1)}, u32[]{:S(2)}, u32[]{:S(2)}) collective-permute-start(bf16[4,128,128]{2,1,0:T(8,128)(2,1)S(1)} %get-tuple-element.19), channel_id=1, source_target_pairs={{0,4},{2,6},{4,0},{6,2},{8,12},{10,14},{12,8},{14,10},{1,5},{3,7},... | collective-permute-start | bytes 393224 | tf_op jit(solution)/shard_map/ppermute | solution.py:187
  31.9 1.3 %collective-permute-start.12 = (bf16[4,128,128]{2,1,0:T(8,128)(2,1)S(1)}, bf16[4,128,128]{2,1,0:T(8,128)(2,1)S(1)}, u32[]{:S(2)}, u32[]{:S(2)}) collective-permute-start(bf16[4,128,128]{2,1,0:T(8,128)(2,1)S(1)} %get-tuple-element.18), channel_id=1, source_target_pairs={{0,6},{2,4},{4,2},{6,0},{8,14},{10,12},{12,10},{14,8},{1,7},{3,5},... | collective-permute-start | bytes 393224 | tf_op jit(solution)/shard_map/ppermute | solution.py:187
  33.2 0.5 %collective-permute-start.7 = (bf16[4,128,128]{2,1,0:T(8,128)(2,1)S(1)}, bf16[4,128,128]{2,1,0:T(8,128)(2,1)S(1)}, u32[]{:S(2)}, u32[]{:S(2)}) collective-permute-start(bf16[4,128,128]{2,1,0:T(8,128)(2,1)S(1)} %get-tuple-element.17), channel_id=1, source_target_pairs={{0,2},{2,0},{4,6},{6,4},{8,10},{10,8},{12,14},{14,12},{1,3},{3,1},... | collective-permute-start | bytes 393224 | tf_op jit(solution)/shard_map/ppermute | solution.py:191
  33.8 1.7 %collective-permute-start.8 = (bf16[4,128,128]{2,1,0:T(8,128)(2,1)S(1)}, bf16[4,128,128]{2,1,0:T(8,128)(2,1)S(1)}, u32[]{:S(2)}, u32[]{:S(2)}) collective-permute-start(bf16[4,128,128]{2,1,0:T(8,128)(2,1)S(1)} %get-tuple-element.22), channel_id=1, source_target_pairs={{0,4},{2,6},{4,0},{6,2},{8,12},{10,14},{12,8},{14,10},{1,5},{3,7},... | collective-permute-start | bytes 393224 | tf_op jit(solution)/shard_map/ppermute | solution.py:191
  35.4 1.8 %collective-permute-done.10 = bf16[4,128,128]{2,1,0:T(8,128)(2,1)S(1)} collective-permute-done((bf16[4,128,128]{2,1,0:T(8,128)(2,1)S(1)}, bf16[4,128,128]{2,1,0:T(8,128)(2,1)S(1)}, u32[]{:S(2)}, u32[]{:S(2)}) %collective-permute-start.10) | collective-permute-done | bytes 131104 | tf_op jit(solution)/shard_map/ppermute | solution.py:187
  37.2 1.6 %collective-permute-start.9 = (bf16[4,128,128]{2,1,0:T(8,128)(2,1)S(1)}, bf16[4,128,128]{2,1,0:T(8,128)(2,1)S(1)}, u32[]{:S(2)}, u32[]{:S(2)}) collective-permute-start(bf16[4,128,128]{2,1,0:T(8,128)(2,1)S(1)} %get-tuple-element.21), channel_id=1, source_target_pairs={{0,6},{2,4},{4,2},{6,0},{8,14},{10,12},{12,10},{14,8},{1,7},{3,5},... | collective-permute-start | bytes 393224 | tf_op jit(solution)/shard_map/ppermute | solution.py:191
  38.9 0.0 collective-permute-done.11
  38.9 1.6 %collective-permute-done.12 = bf16[4,128,128]{2,1,0:T(8,128)(2,1)S(1)} collective-permute-done((bf16[4,128,128]{2,1,0:T(8,128)(2,1)S(1)}, bf16[4,128,128]{2,1,0:T(8,128)(2,1)S(1)}, u32[]{:S(2)}, u32[]{:S(2)}) %collective-permute-start.12) | collective-permute-done | bytes 131104 | tf_op jit(solution)/shard_map/ppermute | solution.py:187
  40.5 0.1 add_convert_fusion
  40.6 1.7 %collective-permute-start.13 = (bf16[4,128,128]{2,1,0:T(8,128)(2,1)S(1)}, bf16[4,128,128]{2,1,0:T(8,128)(2,1)S(1)}, u32[]{:S(2)}, u32[]{:S(2)}) collective-permute-start(bf16[4,128,128]{2,1,0:T(8,128)(2,1)S(1)} %add_convert_fusion), channel_id=1, source_target_pairs={{0,8},{2,10},{4,12},{6,14},{8,0},{10,2},{12,4},{14,6},{1,9},{3,11}... | collective-permute-start | bytes 393224 | tf_op jit(solution)/shard_map/ppermute | solution.py:193
  42.3 1.1 %copy.20 = f32[128,8,128]{2,1,0:T(8,128)} copy(f32[128,8,128]{2,0,1:T(8,128)S(1)} %bitcast.44) | data formatting | bytes 1048576
  43.4 0.0 collective-permute-done.7
  43.4 0.1 collective-permute-done.8
  43.4 1.4 %collective-permute-done.9 = bf16[4,128,128]{2,1,0:T(8,128)(2,1)S(1)} collective-permute-done((bf16[4,128,128]{2,1,0:T(8,128)(2,1)S(1)}, bf16[4,128,128]{2,1,0:T(8,128)(2,1)S(1)}, u32[]{:S(2)}, u32[]{:S(2)}) %collective-permute-start.9) | collective-permute-done | bytes 131104 | tf_op jit(solution)/shard_map/ppermute | solution.py:191
  44.9 3.0 %collective-permute-done.13 = bf16[4,128,128]{2,1,0:T(8,128)(2,1)S(1)} collective-permute-done((bf16[4,128,128]{2,1,0:T(8,128)(2,1)S(1)}, bf16[4,128,128]{2,1,0:T(8,128)(2,1)S(1)}, u32[]{:S(2)}, u32[]{:S(2)}) %collective-permute-start.13) | collective-permute-done | bytes 131104 | tf_op jit(solution)/shard_map/ppermute | solution.py:193
  47.9 0.1 convert_add_fusion
  48.0 0.8 %copy.21 = f32[128,2,128]{2,1,0:T(2,128)} copy(f32[128,2,128]{2,0,1:T(8,128)S(1)} %get-tuple-element.24) | data formatting | bytes 262144
  48.8 0.8 %copy.22 = f32[128,2,128]{2,1,0:T(2,128)} copy(f32[128,2,128]{2,0,1:T(8,128)S(1)} %get-tuple-element.23) | data formatting | bytes 262144
  (12 shorter events, 0.2 us)
Async XLA Ops:
  0.6 10.1 %copy-start = (bf16[128,8,128]{2,1,0:T(8,128)(2,1)S(1)}, bf16[128,8,128]{2,1,0:T(8,128)(2,1)}, u32[]{:S(2)}) copy-start(bf16[128,8,128]{2,1,0:T(8,128)(2,1)} %param.6) | copy-start | bytes 786436
  2.4 17.2 %collective-permute-start = (bf16[528,128]{1,0:T(8,128)(2,1)S(1)}, bf16[528,128]{1,0:T(8,128)(2,1)S(1)}, u32[]{:S(2)}, u32[]{:S(2)}) collective-permute-start(bf16[528,128]{1,0:T(8,128)(2,1)S(1)} %concatenate.7), channel_id=1, source_target_pairs={{0,2},{2,0},{4,6},{6,4},{8,10},{10,8},{12,14},{14,12},{1,3},{3,1},... | collective-permute-start | bytes 405512 | tf_op jit(solution)/shard_map/ppermute | solution.py:160
  5.4 13.8 %collective-permute-start.1 = (bf16[528,128]{1,0:T(8,128)(2,1)S(1)}, bf16[528,128]{1,0:T(8,128)(2,1)S(1)}, u32[]{:S(2)}, u32[]{:S(2)}) collective-permute-start(bf16[528,128]{1,0:T(8,128)(2,1)S(1)} %concatenate.7), channel_id=1, source_target_pairs={{0,4},{2,6},{4,0},{6,2},{8,12},{10,14},{12,8},{14,10},{1,5},{3,7},... | collective-permute-start | bytes 405512 | tf_op jit(solution)/shard_map/ppermute | solution.py:161
  7.0 8.7 %collective-permute-start.3 = (bf16[528,128]{1,0:T(8,128)(2,1)S(1)}, bf16[528,128]{1,0:T(8,128)(2,1)S(1)}, u32[]{:S(2)}, u32[]{:S(2)}) collective-permute-start(bf16[528,128]{1,0:T(8,128)(2,1)S(1)} %concatenate.7), channel_id=1, source_target_pairs={{0,8},{2,10},{4,12},{6,14},{8,0},{10,2},{12,4},{14,6},{1,9},{3,11}... | collective-permute-start | bytes 405512 | tf_op jit(solution)/shard_map/ppermute | solution.py:158
  15.7 9.4 %collective-permute-start.4 = (bf16[528,128]{1,0:T(8,128)(2,1)S(1)}, bf16[528,128]{1,0:T(8,128)(2,1)S(1)}, u32[]{:S(2)}, u32[]{:S(2)}) collective-permute-start(bf16[528,128]{1,0:T(8,128)(2,1)S(1)} %collective-permute-done.3), channel_id=1, source_target_pairs={{0,2},{2,0},{4,6},{6,4},{8,10},{10,8},{12,14},{14,12},{1,3},{3,1},... | collective-permute-start | bytes 405512 | tf_op jit(solution)/shard_map/ppermute | solution.py:163
  16.1 9.1 %collective-permute-start.5 = (bf16[528,128]{1,0:T(8,128)(2,1)S(1)}, bf16[528,128]{1,0:T(8,128)(2,1)S(1)}, u32[]{:S(2)}, u32[]{:S(2)}) collective-permute-start(bf16[528,128]{1,0:T(8,128)(2,1)S(1)} %collective-permute-done.3), channel_id=1, source_target_pairs={{0,4},{2,6},{4,0},{6,2},{8,12},{10,14},{12,8},{14,10},{1,5},{3,7},... | collective-permute-start | bytes 405512 | tf_op jit(solution)/shard_map/ppermute | solution.py:164
  16.5 8.8 %collective-permute-start.6 = (bf16[528,128]{1,0:T(8,128)(2,1)S(1)}, bf16[528,128]{1,0:T(8,128)(2,1)S(1)}, u32[]{:S(2)}, u32[]{:S(2)}) collective-permute-start(bf16[528,128]{1,0:T(8,128)(2,1)S(1)} %collective-permute-done.3), channel_id=1, source_target_pairs={{0,6},{2,4},{4,2},{6,0},{8,14},{10,12},{12,10},{14,8},{1,7},{3,5},... | collective-permute-start | bytes 405512 | tf_op jit(solution)/shard_map/ppermute | solution.py:165
  19.2 5.9 %collective-permute-start.2 = (bf16[528,128]{1,0:T(8,128)(2,1)S(1)}, bf16[528,128]{1,0:T(8,128)(2,1)S(1)}, u32[]{:S(2)}, u32[]{:S(2)}) collective-permute-start(bf16[528,128]{1,0:T(8,128)(2,1)S(1)} %collective-permute-done.1), channel_id=1, source_target_pairs={{0,2},{2,0},{4,6},{6,4},{8,10},{10,8},{12,14},{14,12},{1,3},{3,1},... | collective-permute-start | bytes 405512 | tf_op jit(solution)/shard_map/ppermute | solution.py:162
  29.7 7.6 %collective-permute-start.10 = (bf16[4,128,128]{2,1,0:T(8,128)(2,1)S(1)}, bf16[4,128,128]{2,1,0:T(8,128)(2,1)S(1)}, u32[]{:S(2)}, u32[]{:S(2)}) collective-permute-start(bf16[4,128,128]{2,1,0:T(8,128)(2,1)S(1)} %get-tuple-element.20), channel_id=1, source_target_pairs={{0,2},{2,0},{4,6},{6,4},{8,10},{10,8},{12,14},{14,12},{1,3},{3,1},... | collective-permute-start | bytes 393224 | tf_op jit(solution)/shard_map/ppermute | solution.py:187
  30.3 8.6 %collective-permute-start.11 = (bf16[4,128,128]{2,1,0:T(8,128)(2,1)S(1)}, bf16[4,128,128]{2,1,0:T(8,128)(2,1)S(1)}, u32[]{:S(2)}, u32[]{:S(2)}) collective-permute-start(bf16[4,128,128]{2,1,0:T(8,128)(2,1)S(1)} %get-tuple-element.19), channel_id=1, source_target_pairs={{0,4},{2,6},{4,0},{6,2},{8,12},{10,14},{12,8},{14,10},{1,5},{3,7},... | collective-permute-start | bytes 393224 | tf_op jit(solution)/shard_map/ppermute | solution.py:187
  31.9 8.6 %collective-permute-start.12 = (bf16[4,128,128]{2,1,0:T(8,128)(2,1)S(1)}, bf16[4,128,128]{2,1,0:T(8,128)(2,1)S(1)}, u32[]{:S(2)}, u32[]{:S(2)}) collective-permute-start(bf16[4,128,128]{2,1,0:T(8,128)(2,1)S(1)} %get-tuple-element.18), channel_id=1, source_target_pairs={{0,6},{2,4},{4,2},{6,0},{8,14},{10,12},{12,10},{14,8},{1,7},{3,5},... | collective-permute-start | bytes 393224 | tf_op jit(solution)/shard_map/ppermute | solution.py:187
  33.2 10.1 %collective-permute-start.7 = (bf16[4,128,128]{2,1,0:T(8,128)(2,1)S(1)}, bf16[4,128,128]{2,1,0:T(8,128)(2,1)S(1)}, u32[]{:S(2)}, u32[]{:S(2)}) collective-permute-start(bf16[4,128,128]{2,1,0:T(8,128)(2,1)S(1)} %get-tuple-element.17), channel_id=1, source_target_pairs={{0,2},{2,0},{4,6},{6,4},{8,10},{10,8},{12,14},{14,12},{1,3},{3,1},... | collective-permute-start | bytes 393224 | tf_op jit(solution)/shard_map/ppermute | solution.py:191
  33.8 9.7 %collective-permute-start.8 = (bf16[4,128,128]{2,1,0:T(8,128)(2,1)S(1)}, bf16[4,128,128]{2,1,0:T(8,128)(2,1)S(1)}, u32[]{:S(2)}, u32[]{:S(2)}) collective-permute-start(bf16[4,128,128]{2,1,0:T(8,128)(2,1)S(1)} %get-tuple-element.22), channel_id=1, source_target_pairs={{0,4},{2,6},{4,0},{6,2},{8,12},{10,14},{12,8},{14,10},{1,5},{3,7},... | collective-permute-start | bytes 393224 | tf_op jit(solution)/shard_map/ppermute | solution.py:191
  37.2 7.6 %collective-permute-start.9 = (bf16[4,128,128]{2,1,0:T(8,128)(2,1)S(1)}, bf16[4,128,128]{2,1,0:T(8,128)(2,1)S(1)}, u32[]{:S(2)}, u32[]{:S(2)}) collective-permute-start(bf16[4,128,128]{2,1,0:T(8,128)(2,1)S(1)} %get-tuple-element.21), channel_id=1, source_target_pairs={{0,6},{2,4},{4,2},{6,0},{8,14},{10,12},{12,10},{14,8},{1,7},{3,5},... | collective-permute-start | bytes 393224 | tf_op jit(solution)/shard_map/ppermute | solution.py:191
  40.6 7.3 %collective-permute-start.13 = (bf16[4,128,128]{2,1,0:T(8,128)(2,1)S(1)}, bf16[4,128,128]{2,1,0:T(8,128)(2,1)S(1)}, u32[]{:S(2)}, u32[]{:S(2)}) collective-permute-start(bf16[4,128,128]{2,1,0:T(8,128)(2,1)S(1)} %add_convert_fusion), channel_id=1, source_target_pairs={{0,8},{2,10},{4,12},{6,14},{8,0},{10,2},{12,4},{14,6},{1,9},{3,11}... | collective-permute-start | bytes 393224 | tf_op jit(solution)/shard_map/ppermute | solution.py:193

commit v18 on v16

--- a/solution.py
+++ b/solution.py
@@ -181,11 +181,12 @@
     for k in range(1, half):
         arrived = lax.ppermute(parts[half + k - 1], "ctx", mate_pairs(cycle_size, k))
         mirror_total = mirror_total + arrived.astype(jnp.float32)
+    crossed = lax.ppermute(mirror_total.astype(jnp.bfloat16), "ctx", mirror_pairs(cycle_size))
+    parts, crossed = lax.optimization_barrier((parts, crossed))
     own_total = own_part
     for k in range(1, half):
         arrived = lax.ppermute(parts[k - 1], "ctx", mate_pairs(cycle_size, k))
         own_total = own_total + arrived.astype(jnp.float32)
-    crossed = lax.ppermute(mirror_total.astype(jnp.bfloat16), "ctx", mirror_pairs(cycle_size))
     total = own_total + crossed.astype(jnp.float32)
     key_grad = total[:kv_heads].transpose(1, 0, 2)
     value_grad = total[kv_heads:].transpose(1, 0, 2)

time: 49.7 us -> 54.8 us (1.10)
  waiting for transfers between devices: 18.3 us -> 23.8 us
    ppermute x1, waiting for transfers between devices: 3.03 us -> 5.6 us  [on_device(): lax.ppermute(mirror_total.astype(jnp.bfloat16), 'ctx', mirror_pairs(cycle...]
    ppermute x3, waiting for transfers between devices: 1.53 us -> 3.24 us  [on_device(): arrived = lax.ppermute(parts[k - 1], 'ctx', mate_pairs(cycle_size, k))]
    ppermute x3, waiting for transfers between devices: 3.42 us -> 4.58 us  [on_device(): lax.ppermute(parts[half + k - 1], 'ctx', mate_pairs(cycle_size, k))]
  transfers between devices with their start and end apart: 14 -> 14, of which waited for: 7 -> 9; matrix products, arithmetic and copies ran while one was open for 5% -> 4% of each run, Pallas kernels for 0% -> 0%
where the time goes in v18:
time: 54.8 us; the launch traced here: 54.6 us
  waiting for transfers between devices  23.8 us (43%)
  starting transfers between devices  19.8 us (36%)
  Pallas kernels  4.1 us (7%)
  local copies, waits for them, and re-layouts  4.03 us (7%)
  between operations  1.5 us (3%)
  other arithmetic  1.39 us (3%)
    ppermute x1, waiting for transfers between devices, on_device(): lax.ppermute(mirror_total.astype(jnp.bfloat16), 'ctx', mirror_pairs(cycle...  5.6 us
    ppermute x1, waiting for transfers between devices, on_device(): from_x3 = lax.ppermute(from_x2, 'ctx', mate_pairs(cycle_size, 1))  5.42 us
    ppermute x1, waiting for transfers between devices, on_device(): from_mirror = lax.ppermute(slab, 'ctx', mirror_pairs(cycle_size))  4.92 us
    ppermute x3, waiting for transfers between devices, on_device(): lax.ppermute(parts[half + k - 1], 'ctx', mate_pairs(cycle_size, k))  4.58 us
    pallas_call x1, Pallas kernels, local_backward(): pl.pallas_call(functools.partial(backward_kernel, kv_heads=kv_heads, chun...  4.1 us
    ppermute x3, starting transfers between devices, on_device(): lax.ppermute(parts[half + k - 1], 'ctx', mate_pairs(cycle_size, k))  3.55 us
    ppermute x3, starting transfers between devices, on_device(): arrived = lax.ppermute(parts[k - 1], 'ctx', mate_pairs(cycle_size, k))  3.55 us
    ppermute x3, waiting for transfers between devices, on_device(): arrived = lax.ppermute(parts[k - 1], 'ctx', mate_pairs(cycle_size, k))  3.24 us
  transfers between devices with their start and end apart: 14, of which 9 were waited for; matrix products, arithmetic and copies ran while one was open for 4% of the time, Pallas kernels for 0%

profile of v18, /device:TPU:0, one launch (start us, length us, event | category | flops | bytes accessed | tf_op | source)
XLA Modules:
  0.0 54.6 jit_solution(10665141809211358795)
XLA Ops:
  0.6 0.0 copy-start
  1.3 1.0 %maximum_bitcast_fusion = bf16[4,128,128]{2,0,1:T(4,128)(2,1)S(1)} fusion(bf16[128,2,128]{2,1,0:T(2,128)(2,1)} %param.8, bf16[128,2,128]{2,1,0:T(2,128)(2,1)} %param.7), kind=kLoop, calls=%fused_computation.15 | loop fusion | flops 262144 | bytes 262144 | tf_op jit(solution)/shard_map/transpose | solution.py:150
  2.4 3.0 %collective-permute-start = (bf16[528,128]{1,0:T(8,128)(2,1)S(1)}, bf16[528,128]{1,0:T(8,128)(2,1)S(1)}, u32[]{:S(2)}, u32[]{:S(2)}) collective-permute-start(bf16[528,128]{1,0:T(8,128)(2,1)S(1)} %concatenate.7), channel_id=1, source_target_pairs={{0,2},{2,0},{4,6},{6,4},{8,10},{10,8},{12,14},{14,12},{1,3},{3,1},... | collective-permute-start | bytes 405512 | tf_op jit(solution)/shard_map/ppermute | solution.py:155
  5.4 1.6 %collective-permute-start.1 = (bf16[528,128]{1,0:T(8,128)(2,1)S(1)}, bf16[528,128]{1,0:T(8,128)(2,1)S(1)}, u32[]{:S(2)}, u32[]{:S(2)}) collective-permute-start(bf16[528,128]{1,0:T(8,128)(2,1)S(1)} %concatenate.7), channel_id=1, source_target_pairs={{0,4},{2,6},{4,0},{6,2},{8,12},{10,14},{12,8},{14,10},{1,5},{3,7},... | collective-permute-start | bytes 405512 | tf_op jit(solution)/shard_map/ppermute | solution.py:156
  7.0 2.6 %collective-permute-start.3 = (bf16[528,128]{1,0:T(8,128)(2,1)S(1)}, bf16[528,128]{1,0:T(8,128)(2,1)S(1)}, u32[]{:S(2)}, u32[]{:S(2)}) collective-permute-start(bf16[528,128]{1,0:T(8,128)(2,1)S(1)} %concatenate.7), channel_id=1, source_target_pairs={{0,8},{2,10},{4,12},{6,14},{8,0},{10,2},{12,4},{14,6},{1,9},{3,11}... | collective-permute-start | bytes 405512 | tf_op jit(solution)/shard_map/ppermute | solution.py:153
  9.6 1.1 %copy_bitcast_fusion = (bf16[8,128,128]{2,1,0:T(8,128)(2,1)S(1)}, bf16[8,128,128]{2,1,0:T(8,128)(2,1)S(1)}) fusion(bf16[128,8,128]{2,1,0:T(8,128)(2,1)} %param.9, bf16[128,8,128]{2,1,0:T(8,128)(2,1)} %param.10), kind=kLoop, calls=%fused_computation | loop fusion | bytes 1048576 | tf_op jit(solution)/shard_map/transpose | solution.py:176
  10.7 0.0 copy-done
  10.8 4.9 %collective-permute-done.3 = bf16[528,128]{1,0:T(8,128)(2,1)S(1)} collective-permute-done((bf16[528,128]{1,0:T(8,128)(2,1)S(1)}, bf16[528,128]{1,0:T(8,128)(2,1)S(1)}, u32[]{:S(2)}, u32[]{:S(2)}) %collective-permute-start.3) | collective-permute-done | bytes 135200 | tf_op jit(solution)/shard_map/ppermute | solution.py:153
  15.7 0.4 collective-permute-start.4
  16.1 0.3 collective-permute-start.5
  16.5 2.7 %collective-permute-start.6 = (bf16[528,128]{1,0:T(8,128)(2,1)S(1)}, bf16[528,128]{1,0:T(8,128)(2,1)S(1)}, u32[]{:S(2)}, u32[]{:S(2)}) collective-permute-start(bf16[528,128]{1,0:T(8,128)(2,1)S(1)} %collective-permute-done.3), channel_id=1, source_target_pairs={{0,6},{2,4},{4,2},{6,0},{8,14},{10,12},{12,10},{14,8},{1,7},{3,5},... | collective-permute-start | bytes 405512 | tf_op jit(solution)/shard_map/ppermute | solution.py:160
  19.2 0.0 collective-permute-done.1
  19.2 0.4 collective-permute-start.2
  19.6 0.0 collective-permute-done
  19.7 5.4 %collective-permute-done.2 = bf16[528,128]{1,0:T(8,128)(2,1)S(1)} collective-permute-done((bf16[528,128]{1,0:T(8,128)(2,1)S(1)}, bf16[528,128]{1,0:T(8,128)(2,1)S(1)}, u32[]{:S(2)}, u32[]{:S(2)}) %collective-permute-start.2) | collective-permute-done | bytes 135200 | tf_op jit(solution)/shard_map/ppermute | solution.py:157
  25.1 0.0 collective-permute-done.4
  25.2 0.0 collective-permute-done.5
  25.2 0.0 collective-permute-done.6
  25.3 0.2 fusion.1.offs_ref
  25.5 4.1 %shard_map.85 = (f32[8,128,128]{2,1,0:T(8,128)S(1)}, f32[4,128,128]{2,1,0:T(8,128)S(1)}, f32[4,128,128]{2,1,0:T(8,128)S(1)}, bf16[7,4,128,128]{3,2,1,0:T(8,128)(2,1)S(1)}) custom-call(s32[8]{0:T(128)S(1)} %fusion.1.offs_ref, s32[1]{0:T(128)S(6)} %copy.34.own_ref, bf16[8,128,128]{2,1,0:T(8,128)(2,1)S(1)} %bitcast.45, ...), custom_call_target="tpu_custom_call" | custom-call | flops 1610612736 | bytes 2654208 | tf_op jit(solution)/shard_map/pallas_call | solution.py:124
  29.6 0.6 %collective-permute-start.7 = (bf16[4,128,128]{2,1,0:T(8,128)(2,1)S(1)}, bf16[4,128,128]{2,1,0:T(8,128)(2,1)S(1)}, u32[]{:S(2)}, u32[]{:S(2)}) collective-permute-start(bf16[4,128,128]{2,1,0:T(8,128)(2,1)S(1)} %get-tuple-element.24), channel_id=1, source_target_pairs={{0,2},{2,0},{4,6},{6,4},{8,10},{10,8},{12,14},{14,12},{1,3},{3,1},... | collective-permute-start | bytes 393224 | tf_op jit(solution)/shard_map/ppermute | solution.py:182
  30.2 1.7 %collective-permute-start.8 = (bf16[4,128,128]{2,1,0:T(8,128)(2,1)S(1)}, bf16[4,128,128]{2,1,0:T(8,128)(2,1)S(1)}, u32[]{:S(2)}, u32[]{:S(2)}) collective-permute-start(bf16[4,128,128]{2,1,0:T(8,128)(2,1)S(1)} %get-tuple-element.26), channel_id=1, source_target_pairs={{0,4},{2,6},{4,0},{6,2},{8,12},{10,14},{12,8},{14,10},{1,5},{3,7},... | collective-permute-start | bytes 393224 | tf_op jit(solution)/shard_map/ppermute | solution.py:182
  31.9 1.3 %collective-permute-start.9 = (bf16[4,128,128]{2,1,0:T(8,128)(2,1)S(1)}, bf16[4,128,128]{2,1,0:T(8,128)(2,1)S(1)}, u32[]{:S(2)}, u32[]{:S(2)}) collective-permute-start(bf16[4,128,128]{2,1,0:T(8,128)(2,1)S(1)} %get-tuple-element.25), channel_id=1, source_target_pairs={{0,6},{2,4},{4,2},{6,0},{8,14},{10,12},{12,10},{14,8},{1,7},{3,5},... | collective-permute-start | bytes 393224 | tf_op jit(solution)/shard_map/ppermute | solution.py:182
  33.2 2.9 %collective-permute-done.7 = bf16[4,128,128]{2,1,0:T(8,128)(2,1)S(1)} collective-permute-done((bf16[4,128,128]{2,1,0:T(8,128)(2,1)S(1)}, bf16[4,128,128]{2,1,0:T(8,128)(2,1)S(1)}, u32[]{:S(2)}, u32[]{:S(2)}) %collective-permute-start.7) | collective-permute-done | bytes 131104 | tf_op jit(solution)/shard_map/ppermute | solution.py:182
  36.1 0.3 collective-permute-done.8
  36.4 1.4 %collective-permute-done.9 = bf16[4,128,128]{2,1,0:T(8,128)(2,1)S(1)} collective-permute-done((bf16[4,128,128]{2,1,0:T(8,128)(2,1)S(1)}, bf16[4,128,128]{2,1,0:T(8,128)(2,1)S(1)}, u32[]{:S(2)}, u32[]{:S(2)}) %collective-permute-start.9) | collective-permute-done | bytes 131104 | tf_op jit(solution)/shard_map/ppermute | solution.py:182
  37.8 0.1 add_convert_fusion
  37.8 1.6 %collective-permute-start.10 = (bf16[4,128,128]{2,1,0:T(8,128)(2,1)S(1)}, bf16[4,128,128]{2,1,0:T(8,128)(2,1)S(1)}, u32[]{:S(2)}, u32[]{:S(2)}) collective-permute-start(bf16[4,128,128]{2,1,0:T(8,128)(2,1)S(1)} %add_convert_fusion), channel_id=1, source_target_pairs={{0,8},{2,10},{4,12},{6,14},{8,0},{10,2},{12,4},{14,6},{1,9},{3,11}... | collective-permute-start | bytes 393224 | tf_op jit(solution)/shard_map/ppermute | solution.py:184
  39.4 5.6 %collective-permute-done.10 = bf16[4,128,128]{2,1,0:T(8,128)(2,1)S(1)} collective-permute-done((bf16[4,128,128]{2,1,0:T(8,128)(2,1)S(1)}, bf16[4,128,128]{2,1,0:T(8,128)(2,1)S(1)}, u32[]{:S(2)}, u32[]{:S(2)}) %collective-permute-start.10) | collective-permute-done | bytes 131104 | tf_op jit(solution)/shard_map/ppermute | solution.py:184
  45.0 1.8 %collective-permute-start.11 = (bf16[4,128,128]{2,1,0:T(8,128)(2,1)S(1)}, bf16[4,128,128]{2,1,0:T(8,128)(2,1)S(1)}, u32[]{:S(2)}, u32[]{:S(2)}) collective-permute-start(bf16[4,128,128]{2,1,0:T(8,128)(2,1)S(1)} %get-tuple-element.21), channel_id=1, source_target_pairs={{0,2},{2,0},{4,6},{6,4},{8,10},{10,8},{12,14},{14,12},{1,3},{3,1},... | collective-permute-start | bytes 393224 | tf_op jit(solution)/shard_map/ppermute | solution.py:188
  46.9 0.0 collective-permute-start.12
  46.9 1.7 %collective-permute-start.13 = (bf16[4,128,128]{2,1,0:T(8,128)(2,1)S(1)}, bf16[4,128,128]{2,1,0:T(8,128)(2,1)S(1)}, u32[]{:S(2)}, u32[]{:S(2)}) collective-permute-start(bf16[4,128,128]{2,1,0:T(8,128)(2,1)S(1)} %get-tuple-element.22), channel_id=1, source_target_pairs={{0,6},{2,4},{4,2},{6,0},{8,14},{10,12},{12,10},{14,8},{1,7},{3,5},... | collective-permute-start | bytes 393224 | tf_op jit(solution)/shard_map/ppermute | solution.py:188
  48.6 1.1 %copy.20 = f32[128,8,128]{2,1,0:T(8,128)} copy(f32[128,8,128]{2,0,1:T(8,128)S(1)} %bitcast.44) | data formatting | bytes 1048576
  49.7 0.6 %collective-permute-done.11 = bf16[4,128,128]{2,1,0:T(8,128)(2,1)S(1)} collective-permute-done((bf16[4,128,128]{2,1,0:T(8,128)(2,1)S(1)}, bf16[4,128,128]{2,1,0:T(8,128)(2,1)S(1)}, u32[]{:S(2)}, u32[]{:S(2)}) %collective-permute-start.11) | collective-permute-done | bytes 131104 | tf_op jit(solution)/shard_map/ppermute | solution.py:188
  50.3 1.5 %collective-permute-done.12 = bf16[4,128,128]{2,1,0:T(8,128)(2,1)S(1)} collective-permute-done((bf16[4,128,128]{2,1,0:T(8,128)(2,1)S(1)}, bf16[4,128,128]{2,1,0:T(8,128)(2,1)S(1)}, u32[]{:S(2)}, u32[]{:S(2)}) %collective-permute-start.12) | collective-permute-done | bytes 131104 | tf_op jit(solution)/shard_map/ppermute | solution.py:188
  51.9 1.1 %collective-permute-done.13 = bf16[4,128,128]{2,1,0:T(8,128)(2,1)S(1)} collective-permute-done((bf16[4,128,128]{2,1,0:T(8,128)(2,1)S(1)}, bf16[4,128,128]{2,1,0:T(8,128)(2,1)S(1)}, u32[]{:S(2)}, u32[]{:S(2)}) %collective-permute-start.13) | collective-permute-done | bytes 131104 | tf_op jit(solution)/shard_map/ppermute | solution.py:188
  52.9 0.1 convert_add_fusion
  53.1 0.8 %copy.21 = f32[128,2,128]{2,1,0:T(2,128)} copy(f32[128,2,128]{2,0,1:T(8,128)S(1)} %get-tuple-element.28) | data formatting | bytes 262144
  53.8 0.8 %copy.22 = f32[128,2,128]{2,1,0:T(2,128)} copy(f32[128,2,128]{2,0,1:T(8,128)S(1)} %get-tuple-element.27) | data formatting | bytes 262144
  (14 shorter events, 0.3 us)
Async XLA Ops:
  0.6 10.1 %copy-start = (bf16[128,8,128]{2,1,0:T(8,128)(2,1)S(1)}, bf16[128,8,128]{2,1,0:T(8,128)(2,1)}, u32[]{:S(2)}) copy-start(bf16[128,8,128]{2,1,0:T(8,128)(2,1)} %param.6) | copy-start | bytes 786436
  2.4 17.2 %collective-permute-start = (bf16[528,128]{1,0:T(8,128)(2,1)S(1)}, bf16[528,128]{1,0:T(8,128)(2,1)S(1)}, u32[]{:S(2)}, u32[]{:S(2)}) collective-permute-start(bf16[528,128]{1,0:T(8,128)(2,1)S(1)} %concatenate.7), channel_id=1, source_target_pairs={{0,2},{2,0},{4,6},{6,4},{8,10},{10,8},{12,14},{14,12},{1,3},{3,1},... | collective-permute-start | bytes 405512 | tf_op jit(solution)/shard_map/ppermute | solution.py:155
  5.4 13.8 %collective-permute-start.1 = (bf16[528,128]{1,0:T(8,128)(2,1)S(1)}, bf16[528,128]{1,0:T(8,128)(2,1)S(1)}, u32[]{:S(2)}, u32[]{:S(2)}) collective-permute-start(bf16[528,128]{1,0:T(8,128)(2,1)S(1)} %concatenate.7), channel_id=1, source_target_pairs={{0,4},{2,6},{4,0},{6,2},{8,12},{10,14},{12,8},{14,10},{1,5},{3,7},... | collective-permute-start | bytes 405512 | tf_op jit(solution)/shard_map/ppermute | solution.py:156
  7.0 8.7 %collective-permute-start.3 = (bf16[528,128]{1,0:T(8,128)(2,1)S(1)}, bf16[528,128]{1,0:T(8,128)(2,1)S(1)}, u32[]{:S(2)}, u32[]{:S(2)}) collective-permute-start(bf16[528,128]{1,0:T(8,128)(2,1)S(1)} %concatenate.7), channel_id=1, source_target_pairs={{0,8},{2,10},{4,12},{6,14},{8,0},{10,2},{12,4},{14,6},{1,9},{3,11}... | collective-permute-start | bytes 405512 | tf_op jit(solution)/shard_map/ppermute | solution.py:153
  15.7 9.4 %collective-permute-start.4 = (bf16[528,128]{1,0:T(8,128)(2,1)S(1)}, bf16[528,128]{1,0:T(8,128)(2,1)S(1)}, u32[]{:S(2)}, u32[]{:S(2)}) collective-permute-start(bf16[528,128]{1,0:T(8,128)(2,1)S(1)} %collective-permute-done.3), channel_id=1, source_target_pairs={{0,2},{2,0},{4,6},{6,4},{8,10},{10,8},{12,14},{14,12},{1,3},{3,1},... | collective-permute-start | bytes 405512 | tf_op jit(solution)/shard_map/ppermute | solution.py:158
  16.1 9.1 %collective-permute-start.5 = (bf16[528,128]{1,0:T(8,128)(2,1)S(1)}, bf16[528,128]{1,0:T(8,128)(2,1)S(1)}, u32[]{:S(2)}, u32[]{:S(2)}) collective-permute-start(bf16[528,128]{1,0:T(8,128)(2,1)S(1)} %collective-permute-done.3), channel_id=1, source_target_pairs={{0,4},{2,6},{4,0},{6,2},{8,12},{10,14},{12,8},{14,10},{1,5},{3,7},... | collective-permute-start | bytes 405512 | tf_op jit(solution)/shard_map/ppermute | solution.py:159
  16.5 8.8 %collective-permute-start.6 = (bf16[528,128]{1,0:T(8,128)(2,1)S(1)}, bf16[528,128]{1,0:T(8,128)(2,1)S(1)}, u32[]{:S(2)}, u32[]{:S(2)}) collective-permute-start(bf16[528,128]{1,0:T(8,128)(2,1)S(1)} %collective-permute-done.3), channel_id=1, source_target_pairs={{0,6},{2,4},{4,2},{6,0},{8,14},{10,12},{12,10},{14,8},{1,7},{3,5},... | collective-permute-start | bytes 405512 | tf_op jit(solution)/shard_map/ppermute | solution.py:160
  19.2 5.9 %collective-permute-start.2 = (bf16[528,128]{1,0:T(8,128)(2,1)S(1)}, bf16[528,128]{1,0:T(8,128)(2,1)S(1)}, u32[]{:S(2)}, u32[]{:S(2)}) collective-permute-start(bf16[528,128]{1,0:T(8,128)(2,1)S(1)} %collective-permute-done.1), channel_id=1, source_target_pairs={{0,2},{2,0},{4,6},{6,4},{8,10},{10,8},{12,14},{14,12},{1,3},{3,1},... | collective-permute-start | bytes 405512 | tf_op jit(solution)/shard_map/ppermute | solution.py:157
  29.6 6.4 %collective-permute-start.7 = (bf16[4,128,128]{2,1,0:T(8,128)(2,1)S(1)}, bf16[4,128,128]{2,1,0:T(8,128)(2,1)S(1)}, u32[]{:S(2)}, u32[]{:S(2)}) collective-permute-start(bf16[4,128,128]{2,1,0:T(8,128)(2,1)S(1)} %get-tuple-element.24), channel_id=1, source_target_pairs={{0,2},{2,0},{4,6},{6,4},{8,10},{10,8},{12,14},{14,12},{1,3},{3,1},... | collective-permute-start | bytes 393224 | tf_op jit(solution)/shard_map/ppermute | solution.py:182
  30.2 6.1 %collective-permute-start.8 = (bf16[4,128,128]{2,1,0:T(8,128)(2,1)S(1)}, bf16[4,128,128]{2,1,0:T(8,128)(2,1)S(1)}, u32[]{:S(2)}, u32[]{:S(2)}) collective-permute-start(bf16[4,128,128]{2,1,0:T(8,128)(2,1)S(1)} %get-tuple-element.26), channel_id=1, source_target_pairs={{0,4},{2,6},{4,0},{6,2},{8,12},{10,14},{12,8},{14,10},{1,5},{3,7},... | collective-permute-start | bytes 393224 | tf_op jit(solution)/shard_map/ppermute | solution.py:182
  31.9 5.9 %collective-permute-start.9 = (bf16[4,128,128]{2,1,0:T(8,128)(2,1)S(1)}, bf16[4,128,128]{2,1,0:T(8,128)(2,1)S(1)}, u32[]{:S(2)}, u32[]{:S(2)}) collective-permute-start(bf16[4,128,128]{2,1,0:T(8,128)(2,1)S(1)} %get-tuple-element.25), channel_id=1, source_target_pairs={{0,6},{2,4},{4,2},{6,0},{8,14},{10,12},{12,10},{14,8},{1,7},{3,5},... | collective-permute-start | bytes 393224 | tf_op jit(solution)/shard_map/ppermute | solution.py:182
  37.8 7.2 %collective-permute-start.10 = (bf16[4,128,128]{2,1,0:T(8,128)(2,1)S(1)}, bf16[4,128,128]{2,1,0:T(8,128)(2,1)S(1)}, u32[]{:S(2)}, u32[]{:S(2)}) collective-permute-start(bf16[4,128,128]{2,1,0:T(8,128)(2,1)S(1)} %add_convert_fusion), channel_id=1, source_target_pairs={{0,8},{2,10},{4,12},{6,14},{8,0},{10,2},{12,4},{14,6},{1,9},{3,11}... | collective-permute-start | bytes 393224 | tf_op jit(solution)/shard_map/ppermute | solution.py:184
  45.0 5.3 %collective-permute-start.11 = (bf16[4,128,128]{2,1,0:T(8,128)(2,1)S(1)}, bf16[4,128,128]{2,1,0:T(8,128)(2,1)S(1)}, u32[]{:S(2)}, u32[]{:S(2)}) collective-permute-start(bf16[4,128,128]{2,1,0:T(8,128)(2,1)S(1)} %get-tuple-element.21), channel_id=1, source_target_pairs={{0,2},{2,0},{4,6},{6,4},{8,10},{10,8},{12,14},{14,12},{1,3},{3,1},... | collective-permute-start | bytes 393224 | tf_op jit(solution)/shard_map/ppermute | solution.py:188
  46.9 5.0 %collective-permute-start.12 = (bf16[4,128,128]{2,1,0:T(8,128)(2,1)S(1)}, bf16[4,128,128]{2,1,0:T(8,128)(2,1)S(1)}, u32[]{:S(2)}, u32[]{:S(2)}) collective-permute-start(bf16[4,128,128]{2,1,0:T(8,128)(2,1)S(1)} %get-tuple-element.23), channel_id=1, source_target_pairs={{0,4},{2,6},{4,0},{6,2},{8,12},{10,14},{12,8},{14,10},{1,5},{3,7},... | collective-permute-start | bytes 393224 | tf_op jit(solution)/shard_map/ppermute | solution.py:188
  46.9 6.1 %collective-permute-start.13 = (bf16[4,128,128]{2,1,0:T(8,128)(2,1)S(1)}, bf16[4,128,128]{2,1,0:T(8,128)(2,1)S(1)}, u32[]{:S(2)}, u32[]{:S(2)}) collective-permute-start(bf16[4,128,128]{2,1,0:T(8,128)(2,1)S(1)} %get-tuple-element.22), channel_id=1, source_target_pairs={{0,6},{2,4},{4,2},{6,0},{8,14},{10,12},{12,10},{14,8},{1,7},{3,5},... | collective-permute-start | bytes 393224 | tf_op jit(solution)/shard_map/ppermute | solution.py:188
